TPU v7x, 32 devices: a whole 2x2x4 slice. The times are simulated.
32 devices in a mesh: gx: 4 (over y, x), gy: 4 (over z), gz: 2 (over core).
Axes of the slice: x: 2, y: 2, z: 4, core: 2. Of those that a mesh axis runs over, the one named last changes fastest.
Arguments:
- concentration: bfloat16 [256, 128, 256], P(('gx', 'gy'), None, 'gz'), may hold values from 0.00016 to 10.5
- turbulence: bfloat16 [256, 128, 256], P(('gx', 'gy'), None, 'gz'), may hold values from 0.049804688 to 2
- src_list: int32 [256, 4], P(('gx', 'gy')), may hold values from 0 to 255, as said below
- interp_weights: bfloat16 [256, 4, 128, 128], P(('gx', 'gy')), may hold values from 0 to 0.5
- settle_class: int32 [256, 8], P(('gx', 'gy'), 'gz'), may hold values from 0 to 7
- kappa_table: float32 [2, 8], replicated, may hold values from 3 to 30000
- fall_table: float32 [8], replicated, may hold values from 1 to 4
Outputs:
- concentration_out: bfloat16 [256, 128, 256], P(('gx', 'gy'), None, 'gz')
- turbulence_out: bfloat16 [256, 128, 256], P(('gx', 'gy'), None, 'gz')
- mass_ratio: float32 [2], replicated
Inputs may be any that keep to these rules, and one draw needn't show every extreme that they name: `src_list`: every entry names a tile held by a device with the same gx index as the entry's own tile. Of the 64 entries of one device, exactly 8 name tiles of other devices; at most 4 of them name tiles of any one device, and on every device exactly 4 name tiles of some one device.
All inputs are finite; a program needn't handle non-finite values.
Results may differ from a plain program's by a relative error of at most 0.0026.
Values may be sent and summed in bfloat16 or wider, within the bound.
No kernel may reach another device: no remote copies, remote signals or barrier semaphores. Data moves between devices by JAX's collectives and lax.ppermute only.
A program may use at most 64 MiB of HBM per device.

v0:
```python
import jax
import jax.numpy as jnp
from jax import lax
from jax.sharding import PartitionSpec as P
from jax.experimental import pallas as pl
from jax.experimental.pallas import tpu as pltpu

STEPS = 2


HIGHEST = lax.Precision.HIGHEST


def passed_along(array, axis, by):
    devices = lax.axis_size(axis)
    pairs = [(i, i + by) for i in range(devices) if 0 <= i + by < devices]
    return lax.ppermute(array, axis, pairs)


def from_partner(array, axis, apart):
    return lax.ppermute(array, axis, [(i, i ^ 1 << apart) for i in range(lax.axis_size(axis))])


def bucket_ranks(owners, wanted, buckets):
    onehot = (
        (owners[..., None] == jnp.arange(buckets, dtype=jnp.int32)) & wanted[..., None]
    ).astype(jnp.int32)
    running = jnp.cumsum(onehot, axis=-2) - 1
    return jnp.sum(onehot * running, axis=-1)


def table_lookup(level_class, lookup_table):
    classes = lookup_table.shape[-1]
    onehot = (level_class[..., None] == jnp.arange(classes, dtype=jnp.int32)).astype(jnp.float32)
    return jnp.einsum("tzq,fq->tfz", onehot, lookup_table, precision=HIGHEST)


def thomas_inverse_kernel(lower_ref, diagonal_ref, upper_ref, inverse_ref, ratio_ref):
    levels = inverse_ref.shape[0]
    lane = lax.broadcasted_iota(jnp.int32, inverse_ref.shape[1:], 1)
    pivot = 1.0 / diagonal_ref[0]
    ratio = upper_ref[0] * pivot
    row = jnp.where(lane == 0, 1.0, 0.0) * pivot
    ratio_ref[0] = ratio
    inverse_ref[0] = row

    def forward(z, carry):
        ratio, row = carry
        below = lower_ref[z]
        pivot = 1.0 / (diagonal_ref[z] - below * ratio)
        ratio = upper_ref[z] * pivot
        row = (jnp.where(lane == z, 1.0, 0.0) - below * row) * pivot
        ratio_ref[z] = ratio
        inverse_ref[z] = row
        return ratio, row

    _, row = lax.fori_loop(1, levels, forward, (ratio, row))

    def backward(step, row):
        z = levels - 2 - step
        row = inverse_ref[z] - ratio_ref[z] * row
        inverse_ref[z] = row
        return row

    lax.fori_loop(0, levels - 1, backward, row)


def block_inverse(lower, diagonal, upper):
    lead = diagonal.shape[:-1]
    levels = diagonal.shape[-1]
    systems = diagonal.size // levels

    def level_major(band):
        return jnp.transpose(band.reshape(systems, levels))[:, :, None]

    inverse = pl.pallas_call(
        thomas_inverse_kernel,
        out_shape=jax.ShapeDtypeStruct((levels, systems, levels), jnp.float32),
        scratch_shapes=[pltpu.VMEM((levels, systems, 1), jnp.float32)],
    )(level_major(lower), level_major(diagonal), level_major(upper))
    return jnp.transpose(inverse, (1, 0, 2)).reshape(lead + (levels, levels))


def interface_values(low_value, low_spike, high_value, high_spike):
    lower_end = (low_value - low_spike[..., None] * high_value) / (1.0 - low_spike * high_spike)[
        ..., None
    ]
    upper_end = high_value - high_spike[..., None] * lower_end
    return (lower_end, upper_end)


def per_device(
    concentration, turbulence, src_list, interp_weights, settle_class, kappa_table, fall_table
):
    tiles_here, columns, levels = concentration.shape
    sources_per = src_list.shape[1]
    lane_count = lax.axis_size("gy")
    my_lane = lax.axis_index("gy")
    layers = lax.axis_size("gz")
    my_layer = lax.axis_index("gz")
    remote_count = tiles_here // 2
    capacity = max(2, 3 * remote_count // (2 * (lane_count - 1)))
    entries = src_list.reshape(-1)
    owner_lane = entries // tiles_here % lane_count
    local_tile = entries % tiles_here
    remote = owner_lane != my_lane
    slot_index = bucket_ranks(owner_lane, remote, lane_count)
    requests = (
        jnp.zeros((lane_count, capacity), jnp.int32)
        .at[jnp.where(remote, owner_lane, lane_count), slot_index]
        .set(local_tile, mode="drop")
    )
    pool_index = jnp.where(
        remote, tiles_here + owner_lane * capacity + slot_index, local_tile
    ).reshape(tiles_here, sources_per)
    level_class = jnp.repeat(settle_class, levels // settle_class.shape[1], axis=1)
    both_fall = jnp.stack([fall_table, jnp.zeros_like(fall_table)])
    diffusion = table_lookup(level_class, kappa_table)
    falling = table_lookup(level_class, both_fall)
    global_level = my_layer * levels + jnp.arange(levels, dtype=jnp.int32)
    diffusion = jnp.where(global_level >= 1, diffusion, 0.0)
    above_class = passed_along(settle_class[:, :1], "gz", -1)
    at_top = my_layer == layers - 1
    diffusion_above = jnp.where(at_top, 0.0, table_lookup(above_class, kappa_table))
    fall_above = jnp.where(at_top, 0.0, table_lookup(above_class, both_fall))
    diffusion_up = jnp.concatenate([diffusion[..., 1:], diffusion_above], axis=-1)
    fall_up = jnp.concatenate([falling[..., 1:], fall_above], axis=-1)
    diagonal = 1.0 + diffusion + diffusion_up + falling
    lower_band = -diffusion
    upper_band = -(diffusion_up + fall_up)
    level_index = jnp.arange(levels, dtype=jnp.int32)
    block_lower = jnp.where(level_index == 0, 0.0, lower_band)
    block_upper = jnp.where(level_index == levels - 1, 0.0, upper_band)
    inverse = block_inverse(block_lower, diagonal, block_upper)
    spike_column = jnp.where(
        my_layer == 0,
        upper_band[..., -1:] * inverse[..., :, levels - 1],
        lower_band[..., :1] * inverse[..., :, 0],
    )
    edge_spike = jnp.where(my_layer == 0, spike_column[..., -1], spike_column[..., 0])
    fields = jnp.stack([concentration, turbulence], axis=1)
    field_ids = jnp.arange(2, dtype=jnp.int32)[None, :, None]
    ratios = []
    for step_index in range(STEPS):
        arrived = lax.all_to_all(
            fields[lax.all_to_all(requests, "gy", split_axis=0, concat_axis=0, tiled=True)],
            "gy",
            split_axis=0,
            concat_axis=0,
            tiled=True,
        )
        tile_pool = jnp.concatenate([fields, arrived.reshape((-1,) + fields.shape[1:])], axis=0)
        advected = jnp.zeros(fields.shape, jnp.float32)
        for entry_k in range(sources_per):
            advected = advected + jnp.einsum(
                "tcd,tfdz->tfcz",
                interp_weights[:, entry_k],
                tile_pool[pool_index[:, entry_k]],
                preferred_element_type=jnp.float32,
            )
        totals = lax.psum(
            (jnp.sum(fields[:, 0], dtype=jnp.float32), jnp.sum(advected[:, 0])), ("gx", "gy", "gz")
        )
        mass_fixer = totals[0] / totals[1]
        ratios.append(mass_fixer)
        advected = advected * jnp.where(field_ids == 0, mass_fixer, 1.0)[..., None]
        solved = jnp.einsum(
            "tfzy,tfcy->tfcz",
            inverse,
            advected,
            precision=HIGHEST,
            preferred_element_type=jnp.float32,
        )
        edge_value = jnp.where(my_layer == 0, solved[..., -1], solved[..., 0])
        partner_field = 1 - my_layer
        send_value = lax.dynamic_index_in_dim(edge_value, partner_field, 1, keepdims=False)
        send_spike = lax.dynamic_index_in_dim(edge_spike, partner_field, 1, keepdims=False)
        other_value, other_spike = from_partner((send_value, send_spike), "gz", 0)
        own_value = lax.dynamic_index_in_dim(edge_value, my_layer, 1, keepdims=False)
        own_spike = lax.dynamic_index_in_dim(edge_spike, my_layer, 1, keepdims=False)
        low_value = jnp.where(my_layer == 0, own_value, other_value)
        low_spike = jnp.where(my_layer == 0, own_spike, other_spike)
        high_value = jnp.where(my_layer == 0, other_value, own_value)
        high_spike = jnp.where(my_layer == 0, other_spike, own_spike)
        lower_end, upper_end = interface_values(low_value, low_spike, high_value, high_spike)
        keeping = jnp.where(my_layer == 0, upper_end, lower_end)
        giving = jnp.where(my_layer == 0, lower_end, upper_end)
        received = from_partner(giving, "gz", 0)
        needed = jnp.where(field_ids == my_layer, keeping[:, None, :], received[:, None, :])
        fields = (solved - spike_column[:, :, None, :] * needed[..., None]).astype(jnp.bfloat16)
    return (fields[:, 0], fields[:, 1], jnp.stack(ratios))


def solution(mesh):
    return jax.shard_map(
        per_device,
        mesh=mesh,
        in_specs=(
            P(("gx", "gy"), None, "gz"),
            P(("gx", "gy"), None, "gz"),
            P(("gx", "gy"), None),
            P(("gx", "gy"), None, None, None),
            P(("gx", "gy"), "gz"),
            P(),
            P(),
        ),
        out_specs=(P(("gx", "gy"), None, "gz"), P(("gx", "gy"), None, "gz"), P()),
        check_vma=False,
    )
```

profile of v0, /device:TPU:0, one launch (start us, length us, event | category | flops | bytes accessed | tf_op | source)
XLA Modules:
  0.0 251.1 jit_solution(699449341864094952)
XLA Ops:
  0.7 0.8 slice.96
  1.4 1.3 collective-permute-start
  2.7 0.8 copy.111
  4.1 0.6 broadcast.402
  4.7 9.8 %scatter_fusion = s32[4,4]{1,0:T(4,128)} fusion(s32[4,4]{1,0:T(4,128)} %broadcast.402, s32[64]{0:T(128)S(1)} %fusion.63, s32[64]{0:T(128)S(1)} %and_select_fusion), kind=kCustom, calls=%fused_computation.10 | custom fusion | bytes 1280 | tf_op jit(solution)/shard_map/scatter | solution.py:111
  14.5 5.8 %all-to-all-start = ((s32[4,1,4]{2,1,0:T(1,128)}), s32[4,1,4]{2,1,0:T(1,128)S(1)}, u32[]{:S(2)}, u32[]{:S(2)}) async-start(s32[4,1,4]{2,1,0:T(1,128)} %bitcast.5), calls=%async_computation | async-start | bytes 4096 | tf_op jit(solution)/shard_map/all_to_all | solution.py:146
  20.2 0.8 copy.128
  21.1 1.9 convert_reduce_fusion.1
  23.7 0.6 pad_clamp_fusion.2
  24.6 1.0 all-to-all-done
  25.7 0.7 gather_fusion
  26.5 1.0 copy.114
  27.5 4.4 %all-to-all-start.1 = ((bf16[4,4,2,128,128]{4,3,1,2,0:T(8,128)(2,1)}), bf16[4,4,2,128,128]{4,3,1,2,0:T(8,128)(2,1)}, u32[]{:S(2)}, u32[]{:S(2)}) async-start(bf16[4,4,2,128,128]{4,3,1,2,0:T(8,128)(2,1)} %copy.114), calls=%async_computation.1 | async-start | bytes 2097152 | tf_op jit(solution)/shard_map/all_to_all | solution.py:145
  32.5 0.7 copy.140
  33.4 0.6 copy.138
  34.1 2.9 %copy.135.upper_ref = f32[128,32,1]{2,1,0:T(8,128)} copy(f32[128,32,1]{0,1,2:T(8,128)S(1)} %fusion.42) | data formatting | bytes 32768 | tf_op jit(solution)/shard_map/broadcast_in_dim | solution.py:74
  37.0 2.8 %copy.133.lower_ref = f32[128,32,1]{2,1,0:T(8,128)} copy(f32[128,32,1]{0,1,2:T(8,128)S(1)} %bitcast.168) | data formatting | bytes 32768 | tf_op jit(solution)/shard_map/broadcast_in_dim | solution.py:74
  39.8 2.9 %copy.134.diagonal_ref = f32[128,32,1]{2,1,0:T(8,128)} copy(f32[128,32,1]{0,1,2:T(8,128)S(1)} %bitcast.167) | data formatting | bytes 32768 | tf_op jit(solution)/shard_map/broadcast_in_dim | solution.py:74
  42.7 24.1 %shard_map.94 = f32[128,32,128]{2,1,0:T(8,128)} custom-call(f32[128,32,1]{2,1,0:T(8,128)} %copy.133.lower_ref, f32[128,32,1]{2,1,0:T(8,128)} %copy.134.diagonal_ref, f32[128,32,1]{2,1,0:T(8,128)} %copy.135.upper_ref), custom_call_target="tpu_custom_call" | custom-call | tf_op jit(solution)/shard_map/pallas_call | solution.py:76
  66.7 5.8 %fusion.66 = (f32[16,2,128,1]{3,1,0,2:T(2,128)}, f32[16,2,128,1]{3,1,0,2:T(2,128)S(1)}) fusion(f32[16,2,128,128]{3,1,0,2:T(2,128)} %bitcast.148), kind=kLoop, calls=%fused_computation.174 | loop fusion | bytes 65536 | tf_op jit(solution)/shard_map/slice | solution.py:137
  72.6 3.4 %copy.161 = f32[16,2,128,1]{0,2,1,3:T(8,128)S(1)} copy(f32[16,2,128,1]{3,1,0,2:T(2,128)} %get-tuple-element.28) | data formatting | bytes 32768
  76.0 1.9 copy.162
  78.0 0.7 fusion.33
  78.7 1.3 copy.115
  80.3 0.7 gather_fusion.4
  81.0 1.7 gather_fusion.3
  82.7 1.8 gather_fusion.2
  84.5 1.8 gather_fusion.1
  86.3 2.0 fusion.15
  88.6 0.5 fusion.23
  89.1 0.7 copy-done.9
  89.8 0.5 fusion.19
  90.3 0.6 add_bitcast_fusion.1
  90.9 1.3 copy-done.2
  92.2 0.9 slice_reduce_fusion.1
  93.1 41.6 %all-reduce.2 = (f32[]{:T(128)}, f32[]{:T(128)}) all-reduce(f32[]{:T(128)} %convert_reduce_fusion.1, f32[]{:T(128)} %slice_reduce_fusion.1), channel_id=1, replica_groups=mesh['gx'=4,'gy'=4,'gz'=2] {'gx','gy','gz'}, use_global_device_ids=true, to_apply=%region_4.5 | all-reduce | flops 2 | bytes 16 | tf_op jit(solution)/shard_map/psum | solution.py:161
  136.0 4.9 %fusion.2 = f32[16,2,128,128]{2,3,1,0:T(8,128)S(1)} fusion(f32[16,2,128,128]{2,3,1,0:T(8,128)} %copy-done.2, f32[16,2,128,128]{3,1,0,2:T(2,128)S(1)} %bitcast.149, f32[2]{0:T(128)S(1)} %compare_select_fusion.19), kind=kOutput, calls=%fused_computation.18 | convolution fusion | flops 805830656 | bytes 6291464 | tf_op jit(solution)/shard_map/tfzy,tfcy->tfcz/dot_general | solution.py:167
  140.9 1.3 copy-done.4
  142.4 1.1 collective-permute-done.1
  143.9 0.9 collective-permute-done.3
  144.9 1.9 subtract_convert_fusion.1
  146.8 1.7 gather_fusion.5
  148.5 4.3 %all-to-all-start.2 = ((bf16[4,4,2,128,128]{3,4,2,1,0:T(8,128)(2,1)}), bf16[4,4,2,128,128]{3,4,2,1,0:T(8,128)(2,1)}, u32[]{:S(2)}, u32[]{:S(2)}) async-start(bf16[4,4,2,128,128]{3,4,2,1,0:T(8,128)(2,1)} %bitcast.153), calls=%async_computation.2 | async-start | bytes 2097152 | tf_op jit(solution)/shard_map/all_to_all | solution.py:145
  152.8 0.9 convert_reduce_fusion
  153.6 25.5 %all-to-all-done.2 = bf16[4,4,2,128,128]{3,4,2,1,0:T(8,128)(2,1)} async-done(((bf16[4,4,2,128,128]{3,4,2,1,0:T(8,128)(2,1)}), bf16[4,4,2,128,128]{3,4,2,1,0:T(8,128)(2,1)}, u32[]{:S(2)}, u32[]{:S(2)}) %all-to-all-start.2) | async-done | bytes 1048608 | tf_op jit(solution)/shard_map/all_to_all | solution.py:145
  179.2 2.7 %pad_maximum_fusion.1 = bf16[32,2,128,128]{2,3,1,0:T(8,128)(2,1)} fusion(bf16[16,2,128,128]{2,3,1,0:T(8,128)(2,1)} %bitcast.57, bf16[16,2,128,128]{2,3,1,0:T(8,128)(2,1)S(1)} %subtract_convert_fusion.1), kind=kLoop, calls=%fused_computation.12 | loop fusion | flops 1048576 | bytes 4194304 | tf_op jit(solution)/shard_map/concatenate | solution.py:152
  181.9 2.3 gather_fusion.9
  184.3 3.3 %gather_fusion.8 = bf16[16,2,128,128]{2,3,1,0:T(8,128)(2,1)} fusion(bf16[32,2,128,128]{2,3,1,0:T(8,128)(2,1)} %pad_maximum_fusion.1, s32[1024]{0:T(1024)S(1)} %get-tuple-element.45), kind=kCustom, calls=%fused_computation.8 | custom fusion | bytes 2097216 | tf_op jit(solution)/shard_map/gather | solution.py:158
  187.5 3.4 %gather_fusion.7 = bf16[16,2,128,128]{2,3,1,0:T(8,128)(2,1)} fusion(bf16[32,2,128,128]{2,3,1,0:T(8,128)(2,1)} %pad_maximum_fusion.1, s32[1024]{0:T(1024)} %get-tuple-element.46), kind=kCustom, calls=%fused_computation.7 | custom fusion | bytes 2097216 | tf_op jit(solution)/shard_map/gather | solution.py:158
  190.9 3.4 %gather_fusion.6 = bf16[16,2,128,128]{2,3,1,0:T(8,128)(2,1)} fusion(bf16[32,2,128,128]{2,3,1,0:T(8,128)(2,1)} %pad_maximum_fusion.1, s32[1024]{0:T(1024)} %get-tuple-element.47), kind=kCustom, calls=%fused_computation.6 | custom fusion | bytes 2097216 | tf_op jit(solution)/shard_map/gather | solution.py:158
  194.3 1.9 fusion.21
  196.6 0.4 fusion.17
  197.0 0.8 copy-done.8
  197.8 0.4 fusion.13
  198.3 0.6 add_bitcast_fusion
  198.9 1.3 copy-done.3
  200.2 0.9 slice_reduce_fusion
  201.1 38.3 %all-reduce.1 = (f32[]{:T(128)}, f32[]{:T(128)}) all-reduce(f32[]{:T(128)} %convert_reduce_fusion, f32[]{:T(128)} %slice_reduce_fusion), channel_id=1, replica_groups=mesh['gx'=4,'gy'=4,'gz'=2] {'gx','gy','gz'}, use_global_device_ids=true, to_apply=%region_8.9 | all-reduce | flops 2 | bytes 16 | tf_op jit(solution)/shard_map/psum | solution.py:161
  240.7 4.8 %fusion = f32[16,2,128,128]{2,3,1,0:T(8,128)S(1)} fusion(f32[16,2,128,128]{2,3,1,0:T(8,128)} %copy-done.3, f32[16,2,128,128]{3,1,0,2:T(2,128)S(1)} %bitcast.150, f32[2]{0:T(128)S(1)} %compare_select_fusion.18), kind=kOutput, calls=%fused_computation.14 | convolution fusion | flops 805830656 | bytes 6291464 | tf_op jit(solution)/shard_map/tfzy,tfcy->tfcz/dot_general | solution.py:167
  245.7 1.2 collective-permute-done.4
  247.2 0.6 pad_maximum_fusion.4
  248.2 0.7 subtract_convert_fusion
  249.1 1.0 copy.146
  250.1 1.0 copy.145
  (80 shorter events, 5.1 us)
Async XLA Ops:
  0.6 22.6 %copy-start = (f32[2,8]{1,0:T(2,128)S(1)}, f32[2,8]{1,0:T(2,128)}, u32[]{:S(2)}) copy-start(f32[2,8]{1,0:T(2,128)} %param.12) | copy-start | bytes 196
  0.6 23.7 %copy-start.7 = (bf16[16,128,128]{2,1,0:T(8,128)(2,1)S(1)}, bf16[16,128,128]{2,1,0:T(8,128)(2,1)}, u32[]{:S(2)}) copy-start(bf16[16,128,128]{2,1,0:T(8,128)(2,1)} %param.7) | copy-start | bytes 1572868
  0.7 23.7 %copy-start.12 = (bf16[16,128,128]{2,1,0:T(8,128)(2,1)S(1)}, bf16[16,128,128]{2,1,0:T(8,128)(2,1)}, u32[]{:S(2)}) copy-start(bf16[16,128,128]{2,1,0:T(8,128)(2,1)} %param.8) | copy-start | bytes 1572868
  1.4 23.0 %collective-permute-start = (s32[16,1]{0,1:T(1,128)S(1)}, s32[16,1]{0,1:T(1,128)S(1)}, u32[]{:S(2)}, u32[]{:S(2)}) collective-permute-start(s32[16,1]{0,1:T(1,128)S(1)} %slice.96), channel_id=1, source_target_pairs={{1,0},{3,2},{5,4},{7,6},{9,8},{11,10},{13,12},{15,14},{17,16},{19,... | collective-permute-start | bytes 200 | tf_op jit(solution)/shard_map/ppermute | solution.py:17
  14.5 11.2 %all-to-all-start = ((s32[4,1,4]{2,1,0:T(1,128)}), s32[4,1,4]{2,1,0:T(1,128)S(1)}, u32[]{:S(2)}, u32[]{:S(2)}) async-start(s32[4,1,4]{2,1,0:T(1,128)} %bitcast.5), calls=%async_computation | async-start | bytes 4096 | tf_op jit(solution)/shard_map/all_to_all | solution.py:146
  26.5 5.5 %copy-start.13 = (f32[8]{0:T(128)S(1)}, f32[8]{0:T(128)}, u32[]{:S(2)}) copy-start(f32[8]{0:T(128)} %param.13) | copy-start | bytes 100
  27.5 51.2 %all-to-all-start.1 = ((bf16[4,4,2,128,128]{4,3,1,2,0:T(8,128)(2,1)}), bf16[4,4,2,128,128]{4,3,1,2,0:T(8,128)(2,1)}, u32[]{:S(2)}, u32[]{:S(2)}) async-start(bf16[4,4,2,128,128]{4,3,1,2,0:T(8,128)(2,1)} %copy.114), calls=%async_computation.1 | async-start | bytes 2097152 | tf_op jit(solution)/shard_map/all_to_all | solution.py:145
  86.3 2.1 copy-start.5
  86.3 2.3 copy-start.11
  88.6 1.2 copy-start.9
  90.3 45.7 %copy-start.1 = (f32[128,32,128]{2,1,0:T(8,128)S(1)}, f32[128,32,128]{2,1,0:T(8,128)}, u32[]{:S(2)}) copy-start(f32[128,32,128]{2,1,0:T(8,128)} %shard_map.94) | copy-start | bytes 6291460
  90.9 1.3 copy-start.2
  93.1 49.2 %collective-permute-start.2 = (f32[16]{0:T(128)S(1)}, f32[16]{0:T(128)S(1)}, u32[]{:S(2)}, u32[]{:S(2)}) collective-permute-start(f32[16]{0:T(128)S(1)} %fusion.59), channel_id=1, source_target_pairs={{0,1},{1,0},{2,3},{3,2},{4,5},{5,4},{6,7},{7,6},{8,9},{9,8},{10,11... | collective-permute-start | bytes 200 | tf_op jit(solution)/shard_map/ppermute | solution.py:21
  140.9 1.3 copy-start.4
  142.3 1.2 collective-permute-start.1
  143.6 1.2 collective-permute-start.3
  148.5 30.7 %all-to-all-start.2 = ((bf16[4,4,2,128,128]{3,4,2,1,0:T(8,128)(2,1)}), bf16[4,4,2,128,128]{3,4,2,1,0:T(8,128)(2,1)}, u32[]{:S(2)}, u32[]{:S(2)}) async-start(bf16[4,4,2,128,128]{3,4,2,1,0:T(8,128)(2,1)} %bitcast.153), calls=%async_computation.2 | async-start | bytes 2097152 | tf_op jit(solution)/shard_map/all_to_all | solution.py:145
  194.3 2.1 copy-start.6
  194.3 2.3 copy-start.10
  196.6 1.2 copy-start.8
  198.8 1.3 copy-start.3
  245.6 1.2 collective-permute-start.4
  246.9 1.2 collective-permute-start.5
where the time goes:
time: 254 us; the launch traced here: 251 us
  blocking collectives  79.9 us (31%)
  local copies, waits for them, and re-layouts  66.2 us (26%)
  waiting for transfers between devices  30.2 us (12%)
  Pallas kernels  24.1 us (9%)
  matrix products  17.4 us (7%)
  starting transfers between devices  16.3 us (6%)
  other arithmetic  13.4 us (5%)
  between operations  3.69 us (1%)
    psum x2, blocking collectives, per_device(): lax.psum((jnp.sum(fields[:, 0], dtype=jnp.float32), jnp.sum(advected[:, 0...  79.9 us
    all_to_all x2, waiting for transfers between devices, per_device(): lax.all_to_all(fields[lax.all_to_all(requests, 'gy', split_axis=0, concat...  25.5 us
    pallas_call x1, Pallas kernels, block_inverse(): pl.pallas_call(thomas_inverse_kernel, out_shape=jax.ShapeDtypeStruct((lev...  24.1 us
    gather x8, local copies, waits for them, and re-layouts, per_device(): tile_pool[pool_index[:, entry_k]]  18.3 us
    unnamed x34, local copies, waits for them, and re-layouts  15.2 us
    scatter x1, local copies, waits for them, and re-layouts, per_device(): requests = jnp.zeros((lane_count, capacity), jnp.int32).at[jnp.where(remo...  9.78 us
    dot_general x2, matrix products, per_device(): jnp.einsum('tfzy,tfcy->tfcz', inverse, advected, precision=HIGHEST, prefe...  9.7 us
    all_to_all x2, starting transfers between devices, per_device(): lax.all_to_all(fields[lax.all_to_all(requests, 'gy', split_axis=0, concat...  8.71 us
  transfers between devices with their start and end apart: 9, of which 6 were waited for; matrix products, arithmetic and copies ran while one was open for 18% of the time, Pallas kernels for 10%

commit v1 on v0

--- a/solution.py
+++ b/solution.py
@@ -19,6 +19,19 @@
 
 def from_partner(array, axis, apart):
     return lax.ppermute(array, axis, [(i, i ^ 1 << apart) for i in range(lax.axis_size(axis))])
+
+
+def butterfly_sum(value, axes):
+    for axis in axes:
+        devices = lax.axis_size(axis)
+        if devices & (devices - 1):
+            value = lax.psum(value, axis)
+            continue
+        bit = 1
+        while bit < devices:
+            value = value + lax.ppermute(value, axis, [(i, i ^ bit) for i in range(devices)])
+            bit *= 2
+    return value
 
 
 def bucket_ranks(owners, wanted, buckets):
@@ -105,11 +118,12 @@
     local_tile = entries % tiles_here
     remote = owner_lane != my_lane
     slot_index = bucket_ranks(owner_lane, remote, lane_count)
-    requests = (
-        jnp.zeros((lane_count, capacity), jnp.int32)
-        .at[jnp.where(remote, owner_lane, lane_count), slot_index]
-        .set(local_tile, mode="drop")
+    match = (
+        remote[None, None, :]
+        & (owner_lane[None, None, :] == jnp.arange(lane_count, dtype=jnp.int32)[:, None, None])
+        & (slot_index[None, None, :] == jnp.arange(capacity, dtype=jnp.int32)[None, :, None])
     )
+    requests = jnp.sum(jnp.where(match, local_tile[None, None, :], 0), axis=-1, dtype=jnp.int32)
     pool_index = jnp.where(
         remote, tiles_here + owner_lane * capacity + slot_index, local_tile
     ).reshape(tiles_here, sources_per)
@@ -158,8 +172,9 @@
                 tile_pool[pool_index[:, entry_k]],
                 preferred_element_type=jnp.float32,
             )
-        totals = lax.psum(
-            (jnp.sum(fields[:, 0], dtype=jnp.float32), jnp.sum(advected[:, 0])), ("gx", "gy", "gz")
+        totals = butterfly_sum(
+            jnp.stack([jnp.sum(fields[:, 0], dtype=jnp.float32), jnp.sum(advected[:, 0])]),
+            ("gz", "gy", "gx"),
         )
         mass_fixer = totals[0] / totals[1]
         ratios.append(mass_fixer)

time: 254 us -> 201 us (0.79)
  blocking collectives: 79.9 us -> 0 us
  waiting for transfers between devices: 30.2 us -> 50.2 us
  starting transfers between devices: 16.3 us -> 29.7 us
  local copies, waits for them, and re-layouts: 66.2 us -> 54.5 us
  other arithmetic: 13.4 us -> 23.4 us
  matrix products: 17.4 us -> 14.2 us
    psum x2 -> x0, blocking collectives: 79.9 us -> none  [per_device(): lax.psum((jnp.sum(fields[:, 0], dtype=jnp.float32), jnp.sum(advected[:, 0...]
    ppermute x0 -> x10, waiting for transfers between devices: none -> 21.3 us  [butterfly_sum(): lax.ppermute(value, axis, [(i, i ^ bit) for i in range(devices)])]
    ppermute x0 -> x10, starting transfers between devices: none -> 11.1 us  [butterfly_sum(): lax.ppermute(value, axis, [(i, i ^ bit) for i in range(devices)])]
    scatter x1 -> x0, local copies, waits for them, and re-layouts: 9.78 us -> none  [per_device(): requests = jnp.zeros((lane_count, capacity), jnp.int32).at[jnp.where(remo...]
    add x0 -> x10, other arithmetic: none -> 5.38 us  [butterfly_sum(): value + lax.ppermute(value, axis, [(i, i ^ bit) for i in range(devices)])]
    dot_general x2, matrix products: 9.7 us -> 6.54 us  [per_device(): jnp.einsum('tfzy,tfcy->tfcz', inverse, advected, precision=HIGHEST, prefe...]
    another operation x0 -> x2, other arithmetic: none -> 2.68 us  [per_device(): jnp.stack([jnp.sum(fields[:, 0], dtype=jnp.float32), jnp.sum(advected[:,...]
    unnamed x34 -> x30, local copies, waits for them, and re-layouts: 15.2 us -> 12.7 us
  transfers between devices with their start and end apart: 9 -> 19, of which waited for: 6 -> 15; matrix products, arithmetic and copies ran while one was open for 18% -> 26% of each run, Pallas kernels for 10% -> 12%
where the time goes in v1:
time: 201 us; the launch traced here: 200 us
  local copies, waits for them, and re-layouts  54.5 us (27%)
  waiting for transfers between devices  50.2 us (25%)
  starting transfers between devices  29.7 us (15%)
  Pallas kernels  24.1 us (12%)
  other arithmetic  23.4 us (12%)
  matrix products  14.2 us (7%)
  between operations  3.75 us (2%)
    all_to_all x2, waiting for transfers between devices, per_device(): lax.all_to_all(fields[lax.all_to_all(requests, 'gy', split_axis=0, concat...  25.3 us
    pallas_call x1, Pallas kernels, block_inverse(): pl.pallas_call(thomas_inverse_kernel, out_shape=jax.ShapeDtypeStruct((lev...  24.1 us
    ppermute x10, waiting for transfers between devices, butterfly_sum(): lax.ppermute(value, axis, [(i, i ^ bit) for i in range(devices)])  21.3 us
    gather x8, local copies, waits for them, and re-layouts, per_device(): tile_pool[pool_index[:, entry_k]]  18.4 us
    unnamed x30, local copies, waits for them, and re-layouts  12.7 us
    ppermute x10, starting transfers between devices, butterfly_sum(): lax.ppermute(value, axis, [(i, i ^ bit) for i in range(devices)])  11.1 us
    all_to_all x2, starting transfers between devices, per_device(): lax.all_to_all(fields[lax.all_to_all(requests, 'gy', split_axis=0, concat...  10.1 us
    broadcast_in_dim x3, local copies, waits for them, and re-layouts, level_major(): return jnp.transpose(band.reshape(systems, levels))[:, :, None]  8.65 us
  transfers between devices with their start and end apart: 19, of which 15 were waited for; matrix products, arithmetic and copies ran while one was open for 26% of the time, Pallas kernels for 12%

profile of v1, /device:TPU:0, one launch (start us, length us, event | category | flops | bytes accessed | tf_op | source)
XLA Modules:
  0.0 199.9 jit_solution(4413768472292876980)
XLA Ops:
  1.3 1.3 collective-permute-start.5
  2.6 0.8 copy.143
  4.6 6.3 %all-to-all-start = ((s32[4,1,4]{2,1,0:T(1,128)}), s32[4,1,4]{2,1,0:T(1,128)S(1)}, u32[]{:S(2)}, u32[]{:S(2)}) async-start(s32[4,1,4]{2,1,0:T(1,128)} %bitcast.3), calls=%async_computation | async-start | bytes 4096 | tf_op jit(solution)/shard_map/all_to_all | solution.py:160
  11.0 0.8 copy.159
  11.8 2.0 convert_reduce_fusion.1
  15.1 1.3 pad_maximum_fusion.2
  17.5 1.1 copy.145
  18.5 5.1 %all-to-all-start.1 = ((bf16[4,4,2,128,128]{4,3,1,2,0:T(8,128)(2,1)}), bf16[4,4,2,128,128]{4,3,1,2,0:T(8,128)(2,1)}, u32[]{:S(2)}, u32[]{:S(2)}) async-start(bf16[4,4,2,128,128]{4,3,1,2,0:T(8,128)(2,1)} %copy.145), calls=%async_computation.1 | async-start | bytes 2097152 | tf_op jit(solution)/shard_map/all_to_all | solution.py:159
  25.7 2.9 %copy.166.upper_ref = f32[128,32,1]{2,1,0:T(8,128)} copy(f32[128,32,1]{0,1,2:T(8,128)S(1)} %fusion.42) | data formatting | bytes 32768 | tf_op jit(solution)/shard_map/broadcast_in_dim | solution.py:87
  28.6 2.9 %copy.164.lower_ref = f32[128,32,1]{2,1,0:T(8,128)} copy(f32[128,32,1]{0,1,2:T(8,128)S(1)} %bitcast.165) | data formatting | bytes 32768 | tf_op jit(solution)/shard_map/broadcast_in_dim | solution.py:87
  31.5 2.9 %copy.165.diagonal_ref = f32[128,32,1]{2,1,0:T(8,128)} copy(f32[128,32,1]{0,1,2:T(8,128)S(1)} %bitcast.164) | data formatting | bytes 32768 | tf_op jit(solution)/shard_map/broadcast_in_dim | solution.py:87
  34.4 24.1 %shard_map.94 = f32[128,32,128]{2,1,0:T(8,128)} custom-call(f32[128,32,1]{2,1,0:T(8,128)} %copy.164.lower_ref, f32[128,32,1]{2,1,0:T(8,128)} %copy.165.diagonal_ref, f32[128,32,1]{2,1,0:T(8,128)} %copy.166.upper_ref), custom_call_target="tpu_custom_call" | custom-call | tf_op jit(solution)/shard_map/pallas_call | solution.py:89
  58.4 5.9 %fusion.64 = (f32[16,2,128,1]{3,1,0,2:T(2,128)}, f32[16,2,128,1]{3,1,0,2:T(2,128)S(1)}) fusion(f32[16,2,128,128]{3,1,0,2:T(2,128)} %bitcast.145), kind=kLoop, calls=%fused_computation.163 | loop fusion | bytes 65536 | tf_op jit(solution)/shard_map/slice | solution.py:151
  64.3 3.4 %copy.192 = f32[16,2,128,1]{0,2,1,3:T(8,128)S(1)} copy(f32[16,2,128,1]{3,1,0,2:T(2,128)} %get-tuple-element.27) | data formatting | bytes 32768
  67.8 2.1 %copy.193 = f32[16,2,128,1]{0,2,1,3:T(8,128)S(1)} copy(f32[16,2,128,1]{3,1,0,2:T(2,128)S(1)} %get-tuple-element.28) | data formatting | bytes 32768
  71.0 1.3 copy.146
  73.3 1.7 gather_fusion.3
  75.0 1.8 gather_fusion.2
  76.7 1.8 gather_fusion.1
  78.5 2.0 fusion.15
  83.2 0.9 slice_reduce_fusion.1
  84.1 1.3 pad_maximum_fusion.4
  85.6 0.9 collective-permute-done
  86.5 1.3 fusion.78
  87.9 2.0 collective-permute-start.1
  89.8 1.6 collective-permute-done.1
  91.4 1.3 fusion.80
  92.8 2.9 %collective-permute-start.2 = (f32[2]{0:T(128)S(1)}, f32[2]{0:T(128)S(1)}, u32[]{:S(2)}, u32[]{:S(2)}) collective-permute-start(f32[2]{0:T(128)S(1)} %fusion.80), channel_id=1, source_target_pairs={{0,4},{2,6},{4,0},{6,2},{1,5},{3,7},{5,1},{7,3},{8,12},{10,14},{12... | collective-permute-start | bytes 32 | tf_op jit(solution)/shard_map/ppermute | solution.py:32
  95.6 1.6 collective-permute-done.2
  97.2 1.5 collective-permute-start.3
  98.7 2.0 %collective-permute-done.3 = f32[2]{0:T(128)S(1)} collective-permute-done((f32[2]{0:T(128)S(1)}, f32[2]{0:T(128)S(1)}, u32[]{:S(2)}, u32[]{:S(2)}) %collective-permute-start.3) | collective-permute-done | bytes 40 | tf_op jit(solution)/shard_map/ppermute | solution.py:32
  100.8 1.5 collective-permute-start.4
  102.3 2.0 %collective-permute-done.4 = f32[2]{0:T(128)S(1)} collective-permute-done((f32[2]{0:T(128)S(1)}, f32[2]{0:T(128)S(1)}, u32[]{:S(2)}, u32[]{:S(2)}) %collective-permute-start.4) | collective-permute-done | bytes 40 | tf_op jit(solution)/shard_map/ppermute | solution.py:32
  106.2 3.3 %fusion.2 = f32[16,2,128,128]{2,3,1,0:T(8,128)S(1)} fusion(f32[16,2,128,128]{2,3,1,0:T(8,128)S(1)} %add_bitcast_fusion.1, f32[16,2,128,128]{3,1,0,2:T(2,128)S(1)} %bitcast.146, f32[2]{0:T(128)S(1)} %compare_select_fusion.11), kind=kOutput, calls=%fused_computation.17 | convolution fusion | flops 805830656 | bytes 6291464 | tf_op jit(solution)/shard_map/tfzy,tfcy->tfcz/dot_general | solution.py:182
  109.5 1.3 copy-done.2
  111.0 1.1 collective-permute-done.6
  112.5 0.9 collective-permute-done.8
  113.5 1.9 subtract_convert_fusion.1
  115.5 1.7 gather_fusion.5
  117.1 5.0 %all-to-all-start.2 = ((bf16[4,4,2,128,128]{3,4,2,1,0:T(8,128)(2,1)}), bf16[4,4,2,128,128]{3,4,2,1,0:T(8,128)(2,1)}, u32[]{:S(2)}, u32[]{:S(2)}) async-start(bf16[4,4,2,128,128]{3,4,2,1,0:T(8,128)(2,1)} %bitcast.150), calls=%async_computation.2 | async-start | bytes 2097152 | tf_op jit(solution)/shard_map/all_to_all | solution.py:159
  122.1 0.9 convert_reduce_fusion
  123.0 25.3 %all-to-all-done.2 = bf16[4,4,2,128,128]{3,4,2,1,0:T(8,128)(2,1)} async-done(((bf16[4,4,2,128,128]{3,4,2,1,0:T(8,128)(2,1)}), bf16[4,4,2,128,128]{3,4,2,1,0:T(8,128)(2,1)}, u32[]{:S(2)}, u32[]{:S(2)}) %all-to-all-start.2) | async-done | bytes 1048608 | tf_op jit(solution)/shard_map/all_to_all | solution.py:159
  148.3 2.7 %pad_maximum_fusion.1 = bf16[32,2,128,128]{2,3,1,0:T(8,128)(2,1)} fusion(bf16[16,2,128,128]{2,3,1,0:T(8,128)(2,1)} %bitcast.58, bf16[16,2,128,128]{2,3,1,0:T(8,128)(2,1)S(1)} %subtract_convert_fusion.1), kind=kLoop, calls=%fused_computation.11 | loop fusion | flops 1048576 | bytes 4194304 | tf_op jit(solution)/shard_map/concatenate | solution.py:166
  151.0 2.3 %gather_fusion.9 = bf16[16,2,128,128]{2,3,1,0:T(8,128)(2,1)S(1)} fusion(bf16[32,2,128,128]{2,3,1,0:T(8,128)(2,1)} %pad_maximum_fusion.1, s32[1024]{0:T(1024)S(1)} %get-tuple-element.49), kind=kCustom, calls=%fused_computation.9 | custom fusion | bytes 2097216 | tf_op jit(solution)/shard_map/gather | solution.py:172
  153.4 3.2 %gather_fusion.8 = bf16[16,2,128,128]{2,3,1,0:T(8,128)(2,1)} fusion(bf16[32,2,128,128]{2,3,1,0:T(8,128)(2,1)} %pad_maximum_fusion.1, s32[1024]{0:T(1024)S(1)} %get-tuple-element.50), kind=kCustom, calls=%fused_computation.8 | custom fusion | bytes 2097216 | tf_op jit(solution)/shard_map/gather | solution.py:172
  156.6 3.4 %gather_fusion.7 = bf16[16,2,128,128]{2,3,1,0:T(8,128)(2,1)} fusion(bf16[32,2,128,128]{2,3,1,0:T(8,128)(2,1)} %pad_maximum_fusion.1, s32[1024]{0:T(1024)} %get-tuple-element.51), kind=kCustom, calls=%fused_computation.7 | custom fusion | bytes 2097216 | tf_op jit(solution)/shard_map/gather | solution.py:172
  160.0 3.4 %gather_fusion.6 = bf16[16,2,128,128]{2,3,1,0:T(8,128)(2,1)} fusion(bf16[32,2,128,128]{2,3,1,0:T(8,128)(2,1)} %pad_maximum_fusion.1, s32[1024]{0:T(1024)} %get-tuple-element.52), kind=kCustom, calls=%fused_computation.6 | custom fusion | bytes 2097216 | tf_op jit(solution)/shard_map/gather | solution.py:172
  163.4 1.9 fusion.21
  166.2 0.8 copy-done.6
  168.0 0.9 slice_reduce_fusion
  168.9 1.3 pad_maximum_fusion.5
  170.2 1.1 collective-permute-done.9
  171.3 1.3 fusion.77
  172.7 3.5 %collective-permute-done.10 = f32[2]{0:T(128)S(1)} collective-permute-done((f32[2]{0:T(128)S(1)}, f32[2]{0:T(128)S(1)}, u32[]{:S(2)}, u32[]{:S(2)}) %collective-permute-start.10) | collective-permute-done | bytes 40 | tf_op jit(solution)/shard_map/ppermute | solution.py:32
  176.2 1.3 fusion.79
  177.6 4.4 %collective-permute-done.11 = f32[2]{0:T(128)S(1)} collective-permute-done((f32[2]{0:T(128)S(1)}, f32[2]{0:T(128)S(1)}, u32[]{:S(2)}, u32[]{:S(2)}) %collective-permute-start.11) | collective-permute-done | bytes 40 | tf_op jit(solution)/shard_map/ppermute | solution.py:32
  182.0 1.5 collective-permute-start.12
  183.5 2.1 %collective-permute-done.12 = f32[2]{0:T(128)S(1)} collective-permute-done((f32[2]{0:T(128)S(1)}, f32[2]{0:T(128)S(1)}, u32[]{:S(2)}, u32[]{:S(2)}) %collective-permute-start.12) | collective-permute-done | bytes 40 | tf_op jit(solution)/shard_map/ppermute | solution.py:32
  185.6 1.5 collective-permute-start.13
  187.1 2.0 %collective-permute-done.13 = f32[2]{0:T(128)S(1)} collective-permute-done((f32[2]{0:T(128)S(1)}, f32[2]{0:T(128)S(1)}, u32[]{:S(2)}, u32[]{:S(2)}) %collective-permute-start.13) | collective-permute-done | bytes 40 | tf_op jit(solution)/shard_map/ppermute | solution.py:32
  191.0 3.3 %fusion = f32[16,2,128,128]{2,3,1,0:T(8,128)S(1)} fusion(f32[16,2,128,128]{2,3,1,0:T(8,128)S(1)} %add_bitcast_fusion, f32[16,2,128,128]{3,1,0,2:T(2,128)S(1)} %bitcast.147, f32[2]{0:T(128)S(1)} %compare_select_fusion.10), kind=kOutput, calls=%fused_computation.13 | convolution fusion | flops 805830656 | bytes 6291464 | tf_op jit(solution)/shard_map/tfzy,tfcy->tfcz/dot_general | solution.py:182
  194.4 1.2 collective-permute-done.14
  197.8 1.0 copy.177
  198.8 1.0 copy.176
  (106 shorter events, 17.3 us)
Async XLA Ops:
  0.6 13.3 %copy-start = (f32[2,8]{1,0:T(2,128)S(1)}, f32[2,8]{1,0:T(2,128)}, u32[]{:S(2)}) copy-start(f32[2,8]{1,0:T(2,128)} %param.12) | copy-start | bytes 196
  1.3 15.0 %collective-permute-start.5 = (s32[16,1]{0,1:T(1,128)S(1)}, s32[16,1]{0,1:T(1,128)S(1)}, u32[]{:S(2)}, u32[]{:S(2)}) collective-permute-start(s32[16,1]{0,1:T(1,128)S(1)} %slice.110), channel_id=1, source_target_pairs={{1,0},{3,2},{5,4},{7,6},{9,8},{11,10},{13,12},{15,14},{17,16},{19,... | collective-permute-start | bytes 200 | tf_op jit(solution)/shard_map/ppermute | solution.py:17
  4.6 11.9 %all-to-all-start = ((s32[4,1,4]{2,1,0:T(1,128)}), s32[4,1,4]{2,1,0:T(1,128)S(1)}, u32[]{:S(2)}, u32[]{:S(2)}) async-start(s32[4,1,4]{2,1,0:T(1,128)} %bitcast.3), calls=%async_computation | async-start | bytes 4096 | tf_op jit(solution)/shard_map/all_to_all | solution.py:160
  17.4 6.2 %copy-start.11 = (f32[8]{0:T(128)S(1)}, f32[8]{0:T(128)}, u32[]{:S(2)}) copy-start(f32[8]{0:T(128)} %param.13) | copy-start | bytes 100
  18.5 52.4 %all-to-all-start.1 = ((bf16[4,4,2,128,128]{4,3,1,2,0:T(8,128)(2,1)}), bf16[4,4,2,128,128]{4,3,1,2,0:T(8,128)(2,1)}, u32[]{:S(2)}, u32[]{:S(2)}) async-start(bf16[4,4,2,128,128]{4,3,1,2,0:T(8,128)(2,1)} %copy.145), calls=%async_computation.1 | async-start | bytes 2097152 | tf_op jit(solution)/shard_map/all_to_all | solution.py:159
  67.7 4.6 %copy-start.5 = (bf16[16,128,128]{2,1,0:T(8,128)(2,1)S(1)}, bf16[16,128,128]{2,1,0:T(8,128)(2,1)}, u32[]{:S(2)}) copy-start(bf16[16,128,128]{2,1,0:T(8,128)(2,1)} %param.7) | copy-start | bytes 1572868
  67.8 4.5 %copy-start.10 = (bf16[16,128,128]{2,1,0:T(8,128)(2,1)S(1)}, bf16[16,128,128]{2,1,0:T(8,128)(2,1)}, u32[]{:S(2)}) copy-start(bf16[16,128,128]{2,1,0:T(8,128)(2,1)} %param.8) | copy-start | bytes 1572868
  70.6 40.4 %collective-permute-start.7 = (f32[16]{0:T(128)S(1)}, f32[16]{0:T(128)S(1)}, u32[]{:S(2)}, u32[]{:S(2)}) collective-permute-start(f32[16]{0:T(128)S(1)} %fusion.59), channel_id=1, source_target_pairs={{0,1},{1,0},{2,3},{3,2},{4,5},{5,4},{6,7},{7,6},{8,9},{9,8},{10,11... | collective-permute-start | bytes 200 | tf_op jit(solution)/shard_map/ppermute | solution.py:21
  78.5 2.1 %copy-start.3 = (bf16[16,4,128,128]{3,2,1,0:T(8,128)(2,1)S(1)}, bf16[16,4,128,128]{3,2,1,0:T(8,128)(2,1)}, u32[]{:S(2)}) copy-start(bf16[16,4,128,128]{3,2,1,0:T(8,128)(2,1)} %param.10) | copy-start | bytes 6291460
  78.5 2.3 %copy-start.9 = (bf16[16,2,128,128]{3,2,1,0:T(8,128)(2,1)S(1)}, bf16[16,2,128,128]{3,2,1,0:T(8,128)(2,1)}, u32[]{:S(2)}) copy-start(bf16[16,2,128,128]{3,2,1,0:T(8,128)(2,1)} %gather_fusion.1) | copy-start | bytes 3145732
  80.9 1.2 copy-start.7
  82.6 23.6 %copy-start.1 = (f32[128,32,128]{2,1,0:T(8,128)S(1)}, f32[128,32,128]{2,1,0:T(8,128)}, u32[]{:S(2)}) copy-start(f32[128,32,128]{2,1,0:T(8,128)} %shard_map.94) | copy-start | bytes 6291460
  85.4 1.1 collective-permute-start
  87.9 3.5 %collective-permute-start.1 = (f32[2]{0:T(128)S(1)}, f32[2]{0:T(128)S(1)}, u32[]{:S(2)}, u32[]{:S(2)}) collective-permute-start(f32[2]{0:T(128)S(1)} %fusion.78), channel_id=1, source_target_pairs={{0,2},{2,0},{4,6},{6,4},{1,3},{3,1},{5,7},{7,5},{8,10},{10,8},{12,... | collective-permute-start | bytes 32 | tf_op jit(solution)/shard_map/ppermute | solution.py:32
  92.8 4.4 %collective-permute-start.2 = (f32[2]{0:T(128)S(1)}, f32[2]{0:T(128)S(1)}, u32[]{:S(2)}, u32[]{:S(2)}) collective-permute-start(f32[2]{0:T(128)S(1)} %fusion.80), channel_id=1, source_target_pairs={{0,4},{2,6},{4,0},{6,2},{1,5},{3,7},{5,1},{7,3},{8,12},{10,14},{12... | collective-permute-start | bytes 32 | tf_op jit(solution)/shard_map/ppermute | solution.py:32
  97.2 3.5 %collective-permute-start.3 = (f32[2]{0:T(128)S(1)}, f32[2]{0:T(128)S(1)}, u32[]{:S(2)}, u32[]{:S(2)}) collective-permute-start(f32[2]{0:T(128)S(1)} %add.207), channel_id=1, source_target_pairs={{0,8},{8,0},{16,24},{24,16},{1,9},{9,1},{17,25},{25,17},{2,10},{10... | collective-permute-start | bytes 32 | tf_op jit(solution)/shard_map/ppermute | solution.py:32
  100.8 3.5 %collective-permute-start.4 = (f32[2]{0:T(128)S(1)}, f32[2]{0:T(128)S(1)}, u32[]{:S(2)}, u32[]{:S(2)}) collective-permute-start(f32[2]{0:T(128)S(1)} %add.208), channel_id=1, source_target_pairs={{0,16},{8,24},{16,0},{24,8},{1,17},{9,25},{17,1},{25,9},{2,18},{10... | collective-permute-start | bytes 32 | tf_op jit(solution)/shard_map/ppermute | solution.py:32
  109.5 1.3 copy-start.2
  110.9 1.2 collective-permute-start.6
  112.2 1.2 collective-permute-start.8
  117.1 31.2 %all-to-all-start.2 = ((bf16[4,4,2,128,128]{3,4,2,1,0:T(8,128)(2,1)}), bf16[4,4,2,128,128]{3,4,2,1,0:T(8,128)(2,1)}, u32[]{:S(2)}, u32[]{:S(2)}) async-start(bf16[4,4,2,128,128]{3,4,2,1,0:T(8,128)(2,1)} %bitcast.150), calls=%async_computation.2 | async-start | bytes 2097152 | tf_op jit(solution)/shard_map/all_to_all | solution.py:159
  163.4 2.1 %copy-start.4 = (bf16[16,4,128,128]{3,2,1,0:T(8,128)(2,1)S(1)}, bf16[16,4,128,128]{3,2,1,0:T(8,128)(2,1)}, u32[]{:S(2)}) copy-start(bf16[16,4,128,128]{3,2,1,0:T(8,128)(2,1)} %param.10) | copy-start | bytes 6291460
  163.4 2.3 %copy-start.8 = (bf16[16,2,128,128]{2,3,1,0:T(8,128)(2,1)S(1)}, bf16[16,2,128,128]{2,3,1,0:T(8,128)(2,1)}, u32[]{:S(2)}) copy-start(bf16[16,2,128,128]{2,3,1,0:T(8,128)(2,1)} %gather_fusion.7) | copy-start | bytes 3145732
  165.7 1.2 copy-start.6
  170.2 1.1 collective-permute-start.9
  172.7 3.5 %collective-permute-start.10 = (f32[2]{0:T(128)S(1)}, f32[2]{0:T(128)S(1)}, u32[]{:S(2)}, u32[]{:S(2)}) collective-permute-start(f32[2]{0:T(128)S(1)} %fusion.77), channel_id=1, source_target_pairs={{0,2},{2,0},{4,6},{6,4},{1,3},{3,1},{5,7},{7,5},{8,10},{10,8},{12,... | collective-permute-start | bytes 32 | tf_op jit(solution)/shard_map/ppermute | solution.py:32
  177.6 4.4 %collective-permute-start.11 = (f32[2]{0:T(128)S(1)}, f32[2]{0:T(128)S(1)}, u32[]{:S(2)}, u32[]{:S(2)}) collective-permute-start(f32[2]{0:T(128)S(1)} %fusion.79), channel_id=1, source_target_pairs={{0,4},{2,6},{4,0},{6,2},{1,5},{3,7},{5,1},{7,3},{8,12},{10,14},{12... | collective-permute-start | bytes 32 | tf_op jit(solution)/shard_map/ppermute | solution.py:32
  182.0 3.5 %collective-permute-start.12 = (f32[2]{0:T(128)S(1)}, f32[2]{0:T(128)S(1)}, u32[]{:S(2)}, u32[]{:S(2)}) collective-permute-start(f32[2]{0:T(128)S(1)} %add.226), channel_id=1, source_target_pairs={{0,8},{8,0},{16,24},{24,16},{1,9},{9,1},{17,25},{25,17},{2,10},{10... | collective-permute-start | bytes 32 | tf_op jit(solution)/shard_map/ppermute | solution.py:32
  185.6 3.5 %collective-permute-start.13 = (f32[2]{0:T(128)S(1)}, f32[2]{0:T(128)S(1)}, u32[]{:S(2)}, u32[]{:S(2)}) collective-permute-start(f32[2]{0:T(128)S(1)} %add.227), channel_id=1, source_target_pairs={{0,16},{8,24},{16,0},{24,8},{1,17},{9,25},{17,1},{25,9},{2,18},{10... | collective-permute-start | bytes 32 | tf_op jit(solution)/shard_map/ppermute | solution.py:32
  194.4 1.2 collective-permute-start.14
  195.7 1.2 collective-permute-start.15

commit v2 on v1

--- a/solution.py
+++ b/solution.py
@@ -124,8 +124,9 @@
         & (slot_index[None, None, :] == jnp.arange(capacity, dtype=jnp.int32)[None, :, None])
     )
     requests = jnp.sum(jnp.where(match, local_tile[None, None, :], 0), axis=-1, dtype=jnp.int32)
+    shift = (my_lane - owner_lane) % lane_count
     pool_index = jnp.where(
-        remote, tiles_here + owner_lane * capacity + slot_index, local_tile
+        remote, tiles_here + (shift - 1) * capacity + slot_index, local_tile
     ).reshape(tiles_here, sources_per)
     level_class = jnp.repeat(settle_class, levels // settle_class.shape[1], axis=1)
     both_fall = jnp.stack([fall_table, jnp.zeros_like(fall_table)])
@@ -152,18 +153,26 @@
         lower_band[..., :1] * inverse[..., :, 0],
     )
     edge_spike = jnp.where(my_layer == 0, spike_column[..., -1], spike_column[..., 0])
+    other_spike = from_partner(edge_spike, "gz", 0)
+    low_spike = jnp.where(my_layer == 0, edge_spike, other_spike)
+    high_spike = jnp.where(my_layer == 0, other_spike, edge_spike)
     fields = jnp.stack([concentration, turbulence], axis=1)
-    field_ids = jnp.arange(2, dtype=jnp.int32)[None, :, None]
+    wanted = lax.all_to_all(requests, "gy", split_axis=0, concat_axis=0, tiled=True)
+
+    def exchange(tiles):
+        received = []
+        for hop in range(1, lane_count):
+            target = (my_lane + hop) % lane_count
+            block = tiles[lax.dynamic_index_in_dim(wanted, target, 0, keepdims=False)]
+            received.append(
+                lax.ppermute(block, "gy", [(i, (i + hop) % lane_count) for i in range(lane_count)])
+            )
+        return jnp.concatenate(received, axis=0)
+
+    arrived = exchange(fields)
     ratios = []
     for step_index in range(STEPS):
-        arrived = lax.all_to_all(
-            fields[lax.all_to_all(requests, "gy", split_axis=0, concat_axis=0, tiled=True)],
-            "gy",
-            split_axis=0,
-            concat_axis=0,
-            tiled=True,
-        )
-        tile_pool = jnp.concatenate([fields, arrived.reshape((-1,) + fields.shape[1:])], axis=0)
+        tile_pool = jnp.concatenate([fields, arrived], axis=0)
         advected = jnp.zeros(fields.shape, jnp.float32)
         for entry_k in range(sources_per):
             advected = advected + jnp.einsum(
@@ -176,9 +185,6 @@
             jnp.stack([jnp.sum(fields[:, 0], dtype=jnp.float32), jnp.sum(advected[:, 0])]),
             ("gz", "gy", "gx"),
         )
-        mass_fixer = totals[0] / totals[1]
-        ratios.append(mass_fixer)
-        advected = advected * jnp.where(field_ids == 0, mass_fixer, 1.0)[..., None]
         solved = jnp.einsum(
             "tfzy,tfcy->tfcz",
             inverse,
@@ -187,22 +193,26 @@
             preferred_element_type=jnp.float32,
         )
         edge_value = jnp.where(my_layer == 0, solved[..., -1], solved[..., 0])
-        partner_field = 1 - my_layer
-        send_value = lax.dynamic_index_in_dim(edge_value, partner_field, 1, keepdims=False)
-        send_spike = lax.dynamic_index_in_dim(edge_spike, partner_field, 1, keepdims=False)
-        other_value, other_spike = from_partner((send_value, send_spike), "gz", 0)
-        own_value = lax.dynamic_index_in_dim(edge_value, my_layer, 1, keepdims=False)
-        own_spike = lax.dynamic_index_in_dim(edge_spike, my_layer, 1, keepdims=False)
-        low_value = jnp.where(my_layer == 0, own_value, other_value)
-        low_spike = jnp.where(my_layer == 0, own_spike, other_spike)
-        high_value = jnp.where(my_layer == 0, other_value, own_value)
-        high_spike = jnp.where(my_layer == 0, other_spike, own_spike)
+        other_value = from_partner(edge_value, "gz", 0)
+        low_value = jnp.where(my_layer == 0, edge_value, other_value)
+        high_value = jnp.where(my_layer == 0, other_value, edge_value)
         lower_end, upper_end = interface_values(low_value, low_spike, high_value, high_spike)
-        keeping = jnp.where(my_layer == 0, upper_end, lower_end)
-        giving = jnp.where(my_layer == 0, lower_end, upper_end)
-        received = from_partner(giving, "gz", 0)
-        needed = jnp.where(field_ids == my_layer, keeping[:, None, :], received[:, None, :])
-        fields = (solved - spike_column[:, :, None, :] * needed[..., None]).astype(jnp.bfloat16)
+        needed = jnp.where(my_layer == 0, upper_end, lower_end)
+        unscaled = solved - spike_column[:, :, None, :] * needed[..., None]
+        mass_fixer = totals[0] / totals[1]
+        ratios.append(mass_fixer)
+        next_turbulence = unscaled[:, 1].astype(jnp.bfloat16)
+        if step_index + 1 < STEPS:
+            sent = exchange(
+                jnp.stack([unscaled[:, 0], next_turbulence.astype(jnp.float32)], axis=1)
+            )
+            arrived = jnp.stack(
+                [(mass_fixer * sent[:, 0]).astype(jnp.bfloat16), sent[:, 1].astype(jnp.bfloat16)],
+                axis=1,
+            )
+        fields = jnp.stack(
+            [(mass_fixer * unscaled[:, 0]).astype(jnp.bfloat16), next_turbulence], axis=1
+        )
     return (fields[:, 0], fields[:, 1], jnp.stack(ratios))
 
 

time: 201 us -> 232 us (1.15)
  starting transfers between devices: 29.7 us -> 45.9 us
  local copies, waits for them, and re-layouts: 54.5 us -> 62.5 us
  waiting for transfers between devices: 50.2 us -> 56.1 us
    ppermute x0 -> x6, waiting for transfers between devices: none -> 38.5 us  [exchange(): lax.ppermute(block, 'gy', [(i, (i + hop) % lane_count) for i in range(lan...]
    all_to_all x2 -> x0, waiting for transfers between devices: 25.3 us -> none  [per_device(): lax.all_to_all(fields[lax.all_to_all(requests, 'gy', split_axis=0, concat...]
    ppermute x10, starting transfers between devices: 11.1 us -> 26.2 us  [butterfly_sum(): lax.ppermute(value, axis, [(i, i ^ bit) for i in range(devices)])]
    gather x3 -> x6, local copies, waits for them, and re-layouts: 3.46 us -> 14.4 us  [exchange(): block = tiles[lax.dynamic_index_in_dim(wanted, target, 0, keepdims=False)]]
    ppermute x0 -> x6, starting transfers between devices: none -> 10.1 us  [exchange(): lax.ppermute(block, 'gy', [(i, (i + hop) % lane_count) for i in range(lan...]
    all_to_all x2 -> x0, starting transfers between devices: 10.1 us -> none  [per_device(): lax.all_to_all(fields[lax.all_to_all(requests, 'gy', split_axis=0, concat...]
    ppermute x10, waiting for transfers between devices: 21.3 us -> 17.6 us  [butterfly_sum(): lax.ppermute(value, axis, [(i, i ^ bit) for i in range(devices)])]
    ppermute x5 -> x3, waiting for transfers between devices: 3.65 us -> 0.01 us  [from_partner(): lax.ppermute(array, axis, [(i, i ^ 1 << apart) for i in range(lax.axis_si...]
  transfers between devices with their start and end apart: 19 -> 21, of which waited for: 15 -> 14; matrix products, arithmetic and copies ran while one was open for 26% -> 21% of each run, Pallas kernels for 12% -> 10%
where the time goes in v2:
time: 232 us; the launch traced here: 230 us
  local copies, waits for them, and re-layouts  62.5 us (27%)
  waiting for transfers between devices  56.1 us (24%)
  starting transfers between devices  45.9 us (20%)
  Pallas kernels  24.1 us (10%)
  other arithmetic  23.8 us (10%)
  matrix products  14.3 us (6%)
  between operations  3.8 us (2%)
    ppermute x6, waiting for transfers between devices, exchange(): lax.ppermute(block, 'gy', [(i, (i + hop) % lane_count) for i in range(lan...  38.5 us
    ppermute x10, starting transfers between devices, butterfly_sum(): lax.ppermute(value, axis, [(i, i ^ bit) for i in range(devices)])  26.2 us
    pallas_call x1, Pallas kernels, block_inverse(): pl.pallas_call(thomas_inverse_kernel, out_shape=jax.ShapeDtypeStruct((lev...  24.1 us
    ppermute x10, waiting for transfers between devices, butterfly_sum(): lax.ppermute(value, axis, [(i, i ^ bit) for i in range(devices)])  17.6 us
    gather x8, local copies, waits for them, and re-layouts, per_device(): tile_pool[pool_index[:, entry_k]]  17.5 us
    gather x6, local copies, waits for them, and re-layouts, exchange(): block = tiles[lax.dynamic_index_in_dim(wanted, target, 0, keepdims=False)]  14.4 us
    unnamed x32, local copies, waits for them, and re-layouts  12.8 us
    ppermute x6, starting transfers between devices, exchange(): lax.ppermute(block, 'gy', [(i, (i + hop) % lane_count) for i in range(lan...  10.1 us
  transfers between devices with their start and end apart: 21, of which 14 were waited for; matrix products, arithmetic and copies ran while one was open for 21% of the time, Pallas kernels for 10%

profile of v2, /device:TPU:0, one launch (start us, length us, event | category | flops | bytes accessed | tf_op | source)
XLA Modules:
  0.0 230.4 jit_solution(16643910226222132934)
XLA Ops:
  1.4 1.3 collective-permute-start.8
  4.6 6.3 %all-to-all-start = ((s32[4,1,4]{2,1,0:T(1,128)}), s32[4,1,4]{2,1,0:T(1,128)S(1)}, u32[]{:S(2)}, u32[]{:S(2)}) async-start(s32[4,1,4]{2,1,0:T(1,128)} %bitcast.4), calls=%async_computation | async-start | bytes 4096 | tf_op jit(solution)/shard_map/all_to_all | solution.py:160
  11.8 1.9 convert_reduce_fusion.1
  14.5 2.4 %pad_maximum_fusion.2 = bf16[16,2,128,128]{3,2,1,0:T(8,128)(2,1)} fusion(bf16[16,1,128,128]{3,2,1,0:T(8,128)(2,1)} %bitcast.167, bf16[16,1,128,128]{3,2,1,0:T(8,128)(2,1)} %bitcast.165), kind=kLoop, calls=%fused_computation.38 | loop fusion | flops 524288 | bytes 2097152 | tf_op jit(solution)/shard_map/stack | solution.py:159
  18.2 2.9 %copy.145.upper_ref = f32[128,32,1]{2,1,0:T(8,128)} copy(f32[128,32,1]{0,1,2:T(8,128)S(1)} %fusion.44) | data formatting | bytes 32768 | tf_op jit(solution)/shard_map/broadcast_in_dim | solution.py:87
  21.1 2.9 %copy.143.lower_ref = f32[128,32,1]{2,1,0:T(8,128)} copy(f32[128,32,1]{0,1,2:T(8,128)S(1)} %bitcast.181) | data formatting | bytes 32768 | tf_op jit(solution)/shard_map/broadcast_in_dim | solution.py:87
  24.0 2.9 %copy.144.diagonal_ref = f32[128,32,1]{2,1,0:T(8,128)} copy(f32[128,32,1]{0,1,2:T(8,128)S(1)} %bitcast.180) | data formatting | bytes 32768 | tf_op jit(solution)/shard_map/broadcast_in_dim | solution.py:87
  26.8 24.1 %shard_map.94 = f32[128,32,128]{2,1,0:T(8,128)} custom-call(f32[128,32,1]{2,1,0:T(8,128)} %copy.143.lower_ref, f32[128,32,1]{2,1,0:T(8,128)} %copy.144.diagonal_ref, f32[128,32,1]{2,1,0:T(8,128)} %copy.145.upper_ref), custom_call_target="tpu_custom_call" | custom-call | tf_op jit(solution)/shard_map/pallas_call | solution.py:89
  50.9 5.9 %fusion.74 = (f32[16,2,128,1]{3,1,0,2:T(2,128)}, f32[16,2,128,1]{3,1,0,2:T(2,128)S(1)}) fusion(f32[16,2,128,128]{3,1,0,2:T(2,128)} %bitcast.160), kind=kLoop, calls=%fused_computation.178 | loop fusion | bytes 65536 | tf_op jit(solution)/shard_map/slice | solution.py:152
  56.7 2.7 %copy.175 = f32[16,2,128,1]{2,1,0,3:T(2,128)S(1)} copy(f32[16,2,128,1]{3,1,0,2:T(2,128)} %get-tuple-element.31) | data formatting | bytes 32768
  59.5 1.1 copy.176
  61.8 1.8 gather_fusion.2
  63.6 1.8 gather_fusion.1
  65.4 1.8 gather_fusion
  67.3 1.8 collective-permute-start
  69.1 2.4 %collective-permute-start.1 = (bf16[4,2,128,128]{3,2,1,0:T(8,128)(2,1)S(1)}, bf16[4,2,128,128]{3,2,1,0:T(8,128)(2,1)S(1)}, u32[]{:S(2)}, u32[]{:S(2)}) collective-permute-start(bf16[4,2,128,128]{3,2,1,0:T(8,128)(2,1)S(1)} %gather_fusion.1), channel_id=1, source_target_pairs={{0,4},{2,6},{4,0},{6,2},{1,5},{3,7},{5,1},{7,3},{8,12},{10,14},{12... | collective-permute-start | bytes 786440 | tf_op jit(solution)/shard_map/ppermute | solution.py:168
  71.4 1.5 collective-permute-start.2
  73.2 5.3 %collective-permute-done = bf16[4,2,128,128]{3,2,1,0:T(8,128)(2,1)S(1)} collective-permute-done((bf16[4,2,128,128]{3,2,1,0:T(8,128)(2,1)S(1)}, bf16[4,2,128,128]{3,2,1,0:T(8,128)(2,1)S(1)}, u32[]{:S(2)}, u32[]{:S(2)}) %collective-permute-start) | collective-permute-done | bytes 262176 | tf_op jit(solution)/shard_map/ppermute | solution.py:168
  78.4 10.3 %collective-permute-done.1 = bf16[4,2,128,128]{3,2,1,0:T(8,128)(2,1)S(1)} collective-permute-done((bf16[4,2,128,128]{3,2,1,0:T(8,128)(2,1)S(1)}, bf16[4,2,128,128]{3,2,1,0:T(8,128)(2,1)S(1)}, u32[]{:S(2)}, u32[]{:S(2)}) %collective-permute-start.1) | collective-permute-done | bytes 262176 | tf_op jit(solution)/shard_map/ppermute | solution.py:168
  88.7 1.3 pad_maximum_fusion.1
  90.7 1.7 gather_fusion.5
  92.4 1.6 gather_fusion.4
  94.1 1.6 gather_fusion.3
  95.7 2.0 fusion.18
  101.4 3.3 %fusion.2 = f32[16,2,128,128]{2,3,1,0:T(8,128)S(1)} fusion(f32[16,2,128,128]{3,2,1,0:T(8,128)S(1)} %add_add_fusion.1, f32[16,2,128,128]{3,1,0,2:T(2,128)S(1)} %bitcast.161), kind=kOutput, calls=%fused_computation.21 | convolution fusion | flops 805306368 | bytes 6291456 | tf_op jit(solution)/shard_map/tfzy,tfcy->tfcz/dot_general | solution.py:188
  105.5 1.4 pad_maximum_fusion.4
  108.0 1.4 fusion.90
  109.4 6.2 %collective-permute-start.4 = (f32[2]{0:T(128)S(1)}, f32[2]{0:T(128)S(1)}, u32[]{:S(2)}, u32[]{:S(2)}) collective-permute-start(f32[2]{0:T(128)S(1)} %fusion.90), channel_id=1, source_target_pairs={{0,2},{2,0},{4,6},{6,4},{1,3},{3,1},{5,7},{7,5},{8,10},{10,8},{12,... | collective-permute-start | bytes 32 | tf_op jit(solution)/shard_map/ppermute | solution.py:32
  115.6 1.5 collective-permute-done.4
  117.1 1.4 fusion.92
  118.5 1.6 collective-permute-start.5
  120.1 2.8 %collective-permute-done.5 = f32[2]{0:T(128)S(1)} collective-permute-done((f32[2]{0:T(128)S(1)}, f32[2]{0:T(128)S(1)}, u32[]{:S(2)}, u32[]{:S(2)}) %collective-permute-start.5) | collective-permute-done | bytes 40 | tf_op jit(solution)/shard_map/ppermute | solution.py:32
  122.9 1.5 collective-permute-start.6
  124.4 2.0 collective-permute-done.6
  126.5 1.5 collective-permute-start.7
  128.0 2.0 collective-permute-done.7
  133.9 1.5 pad_maximum_fusion
  135.4 3.0 %gather_fusion.7 = f32[4,2,128,128]{2,3,1,0:T(8,128)} fusion(f32[16,2,128,128]{2,3,1,0:T(8,128)} %pad_maximum_fusion, s32[1024]{0:T(1024)S(1)} %pad_clamp_fusion.6), kind=kCustom, calls=%fused_computation.7 | custom fusion | bytes 1048592 | tf_op jit(solution)/shard_map/gather | solution.py:166
  138.3 2.0 collective-permute-start.11
  140.4 3.0 %gather_fusion.8 = f32[4,2,128,128]{2,3,1,0:T(8,128)} fusion(f32[16,2,128,128]{2,3,1,0:T(8,128)} %pad_maximum_fusion, s32[1024]{0:T(1024)S(1)} %pad_clamp_fusion.5), kind=kCustom, calls=%fused_computation.8 | custom fusion | bytes 1048592 | tf_op jit(solution)/shard_map/gather | solution.py:166
  143.3 1.6 collective-permute-start.12
  144.9 3.0 %gather_fusion.9 = f32[4,2,128,128]{2,3,1,0:T(8,128)} fusion(f32[16,2,128,128]{2,3,1,0:T(8,128)} %pad_maximum_fusion, s32[1024]{0:T(1024)S(1)} %pad_clamp_fusion.4), kind=kCustom, calls=%fused_computation.9 | custom fusion | bytes 1048592 | tf_op jit(solution)/shard_map/gather | solution.py:166
  148.8 6.6 %collective-permute-done.11 = f32[4,2,128,128]{2,3,1,0:T(8,128)} collective-permute-done((f32[4,2,128,128]{2,3,1,0:T(8,128)}, f32[4,2,128,128]{2,3,1,0:T(8,128)}, u32[]{:S(2)}, u32[]{:S(2)}) %collective-permute-start.11) | collective-permute-done | bytes 524320 | tf_op jit(solution)/shard_map/ppermute | solution.py:168
  155.4 1.1 constant_dynamic-update-slice_fusion.2
  156.5 16.3 %collective-permute-done.12 = f32[4,2,128,128]{2,3,1,0:T(8,128)} collective-permute-done((f32[4,2,128,128]{2,3,1,0:T(8,128)}, f32[4,2,128,128]{2,3,1,0:T(8,128)}, u32[]{:S(2)}, u32[]{:S(2)}) %collective-permute-start.12) | collective-permute-done | bytes 524320 | tf_op jit(solution)/shard_map/ppermute | solution.py:168
  172.8 1.1 constant_dynamic-update-slice_fusion.1
  174.1 1.4 maximum_maximum_fusion
  175.5 2.2 gather_fusion.13
  177.8 3.2 %gather_fusion.12 = bf16[16,2,128,128]{2,3,1,0:T(8,128)(2,1)} fusion(bf16[28,2,128,128]{2,3,1,0:T(8,128)(2,1)} %maximum_maximum_fusion, s32[1024]{0:T(1024)S(1)} %get-tuple-element.47), kind=kCustom, calls=%fused_computation.12 | custom fusion | bytes 2097216 | tf_op jit(solution)/shard_map/gather | solution.py:181
  180.9 3.2 %gather_fusion.11 = bf16[16,2,128,128]{2,3,1,0:T(8,128)(2,1)} fusion(bf16[28,2,128,128]{2,3,1,0:T(8,128)(2,1)} %maximum_maximum_fusion, s32[1024]{0:T(1024)S(1)} %get-tuple-element.48), kind=kCustom, calls=%fused_computation.11 | custom fusion | bytes 2097216 | tf_op jit(solution)/shard_map/gather | solution.py:181
  184.1 3.2 %gather_fusion.10 = bf16[16,2,128,128]{2,3,1,0:T(8,128)(2,1)} fusion(bf16[28,2,128,128]{2,3,1,0:T(8,128)(2,1)} %maximum_maximum_fusion, s32[1024]{0:T(1024)S(1)} %get-tuple-element.49), kind=kCustom, calls=%fused_computation.10 | custom fusion | bytes 2097216 | tf_op jit(solution)/shard_map/gather | solution.py:181
  187.2 1.9 fusion.24
  191.8 3.3 %fusion = f32[16,2,128,128]{2,3,1,0:T(8,128)S(1)} fusion(f32[16,2,128,128]{3,2,1,0:T(8,128)S(1)} %add_add_fusion, f32[16,2,128,128]{3,1,0,2:T(2,128)S(1)} %bitcast.162), kind=kOutput, calls=%fused_computation.19 | convolution fusion | flops 805306368 | bytes 6291456 | tf_op jit(solution)/shard_map/tfzy,tfcy->tfcz/dot_general | solution.py:188
  196.0 1.4 pad_maximum_fusion.5
  198.5 1.4 fusion.89
  199.9 10.5 %collective-permute-start.15 = (f32[2]{0:T(128)S(1)}, f32[2]{0:T(128)S(1)}, u32[]{:S(2)}, u32[]{:S(2)}) collective-permute-start(f32[2]{0:T(128)S(1)} %fusion.89), channel_id=1, source_target_pairs={{0,2},{2,0},{4,6},{6,4},{1,3},{3,1},{5,7},{7,5},{8,10},{10,8},{12,... | collective-permute-start | bytes 32 | tf_op jit(solution)/shard_map/ppermute | solution.py:32
  210.4 1.5 collective-permute-done.15
  211.9 1.4 fusion.91
  213.3 1.9 collective-permute-start.16
  215.1 2.6 %collective-permute-done.16 = f32[2]{0:T(128)S(1)} collective-permute-done((f32[2]{0:T(128)S(1)}, f32[2]{0:T(128)S(1)}, u32[]{:S(2)}, u32[]{:S(2)}) %collective-permute-start.16) | collective-permute-done | bytes 40 | tf_op jit(solution)/shard_map/ppermute | solution.py:32
  217.7 1.5 collective-permute-start.17
  219.2 2.0 collective-permute-done.17
  221.2 1.5 collective-permute-start.18
  222.8 2.0 collective-permute-done.18
  (119 shorter events, 25.8 us)
Async XLA Ops:
  0.6 13.3 %copy-start = (f32[2,8]{1,0:T(2,128)S(1)}, f32[2,8]{1,0:T(2,128)}, u32[]{:S(2)}) copy-start(f32[2,8]{1,0:T(2,128)} %param.12) | copy-start | bytes 196
  0.6 16.4 %copy-start.11 = (f32[8]{0:T(128)S(1)}, f32[8]{0:T(128)}, u32[]{:S(2)}) copy-start(f32[8]{0:T(128)} %param.13) | copy-start | bytes 100
  1.4 15.5 %collective-permute-start.8 = (s32[16,1]{0,1:T(1,128)S(1)}, s32[16,1]{0,1:T(1,128)S(1)}, u32[]{:S(2)}, u32[]{:S(2)}) collective-permute-start(s32[16,1]{0,1:T(1,128)S(1)} %slice.123), channel_id=1, source_target_pairs={{1,0},{3,2},{5,4},{7,6},{9,8},{11,10},{13,12},{15,14},{17,16},{19,... | collective-permute-start | bytes 200 | tf_op jit(solution)/shard_map/ppermute | solution.py:17
  4.6 57.1 %all-to-all-start = ((s32[4,1,4]{2,1,0:T(1,128)}), s32[4,1,4]{2,1,0:T(1,128)S(1)}, u32[]{:S(2)}, u32[]{:S(2)}) async-start(s32[4,1,4]{2,1,0:T(1,128)} %bitcast.4), calls=%async_computation | async-start | bytes 4096 | tf_op jit(solution)/shard_map/all_to_all | solution.py:160
  59.5 29.3 %copy-start.5 = (bf16[16,128,128]{2,1,0:T(8,128)(2,1)S(1)}, bf16[16,128,128]{2,1,0:T(8,128)(2,1)}, u32[]{:S(2)}) copy-start(bf16[16,128,128]{2,1,0:T(8,128)(2,1)} %param.7) | copy-start | bytes 1572868
  59.5 29.2 %copy-start.10 = (bf16[16,128,128]{2,1,0:T(8,128)(2,1)S(1)}, bf16[16,128,128]{2,1,0:T(8,128)(2,1)}, u32[]{:S(2)}) copy-start(bf16[16,128,128]{2,1,0:T(8,128)(2,1)} %param.8) | copy-start | bytes 1572868
  60.9 12.0 %collective-permute-start.10 = (f32[16,2]{0,1:T(2,128)S(1)}, f32[16,2]{0,1:T(2,128)S(1)}, u32[]{:S(2)}, u32[]{:S(2)}) collective-permute-start(f32[16,2]{0,1:T(2,128)S(1)} %bitcast.185), channel_id=1, source_target_pairs={{0,1},{1,0},{2,3},{3,2},{4,5},{5,4},{6,7},{7,6},{8,9},{9,8},{10,11... | collective-permute-start | bytes 392 | tf_op jit(solution)/shard_map/ppermute | solution.py:21
  67.3 11.2 %collective-permute-start = (bf16[4,2,128,128]{3,2,1,0:T(8,128)(2,1)S(1)}, bf16[4,2,128,128]{3,2,1,0:T(8,128)(2,1)S(1)}, u32[]{:S(2)}, u32[]{:S(2)}) collective-permute-start(bf16[4,2,128,128]{3,2,1,0:T(8,128)(2,1)S(1)} %gather_fusion), channel_id=1, source_target_pairs={{0,2},{2,4},{4,6},{6,0},{1,3},{3,5},{5,7},{7,1},{8,10},{10,12},{12... | collective-permute-start | bytes 786440 | tf_op jit(solution)/shard_map/ppermute | solution.py:168
  69.1 19.7 %collective-permute-start.1 = (bf16[4,2,128,128]{3,2,1,0:T(8,128)(2,1)S(1)}, bf16[4,2,128,128]{3,2,1,0:T(8,128)(2,1)S(1)}, u32[]{:S(2)}, u32[]{:S(2)}) collective-permute-start(bf16[4,2,128,128]{3,2,1,0:T(8,128)(2,1)S(1)} %gather_fusion.1), channel_id=1, source_target_pairs={{0,4},{2,6},{4,0},{6,2},{1,5},{3,7},{5,1},{7,3},{8,12},{10,14},{12... | collective-permute-start | bytes 786440 | tf_op jit(solution)/shard_map/ppermute | solution.py:168
  71.4 17.3 %collective-permute-start.2 = (bf16[4,2,128,128]{3,2,1,0:T(8,128)(2,1)S(1)}, bf16[4,2,128,128]{3,2,1,0:T(8,128)(2,1)}, u32[]{:S(2)}, u32[]{:S(2)}) collective-permute-start(bf16[4,2,128,128]{3,2,1,0:T(8,128)(2,1)S(1)} %gather_fusion.2), channel_id=1, source_target_pairs={{0,6},{2,0},{4,2},{6,4},{1,7},{3,1},{5,3},{7,5},{8,14},{10,8},{12,... | collective-permute-start | bytes 786440 | tf_op jit(solution)/shard_map/ppermute | solution.py:168
  95.7 2.1 copy-start.3
  95.7 2.3 %copy-start.9 = (bf16[16,2,128,128]{3,2,1,0:T(8,128)(2,1)S(1)}, bf16[16,2,128,128]{3,2,1,0:T(8,128)(2,1)}, u32[]{:S(2)}) copy-start(bf16[16,2,128,128]{3,2,1,0:T(8,128)(2,1)} %gather_fusion.3) | copy-start | bytes 3145732
  98.1 1.2 copy-start.7
  99.8 1.6 copy-start.2
  106.9 1.1 collective-permute-start.3
  107.0 25.0 %collective-permute-start.9 = (f32[16,2,128]{2,1,0:T(2,128)S(1)}, f32[16,2,128]{2,1,0:T(2,128)S(1)}, u32[]{:S(2)}, u32[]{:S(2)}) collective-permute-start(f32[16,2,128]{2,1,0:T(2,128)S(1)} %bitcast.176), channel_id=1, source_target_pairs={{0,1},{1,0},{2,3},{3,2},{4,5},{5,4},{6,7},{7,6},{8,9},{9,8},{10,11... | collective-permute-start | bytes 49160 | tf_op jit(solution)/shard_map/ppermute | solution.py:21
  109.4 7.7 %collective-permute-start.4 = (f32[2]{0:T(128)S(1)}, f32[2]{0:T(128)S(1)}, u32[]{:S(2)}, u32[]{:S(2)}) collective-permute-start(f32[2]{0:T(128)S(1)} %fusion.90), channel_id=1, source_target_pairs={{0,2},{2,0},{4,6},{6,4},{1,3},{3,1},{5,7},{7,5},{8,10},{10,8},{12,... | collective-permute-start | bytes 32 | tf_op jit(solution)/shard_map/ppermute | solution.py:32
  118.5 4.4 %collective-permute-start.5 = (f32[2]{0:T(128)S(1)}, f32[2]{0:T(128)S(1)}, u32[]{:S(2)}, u32[]{:S(2)}) collective-permute-start(f32[2]{0:T(128)S(1)} %fusion.92), channel_id=1, source_target_pairs={{0,4},{2,6},{4,0},{6,2},{1,5},{3,7},{5,1},{7,3},{8,12},{10,14},{12... | collective-permute-start | bytes 32 | tf_op jit(solution)/shard_map/ppermute | solution.py:32
  122.9 3.5 %collective-permute-start.6 = (f32[2]{0:T(128)S(1)}, f32[2]{0:T(128)S(1)}, u32[]{:S(2)}, u32[]{:S(2)}) collective-permute-start(f32[2]{0:T(128)S(1)} %add.271), channel_id=1, source_target_pairs={{0,8},{8,0},{16,24},{24,16},{1,9},{9,1},{17,25},{25,17},{2,10},{10... | collective-permute-start | bytes 32 | tf_op jit(solution)/shard_map/ppermute | solution.py:32
  126.5 3.5 %collective-permute-start.7 = (f32[2]{0:T(128)S(1)}, f32[2]{0:T(128)S(1)}, u32[]{:S(2)}, u32[]{:S(2)}) collective-permute-start(f32[2]{0:T(128)S(1)} %add.272), channel_id=1, source_target_pairs={{0,16},{8,24},{16,0},{24,8},{1,17},{9,25},{17,1},{25,9},{2,18},{10... | collective-permute-start | bytes 32 | tf_op jit(solution)/shard_map/ppermute | solution.py:32
  138.3 17.1 %collective-permute-start.11 = (f32[4,2,128,128]{2,3,1,0:T(8,128)}, f32[4,2,128,128]{2,3,1,0:T(8,128)}, u32[]{:S(2)}, u32[]{:S(2)}) collective-permute-start(f32[4,2,128,128]{2,3,1,0:T(8,128)} %gather_fusion.7), channel_id=1, source_target_pairs={{0,2},{2,4},{4,6},{6,0},{1,3},{3,5},{5,7},{7,1},{8,10},{10,12},{12... | collective-permute-start | bytes 1572872 | tf_op jit(solution)/shard_map/ppermute | solution.py:168
  143.3 29.5 %collective-permute-start.12 = (f32[4,2,128,128]{2,3,1,0:T(8,128)}, f32[4,2,128,128]{2,3,1,0:T(8,128)}, u32[]{:S(2)}, u32[]{:S(2)}) collective-permute-start(f32[4,2,128,128]{2,3,1,0:T(8,128)} %gather_fusion.8), channel_id=1, source_target_pairs={{0,4},{2,6},{4,0},{6,2},{1,5},{3,7},{5,1},{7,3},{8,12},{10,14},{12... | collective-permute-start | bytes 1572872 | tf_op jit(solution)/shard_map/ppermute | solution.py:168
  147.9 26.0 %collective-permute-start.13 = (f32[4,2,128,128]{2,3,1,0:T(8,128)}, f32[4,2,128,128]{2,3,1,0:T(8,128)S(1)}, u32[]{:S(2)}, u32[]{:S(2)}) collective-permute-start(f32[4,2,128,128]{2,3,1,0:T(8,128)} %gather_fusion.9), channel_id=1, source_target_pairs={{0,6},{2,0},{4,2},{6,4},{1,7},{3,1},{5,3},{7,5},{8,14},{10,8},{12,... | collective-permute-start | bytes 1572872 | tf_op jit(solution)/shard_map/ppermute | solution.py:168
  187.2 2.1 copy-start.4
  187.2 2.3 %copy-start.8 = (bf16[16,2,128,128]{2,3,1,0:T(8,128)(2,1)S(1)}, bf16[16,2,128,128]{2,3,1,0:T(8,128)(2,1)}, u32[]{:S(2)}) copy-start(bf16[16,2,128,128]{2,3,1,0:T(8,128)(2,1)} %gather_fusion.11) | copy-start | bytes 3145732
  189.6 1.2 copy-start.6
  197.4 1.1 collective-permute-start.14
  197.4 29.9 %collective-permute-start.19 = (f32[16,2,128]{2,1,0:T(2,128)S(1)}, f32[16,2,128]{2,1,0:T(2,128)S(1)}, u32[]{:S(2)}, u32[]{:S(2)}) collective-permute-start(f32[16,2,128]{2,1,0:T(2,128)S(1)} %select_bitcast_fusion), channel_id=1, source_target_pairs={{0,1},{1,0},{2,3},{3,2},{4,5},{5,4},{6,7},{7,6},{8,9},{9,8},{10,11... | collective-permute-start | bytes 49160 | tf_op jit(solution)/shard_map/ppermute | solution.py:21
  199.9 12.0 %collective-permute-start.15 = (f32[2]{0:T(128)S(1)}, f32[2]{0:T(128)S(1)}, u32[]{:S(2)}, u32[]{:S(2)}) collective-permute-start(f32[2]{0:T(128)S(1)} %fusion.89), channel_id=1, source_target_pairs={{0,2},{2,0},{4,6},{6,4},{1,3},{3,1},{5,7},{7,5},{8,10},{10,8},{12,... | collective-permute-start | bytes 32 | tf_op jit(solution)/shard_map/ppermute | solution.py:32
  213.3 4.4 %collective-permute-start.16 = (f32[2]{0:T(128)S(1)}, f32[2]{0:T(128)S(1)}, u32[]{:S(2)}, u32[]{:S(2)}) collective-permute-start(f32[2]{0:T(128)S(1)} %fusion.91), channel_id=1, source_target_pairs={{0,4},{2,6},{4,0},{6,2},{1,5},{3,7},{5,1},{7,3},{8,12},{10,14},{12... | collective-permute-start | bytes 32 | tf_op jit(solution)/shard_map/ppermute | solution.py:32
  217.7 3.5 %collective-permute-start.17 = (f32[2]{0:T(128)S(1)}, f32[2]{0:T(128)S(1)}, u32[]{:S(2)}, u32[]{:S(2)}) collective-permute-start(f32[2]{0:T(128)S(1)} %add.288), channel_id=1, source_target_pairs={{0,8},{8,0},{16,24},{24,16},{1,9},{9,1},{17,25},{25,17},{2,10},{10... | collective-permute-start | bytes 32 | tf_op jit(solution)/shard_map/ppermute | solution.py:32
  221.2 3.5 %collective-permute-start.18 = (f32[2]{0:T(128)S(1)}, f32[2]{0:T(128)S(1)}, u32[]{:S(2)}, u32[]{:S(2)}) collective-permute-start(f32[2]{0:T(128)S(1)} %add.289), channel_id=1, source_target_pairs={{0,16},{8,24},{16,0},{24,8},{1,17},{9,25},{17,1},{25,9},{2,18},{10... | collective-permute-start | bytes 32 | tf_op jit(solution)/shard_map/ppermute | solution.py:32
  228.1 2.3 copy-start.1

commit v3 on v2

--- a/solution.py
+++ b/solution.py
@@ -67,7 +67,7 @@
         inverse_ref[z] = row
         return ratio, row
 
-    _, row = lax.fori_loop(1, levels, forward, (ratio, row))
+    _, row = lax.fori_loop(1, levels, forward, (ratio, row), unroll=8)
 
     def backward(step, row):
         z = levels - 2 - step
@@ -75,10 +75,10 @@
         inverse_ref[z] = row
         return row
 
-    lax.fori_loop(0, levels - 1, backward, row)
-
-
-def block_inverse(lower, diagonal, upper):
+    lax.fori_loop(0, levels - 1, backward, row, unroll=8)
+
+
+def block_inverse(lower, diagonal, upper, ready):
     lead = diagonal.shape[:-1]
     levels = diagonal.shape[-1]
     systems = diagonal.size // levels
@@ -86,12 +86,20 @@
     def level_major(band):
         return jnp.transpose(band.reshape(systems, levels))[:, :, None]
 
+    bands, ready = lax.optimization_barrier(
+        ((level_major(lower), level_major(diagonal), level_major(upper)), ready)
+    )
     inverse = pl.pallas_call(
         thomas_inverse_kernel,
         out_shape=jax.ShapeDtypeStruct((levels, systems, levels), jnp.float32),
         scratch_shapes=[pltpu.VMEM((levels, systems, 1), jnp.float32)],
-    )(level_major(lower), level_major(diagonal), level_major(upper))
-    return jnp.transpose(inverse, (1, 0, 2)).reshape(lead + (levels, levels))
+        cost_estimate=pl.CostEstimate(
+            flops=16 * levels * systems * levels,
+            transcendentals=levels * systems,
+            bytes_accessed=64 * levels * systems * levels,
+        ),
+    )(*bands)
+    return jnp.transpose(inverse, (1, 0, 2)).reshape(lead + (levels, levels)), ready
 
 
 def interface_values(low_value, low_spike, high_value, high_spike):
@@ -146,7 +154,33 @@
     level_index = jnp.arange(levels, dtype=jnp.int32)
     block_lower = jnp.where(level_index == 0, 0.0, lower_band)
     block_upper = jnp.where(level_index == levels - 1, 0.0, upper_band)
-    inverse = block_inverse(block_lower, diagonal, block_upper)
+    fields = jnp.stack([concentration, turbulence], axis=1)
+    wanted = lax.all_to_all(requests, "gy", split_axis=0, concat_axis=0, tiled=True)
+
+    def exchange(tiles, extra=None):
+        received = []
+        for hop in range(1, lane_count):
+            target = (my_lane + hop) % lane_count
+            block = tiles[lax.dynamic_index_in_dim(wanted, target, 0, keepdims=False)]
+            if extra is not None:
+                block = jnp.concatenate([block.reshape(-1), extra])
+            received.append(
+                lax.ppermute(block, "gy", [(i, (i + hop) % lane_count) for i in range(lane_count)])
+            )
+        if extra is None:
+            return jnp.concatenate(received, axis=0), None
+        tail = extra.shape[0]
+        shape = (-1,) + tiles.shape[1:]
+        tiles_in = jnp.concatenate([r[:-tail].reshape(shape) for r in received], axis=0)
+        extras_in = jnp.stack([extra] + [r[-tail:] for r in received])
+        by_lane = extras_in[(my_lane - jnp.arange(lane_count)) % lane_count]
+        total = by_lane[0]
+        for lane in range(1, lane_count):
+            total = total + by_lane[lane]
+        return tiles_in, total
+
+    arrived, _ = exchange(fields)
+    inverse, wanted = block_inverse(block_lower, diagonal, block_upper, wanted)
     spike_column = jnp.where(
         my_layer == 0,
         upper_band[..., -1:] * inverse[..., :, levels - 1],
@@ -156,20 +190,6 @@
     other_spike = from_partner(edge_spike, "gz", 0)
     low_spike = jnp.where(my_layer == 0, edge_spike, other_spike)
     high_spike = jnp.where(my_layer == 0, other_spike, edge_spike)
-    fields = jnp.stack([concentration, turbulence], axis=1)
-    wanted = lax.all_to_all(requests, "gy", split_axis=0, concat_axis=0, tiled=True)
-
-    def exchange(tiles):
-        received = []
-        for hop in range(1, lane_count):
-            target = (my_lane + hop) % lane_count
-            block = tiles[lax.dynamic_index_in_dim(wanted, target, 0, keepdims=False)]
-            received.append(
-                lax.ppermute(block, "gy", [(i, (i + hop) % lane_count) for i in range(lane_count)])
-            )
-        return jnp.concatenate(received, axis=0)
-
-    arrived = exchange(fields)
     ratios = []
     for step_index in range(STEPS):
         tile_pool = jnp.concatenate([fields, arrived], axis=0)
@@ -181,10 +201,12 @@
                 tile_pool[pool_index[:, entry_k]],
                 preferred_element_type=jnp.float32,
             )
-        totals = butterfly_sum(
-            jnp.stack([jnp.sum(fields[:, 0], dtype=jnp.float32), jnp.sum(advected[:, 0])]),
-            ("gz", "gy", "gx"),
-        )
+        partial = jnp.stack([jnp.sum(fields[:, 0], dtype=jnp.float32), jnp.sum(advected[:, 0])])
+        last = step_index + 1 == STEPS
+        if last:
+            totals = butterfly_sum(partial, ("gz", "gy", "gx"))
+        else:
+            partial = butterfly_sum(partial, ("gz", "gx"))
         solved = jnp.einsum(
             "tfzy,tfcy->tfcz",
             inverse,
@@ -199,13 +221,14 @@
         lower_end, upper_end = interface_values(low_value, low_spike, high_value, high_spike)
         needed = jnp.where(my_layer == 0, upper_end, lower_end)
         unscaled = solved - spike_column[:, :, None, :] * needed[..., None]
+        next_turbulence = unscaled[:, 1].astype(jnp.bfloat16)
+        if not last:
+            sent, totals = exchange(
+                jnp.stack([unscaled[:, 0], next_turbulence.astype(jnp.float32)], axis=1), partial
+            )
         mass_fixer = totals[0] / totals[1]
         ratios.append(mass_fixer)
-        next_turbulence = unscaled[:, 1].astype(jnp.bfloat16)
-        if step_index + 1 < STEPS:
-            sent = exchange(
-                jnp.stack([unscaled[:, 0], next_turbulence.astype(jnp.float32)], axis=1)
-            )
+        if not last:
             arrived = jnp.stack(
                 [(mass_fixer * sent[:, 0]).astype(jnp.bfloat16), sent[:, 1].astype(jnp.bfloat16)],
                 axis=1,

time: 232 us -> 208 us (0.90)
  Pallas kernels: 24.1 us -> 9.26 us
  waiting for transfers between devices: 56.1 us -> 45.3 us
  starting transfers between devices: 45.9 us -> 35.5 us
  local copies, waits for them, and re-layouts: 62.5 us -> 70.9 us
  other arithmetic: 23.8 us -> 28 us
    pallas_call x1, Pallas kernels: 24.1 us -> 9.26 us  [block_inverse(): pl.pallas_call(thomas_inverse_kernel, out_shape=jax.ShapeDtypeStruct((lev...]
    ppermute x10 -> x8, starting transfers between devices: 26.2 us -> 17.3 us  [butterfly_sum(): lax.ppermute(value, axis, [(i, i ^ bit) for i in range(devices)])]
    broadcast_in_dim x3 -> x0, local copies, waits for them, and re-layouts: 8.61 us -> none  [level_major(): return jnp.transpose(band.reshape(systems, levels))[:, :, None]]
    optimization_barrier x0 -> x3, local copies, waits for them, and re-layouts: none -> 8.6 us  [block_inverse(): lax.optimization_barrier(((level_major(lower), level_major(diagonal), lev...]
    ppermute x6, waiting for transfers between devices: 38.5 us -> 30.9 us  [exchange(): lax.ppermute(block, 'gy', [(i, (i + hop) % lane_count) for i in range(lan...]
    ppermute x10 -> x8, waiting for transfers between devices: 17.6 us -> 13.3 us  [butterfly_sum(): lax.ppermute(value, axis, [(i, i ^ bit) for i in range(devices)])]
    concatenate x0 -> x2, other arithmetic: none -> 3.89 us  [the longest x1 2.43 us: exchange(): block = jnp.concatenate([block.reshape(-1), extra])]
    reshape x0 -> x3, local copies, waits for them, and re-layouts: none -> 2.99 us  [exchange(): r[:-tail].reshape(shape)]
  transfers between devices with their start and end apart: 21 -> 19, of which waited for: 14 -> 11; matrix products, arithmetic and copies ran while one was open for 21% -> 18% of each run, Pallas kernels for 10% -> 4%
where the time goes in v3:
time: 208 us; the launch traced here: 207 us
  local copies, waits for them, and re-layouts  70.9 us (34%)
  waiting for transfers between devices  45.3 us (22%)
  starting transfers between devices  35.5 us (17%)
  other arithmetic  28 us (13%)
  matrix products  14.3 us (7%)
  Pallas kernels  9.26 us (4%)
  between operations  3.76 us (2%)
    ppermute x6, waiting for transfers between devices, exchange(): lax.ppermute(block, 'gy', [(i, (i + hop) % lane_count) for i in range(lan...  30.9 us
    gather x8, local copies, waits for them, and re-layouts, per_device(): tile_pool[pool_index[:, entry_k]]  17.5 us
    ppermute x8, starting transfers between devices, butterfly_sum(): lax.ppermute(value, axis, [(i, i ^ bit) for i in range(devices)])  17.3 us
    gather x9, local copies, waits for them, and re-layouts, exchange(): block = tiles[lax.dynamic_index_in_dim(wanted, target, 0, keepdims=False)]  15.2 us
    ppermute x8, waiting for transfers between devices, butterfly_sum(): lax.ppermute(value, axis, [(i, i ^ bit) for i in range(devices)])  13.3 us
    unnamed x34, local copies, waits for them, and re-layouts  12.6 us
    ppermute x6, starting transfers between devices, exchange(): lax.ppermute(block, 'gy', [(i, (i + hop) % lane_count) for i in range(lan...  9.67 us
    pallas_call x1, Pallas kernels, block_inverse(): pl.pallas_call(thomas_inverse_kernel, out_shape=jax.ShapeDtypeStruct((lev...  9.26 us
  transfers between devices with their start and end apart: 19, of which 11 were waited for; matrix products, arithmetic and copies ran while one was open for 18% of the time, Pallas kernels for 4%

profile of v3, /device:TPU:0, one launch (start us, length us, event | category | flops | bytes accessed | tf_op | source)
XLA Modules:
  0.0 207.0 jit_solution(2869542763518723629)
XLA Ops:
  1.4 1.3 collective-permute-start.6
  4.7 6.3 %all-to-all-start = ((s32[4,1,4]{2,1,0:T(1,128)}), s32[4,1,4]{2,1,0:T(1,128)S(1)}, u32[]{:S(2)}, u32[]{:S(2)}) async-start(s32[4,1,4]{2,1,0:T(1,128)} %bitcast.4), calls=%async_computation | async-start | bytes 4096 | tf_op jit(solution)/shard_map/all_to_all | solution.py:158
  11.8 2.0 convert_reduce_fusion.1
  14.5 1.3 pad_maximum_fusion.3
  17.3 1.3 gather_fusion.2
  18.6 1.3 gather_fusion.1
  19.9 1.3 gather_fusion
  21.2 2.0 collective-permute-start
  23.2 2.4 %collective-permute-start.1 = (bf16[4,2,128,128]{3,2,1,0:T(8,128)(2,1)}, bf16[4,2,128,128]{3,2,1,0:T(8,128)(2,1)}, u32[]{:S(2)}, u32[]{:S(2)}) collective-permute-start(bf16[4,2,128,128]{3,2,1,0:T(8,128)(2,1)} %gather_fusion.1), channel_id=1, source_target_pairs={{0,4},{2,6},{4,0},{6,2},{1,5},{3,7},{5,1},{7,3},{8,12},{10,14},{12... | collective-permute-start | bytes 786440 | tf_op jit(solution)/shard_map/ppermute | solution.py:168
  25.6 1.5 collective-permute-start.2
  27.1 2.9 %copy.155.lower_ref = f32[128,32,1]{2,1,0:T(8,128)} copy(f32[128,32,1]{0,1,2:T(8,128)S(1)} %bitcast.228) | data formatting | bytes 32768 | tf_op jit(solution)/shard_map/optimization_barrier | solution.py:89
  29.9 2.9 %copy.156.diagonal_ref = f32[128,32,1]{2,1,0:T(8,128)} copy(f32[128,32,1]{0,1,2:T(8,128)S(1)} %bitcast.227) | data formatting | bytes 32768 | tf_op jit(solution)/shard_map/optimization_barrier | solution.py:89
  32.8 2.9 %copy.157.upper_ref = f32[128,32,1]{2,1,0:T(8,128)} copy(f32[128,32,1]{0,1,2:T(8,128)S(1)} %fusion.44) | data formatting | bytes 32768 | tf_op jit(solution)/shard_map/optimization_barrier | solution.py:89
  35.7 9.3 %shard_map.94 = f32[128,32,128]{2,1,0:T(8,128)} custom-call(f32[128,32,1]{2,1,0:T(8,128)} %copy.155.lower_ref, f32[128,32,1]{2,1,0:T(8,128)} %copy.156.diagonal_ref, f32[128,32,1]{2,1,0:T(8,128)} %copy.157.upper_ref), custom_call_target="tpu_custom_call" | custom-call | flops 8388608 | bytes 33554432 | tf_op jit(solution)/shard_map/pallas_call | solution.py:92
  44.9 5.9 %fusion.82 = (f32[16,2,128,1]{3,1,0,2:T(2,128)}, f32[16,2,128,1]{3,1,0,2:T(2,128)S(1)}) fusion(f32[16,2,128,128]{3,1,0,2:T(2,128)} %bitcast.201), kind=kLoop, calls=%fused_computation.207 | loop fusion | bytes 65536 | tf_op jit(solution)/shard_map/slice | solution.py:186
  50.8 2.8 %copy.193 = f32[16,2,128,1]{2,1,0,3:T(2,128)S(1)} copy(f32[16,2,128,1]{3,1,0,2:T(2,128)} %get-tuple-element.38) | data formatting | bytes 32768
  53.6 1.1 copy.194
  55.0 1.1 collective-permute-done.8
  56.4 1.3 pad_maximum_fusion.1
  58.5 1.7 gather_fusion.5
  60.2 1.6 gather_fusion.4
  61.8 1.6 gather_fusion.3
  63.5 2.0 fusion.18
  69.1 3.3 %fusion.2 = f32[16,2,128,128]{2,3,1,0:T(8,128)S(1)} fusion(f32[16,2,128,128]{3,2,1,0:T(8,128)S(1)} %add_add_fusion.1, f32[16,2,128,128]{3,1,0,2:T(2,128)S(1)} %bitcast.202), kind=kOutput, calls=%fused_computation.22 | convolution fusion | flops 805306368 | bytes 6291456 | tf_op jit(solution)/shard_map/tfzy,tfcy->tfcz/dot_general | solution.py:210
  73.3 1.3 pad_maximum_fusion.9
  75.8 1.3 fusion.98
  77.1 1.5 collective-permute-start.4
  78.6 2.0 collective-permute-done.4
  80.7 1.3 fusion.100
  82.0 1.5 collective-permute-start.5
  83.5 2.0 collective-permute-done.5
  86.7 1.0 copy-done.3
  87.7 1.5 pad_maximum_fusion
  89.2 2.2 %gather_fusion.9 = f32[4,2,128,128]{2,3,1,0:T(8,128)S(1)} fusion(f32[16,2,128,128]{2,3,1,0:T(8,128)} %pad_maximum_fusion, s32[1024]{0:T(1024)S(1)} %pad_clamp_fusion.1), kind=kCustom, calls=%fused_computation.9 | custom fusion | bytes 1048592 | tf_op jit(solution)/shard_map/gather | solution.py:164
  92.4 2.2 %gather_fusion.8 = f32[4,2,128,128]{2,3,1,0:T(8,128)S(1)} fusion(f32[16,2,128,128]{2,3,1,0:T(8,128)} %pad_maximum_fusion, s32[1024]{0:T(1024)S(1)} %pad_clamp_fusion.2), kind=kCustom, calls=%fused_computation.8 | custom fusion | bytes 1048592 | tf_op jit(solution)/shard_map/gather | solution.py:164
  94.5 3.0 %gather_fusion.7 = f32[4,2,128,128]{2,3,1,0:T(8,128)} fusion(f32[16,2,128,128]{2,3,1,0:T(8,128)} %pad_maximum_fusion, s32[1024]{0:T(1024)S(1)} %pad_clamp_fusion.3), kind=kCustom, calls=%fused_computation.7 | custom fusion | bytes 1048592 | tf_op jit(solution)/shard_map/gather | solution.py:164
  97.5 2.0 copy.170
  100.5 2.4 %pad_maximum_fusion.6 = (f32[131074]{0:T(1024)S(1)}, f32[131074]{0:T(1024)}, f32[131074]{0:T(1024)}) fusion(f32[2]{0:T(128)S(1)} %add.327, f32[131072]{0:T(1024)} %bitcast.214, f32[131072]{0:T(1024)} %bitcast.215, f32[131072]{0:T(1024)} %bitcast.213), kind=kLoop, calls=%fused_computation.46 | loop fusion | flops 393222 | bytes 3145760 | tf_op jit(solution)/shard_map/concatenate | solution.py:166
  104.1 2.7 %collective-permute-start.11 = (f32[131074]{0:T(1024)}, f32[131074]{0:T(1024)}, u32[]{:S(2)}, u32[]{:S(2)}) collective-permute-start(f32[131074]{0:T(1024)} %get-tuple-element.55), channel_id=1, source_target_pairs={{0,6},{2,0},{4,2},{6,4},{1,7},{3,1},{5,3},{7,5},{8,14},{10,8},{12,... | collective-permute-start | bytes 1572896 | tf_op jit(solution)/shard_map/ppermute | solution.py:168
  106.8 13.0 %collective-permute-done.9 = f32[131074]{0:T(1024)S(1)} collective-permute-done((f32[131074]{0:T(1024)S(1)}, f32[131074]{0:T(1024)S(1)}, u32[]{:S(2)}, u32[]{:S(2)}) %collective-permute-start.9) | collective-permute-done | bytes 524328 | tf_op jit(solution)/shard_map/ppermute | solution.py:168
  121.6 17.9 %collective-permute-done.10 = f32[131074]{0:T(1024)} collective-permute-done((f32[131074]{0:T(1024)}, f32[131074]{0:T(1024)}, u32[]{:S(2)}, u32[]{:S(2)}) %collective-permute-start.10) | collective-permute-done | bytes 524328 | tf_op jit(solution)/shard_map/ppermute | solution.py:168
  139.5 1.1 slice.238
  141.6 1.1 slice.239
  148.2 2.1 %convert_reduce_fusion = (f32[]{:T(128)}, bf16[16,1,128,128]{2,3,1,0:T(8,128)(2,1)S(1)}) fusion(f32[16,2,128,128]{2,3,1,0:T(8,128)} %copy-done.3, f32[]{:T(128)} %bitcast.72), kind=kLoop, calls=%fused_computation.41 | loop fusion | flops 1048575 | bytes 1572872 | tf_op jit(solution)/shard_map/reduce_sum | solution.py:204
  150.3 1.5 pad_maximum_fusion.2
  151.9 1.4 maximum_maximum_fusion
  153.3 2.2 %gather_fusion.14 = bf16[16,2,128,128]{2,3,1,0:T(8,128)(2,1)S(1)} fusion(bf16[28,2,128,128]{2,3,1,0:T(8,128)(2,1)} %maximum_maximum_fusion, s32[1024]{0:T(1024)S(1)} %get-tuple-element.60), kind=kCustom, calls=%fused_computation.14 | custom fusion | bytes 2097216 | tf_op jit(solution)/shard_map/gather | solution.py:201
  155.6 3.2 %gather_fusion.13 = bf16[16,2,128,128]{2,3,1,0:T(8,128)(2,1)} fusion(bf16[28,2,128,128]{2,3,1,0:T(8,128)(2,1)} %maximum_maximum_fusion, s32[1024]{0:T(1024)S(1)} %get-tuple-element.61), kind=kCustom, calls=%fused_computation.13 | custom fusion | bytes 2097216 | tf_op jit(solution)/shard_map/gather | solution.py:201
  158.8 3.2 %gather_fusion.12 = bf16[16,2,128,128]{2,3,1,0:T(8,128)(2,1)} fusion(bf16[28,2,128,128]{2,3,1,0:T(8,128)(2,1)} %maximum_maximum_fusion, s32[1024]{0:T(1024)S(1)} %get-tuple-element.62), kind=kCustom, calls=%fused_computation.12 | custom fusion | bytes 2097216 | tf_op jit(solution)/shard_map/gather | solution.py:201
  161.9 3.2 %gather_fusion.11 = bf16[16,2,128,128]{2,3,1,0:T(8,128)(2,1)} fusion(bf16[28,2,128,128]{2,3,1,0:T(8,128)(2,1)} %maximum_maximum_fusion, s32[1024]{0:T(1024)S(1)} %get-tuple-element.63), kind=kCustom, calls=%fused_computation.11 | custom fusion | bytes 2097216 | tf_op jit(solution)/shard_map/gather | solution.py:201
  165.1 1.9 fusion.24
  169.7 3.3 %fusion = f32[16,2,128,128]{2,3,1,0:T(8,128)S(1)} fusion(f32[16,2,128,128]{3,2,1,0:T(8,128)S(1)} %add_add_fusion, f32[16,2,128,128]{3,1,0,2:T(2,128)S(1)} %bitcast.203), kind=kOutput, calls=%fused_computation.20 | convolution fusion | flops 805306368 | bytes 6291456 | tf_op jit(solution)/shard_map/tfzy,tfcy->tfcz/dot_general | solution.py:210
  173.8 1.4 pad_maximum_fusion.10
  176.3 1.4 fusion.97
  177.7 9.2 %collective-permute-start.13 = (f32[2]{0:T(128)S(1)}, f32[2]{0:T(128)S(1)}, u32[]{:S(2)}, u32[]{:S(2)}) collective-permute-start(f32[2]{0:T(128)S(1)} %fusion.97), channel_id=1, source_target_pairs={{0,2},{2,0},{4,6},{6,4},{1,3},{3,1},{5,7},{7,5},{8,10},{10,8},{12,... | collective-permute-start | bytes 32 | tf_op jit(solution)/shard_map/ppermute | solution.py:32
  186.9 1.5 collective-permute-done.13
  188.5 1.4 fusion.99
  189.8 1.8 collective-permute-start.14
  191.7 2.6 %collective-permute-done.14 = f32[2]{0:T(128)S(1)} collective-permute-done((f32[2]{0:T(128)S(1)}, f32[2]{0:T(128)S(1)}, u32[]{:S(2)}, u32[]{:S(2)}) %collective-permute-start.14) | collective-permute-done | bytes 40 | tf_op jit(solution)/shard_map/ppermute | solution.py:32
  194.3 1.5 collective-permute-start.15
  195.8 2.0 collective-permute-done.15
  197.8 1.5 collective-permute-start.16
  199.3 2.0 collective-permute-done.16
  205.0 1.0 copy.180
  (138 shorter events, 31.8 us)
Async XLA Ops:
  0.6 13.3 %copy-start = (f32[2,8]{1,0:T(2,128)S(1)}, f32[2,8]{1,0:T(2,128)}, u32[]{:S(2)}) copy-start(f32[2,8]{1,0:T(2,128)} %param.12) | copy-start | bytes 196
  0.6 15.4 %copy-start.13 = (f32[8]{0:T(128)S(1)}, f32[8]{0:T(128)}, u32[]{:S(2)}) copy-start(f32[8]{0:T(128)} %param.13) | copy-start | bytes 100
  1.4 14.5 %collective-permute-start.6 = (s32[16,1]{0,1:T(1,128)S(1)}, s32[16,1]{0,1:T(1,128)S(1)}, u32[]{:S(2)}, u32[]{:S(2)}) collective-permute-start(s32[16,1]{0,1:T(1,128)S(1)} %slice.153), channel_id=1, source_target_pairs={{1,0},{3,2},{5,4},{7,6},{9,8},{11,10},{13,12},{15,14},{17,16},{19,... | collective-permute-start | bytes 200 | tf_op jit(solution)/shard_map/ppermute | solution.py:17
  4.7 12.6 %all-to-all-start = ((s32[4,1,4]{2,1,0:T(1,128)}), s32[4,1,4]{2,1,0:T(1,128)S(1)}, u32[]{:S(2)}, u32[]{:S(2)}) async-start(s32[4,1,4]{2,1,0:T(1,128)} %bitcast.4), calls=%async_computation | async-start | bytes 4096 | tf_op jit(solution)/shard_map/all_to_all | solution.py:158
  21.2 35.2 %collective-permute-start = (bf16[4,2,128,128]{3,2,1,0:T(8,128)(2,1)}, bf16[4,2,128,128]{3,2,1,0:T(8,128)(2,1)S(1)}, u32[]{:S(2)}, u32[]{:S(2)}) collective-permute-start(bf16[4,2,128,128]{3,2,1,0:T(8,128)(2,1)} %gather_fusion), channel_id=1, source_target_pairs={{0,2},{2,4},{4,6},{6,0},{1,3},{3,5},{5,7},{7,1},{8,10},{10,12},{12... | collective-permute-start | bytes 786440 | tf_op jit(solution)/shard_map/ppermute | solution.py:168
  23.2 33.2 %collective-permute-start.1 = (bf16[4,2,128,128]{3,2,1,0:T(8,128)(2,1)}, bf16[4,2,128,128]{3,2,1,0:T(8,128)(2,1)}, u32[]{:S(2)}, u32[]{:S(2)}) collective-permute-start(bf16[4,2,128,128]{3,2,1,0:T(8,128)(2,1)} %gather_fusion.1), channel_id=1, source_target_pairs={{0,4},{2,6},{4,0},{6,2},{1,5},{3,7},{5,1},{7,3},{8,12},{10,14},{12... | collective-permute-start | bytes 786440 | tf_op jit(solution)/shard_map/ppermute | solution.py:168
  25.6 30.8 %collective-permute-start.2 = (bf16[4,2,128,128]{3,2,1,0:T(8,128)(2,1)}, bf16[4,2,128,128]{3,2,1,0:T(8,128)(2,1)}, u32[]{:S(2)}, u32[]{:S(2)}) collective-permute-start(bf16[4,2,128,128]{3,2,1,0:T(8,128)(2,1)} %gather_fusion.2), channel_id=1, source_target_pairs={{0,6},{2,0},{4,2},{6,4},{1,7},{3,1},{5,3},{7,5},{8,14},{10,8},{12,... | collective-permute-start | bytes 786440 | tf_op jit(solution)/shard_map/ppermute | solution.py:168
  50.8 5.6 %copy-start.6 = (bf16[16,128,128]{2,1,0:T(8,128)(2,1)S(1)}, bf16[16,128,128]{2,1,0:T(8,128)(2,1)}, u32[]{:S(2)}) copy-start(bf16[16,128,128]{2,1,0:T(8,128)(2,1)} %param.7) | copy-start | bytes 1572868
  50.8 5.6 %copy-start.11 = (bf16[16,128,128]{2,1,0:T(8,128)(2,1)S(1)}, bf16[16,128,128]{2,1,0:T(8,128)(2,1)}, u32[]{:S(2)}) copy-start(bf16[16,128,128]{2,1,0:T(8,128)(2,1)} %param.8) | copy-start | bytes 1572868
  55.0 1.1 collective-permute-start.8
  63.5 2.1 copy-start.4
  63.5 2.3 %copy-start.10 = (bf16[16,2,128,128]{3,2,1,0:T(8,128)(2,1)S(1)}, bf16[16,2,128,128]{3,2,1,0:T(8,128)(2,1)}, u32[]{:S(2)}) copy-start(bf16[16,2,128,128]{3,2,1,0:T(8,128)(2,1)} %gather_fusion.3) | copy-start | bytes 3145732
  65.8 1.2 copy-start.8
  67.5 1.6 copy-start.2
  74.6 1.1 collective-permute-start.3
  74.9 10.7 %collective-permute-start.7 = (f32[16,2,128]{2,1,0:T(2,128)S(1)}, f32[16,2,128]{2,1,0:T(2,128)S(1)}, u32[]{:S(2)}, u32[]{:S(2)}) collective-permute-start(f32[16,2,128]{2,1,0:T(2,128)S(1)} %bitcast.223), channel_id=1, source_target_pairs={{0,1},{1,0},{2,3},{3,2},{4,5},{5,4},{6,7},{7,6},{8,9},{9,8},{10,11... | collective-permute-start | bytes 49160 | tf_op jit(solution)/shard_map/ppermute | solution.py:21
  77.1 3.5 %collective-permute-start.4 = (f32[2]{0:T(128)S(1)}, f32[2]{0:T(128)S(1)}, u32[]{:S(2)}, u32[]{:S(2)}) collective-permute-start(f32[2]{0:T(128)S(1)} %fusion.98), channel_id=1, source_target_pairs={{0,8},{8,0},{16,24},{24,16},{1,9},{9,1},{17,25},{25,17},{2,10},{10... | collective-permute-start | bytes 32 | tf_op jit(solution)/shard_map/ppermute | solution.py:32
  82.0 3.5 %collective-permute-start.5 = (f32[2]{0:T(128)S(1)}, f32[2]{0:T(128)S(1)}, u32[]{:S(2)}, u32[]{:S(2)}) collective-permute-start(f32[2]{0:T(128)S(1)} %fusion.100), channel_id=1, source_target_pairs={{0,16},{8,24},{16,0},{24,8},{1,17},{9,25},{17,1},{25,9},{2,18},{10... | collective-permute-start | bytes 32 | tf_op jit(solution)/shard_map/ppermute | solution.py:32
  86.4 1.3 copy-start.3
  103.0 16.8 %collective-permute-start.9 = (f32[131074]{0:T(1024)S(1)}, f32[131074]{0:T(1024)S(1)}, u32[]{:S(2)}, u32[]{:S(2)}) collective-permute-start(f32[131074]{0:T(1024)S(1)} %get-tuple-element.53), channel_id=1, source_target_pairs={{0,2},{2,4},{4,6},{6,0},{1,3},{3,5},{5,7},{7,1},{8,10},{10,12},{12... | collective-permute-start | bytes 1572896 | tf_op jit(solution)/shard_map/ppermute | solution.py:168
  103.5 36.0 %collective-permute-start.10 = (f32[131074]{0:T(1024)}, f32[131074]{0:T(1024)}, u32[]{:S(2)}, u32[]{:S(2)}) collective-permute-start(f32[131074]{0:T(1024)} %get-tuple-element.54), channel_id=1, source_target_pairs={{0,4},{2,6},{4,0},{6,2},{1,5},{3,7},{5,1},{7,3},{8,12},{10,14},{12... | collective-permute-start | bytes 1572896 | tf_op jit(solution)/shard_map/ppermute | solution.py:168
  104.1 37.5 %collective-permute-start.11 = (f32[131074]{0:T(1024)}, f32[131074]{0:T(1024)}, u32[]{:S(2)}, u32[]{:S(2)}) collective-permute-start(f32[131074]{0:T(1024)} %get-tuple-element.55), channel_id=1, source_target_pairs={{0,6},{2,0},{4,2},{6,4},{1,7},{3,1},{5,3},{7,5},{8,14},{10,8},{12,... | collective-permute-start | bytes 1572896 | tf_op jit(solution)/shard_map/ppermute | solution.py:168
  119.8 0.8 copy-start.12
  165.1 2.1 copy-start.5
  165.1 2.3 %copy-start.9 = (bf16[16,2,128,128]{2,3,1,0:T(8,128)(2,1)S(1)}, bf16[16,2,128,128]{2,3,1,0:T(8,128)(2,1)}, u32[]{:S(2)}) copy-start(bf16[16,2,128,128]{2,3,1,0:T(8,128)(2,1)} %gather_fusion.12) | copy-start | bytes 3145732
  167.4 1.2 copy-start.7
  175.2 1.1 collective-permute-start.12
  175.3 28.6 %collective-permute-start.17 = (f32[16,2,128]{2,1,0:T(2,128)S(1)}, f32[16,2,128]{2,1,0:T(2,128)S(1)}, u32[]{:S(2)}, u32[]{:S(2)}) collective-permute-start(f32[16,2,128]{2,1,0:T(2,128)S(1)} %select_bitcast_fusion), channel_id=1, source_target_pairs={{0,1},{1,0},{2,3},{3,2},{4,5},{5,4},{6,7},{7,6},{8,9},{9,8},{10,11... | collective-permute-start | bytes 49160 | tf_op jit(solution)/shard_map/ppermute | solution.py:21
  177.7 10.8 %collective-permute-start.13 = (f32[2]{0:T(128)S(1)}, f32[2]{0:T(128)S(1)}, u32[]{:S(2)}, u32[]{:S(2)}) collective-permute-start(f32[2]{0:T(128)S(1)} %fusion.97), channel_id=1, source_target_pairs={{0,2},{2,0},{4,6},{6,4},{1,3},{3,1},{5,7},{7,5},{8,10},{10,8},{12,... | collective-permute-start | bytes 32 | tf_op jit(solution)/shard_map/ppermute | solution.py:32
  189.8 4.4 %collective-permute-start.14 = (f32[2]{0:T(128)S(1)}, f32[2]{0:T(128)S(1)}, u32[]{:S(2)}, u32[]{:S(2)}) collective-permute-start(f32[2]{0:T(128)S(1)} %fusion.99), channel_id=1, source_target_pairs={{0,4},{2,6},{4,0},{6,2},{1,5},{3,7},{5,1},{7,3},{8,12},{10,14},{12... | collective-permute-start | bytes 32 | tf_op jit(solution)/shard_map/ppermute | solution.py:32
  194.3 3.5 %collective-permute-start.15 = (f32[2]{0:T(128)S(1)}, f32[2]{0:T(128)S(1)}, u32[]{:S(2)}, u32[]{:S(2)}) collective-permute-start(f32[2]{0:T(128)S(1)} %add.350), channel_id=1, source_target_pairs={{0,8},{8,0},{16,24},{24,16},{1,9},{9,1},{17,25},{25,17},{2,10},{10... | collective-permute-start | bytes 32 | tf_op jit(solution)/shard_map/ppermute | solution.py:32
  197.8 3.5 %collective-permute-start.16 = (f32[2]{0:T(128)S(1)}, f32[2]{0:T(128)S(1)}, u32[]{:S(2)}, u32[]{:S(2)}) collective-permute-start(f32[2]{0:T(128)S(1)} %add.351), channel_id=1, source_target_pairs={{0,16},{8,24},{16,0},{24,8},{1,17},{9,25},{17,1},{25,9},{2,18},{10... | collective-permute-start | bytes 32 | tf_op jit(solution)/shard_map/ppermute | solution.py:32
  204.7 2.3 %copy-start.1 = (f32[2,8]{1,0:T(2,128)S(1)}, f32[2,8]{1,0:T(2,128)}, u32[]{:S(2)}) copy-start(f32[2,8]{1,0:T(2,128)} %param.12) | copy-start | bytes 196

commit v4 on v3

--- a/solution.py
+++ b/solution.py
@@ -100,6 +100,48 @@
         ),
     )(*bands)
     return jnp.transpose(inverse, (1, 0, 2)).reshape(lead + (levels, levels)), ready
+
+
+def advect_kernel(index_ref, weight_ref, *refs):
+    tile_refs, out_ref = refs[:-1], refs[-1]
+    for field in range(out_ref.shape[1]):
+        total = None
+        for entry_k, tile_ref in enumerate(tile_refs):
+            term = jnp.dot(
+                weight_ref[0, entry_k], tile_ref[0, field], preferred_element_type=jnp.float32
+            )
+            total = term if total is None else total + term
+        out_ref[0, field] = total
+
+
+def advect(weights, tile_pool, pool_index):
+    tiles, sources = pool_index.shape
+    _, fields, columns, levels = tile_pool.shape
+    flat_index = pool_index.reshape(-1)
+
+    def source_spec(entry_k):
+        return pl.BlockSpec(
+            (1, fields, columns, levels),
+            lambda t, index, k=entry_k: (index[t * sources + k], 0, 0, 0),
+        )
+
+    return pl.pallas_call(
+        advect_kernel,
+        out_shape=jax.ShapeDtypeStruct((tiles, fields, columns, levels), jnp.float32),
+        grid_spec=pltpu.PrefetchScalarGridSpec(
+            num_scalar_prefetch=1,
+            grid=(tiles,),
+            in_specs=[pl.BlockSpec((1, sources, columns, columns), lambda t, index: (t, 0, 0, 0))]
+            + [source_spec(k) for k in range(sources)],
+            out_specs=pl.BlockSpec((1, fields, columns, levels), lambda t, index: (t, 0, 0, 0)),
+        ),
+        cost_estimate=pl.CostEstimate(
+            flops=2 * tiles * sources * fields * columns * columns * levels,
+            transcendentals=0,
+            bytes_accessed=tiles * sources * (columns * columns + fields * columns * levels) * 2
+            + tiles * fields * columns * levels * 4,
+        ),
+    )(flat_index, weights, *([tile_pool] * sources))
 
 
 def interface_values(low_value, low_spike, high_value, high_spike):
@@ -193,14 +235,7 @@
     ratios = []
     for step_index in range(STEPS):
         tile_pool = jnp.concatenate([fields, arrived], axis=0)
-        advected = jnp.zeros(fields.shape, jnp.float32)
-        for entry_k in range(sources_per):
-            advected = advected + jnp.einsum(
-                "tcd,tfdz->tfcz",
-                interp_weights[:, entry_k],
-                tile_pool[pool_index[:, entry_k]],
-                preferred_element_type=jnp.float32,
-            )
+        advected = advect(interp_weights, tile_pool, pool_index)
         partial = jnp.stack([jnp.sum(fields[:, 0], dtype=jnp.float32), jnp.sum(advected[:, 0])])
         last = step_index + 1 == STEPS
         if last:

time: 208 us -> 216 us (1.038)
  Pallas kernels: 9.26 us -> 34 us
  local copies, waits for them, and re-layouts: 70.9 us -> 46.8 us
  other arithmetic: 28 us -> 31.7 us
  waiting for transfers between devices: 45.3 us -> 48 us
    pallas_call x0 -> x2, Pallas kernels: none -> 24.7 us  [advect(): pl.pallas_call(advect_kernel, out_shape=jax.ShapeDtypeStruct((tiles, fiel...]
    gather x8 -> x0, local copies, waits for them, and re-layouts: 17.5 us -> none  [per_device(): tile_pool[pool_index[:, entry_k]]]
    dot_general x2, matrix products: 6.61 us -> 13.9 us  [per_device(): jnp.einsum('tfzy,tfcy->tfcz', inverse, advected, precision=HIGHEST, prefe...]
    dot_general x8 -> x0, matrix products: 6.92 us -> none  [per_device(): jnp.einsum('tcd,tfdz->tfcz', interp_weights[:, entry_k], tile_pool[pool_i...]
    dot_general x0 -> x2, local copies, waits for them, and re-layouts: none -> 4.82 us  [per_device(): jnp.einsum('tfzy,tfcy->tfcz', inverse, advected, precision=HIGHEST, prefe...]
    gather x9 -> x6, local copies, waits for them, and re-layouts: 15.2 us -> 12 us  [exchange(): block = tiles[lax.dynamic_index_in_dim(wanted, target, 0, keepdims=False)]]
    reshape x3 -> x0, local copies, waits for them, and re-layouts: 2.99 us -> none  [exchange(): r[:-tail].reshape(shape)]
    reduce_sum x2, other arithmetic: 1.73 us -> 4.2 us  [per_device(): jnp.sum(advected[:, 0])]
  transfers between devices with their start and end apart: 19 -> 19, of which waited for: 11 -> 11; matrix products, arithmetic and copies ran while one was open for 18% -> 16% of each run, Pallas kernels for 4% -> 4%
where the time goes in v4:
time: 216 us; the launch traced here: 215 us
  waiting for transfers between devices  48 us (22%)
  local copies, waits for them, and re-layouts  46.8 us (22%)
  starting transfers between devices  35.8 us (17%)
  Pallas kernels  34 us (16%)
  other arithmetic  31.7 us (15%)
  matrix products  14.6 us (7%)
  between operations  3.74 us (2%)
    ppermute x6, waiting for transfers between devices, exchange(): lax.ppermute(block, 'gy', [(i, (i + hop) % lane_count) for i in range(lan...  32.6 us
    pallas_call x2, Pallas kernels, advect(): pl.pallas_call(advect_kernel, out_shape=jax.ShapeDtypeStruct((tiles, fiel...  24.7 us
    ppermute x8, starting transfers between devices, butterfly_sum(): lax.ppermute(value, axis, [(i, i ^ bit) for i in range(devices)])  17.5 us
    ppermute x8, waiting for transfers between devices, butterfly_sum(): lax.ppermute(value, axis, [(i, i ^ bit) for i in range(devices)])  14.3 us
    dot_general x2, matrix products, per_device(): jnp.einsum('tfzy,tfcy->tfcz', inverse, advected, precision=HIGHEST, prefe...  13.9 us
    gather x6, local copies, waits for them, and re-layouts, exchange(): block = tiles[lax.dynamic_index_in_dim(wanted, target, 0, keepdims=False)]  12 us
    unnamed x28, local copies, waits for them, and re-layouts  10.7 us
    ppermute x6, starting transfers between devices, exchange(): lax.ppermute(block, 'gy', [(i, (i + hop) % lane_count) for i in range(lan...  9.78 us
  transfers between devices with their start and end apart: 19, of which 11 were waited for; matrix products, arithmetic and copies ran while one was open for 16% of the time, Pallas kernels for 4%

profile of v4, /device:TPU:0, one launch (start us, length us, event | category | flops | bytes accessed | tf_op | source)
XLA Modules:
  0.0 214.6 jit_solution(6316513247251171897)
XLA Ops:
  1.4 1.3 collective-permute-start.6
  2.6 0.8 copy.88
  5.2 6.3 %all-to-all-start = ((s32[4,1,4]{2,1,0:T(1,128)}), s32[4,1,4]{2,1,0:T(1,128)S(1)}, u32[]{:S(2)}, u32[]{:S(2)}) async-start(s32[4,1,4]{2,1,0:T(1,128)} %bitcast.4), calls=%async_computation | async-start | bytes 4096 | tf_op jit(solution)/shard_map/all_to_all | solution.py:200
  12.3 2.0 convert_reduce_fusion.1
  14.7 1.3 pad_maximum_fusion.3
  17.5 1.3 gather_fusion.2
  18.8 1.3 gather_fusion.1
  20.1 1.3 gather_fusion
  21.4 2.0 collective-permute-start
  23.4 2.4 %collective-permute-start.1 = (bf16[4,2,128,128]{3,2,1,0:T(8,128)(2,1)}, bf16[4,2,128,128]{3,2,1,0:T(8,128)(2,1)}, u32[]{:S(2)}, u32[]{:S(2)}) collective-permute-start(bf16[4,2,128,128]{3,2,1,0:T(8,128)(2,1)} %gather_fusion.1), channel_id=1, source_target_pairs={{0,4},{2,6},{4,0},{6,2},{1,5},{3,7},{5,1},{7,3},{8,12},{10,14},{12... | collective-permute-start | bytes 786440 | tf_op jit(solution)/shard_map/ppermute | solution.py:210
  25.7 1.5 collective-permute-start.2
  27.2 2.8 %copy.95.lower_ref = f32[128,32,1]{2,1,0:T(8,128)} copy(f32[128,32,1]{0,1,2:T(8,128)S(1)} %bitcast.174) | data formatting | bytes 32768 | tf_op jit(solution)/shard_map/optimization_barrier | solution.py:89
  30.0 2.9 %copy.96.diagonal_ref = f32[128,32,1]{2,1,0:T(8,128)} copy(f32[128,32,1]{0,1,2:T(8,128)S(1)} %bitcast.173) | data formatting | bytes 32768 | tf_op jit(solution)/shard_map/optimization_barrier | solution.py:89
  32.9 2.9 %copy.97.upper_ref = f32[128,32,1]{2,1,0:T(8,128)} copy(f32[128,32,1]{0,1,2:T(8,128)S(1)} %fusion.19) | data formatting | bytes 32768 | tf_op jit(solution)/shard_map/optimization_barrier | solution.py:89
  35.8 9.3 %shard_map.95 = f32[128,32,128]{2,1,0:T(8,128)} custom-call(f32[128,32,1]{2,1,0:T(8,128)} %copy.95.lower_ref, f32[128,32,1]{2,1,0:T(8,128)} %copy.96.diagonal_ref, f32[128,32,1]{2,1,0:T(8,128)} %copy.97.upper_ref), custom_call_target="tpu_custom_call" | custom-call | flops 8388608 | bytes 33554432 | tf_op jit(solution)/shard_map/pallas_call | solution.py:92
  45.1 5.8 %fusion.51 = (f32[16,2,128,1]{3,1,0,2:T(2,128)}, f32[16,2,128,1]{3,1,0,2:T(2,128)S(1)}) fusion(f32[16,2,128,128]{3,1,0,2:T(2,128)} %bitcast.149), kind=kLoop, calls=%fused_computation.151 | loop fusion | bytes 65536 | tf_op jit(solution)/shard_map/slice | solution.py:228
  50.9 2.8 %copy.115 = f32[16,2,128,1]{2,1,0,3:T(2,128)S(1)} copy(f32[16,2,128,1]{3,1,0,2:T(2,128)} %get-tuple-element.24) | data formatting | bytes 32768
  53.7 1.1 copy.116
  55.1 1.1 collective-permute-done.8
  56.5 2.6 %pad_maximum_fusion.1.refs_0_.refs_1_.refs_2_.refs_3_ = bf16[28,2,128,128]{3,2,1,0:T(8,128)(2,1)} fusion(bf16[4,2,128,128]{3,2,1,0:T(8,128)(2,1)} %collective-permute-done.2, bf16[4,2,128,128]{3,2,1,0:T(8,128)(2,1)} %collective-permute-done.1, bf16[4,2,128,128]{3,2,1,0:T(8,128)(2,1)S(1)} %collective-permute-done, bf16[16,1,128,128]{3,2,1,0:T(8,128)(2,1)S(1)} %bitcast.155, ...), kind=kLoop, calls=%fused_computation.14 | loop fusion | flops 3670016 | bytes 3670016 | tf_op jit(solution)/shard_map/concatenate | solution.py:237
  59.1 12.3 %shard_map.94 = f32[16,2,128,128]{3,2,1,0:T(8,128)} custom-call(s32[64]{0:T(128)} %get-tuple-element.18.index_ref, bf16[16,4,128,128]{3,2,1,0:T(8,128)(2,1)} %weight_ref.3, bf16[28,2,128,128]{3,2,1,0:T(8,128)(2,1)} %pad_maximum_fusion.1.refs_0_.refs_1_.refs_2_.refs_3_, bf16[28,2,128,128]{3,2,1,0:T(8,128)(2,1)} %pad_maximum_fusion.1.refs_0_.refs_1_.refs_2_.refs_3_, ...), custom_call_target="tpu_custom_call" | custom-call | flops 536870912 | bytes 8388608 | tf_op jit(solution)/shard_map/pallas_call | solution.py:128
  71.5 2.1 slice_reduce_fusion.1
  73.6 6.9 %fusion.2 = f32[16,2,128,128]{2,3,1,0:T(8,128)S(1)} fusion(f32[16,2,128,128]{3,2,1,0:T(8,128)} %shard_map.94, f32[16,2,128,128]{3,1,0,2:T(2,128)S(1)} %bitcast.150), kind=kOutput, calls=%fused_computation.12 | convolution fusion | flops 805306368 | bytes 6291456 | tf_op jit(solution)/shard_map/tfzy,tfcy->tfcz/dot_general | solution.py:245
  80.5 1.3 copy-done.4
  81.8 2.9 %copy.110 = f32[16,2,128,128]{3,2,1,0:T(8,128)} copy(f32[16,2,128,128]{2,3,1,0:T(8,128)} %copy-done.4) | data formatting | bytes 4194304 | tf_op jit(solution)/shard_map/tfzy,tfcy->tfcz/dot_general | solution.py:245
  84.7 1.4 pad_maximum_fusion.9
  87.3 1.4 fusion.59
  88.7 1.5 collective-permute-start.4
  90.1 2.1 collective-permute-done.4
  92.2 1.4 fusion.61
  93.6 1.5 collective-permute-start.5
  95.1 2.0 collective-permute-done.5
  97.3 1.9 multiply_subtract_fusion.1
  99.5 1.0 copy-done.2
  100.6 1.4 pad_maximum_fusion
  102.0 2.2 %gather_fusion.5 = f32[4,2,128,128]{3,2,1,0:T(8,128)S(1)} fusion(f32[16,2,128,128]{3,2,1,0:T(8,128)} %pad_maximum_fusion, s32[1024]{0:T(1024)S(1)} %pad_clamp_fusion.1), kind=kCustom, calls=%fused_computation.5 | custom fusion | bytes 1048592 | tf_op jit(solution)/shard_map/gather | solution.py:206
  104.2 3.0 %gather_fusion.4 = f32[4,2,128,128]{3,2,1,0:T(8,128)} fusion(f32[16,2,128,128]{3,2,1,0:T(8,128)} %pad_maximum_fusion, s32[1024]{0:T(1024)S(1)} %pad_clamp_fusion.2), kind=kCustom, calls=%fused_computation.4 | custom fusion | bytes 1048592 | tf_op jit(solution)/shard_map/gather | solution.py:206
  107.1 3.0 %gather_fusion.3 = f32[4,2,128,128]{3,2,1,0:T(8,128)} fusion(f32[16,2,128,128]{3,2,1,0:T(8,128)} %pad_maximum_fusion, s32[1024]{0:T(1024)S(1)} %pad_clamp_fusion.3), kind=kCustom, calls=%fused_computation.3 | custom fusion | bytes 1048592 | tf_op jit(solution)/shard_map/gather | solution.py:206
  110.1 1.4 pad_maximum_fusion.6
  112.6 2.8 %collective-permute-start.11 = (f32[131074]{0:T(1024)S(1)}, f32[131074]{0:T(1024)S(1)}, u32[]{:S(2)}, u32[]{:S(2)}) collective-permute-start(f32[131074]{0:T(1024)S(1)} %get-tuple-element.41), channel_id=1, source_target_pairs={{0,6},{2,0},{4,2},{6,4},{1,7},{3,1},{5,3},{7,5},{8,14},{10,8},{12,... | collective-permute-start | bytes 1572896 | tf_op jit(solution)/shard_map/ppermute | solution.py:210
  115.4 12.9 %collective-permute-done.9 = f32[131074]{0:T(1024)S(1)} collective-permute-done((f32[131074]{0:T(1024)S(1)}, f32[131074]{0:T(1024)S(1)}, u32[]{:S(2)}, u32[]{:S(2)}) %collective-permute-start.9) | collective-permute-done | bytes 524328 | tf_op jit(solution)/shard_map/ppermute | solution.py:210
  128.3 19.7 %collective-permute-done.10 = f32[131074]{0:T(1024)S(1)} collective-permute-done((f32[131074]{0:T(1024)S(1)}, f32[131074]{0:T(1024)S(1)}, u32[]{:S(2)}, u32[]{:S(2)}) %collective-permute-start.10) | collective-permute-done | bytes 524328 | tf_op jit(solution)/shard_map/ppermute | solution.py:210
  148.0 0.8 copy-done.7
  148.8 0.8 copy-done.9
  152.1 2.1 convert_reduce_fusion
  154.7 1.4 maximum_maximum_fusion.refs_0_.refs_1_.refs_2_.refs_3_
  156.1 12.4 %shard_map.96 = f32[16,2,128,128]{3,2,1,0:T(8,128)} custom-call(s32[64]{0:T(128)} %get-tuple-element.18.index_ref, bf16[16,4,128,128]{3,2,1,0:T(8,128)(2,1)} %weight_ref.3, bf16[28,2,128,128]{3,2,1,0:T(8,128)(2,1)} %maximum_maximum_fusion.refs_0_.refs_1_.refs_2_.refs_3_, bf16[28,2,128,128]{3,2,1,0:T(8,128)(2,1)} %maximum_maximum_fusion.refs_0_.refs_1_.refs_2_.refs_3_, ...), custom_call_target="tpu_custom_call" | custom-call | flops 536870912 | bytes 8388608 | tf_op jit(solution)/shard_map/pallas_call | solution.py:128
  168.5 2.1 slice_reduce_fusion
  170.6 6.9 %fusion = f32[16,2,128,128]{2,3,1,0:T(8,128)S(1)} fusion(f32[16,2,128,128]{3,2,1,0:T(8,128)} %shard_map.96, f32[16,2,128,128]{3,1,0,2:T(2,128)S(1)} %bitcast.151), kind=kOutput, calls=%fused_computation.10 | convolution fusion | flops 805306368 | bytes 6291456 | tf_op jit(solution)/shard_map/tfzy,tfcy->tfcz/dot_general | solution.py:245
  177.5 1.3 copy-done.3
  178.9 1.9 copy.114
  180.8 1.4 pad_maximum_fusion.10
  183.3 1.4 fusion.58
  184.7 10.3 %collective-permute-start.13 = (f32[2]{0:T(128)S(1)}, f32[2]{0:T(128)S(1)}, u32[]{:S(2)}, u32[]{:S(2)}) collective-permute-start(f32[2]{0:T(128)S(1)} %fusion.58), channel_id=1, source_target_pairs={{0,2},{2,0},{4,6},{6,4},{1,3},{3,1},{5,7},{7,5},{8,10},{10,8},{12,... | collective-permute-start | bytes 32 | tf_op jit(solution)/shard_map/ppermute | solution.py:32
  195.0 1.5 collective-permute-done.13
  196.5 1.4 fusion.60
  197.9 1.0 collective-permute-start.14
  198.9 3.4 %collective-permute-done.14 = f32[2]{0:T(128)S(1)} collective-permute-done((f32[2]{0:T(128)S(1)}, f32[2]{0:T(128)S(1)}, u32[]{:S(2)}, u32[]{:S(2)}) %collective-permute-start.14) | collective-permute-done | bytes 40 | tf_op jit(solution)/shard_map/ppermute | solution.py:32
  202.3 1.5 collective-permute-start.15
  203.8 2.1 collective-permute-done.15
  205.9 1.5 collective-permute-start.16
  207.4 2.0 collective-permute-done.16
  212.8 0.9 fusion.10
  213.7 0.9 fusion.9
  (109 shorter events, 13.1 us)
Async XLA Ops:
  0.6 13.8 %copy-start = (f32[2,8]{1,0:T(2,128)S(1)}, f32[2,8]{1,0:T(2,128)}, u32[]{:S(2)}) copy-start(f32[2,8]{1,0:T(2,128)} %param.12) | copy-start | bytes 196
  0.6 15.6 %copy-start.11 = (f32[8]{0:T(128)S(1)}, f32[8]{0:T(128)}, u32[]{:S(2)}) copy-start(f32[8]{0:T(128)} %param.13) | copy-start | bytes 100
  1.4 14.6 %collective-permute-start.6 = (s32[16,1]{0,1:T(1,128)S(1)}, s32[16,1]{0,1:T(1,128)S(1)}, u32[]{:S(2)}, u32[]{:S(2)}) collective-permute-start(s32[16,1]{0,1:T(1,128)S(1)} %slice.113), channel_id=1, source_target_pairs={{1,0},{3,2},{5,4},{7,6},{9,8},{11,10},{13,12},{15,14},{17,16},{19,... | collective-permute-start | bytes 200 | tf_op jit(solution)/shard_map/ppermute | solution.py:17
  5.2 12.2 %all-to-all-start = ((s32[4,1,4]{2,1,0:T(1,128)}), s32[4,1,4]{2,1,0:T(1,128)S(1)}, u32[]{:S(2)}, u32[]{:S(2)}) async-start(s32[4,1,4]{2,1,0:T(1,128)} %bitcast.4), calls=%async_computation | async-start | bytes 4096 | tf_op jit(solution)/shard_map/all_to_all | solution.py:200
  21.4 35.2 %collective-permute-start = (bf16[4,2,128,128]{3,2,1,0:T(8,128)(2,1)}, bf16[4,2,128,128]{3,2,1,0:T(8,128)(2,1)S(1)}, u32[]{:S(2)}, u32[]{:S(2)}) collective-permute-start(bf16[4,2,128,128]{3,2,1,0:T(8,128)(2,1)} %gather_fusion), channel_id=1, source_target_pairs={{0,2},{2,4},{4,6},{6,0},{1,3},{3,5},{5,7},{7,1},{8,10},{10,12},{12... | collective-permute-start | bytes 786440 | tf_op jit(solution)/shard_map/ppermute | solution.py:210
  23.4 33.1 %collective-permute-start.1 = (bf16[4,2,128,128]{3,2,1,0:T(8,128)(2,1)}, bf16[4,2,128,128]{3,2,1,0:T(8,128)(2,1)}, u32[]{:S(2)}, u32[]{:S(2)}) collective-permute-start(bf16[4,2,128,128]{3,2,1,0:T(8,128)(2,1)} %gather_fusion.1), channel_id=1, source_target_pairs={{0,4},{2,6},{4,0},{6,2},{1,5},{3,7},{5,1},{7,3},{8,12},{10,14},{12... | collective-permute-start | bytes 786440 | tf_op jit(solution)/shard_map/ppermute | solution.py:210
  25.7 30.8 %collective-permute-start.2 = (bf16[4,2,128,128]{3,2,1,0:T(8,128)(2,1)}, bf16[4,2,128,128]{3,2,1,0:T(8,128)(2,1)}, u32[]{:S(2)}, u32[]{:S(2)}) collective-permute-start(bf16[4,2,128,128]{3,2,1,0:T(8,128)(2,1)} %gather_fusion.2), channel_id=1, source_target_pairs={{0,6},{2,0},{4,2},{6,4},{1,7},{3,1},{5,3},{7,5},{8,14},{10,8},{12,... | collective-permute-start | bytes 786440 | tf_op jit(solution)/shard_map/ppermute | solution.py:210
  50.9 5.6 %copy-start.5 = (bf16[16,128,128]{2,1,0:T(8,128)(2,1)S(1)}, bf16[16,128,128]{2,1,0:T(8,128)(2,1)}, u32[]{:S(2)}) copy-start(bf16[16,128,128]{2,1,0:T(8,128)(2,1)} %param.7) | copy-start | bytes 1572868
  50.9 5.6 %copy-start.6 = (bf16[16,128,128]{2,1,0:T(8,128)(2,1)S(1)}, bf16[16,128,128]{2,1,0:T(8,128)(2,1)}, u32[]{:S(2)}) copy-start(bf16[16,128,128]{2,1,0:T(8,128)(2,1)} %param.8) | copy-start | bytes 1572868
  55.1 1.1 collective-permute-start.8
  59.1 14.4 %copy-start.1 = (f32[128,32,128]{2,1,0:T(8,128)S(1)}, f32[128,32,128]{2,1,0:T(8,128)}, u32[]{:S(2)}) copy-start(f32[128,32,128]{2,1,0:T(8,128)} %shard_map.95) | copy-start | bytes 6291460
  80.5 1.3 copy-start.4
  86.1 1.1 collective-permute-start.3
  86.3 10.8 %collective-permute-start.7 = (f32[16,2,128]{2,1,0:T(2,128)S(1)}, f32[16,2,128]{2,1,0:T(2,128)S(1)}, u32[]{:S(2)}, u32[]{:S(2)}) collective-permute-start(f32[16,2,128]{2,1,0:T(2,128)S(1)} %bitcast.169), channel_id=1, source_target_pairs={{0,1},{1,0},{2,3},{3,2},{4,5},{5,4},{6,7},{7,6},{8,9},{9,8},{10,11... | collective-permute-start | bytes 49160 | tf_op jit(solution)/shard_map/ppermute | solution.py:21
  88.7 3.5 %collective-permute-start.4 = (f32[2]{0:T(128)S(1)}, f32[2]{0:T(128)S(1)}, u32[]{:S(2)}, u32[]{:S(2)}) collective-permute-start(f32[2]{0:T(128)S(1)} %fusion.59), channel_id=1, source_target_pairs={{0,8},{8,0},{16,24},{24,16},{1,9},{9,1},{17,25},{25,17},{2,10},{10... | collective-permute-start | bytes 32 | tf_op jit(solution)/shard_map/ppermute | solution.py:32
  93.6 3.5 %collective-permute-start.5 = (f32[2]{0:T(128)S(1)}, f32[2]{0:T(128)S(1)}, u32[]{:S(2)}, u32[]{:S(2)}) collective-permute-start(f32[2]{0:T(128)S(1)} %fusion.61), channel_id=1, source_target_pairs={{0,16},{8,24},{16,0},{24,8},{1,17},{9,25},{17,1},{25,9},{2,18},{10... | collective-permute-start | bytes 32 | tf_op jit(solution)/shard_map/ppermute | solution.py:32
  99.2 1.3 copy-start.2
  111.5 16.9 %collective-permute-start.9 = (f32[131074]{0:T(1024)S(1)}, f32[131074]{0:T(1024)S(1)}, u32[]{:S(2)}, u32[]{:S(2)}) collective-permute-start(f32[131074]{0:T(1024)S(1)} %get-tuple-element.39), channel_id=1, source_target_pairs={{0,2},{2,4},{4,6},{6,0},{1,3},{3,5},{5,7},{7,1},{8,10},{10,12},{12... | collective-permute-start | bytes 1572896 | tf_op jit(solution)/shard_map/ppermute | solution.py:210
  112.1 35.9 %collective-permute-start.10 = (f32[131074]{0:T(1024)S(1)}, f32[131074]{0:T(1024)S(1)}, u32[]{:S(2)}, u32[]{:S(2)}) collective-permute-start(f32[131074]{0:T(1024)S(1)} %get-tuple-element.40), channel_id=1, source_target_pairs={{0,4},{2,6},{4,0},{6,2},{1,5},{3,7},{5,1},{7,3},{8,12},{10,14},{12... | collective-permute-start | bytes 1572896 | tf_op jit(solution)/shard_map/ppermute | solution.py:210
  112.6 35.4 %collective-permute-start.11 = (f32[131074]{0:T(1024)S(1)}, f32[131074]{0:T(1024)S(1)}, u32[]{:S(2)}, u32[]{:S(2)}) collective-permute-start(f32[131074]{0:T(1024)S(1)} %get-tuple-element.41), channel_id=1, source_target_pairs={{0,6},{2,0},{4,2},{6,4},{1,7},{3,1},{5,3},{7,5},{8,14},{10,8},{12,... | collective-permute-start | bytes 1572896 | tf_op jit(solution)/shard_map/ppermute | solution.py:210
  148.0 0.8 copy-start.7
  148.8 0.8 copy-start.9
  150.1 4.1 %copy-start.8 = (f32[131074]{0:T(1024)S(1)}, f32[131074]{0:T(1024)}, u32[]{:S(2)}) copy-start(f32[131074]{0:T(1024)} %copy-done.7) | copy-start | bytes 1572892
  150.2 4.2 %copy-start.10 = (f32[131074]{0:T(1024)S(1)}, f32[131074]{0:T(1024)}, u32[]{:S(2)}) copy-start(f32[131074]{0:T(1024)} %copy-done.9) | copy-start | bytes 1572892
  177.5 1.3 copy-start.3
  182.2 1.1 collective-permute-start.12
  182.2 29.7 %collective-permute-start.17 = (f32[16,2,128]{2,1,0:T(2,128)S(1)}, f32[16,2,128]{2,1,0:T(2,128)S(1)}, u32[]{:S(2)}, u32[]{:S(2)}) collective-permute-start(f32[16,2,128]{2,1,0:T(2,128)S(1)} %select_bitcast_fusion), channel_id=1, source_target_pairs={{0,1},{1,0},{2,3},{3,2},{4,5},{5,4},{6,7},{7,6},{8,9},{9,8},{10,11... | collective-permute-start | bytes 49160 | tf_op jit(solution)/shard_map/ppermute | solution.py:21
  184.7 11.8 %collective-permute-start.13 = (f32[2]{0:T(128)S(1)}, f32[2]{0:T(128)S(1)}, u32[]{:S(2)}, u32[]{:S(2)}) collective-permute-start(f32[2]{0:T(128)S(1)} %fusion.58), channel_id=1, source_target_pairs={{0,2},{2,0},{4,6},{6,4},{1,3},{3,1},{5,7},{7,5},{8,10},{10,8},{12,... | collective-permute-start | bytes 32 | tf_op jit(solution)/shard_map/ppermute | solution.py:32
  197.9 4.4 %collective-permute-start.14 = (f32[2]{0:T(128)S(1)}, f32[2]{0:T(128)S(1)}, u32[]{:S(2)}, u32[]{:S(2)}) collective-permute-start(f32[2]{0:T(128)S(1)} %fusion.60), channel_id=1, source_target_pairs={{0,4},{2,6},{4,0},{6,2},{1,5},{3,7},{5,1},{7,3},{8,12},{10,14},{12... | collective-permute-start | bytes 32 | tf_op jit(solution)/shard_map/ppermute | solution.py:32
  202.3 3.5 %collective-permute-start.15 = (f32[2]{0:T(128)S(1)}, f32[2]{0:T(128)S(1)}, u32[]{:S(2)}, u32[]{:S(2)}) collective-permute-start(f32[2]{0:T(128)S(1)} %add.277), channel_id=1, source_target_pairs={{0,8},{8,0},{16,24},{24,16},{1,9},{9,1},{17,25},{25,17},{2,10},{10... | collective-permute-start | bytes 32 | tf_op jit(solution)/shard_map/ppermute | solution.py:32
  205.9 3.5 %collective-permute-start.16 = (f32[2]{0:T(128)S(1)}, f32[2]{0:T(128)S(1)}, u32[]{:S(2)}, u32[]{:S(2)}) collective-permute-start(f32[2]{0:T(128)S(1)} %add.278), channel_id=1, source_target_pairs={{0,16},{8,24},{16,0},{24,8},{1,17},{9,25},{17,1},{25,9},{2,18},{10... | collective-permute-start | bytes 32 | tf_op jit(solution)/shard_map/ppermute | solution.py:32

commit v5 on v3

--- a/solution.py
+++ b/solution.py
@@ -132,9 +132,8 @@
         & (slot_index[None, None, :] == jnp.arange(capacity, dtype=jnp.int32)[None, :, None])
     )
     requests = jnp.sum(jnp.where(match, local_tile[None, None, :], 0), axis=-1, dtype=jnp.int32)
-    shift = (my_lane - owner_lane) % lane_count
     pool_index = jnp.where(
-        remote, tiles_here + (shift - 1) * capacity + slot_index, local_tile
+        remote, tiles_here + owner_lane * capacity + slot_index, local_tile
     ).reshape(tiles_here, sources_per)
     level_class = jnp.repeat(settle_class, levels // settle_class.shape[1], axis=1)
     both_fall = jnp.stack([fall_table, jnp.zeros_like(fall_table)])
@@ -157,29 +156,11 @@
     fields = jnp.stack([concentration, turbulence], axis=1)
     wanted = lax.all_to_all(requests, "gy", split_axis=0, concat_axis=0, tiled=True)
 
-    def exchange(tiles, extra=None):
-        received = []
-        for hop in range(1, lane_count):
-            target = (my_lane + hop) % lane_count
-            block = tiles[lax.dynamic_index_in_dim(wanted, target, 0, keepdims=False)]
-            if extra is not None:
-                block = jnp.concatenate([block.reshape(-1), extra])
-            received.append(
-                lax.ppermute(block, "gy", [(i, (i + hop) % lane_count) for i in range(lane_count)])
-            )
-        if extra is None:
-            return jnp.concatenate(received, axis=0), None
-        tail = extra.shape[0]
-        shape = (-1,) + tiles.shape[1:]
-        tiles_in = jnp.concatenate([r[:-tail].reshape(shape) for r in received], axis=0)
-        extras_in = jnp.stack([extra] + [r[-tail:] for r in received])
-        by_lane = extras_in[(my_lane - jnp.arange(lane_count)) % lane_count]
-        total = by_lane[0]
-        for lane in range(1, lane_count):
-            total = total + by_lane[lane]
-        return tiles_in, total
-
-    arrived, _ = exchange(fields)
+    def exchange(tiles):
+        sent = lax.all_to_all(tiles[wanted], "gy", split_axis=0, concat_axis=0, tiled=True)
+        return sent.reshape((-1,) + tiles.shape[1:])
+
+    arrived = exchange(fields)
     inverse, wanted = block_inverse(block_lower, diagonal, block_upper, wanted)
     spike_column = jnp.where(
         my_layer == 0,
@@ -201,12 +182,11 @@
                 tile_pool[pool_index[:, entry_k]],
                 preferred_element_type=jnp.float32,
             )
-        partial = jnp.stack([jnp.sum(fields[:, 0], dtype=jnp.float32), jnp.sum(advected[:, 0])])
         last = step_index + 1 == STEPS
-        if last:
-            totals = butterfly_sum(partial, ("gz", "gy", "gx"))
-        else:
-            partial = butterfly_sum(partial, ("gz", "gx"))
+        totals = butterfly_sum(
+            jnp.stack([jnp.sum(fields[:, 0], dtype=jnp.float32), jnp.sum(advected[:, 0])]),
+            ("gz", "gy", "gx"),
+        )
         solved = jnp.einsum(
             "tfzy,tfcy->tfcz",
             inverse,
@@ -223,19 +203,13 @@
         unscaled = solved - spike_column[:, :, None, :] * needed[..., None]
         next_turbulence = unscaled[:, 1].astype(jnp.bfloat16)
         if not last:
-            sent, totals = exchange(
-                jnp.stack([unscaled[:, 0], next_turbulence.astype(jnp.float32)], axis=1), partial
-            )
+            arrived_turbulence = exchange(next_turbulence)
         mass_fixer = totals[0] / totals[1]
         ratios.append(mass_fixer)
+        next_concentration = (mass_fixer * unscaled[:, 0]).astype(jnp.bfloat16)
         if not last:
-            arrived = jnp.stack(
-                [(mass_fixer * sent[:, 0]).astype(jnp.bfloat16), sent[:, 1].astype(jnp.bfloat16)],
-                axis=1,
-            )
-        fields = jnp.stack(
-            [(mass_fixer * unscaled[:, 0]).astype(jnp.bfloat16), next_turbulence], axis=1
-        )
+            arrived = jnp.stack([exchange(next_concentration), arrived_turbulence], axis=1)
+        fields = jnp.stack([next_concentration, next_turbulence], axis=1)
     return (fields[:, 0], fields[:, 1], jnp.stack(ratios))
 
 

time: 208 us -> 175 us (0.84)
  local copies, waits for them, and re-layouts: 70.9 us -> 56 us
  waiting for transfers between devices: 45.3 us -> 32.2 us
  other arithmetic: 28 us -> 22.4 us
    ppermute x6 -> x0, waiting for transfers between devices: 30.9 us -> none  [exchange(): lax.ppermute(block, 'gy', [(i, (i + hop) % lane_count) for i in range(lan...]
    all_to_all x0 -> x3, starting transfers between devices: none -> 14.5 us  [exchange(): lax.all_to_all(tiles[wanted], 'gy', split_axis=0, concat_axis=0, tiled=True)]
    gather x10 -> x4, local copies, waits for them, and re-layouts: 15.8 us -> 4.6 us  [exchange(): tiles[wanted]]
    ppermute x6 -> x0, starting transfers between devices: 9.67 us -> none  [exchange(): lax.ppermute(block, 'gy', [(i, (i + hop) % lane_count) for i in range(lan...]
    ppermute x8 -> x10, waiting for transfers between devices: 13.3 us -> 22.4 us  [butterfly_sum(): lax.ppermute(value, axis, [(i, i ^ bit) for i in range(devices)])]
    all_to_all x0 -> x3, waiting for transfers between devices: none -> 8.84 us  [exchange(): lax.all_to_all(tiles[wanted], 'gy', split_axis=0, concat_axis=0, tiled=True)]
    ppermute x8 -> x10, starting transfers between devices: 17.3 us -> 12.6 us  [butterfly_sum(): lax.ppermute(value, axis, [(i, i ^ bit) for i in range(devices)])]
    concatenate x2 -> x0, other arithmetic: 3.89 us -> none  [the longest x1 2.43 us: exchange(): block = jnp.concatenate([block.reshape(-1), extra])]
  transfers between devices with their start and end apart: 19 -> 18, of which waited for: 11 -> 12; matrix products, arithmetic and copies ran while one was open for 18% -> 24% of each run, Pallas kernels for 4% -> 5%
where the time goes in v5:
time: 175 us; the launch traced here: 174 us
  local copies, waits for them, and re-layouts  56 us (32%)
  starting transfers between devices  35.9 us (21%)
  waiting for transfers between devices  32.2 us (18%)
  other arithmetic  22.4 us (13%)
  matrix products  14.2 us (8%)
  Pallas kernels  9.14 us (5%)
  between operations  3.77 us (2%)
    ppermute x10, waiting for transfers between devices, butterfly_sum(): lax.ppermute(value, axis, [(i, i ^ bit) for i in range(devices)])  22.4 us
    gather x8, local copies, waits for them, and re-layouts, per_device(): tile_pool[pool_index[:, entry_k]]  17.8 us
    all_to_all x3, starting transfers between devices, exchange(): lax.all_to_all(tiles[wanted], 'gy', split_axis=0, concat_axis=0, tiled=True)  14.5 us
    ppermute x10, starting transfers between devices, butterfly_sum(): lax.ppermute(value, axis, [(i, i ^ bit) for i in range(devices)])  12.6 us
    unnamed x30, local copies, waits for them, and re-layouts  12.1 us
    pallas_call x1, Pallas kernels, block_inverse(): pl.pallas_call(thomas_inverse_kernel, out_shape=jax.ShapeDtypeStruct((lev...  9.14 us
    all_to_all x3, waiting for transfers between devices, exchange(): lax.all_to_all(tiles[wanted], 'gy', split_axis=0, concat_axis=0, tiled=True)  8.84 us
    optimization_barrier x3, local copies, waits for them, and re-layouts, block_inverse(): lax.optimization_barrier(((level_major(lower), level_major(diagonal), lev...  8.6 us
  transfers between devices with their start and end apart: 18, of which 12 were waited for; matrix products, arithmetic and copies ran while one was open for 24% of the time, Pallas kernels for 5%

profile of v5, /device:TPU:0, one launch (start us, length us, event | category | flops | bytes accessed | tf_op | source)
XLA Modules:
  0.0 173.6 jit_solution(6346876872932801893)
XLA Ops:
  1.4 1.3 collective-permute-start.5
  2.6 0.8 copy.167
  4.6 6.3 %all-to-all-start = ((s32[4,1,4]{2,1,0:T(1,128)}), s32[4,1,4]{2,1,0:T(1,128)S(1)}, u32[]{:S(2)}, u32[]{:S(2)}) async-start(s32[4,1,4]{2,1,0:T(1,128)} %bitcast.4), calls=%async_computation | async-start | bytes 4096 | tf_op jit(solution)/shard_map/all_to_all | solution.py:157
  11.0 0.8 copy.183
  11.8 1.9 %convert_reduce_fusion.1 = f32[]{:T(128)} fusion(bf16[16,128,128]{2,1,0:T(8,128)(2,1)} %param.7), kind=kLoop, calls=%fused_computation.38 | loop fusion | flops 524287 | bytes 524292 | tf_op jit(solution)/shard_map/reduce_sum | solution.py:187
  14.2 1.3 pad_maximum_fusion.1
  17.9 1.0 copy.169
  19.0 5.1 %all-to-all-start.1 = ((bf16[4,4,2,128,128]{4,3,1,2,0:T(8,128)(2,1)}), bf16[4,4,2,128,128]{4,3,1,2,0:T(8,128)(2,1)}, u32[]{:S(2)}, u32[]{:S(2)}) async-start(bf16[4,4,2,128,128]{4,3,1,2,0:T(8,128)(2,1)} %copy.169), calls=%async_computation.1 | async-start | bytes 2097152 | tf_op jit(solution)/shard_map/all_to_all | solution.py:160
  24.2 2.8 %copy.188.lower_ref = f32[128,32,1]{2,1,0:T(8,128)} copy(f32[128,32,1]{0,1,2:T(8,128)S(1)} %bitcast.175) | data formatting | bytes 32768 | tf_op jit(solution)/shard_map/optimization_barrier | solution.py:89
  27.1 2.9 %copy.189.diagonal_ref = f32[128,32,1]{2,1,0:T(8,128)} copy(f32[128,32,1]{0,1,2:T(8,128)S(1)} %bitcast.174) | data formatting | bytes 32768 | tf_op jit(solution)/shard_map/optimization_barrier | solution.py:89
  30.0 2.9 %copy.190.upper_ref = f32[128,32,1]{2,1,0:T(8,128)} copy(f32[128,32,1]{0,1,2:T(8,128)S(1)} %fusion.41) | data formatting | bytes 32768 | tf_op jit(solution)/shard_map/optimization_barrier | solution.py:89
  32.8 9.1 %shard_map.94 = f32[128,32,128]{2,1,0:T(8,128)} custom-call(f32[128,32,1]{2,1,0:T(8,128)} %copy.188.lower_ref, f32[128,32,1]{2,1,0:T(8,128)} %copy.189.diagonal_ref, f32[128,32,1]{2,1,0:T(8,128)} %copy.190.upper_ref), custom_call_target="tpu_custom_call" | custom-call | flops 8388608 | bytes 33554432 | tf_op jit(solution)/shard_map/pallas_call | solution.py:92
  42.0 5.8 %fusion.60 = (f32[16,2,128,1]{3,1,0,2:T(2,128)}, f32[16,2,128,1]{3,1,0,2:T(2,128)S(1)}) fusion(f32[16,2,128,128]{3,1,0,2:T(2,128)} %bitcast.148), kind=kLoop, calls=%fused_computation.148 | loop fusion | bytes 65536 | tf_op jit(solution)/shard_map/slice | solution.py:167
  47.8 2.7 %copy.220 = f32[16,2,128,1]{2,1,0,3:T(2,128)S(1)} copy(f32[16,2,128,1]{3,1,0,2:T(2,128)} %get-tuple-element.39) | data formatting | bytes 32768
  50.6 1.2 copy.221
  52.4 0.9 collective-permute-done.7
  53.5 1.3 copy.170
  55.8 1.7 gather_fusion.3
  57.5 1.6 gather_fusion.2
  59.2 1.6 gather_fusion.1
  60.8 2.0 %fusion.15 = f32[16,2,128,128]{3,2,1,0:T(8,128)S(1)} fusion(bf16[16,2,128,128]{3,2,1,0:T(8,128)(2,1)} %gather_fusion.3, bf16[16,4,128,128]{3,2,1,0:T(8,128)(2,1)} %param.10), kind=kOutput, calls=%fused_computation.45 | convolution fusion | flops 134217728 | bytes 3670016 | tf_op jit(solution)/shard_map/tcd,tfdz->tfcz/dot_general | solution.py:179
  65.5 1.0 copy-done.1
  66.5 3.3 %fusion.2 = f32[16,2,128,128]{2,3,1,0:T(8,128)S(1)} fusion(f32[16,2,128,128]{3,2,1,0:T(8,128)S(1)} %add_add_fusion.1, f32[16,2,128,128]{3,1,0,2:T(2,128)S(1)} %bitcast.149), kind=kOutput, calls=%fused_computation.19 | convolution fusion | flops 805306368 | bytes 6291456 | tf_op jit(solution)/shard_map/tfzy,tfcy->tfcz/dot_general | solution.py:190
  70.1 0.9 slice_reduce_fusion.1
  71.9 1.3 copy-done.4
  73.3 1.4 gather_fusion.6
  74.7 5.1 %all-to-all-start.3 = ((bf16[4,4,128,128]{2,3,1,0:T(8,128)(2,1)}), bf16[4,4,128,128]{2,3,1,0:T(8,128)(2,1)S(1)}, u32[]{:S(2)}, u32[]{:S(2)}) async-start(bf16[4,4,128,128]{2,3,1,0:T(8,128)(2,1)} %bitcast.61), calls=%async_computation.3 | async-start | bytes 1048576 | tf_op jit(solution)/shard_map/all_to_all | solution.py:160
  79.8 1.4 pad_maximum_fusion.3
  81.2 1.1 collective-permute-done
  82.3 1.4 fusion.76
  83.7 2.0 %collective-permute-start.1 = (f32[2]{0:T(128)S(1)}, f32[2]{0:T(128)S(1)}, u32[]{:S(2)}, u32[]{:S(2)}) collective-permute-start(f32[2]{0:T(128)S(1)} %fusion.76), channel_id=1, source_target_pairs={{0,2},{2,0},{4,6},{6,4},{1,3},{3,1},{5,7},{7,5},{8,10},{10,8},{12,... | collective-permute-start | bytes 32 | tf_op jit(solution)/shard_map/ppermute | solution.py:32
  85.7 3.2 %collective-permute-done.1 = f32[2]{0:T(128)S(1)} collective-permute-done((f32[2]{0:T(128)S(1)}, f32[2]{0:T(128)S(1)}, u32[]{:S(2)}, u32[]{:S(2)}) %collective-permute-start.1) | collective-permute-done | bytes 40 | tf_op jit(solution)/shard_map/ppermute | solution.py:32
  88.9 1.4 fusion.78
  90.3 4.5 %collective-permute-start.2 = (f32[2]{0:T(128)S(1)}, f32[2]{0:T(128)S(1)}, u32[]{:S(2)}, u32[]{:S(2)}) collective-permute-start(f32[2]{0:T(128)S(1)} %fusion.78), channel_id=1, source_target_pairs={{0,4},{2,6},{4,0},{6,2},{1,5},{3,7},{5,1},{7,3},{8,12},{10,14},{12... | collective-permute-start | bytes 32 | tf_op jit(solution)/shard_map/ppermute | solution.py:32
  94.7 1.5 collective-permute-done.2
  96.3 1.5 collective-permute-start.3
  97.8 2.1 %collective-permute-done.3 = f32[2]{0:T(128)S(1)} collective-permute-done((f32[2]{0:T(128)S(1)}, f32[2]{0:T(128)S(1)}, u32[]{:S(2)}, u32[]{:S(2)}) %collective-permute-start.3) | collective-permute-done | bytes 40 | tf_op jit(solution)/shard_map/ppermute | solution.py:32
  99.8 1.5 collective-permute-start.4
  101.3 2.0 %collective-permute-done.4 = f32[2]{0:T(128)S(1)} collective-permute-done((f32[2]{0:T(128)S(1)}, f32[2]{0:T(128)S(1)}, u32[]{:S(2)}, u32[]{:S(2)}) %collective-permute-start.4) | collective-permute-done | bytes 40 | tf_op jit(solution)/shard_map/ppermute | solution.py:32
  105.3 2.1 %convert_reduce_fusion = (f32[]{:T(128)}, bf16[16,1,128,128]{2,3,1,0:T(8,128)(2,1)S(1)}) fusion(f32[16,2,128,128]{2,3,1,0:T(8,128)} %copy-done.4, f32[]{:T(128)} %bitcast.22), kind=kLoop, calls=%fused_computation.37 | loop fusion | flops 1048575 | bytes 1572872 | tf_op jit(solution)/shard_map/reduce_sum | solution.py:187
  107.4 1.4 gather_fusion.5
  108.8 4.4 %all-to-all-start.2 = ((bf16[4,4,128,128]{2,3,1,0:T(8,128)(2,1)}), bf16[4,4,128,128]{2,3,1,0:T(8,128)(2,1)}, u32[]{:S(2)}, u32[]{:S(2)}) async-start(bf16[4,4,128,128]{2,3,1,0:T(8,128)(2,1)} %bitcast.58), calls=%async_computation.2 | async-start | bytes 1048576 | tf_op jit(solution)/shard_map/all_to_all | solution.py:160
  113.2 2.1 %slice.234 = bf16[16,1,128,128]{2,3,1,0:T(8,128)(2,1)} slice(f32[16,2,128,128]{2,3,1,0:T(8,128)} %copy-done.4), slice={[0:16], [1:2], [0:128], [0:128]} | slice | bytes 1048576 | tf_op jit(solution)/shard_map/slice | solution.py:204
  115.3 8.8 %all-to-all-done.2 = bf16[4,4,128,128]{2,3,1,0:T(8,128)(2,1)} async-done(((bf16[4,4,128,128]{2,3,1,0:T(8,128)(2,1)}), bf16[4,4,128,128]{2,3,1,0:T(8,128)(2,1)}, u32[]{:S(2)}, u32[]{:S(2)}) %all-to-all-start.2) | async-done | bytes 524320 | tf_op jit(solution)/shard_map/all_to_all | solution.py:160
  124.1 2.7 %maximum_maximum_fusion = bf16[32,2,128,128]{2,3,1,0:T(8,128)(2,1)} fusion(bf16[16,1,128,128]{2,3,1,0:T(8,128)(2,1)S(1)} %bitcast.158, bf16[16,1,128,128]{2,3,1,0:T(8,128)(2,1)} %bitcast.59, bf16[16,1,128,128]{2,3,1,0:T(8,128)(2,1)} %slice.234, bf16[16,1,128,128]{2,3,1,0:T(8,128)(2,1)S(1)} %get-tuple-element.31), kind=kLoop, calls=%fused_computation.12 | loop fusion | flops 3145728 | bytes 4194304 | tf_op jit(solution)/shard_map/concatenate | solution.py:176
  126.9 2.3 %gather_fusion.10 = bf16[16,2,128,128]{2,3,1,0:T(8,128)(2,1)S(1)} fusion(bf16[32,2,128,128]{2,3,1,0:T(8,128)(2,1)} %maximum_maximum_fusion, s32[1024]{0:T(1024)S(1)} %get-tuple-element.51), kind=kCustom, calls=%fused_computation.10 | custom fusion | bytes 2097216 | tf_op jit(solution)/shard_map/gather | solution.py:182
  129.2 3.2 %gather_fusion.9 = bf16[16,2,128,128]{2,3,1,0:T(8,128)(2,1)} fusion(bf16[32,2,128,128]{2,3,1,0:T(8,128)(2,1)} %maximum_maximum_fusion, s32[1024]{0:T(1024)S(1)} %get-tuple-element.52), kind=kCustom, calls=%fused_computation.9 | custom fusion | bytes 2097216 | tf_op jit(solution)/shard_map/gather | solution.py:182
  132.4 3.3 %gather_fusion.8 = bf16[16,2,128,128]{2,3,1,0:T(8,128)(2,1)} fusion(bf16[32,2,128,128]{2,3,1,0:T(8,128)(2,1)} %maximum_maximum_fusion, s32[1024]{0:T(1024)S(1)} %get-tuple-element.53), kind=kCustom, calls=%fused_computation.8 | custom fusion | bytes 2097216 | tf_op jit(solution)/shard_map/gather | solution.py:182
  135.7 3.2 %gather_fusion.7 = bf16[16,2,128,128]{2,3,1,0:T(8,128)(2,1)} fusion(bf16[32,2,128,128]{2,3,1,0:T(8,128)(2,1)} %maximum_maximum_fusion, s32[1024]{0:T(1024)S(1)} %get-tuple-element.54), kind=kCustom, calls=%fused_computation.7 | custom fusion | bytes 2097216 | tf_op jit(solution)/shard_map/gather | solution.py:182
  139.0 1.9 %fusion.21 = f32[16,2,128,128]{3,2,1,0:T(8,128)S(1)} fusion(bf16[16,2,128,128]{2,3,1,0:T(8,128)(2,1)} %gather_fusion.7, bf16[16,4,128,128]{3,2,1,0:T(8,128)(2,1)} %param.10), kind=kOutput, calls=%fused_computation.51 | convolution fusion | flops 134217728 | bytes 3670016 | tf_op jit(solution)/shard_map/tcd,tfdz->tfcz/dot_general | solution.py:179
  141.7 0.8 copy-done.6
  143.5 3.3 %fusion = f32[16,2,128,128]{2,3,1,0:T(8,128)S(1)} fusion(f32[16,2,128,128]{3,2,1,0:T(8,128)S(1)} %add_add_fusion, f32[16,2,128,128]{3,1,0,2:T(2,128)S(1)} %bitcast.150), kind=kOutput, calls=%fused_computation.17 | convolution fusion | flops 805306368 | bytes 6291456 | tf_op jit(solution)/shard_map/tfzy,tfcy->tfcz/dot_general | solution.py:190
  146.8 0.9 slice_reduce_fusion
  147.7 1.4 pad_maximum_fusion.4
  150.2 1.4 fusion.75
  151.6 3.5 %collective-permute-done.9 = f32[2]{0:T(128)S(1)} collective-permute-done((f32[2]{0:T(128)S(1)}, f32[2]{0:T(128)S(1)}, u32[]{:S(2)}, u32[]{:S(2)}) %collective-permute-start.9) | collective-permute-done | bytes 40 | tf_op jit(solution)/shard_map/ppermute | solution.py:32
  155.1 1.4 fusion.77
  156.5 4.4 %collective-permute-done.10 = f32[2]{0:T(128)S(1)} collective-permute-done((f32[2]{0:T(128)S(1)}, f32[2]{0:T(128)S(1)}, u32[]{:S(2)}, u32[]{:S(2)}) %collective-permute-start.10) | collective-permute-done | bytes 40 | tf_op jit(solution)/shard_map/ppermute | solution.py:32
  160.9 1.5 collective-permute-start.11
  162.4 2.1 %collective-permute-done.11 = f32[2]{0:T(128)S(1)} collective-permute-done((f32[2]{0:T(128)S(1)}, f32[2]{0:T(128)S(1)}, u32[]{:S(2)}, u32[]{:S(2)}) %collective-permute-start.11) | collective-permute-done | bytes 40 | tf_op jit(solution)/shard_map/ppermute | solution.py:32
  164.5 1.5 collective-permute-start.12
  166.0 2.0 %collective-permute-done.12 = f32[2]{0:T(128)S(1)} collective-permute-done((f32[2]{0:T(128)S(1)}, f32[2]{0:T(128)S(1)}, u32[]{:S(2)}, u32[]{:S(2)}) %collective-permute-start.12) | collective-permute-done | bytes 40 | tf_op jit(solution)/shard_map/ppermute | solution.py:32
  171.6 1.0 copy.207
  172.6 1.0 copy.206
  (109 shorter events, 16.5 us)
Async XLA Ops:
  0.6 14.9 %copy-start = (f32[2,8]{1,0:T(2,128)S(1)}, f32[2,8]{1,0:T(2,128)}, u32[]{:S(2)}) copy-start(f32[2,8]{1,0:T(2,128)} %param.12) | copy-start | bytes 196
  0.6 15.3 %copy-start.11 = (f32[8]{0:T(128)S(1)}, f32[8]{0:T(128)}, u32[]{:S(2)}) copy-start(f32[8]{0:T(128)} %param.13) | copy-start | bytes 100
  1.4 14.4 %collective-permute-start.5 = (s32[16,1]{0,1:T(1,128)S(1)}, s32[16,1]{0,1:T(1,128)S(1)}, u32[]{:S(2)}, u32[]{:S(2)}) collective-permute-start(s32[16,1]{0,1:T(1,128)S(1)} %slice.114), channel_id=1, source_target_pairs={{1,0},{3,2},{5,4},{7,6},{9,8},{11,10},{13,12},{15,14},{17,16},{19,... | collective-permute-start | bytes 200 | tf_op jit(solution)/shard_map/ppermute | solution.py:17
  4.6 12.4 %all-to-all-start = ((s32[4,1,4]{2,1,0:T(1,128)}), s32[4,1,4]{2,1,0:T(1,128)S(1)}, u32[]{:S(2)}, u32[]{:S(2)}) async-start(s32[4,1,4]{2,1,0:T(1,128)} %bitcast.4), calls=%async_computation | async-start | bytes 4096 | tf_op jit(solution)/shard_map/all_to_all | solution.py:157
  19.0 34.5 %all-to-all-start.1 = ((bf16[4,4,2,128,128]{4,3,1,2,0:T(8,128)(2,1)}), bf16[4,4,2,128,128]{4,3,1,2,0:T(8,128)(2,1)}, u32[]{:S(2)}, u32[]{:S(2)}) async-start(bf16[4,4,2,128,128]{4,3,1,2,0:T(8,128)(2,1)} %copy.169), calls=%async_computation.1 | async-start | bytes 2097152 | tf_op jit(solution)/shard_map/all_to_all | solution.py:160
  50.6 4.3 %copy-start.5 = (bf16[16,128,128]{2,1,0:T(8,128)(2,1)S(1)}, bf16[16,128,128]{2,1,0:T(8,128)(2,1)}, u32[]{:S(2)}) copy-start(bf16[16,128,128]{2,1,0:T(8,128)(2,1)} %param.7) | copy-start | bytes 1572868
  50.6 4.3 %copy-start.10 = (bf16[16,128,128]{2,1,0:T(8,128)(2,1)S(1)}, bf16[16,128,128]{2,1,0:T(8,128)(2,1)}, u32[]{:S(2)}) copy-start(bf16[16,128,128]{2,1,0:T(8,128)(2,1)} %param.8) | copy-start | bytes 1572868
  52.1 1.1 collective-permute-start.7
  60.8 2.1 %copy-start.2 = (bf16[16,4,128,128]{3,2,1,0:T(8,128)(2,1)S(1)}, bf16[16,4,128,128]{3,2,1,0:T(8,128)(2,1)}, u32[]{:S(2)}) copy-start(bf16[16,4,128,128]{3,2,1,0:T(8,128)(2,1)} %param.10) | copy-start | bytes 6291460
  60.8 2.3 %copy-start.9 = (bf16[16,2,128,128]{3,2,1,0:T(8,128)(2,1)S(1)}, bf16[16,2,128,128]{3,2,1,0:T(8,128)(2,1)}, u32[]{:S(2)}) copy-start(bf16[16,2,128,128]{3,2,1,0:T(8,128)(2,1)} %gather_fusion.1) | copy-start | bytes 3145732
  63.1 1.2 copy-start.7
  64.9 1.6 copy-start.1
  69.8 1.2 collective-permute-start.6
  71.9 1.3 copy-start.4
  74.7 34.1 %all-to-all-start.3 = ((bf16[4,4,128,128]{2,3,1,0:T(8,128)(2,1)}), bf16[4,4,128,128]{2,3,1,0:T(8,128)(2,1)S(1)}, u32[]{:S(2)}, u32[]{:S(2)}) async-start(bf16[4,4,128,128]{2,3,1,0:T(8,128)(2,1)} %bitcast.61), calls=%async_computation.3 | async-start | bytes 1048576 | tf_op jit(solution)/shard_map/all_to_all | solution.py:160
  81.2 1.1 collective-permute-start
  83.7 5.2 %collective-permute-start.1 = (f32[2]{0:T(128)S(1)}, f32[2]{0:T(128)S(1)}, u32[]{:S(2)}, u32[]{:S(2)}) collective-permute-start(f32[2]{0:T(128)S(1)} %fusion.76), channel_id=1, source_target_pairs={{0,2},{2,0},{4,6},{6,4},{1,3},{3,1},{5,7},{7,5},{8,10},{10,8},{12,... | collective-permute-start | bytes 32 | tf_op jit(solution)/shard_map/ppermute | solution.py:32
  90.3 6.0 %collective-permute-start.2 = (f32[2]{0:T(128)S(1)}, f32[2]{0:T(128)S(1)}, u32[]{:S(2)}, u32[]{:S(2)}) collective-permute-start(f32[2]{0:T(128)S(1)} %fusion.78), channel_id=1, source_target_pairs={{0,4},{2,6},{4,0},{6,2},{1,5},{3,7},{5,1},{7,3},{8,12},{10,14},{12... | collective-permute-start | bytes 32 | tf_op jit(solution)/shard_map/ppermute | solution.py:32
  96.3 3.5 %collective-permute-start.3 = (f32[2]{0:T(128)S(1)}, f32[2]{0:T(128)S(1)}, u32[]{:S(2)}, u32[]{:S(2)}) collective-permute-start(f32[2]{0:T(128)S(1)} %add.195), channel_id=1, source_target_pairs={{0,8},{8,0},{16,24},{24,16},{1,9},{9,1},{17,25},{25,17},{2,10},{10... | collective-permute-start | bytes 32 | tf_op jit(solution)/shard_map/ppermute | solution.py:32
  99.8 3.5 %collective-permute-start.4 = (f32[2]{0:T(128)S(1)}, f32[2]{0:T(128)S(1)}, u32[]{:S(2)}, u32[]{:S(2)}) collective-permute-start(f32[2]{0:T(128)S(1)} %add.196), channel_id=1, source_target_pairs={{0,16},{8,24},{16,0},{24,8},{1,17},{9,25},{17,1},{25,9},{2,18},{10... | collective-permute-start | bytes 32 | tf_op jit(solution)/shard_map/ppermute | solution.py:32
  108.8 15.3 %all-to-all-start.2 = ((bf16[4,4,128,128]{2,3,1,0:T(8,128)(2,1)}), bf16[4,4,128,128]{2,3,1,0:T(8,128)(2,1)}, u32[]{:S(2)}, u32[]{:S(2)}) async-start(bf16[4,4,128,128]{2,3,1,0:T(8,128)(2,1)} %bitcast.58), calls=%async_computation.2 | async-start | bytes 1048576 | tf_op jit(solution)/shard_map/all_to_all | solution.py:160
  138.9 2.1 %copy-start.3 = (bf16[16,4,128,128]{3,2,1,0:T(8,128)(2,1)S(1)}, bf16[16,4,128,128]{3,2,1,0:T(8,128)(2,1)}, u32[]{:S(2)}) copy-start(bf16[16,4,128,128]{3,2,1,0:T(8,128)(2,1)} %param.10) | copy-start | bytes 6291460
  138.9 2.3 %copy-start.8 = (bf16[16,2,128,128]{2,3,1,0:T(8,128)(2,1)S(1)}, bf16[16,2,128,128]{2,3,1,0:T(8,128)(2,1)}, u32[]{:S(2)}) copy-start(bf16[16,2,128,128]{2,3,1,0:T(8,128)(2,1)} %gather_fusion.8) | copy-start | bytes 3145732
  141.3 1.2 copy-start.6
  149.1 1.1 collective-permute-start.8
  149.1 21.4 %collective-permute-start.13 = (f32[16,2,128]{2,1,0:T(2,128)S(1)}, f32[16,2,128]{2,1,0:T(2,128)S(1)}, u32[]{:S(2)}, u32[]{:S(2)}) collective-permute-start(f32[16,2,128]{2,1,0:T(2,128)S(1)} %select_bitcast_fusion), channel_id=1, source_target_pairs={{0,1},{1,0},{2,3},{3,2},{4,5},{5,4},{6,7},{7,6},{8,9},{9,8},{10,11... | collective-permute-start | bytes 49160 | tf_op jit(solution)/shard_map/ppermute | solution.py:21
  151.6 3.5 %collective-permute-start.9 = (f32[2]{0:T(128)S(1)}, f32[2]{0:T(128)S(1)}, u32[]{:S(2)}, u32[]{:S(2)}) collective-permute-start(f32[2]{0:T(128)S(1)} %fusion.75), channel_id=1, source_target_pairs={{0,2},{2,0},{4,6},{6,4},{1,3},{3,1},{5,7},{7,5},{8,10},{10,8},{12,... | collective-permute-start | bytes 32 | tf_op jit(solution)/shard_map/ppermute | solution.py:32
  156.5 4.4 %collective-permute-start.10 = (f32[2]{0:T(128)S(1)}, f32[2]{0:T(128)S(1)}, u32[]{:S(2)}, u32[]{:S(2)}) collective-permute-start(f32[2]{0:T(128)S(1)} %fusion.77), channel_id=1, source_target_pairs={{0,4},{2,6},{4,0},{6,2},{1,5},{3,7},{5,1},{7,3},{8,12},{10,14},{12... | collective-permute-start | bytes 32 | tf_op jit(solution)/shard_map/ppermute | solution.py:32
  160.9 3.5 %collective-permute-start.11 = (f32[2]{0:T(128)S(1)}, f32[2]{0:T(128)S(1)}, u32[]{:S(2)}, u32[]{:S(2)}) collective-permute-start(f32[2]{0:T(128)S(1)} %add.213), channel_id=1, source_target_pairs={{0,8},{8,0},{16,24},{24,16},{1,9},{9,1},{17,25},{25,17},{2,10},{10... | collective-permute-start | bytes 32 | tf_op jit(solution)/shard_map/ppermute | solution.py:32
  164.5 3.5 %collective-permute-start.12 = (f32[2]{0:T(128)S(1)}, f32[2]{0:T(128)S(1)}, u32[]{:S(2)}, u32[]{:S(2)}) collective-permute-start(f32[2]{0:T(128)S(1)} %add.214), channel_id=1, source_target_pairs={{0,16},{8,24},{16,0},{24,8},{1,17},{9,25},{17,1},{25,9},{2,18},{10... | collective-permute-start | bytes 32 | tf_op jit(solution)/shard_map/ppermute | solution.py:32

commit v6 on v5

--- a/solution.py
+++ b/solution.py
@@ -99,7 +99,7 @@
             bytes_accessed=64 * levels * systems * levels,
         ),
     )(*bands)
-    return jnp.transpose(inverse, (1, 0, 2)).reshape(lead + (levels, levels)), ready
+    return jnp.transpose(inverse, (1, 2, 0)).reshape(lead + (levels, levels)), ready
 
 
 def interface_values(low_value, low_spike, high_value, high_spike):
@@ -164,8 +164,8 @@
     inverse, wanted = block_inverse(block_lower, diagonal, block_upper, wanted)
     spike_column = jnp.where(
         my_layer == 0,
-        upper_band[..., -1:] * inverse[..., :, levels - 1],
-        lower_band[..., :1] * inverse[..., :, 0],
+        upper_band[..., -1:] * inverse[..., levels - 1, :],
+        lower_band[..., :1] * inverse[..., 0, :],
     )
     edge_spike = jnp.where(my_layer == 0, spike_column[..., -1], spike_column[..., 0])
     other_spike = from_partner(edge_spike, "gz", 0)
@@ -183,19 +183,22 @@
                 preferred_element_type=jnp.float32,
             )
         last = step_index + 1 == STEPS
-        totals = butterfly_sum(
-            jnp.stack([jnp.sum(fields[:, 0], dtype=jnp.float32), jnp.sum(advected[:, 0])]),
-            ("gz", "gy", "gx"),
+        partial = jnp.where(
+            lax.broadcasted_iota(jnp.int32, (128,), 0) == 0,
+            jnp.sum(fields[:, 0], dtype=jnp.float32),
+            jnp.sum(advected[:, 0]),
         )
         solved = jnp.einsum(
-            "tfzy,tfcy->tfcz",
+            "tfcy,tfyz->tfcz",
+            advected,
             inverse,
-            advected,
             precision=HIGHEST,
             preferred_element_type=jnp.float32,
         )
         edge_value = jnp.where(my_layer == 0, solved[..., -1], solved[..., 0])
-        other_value = from_partner(edge_value, "gz", 0)
+        carried = from_partner(jnp.concatenate([edge_value.reshape(-1), partial]), "gz", 0)
+        other_value = carried[: edge_value.size].reshape(edge_value.shape)
+        totals = butterfly_sum(partial + carried[edge_value.size :], ("gy", "gx"))
         low_value = jnp.where(my_layer == 0, edge_value, other_value)
         high_value = jnp.where(my_layer == 0, other_value, edge_value)
         lower_end, upper_end = interface_values(low_value, low_spike, high_value, high_spike)

time: 175 us -> 181 us (1.034)
  local copies, waits for them, and re-layouts: 56 us -> 60 us
  other arithmetic: 22.4 us -> 25.2 us
    unnamed x30 -> x34, local copies, waits for them, and re-layouts: 12.1 us -> 16.3 us
    add x10 -> x8, other arithmetic: 5.49 us -> 2.61 us  [butterfly_sum(): value + lax.ppermute(value, axis, [(i, i ^ bit) for i in range(devices)])]
    another operation x2 -> x0, other arithmetic: 2.73 us -> none  [per_device(): jnp.stack([jnp.sum(fields[:, 0], dtype=jnp.float32), jnp.sum(advected[:,...]
    add x0 -> x2, other arithmetic: none -> 2.59 us  [per_device(): totals = butterfly_sum(partial + carried[edge_value.size:], ('gy', 'gx'))]
    select_n x1 -> x3, other arithmetic: 0.1 us -> 2.68 us  [the longest x2 2.59 us: per_device(): jnp.where(lax.broadcasted_iota(jnp.int32, (128,), 0) == 0, jnp.sum(fields...]
    ppermute x10 -> x8, waiting for transfers between devices: 22.4 us -> 21.3 us  [butterfly_sum(): lax.ppermute(value, axis, [(i, i ^ bit) for i in range(devices)])]
    ppermute x10 -> x8, starting transfers between devices: 12.6 us -> 12.8 us  [butterfly_sum(): lax.ppermute(value, axis, [(i, i ^ bit) for i in range(devices)])]
    slice x4 -> x5, local copies, waits for them, and re-layouts: 6.05 us -> 6.04 us  [the longest x1 5.85 us: per_device(): inverse[..., levels - 1, :]]
  transfers between devices with their start and end apart: 18 -> 16, of which waited for: 12 -> 10; matrix products, arithmetic and copies ran while one was open for 24% -> 32% of each run, Pallas kernels for 5% -> 5%
where the time goes in v6:
time: 181 us; the launch traced here: 179 us
  local copies, waits for them, and re-layouts  60 us (33%)
  starting transfers between devices  35.6 us (20%)
  waiting for transfers between devices  31.4 us (17%)
  other arithmetic  25.2 us (14%)
  matrix products  14.2 us (8%)
  Pallas kernels  9.15 us (5%)
  between operations  3.84 us (2%)
    ppermute x8, waiting for transfers between devices, butterfly_sum(): lax.ppermute(value, axis, [(i, i ^ bit) for i in range(devices)])  21.3 us
    gather x8, local copies, waits for them, and re-layouts, per_device(): tile_pool[pool_index[:, entry_k]]  17.8 us
    unnamed x34, local copies, waits for them, and re-layouts  16.3 us
    all_to_all x3, starting transfers between devices, exchange(): lax.all_to_all(tiles[wanted], 'gy', split_axis=0, concat_axis=0, tiled=True)  14.5 us
    ppermute x8, starting transfers between devices, butterfly_sum(): lax.ppermute(value, axis, [(i, i ^ bit) for i in range(devices)])  12.8 us
    pallas_call x1, Pallas kernels, block_inverse(): pl.pallas_call(thomas_inverse_kernel, out_shape=jax.ShapeDtypeStruct((lev...  9.15 us
    all_to_all x3, waiting for transfers between devices, exchange(): lax.all_to_all(tiles[wanted], 'gy', split_axis=0, concat_axis=0, tiled=True)  8.87 us
    optimization_barrier x3, local copies, waits for them, and re-layouts, block_inverse(): lax.optimization_barrier(((level_major(lower), level_major(diagonal), lev...  8.58 us
  transfers between devices with their start and end apart: 16, of which 10 were waited for; matrix products, arithmetic and copies ran while one was open for 32% of the time, Pallas kernels for 5%

profile of v6, /device:TPU:0, one launch (start us, length us, event | category | flops | bytes accessed | tf_op | source)
XLA Modules:
  0.0 179.4 jit_solution(7994259206039622667)
XLA Ops:
  1.4 1.3 collective-permute-start
  2.6 0.8 copy.147
  4.6 6.3 %all-to-all-start = ((s32[4,1,4]{2,1,0:T(1,128)}), s32[4,1,4]{2,1,0:T(1,128)S(1)}, u32[]{:S(2)}, u32[]{:S(2)}) async-start(s32[4,1,4]{2,1,0:T(1,128)} %bitcast.3), calls=%async_computation | async-start | bytes 4096 | tf_op jit(solution)/shard_map/all_to_all | solution.py:157
  11.8 1.9 %convert_reduce_fusion.1 = f32[]{:T(128)} fusion(bf16[16,128,128]{2,1,0:T(8,128)(2,1)} %param.7), kind=kLoop, calls=%fused_computation.38 | loop fusion | flops 524287 | bytes 524292 | tf_op jit(solution)/shard_map/reduce_sum | solution.py:188
  14.2 1.3 pad_maximum_fusion.1
  17.8 1.0 copy.149
  18.8 5.1 %all-to-all-start.1 = ((bf16[4,4,2,128,128]{4,3,1,2,0:T(8,128)(2,1)}), bf16[4,4,2,128,128]{4,3,1,2,0:T(8,128)(2,1)}, u32[]{:S(2)}, u32[]{:S(2)}) async-start(bf16[4,4,2,128,128]{4,3,1,2,0:T(8,128)(2,1)} %copy.149), calls=%async_computation.1 | async-start | bytes 2097152 | tf_op jit(solution)/shard_map/all_to_all | solution.py:160
  24.1 2.9 %copy.168.lower_ref = f32[128,32,1]{2,1,0:T(8,128)} copy(f32[128,32,1]{0,1,2:T(8,128)S(1)} %bitcast.175) | data formatting | bytes 32768 | tf_op jit(solution)/shard_map/optimization_barrier | solution.py:89
  26.9 2.9 %copy.169.diagonal_ref = f32[128,32,1]{2,1,0:T(8,128)} copy(f32[128,32,1]{0,1,2:T(8,128)S(1)} %bitcast.174) | data formatting | bytes 32768 | tf_op jit(solution)/shard_map/optimization_barrier | solution.py:89
  29.8 2.9 %copy.170.upper_ref = f32[128,32,1]{2,1,0:T(8,128)} copy(f32[128,32,1]{0,1,2:T(8,128)S(1)} %fusion.46) | data formatting | bytes 32768 | tf_op jit(solution)/shard_map/optimization_barrier | solution.py:89
  32.6 9.1 %shard_map.94 = f32[128,32,128]{2,1,0:T(8,128)} custom-call(f32[128,32,1]{2,1,0:T(8,128)} %copy.168.lower_ref, f32[128,32,1]{2,1,0:T(8,128)} %copy.169.diagonal_ref, f32[128,32,1]{2,1,0:T(8,128)} %copy.170.upper_ref), custom_call_target="tpu_custom_call" | custom-call | flops 8388608 | bytes 33554432 | tf_op jit(solution)/shard_map/pallas_call | solution.py:92
  41.8 5.8 %fusion.64 = (f32[16,2,1,128]{2,1,0,3:T(2,128)}, f32[16,2,1,128]{2,1,0,3:T(2,128)S(1)}) fusion(f32[16,2,128,128]{2,1,0,3:T(2,128)} %bitcast.146), kind=kLoop, calls=%fused_computation.161 | loop fusion | bytes 65536 | tf_op jit(solution)/shard_map/slice | solution.py:167
  47.6 3.6 %copy.195 = f32[16,2,1,128]{0,1,3,2:T(2,128)S(1)} copy(f32[16,2,1,128]{2,1,0,3:T(2,128)} %get-tuple-element.37) | data formatting | bytes 32768
  51.3 3.7 %copy.196 = f32[16,2,1,128]{0,1,3,2:T(2,128)S(1)} copy(f32[16,2,1,128]{2,1,0,3:T(2,128)S(1)} %get-tuple-element.38) | data formatting | bytes 32768
  56.2 1.3 copy.150
  58.5 1.7 gather_fusion.3
  60.2 1.7 gather_fusion.2
  61.8 1.6 gather_fusion.1
  63.5 2.0 %fusion.15 = f32[16,2,128,128]{3,2,1,0:T(8,128)S(1)} fusion(bf16[16,2,128,128]{3,2,1,0:T(8,128)(2,1)} %gather_fusion.3, bf16[16,4,128,128]{3,2,1,0:T(8,128)(2,1)} %param.10), kind=kOutput, calls=%fused_computation.45 | convolution fusion | flops 134217728 | bytes 3670016 | tf_op jit(solution)/shard_map/tcd,tfdz->tfcz/dot_general | solution.py:179
  68.2 1.0 copy-done.1
  69.1 3.3 %fusion.2 = f32[16,2,128,128]{2,3,1,0:T(8,128)S(1)} fusion(f32[16,2,128,128]{3,2,1,0:T(8,128)S(1)} %add_add_fusion.1, f32[16,2,128,128]{2,1,0,3:T(2,128)S(1)} %bitcast.147), kind=kOutput, calls=%fused_computation.19 | convolution fusion | flops 805306368 | bytes 6291456 | tf_op jit(solution)/shard_map/tfcy,tfyz->tfcz/dot_general | solution.py:191
  72.4 1.1 slice_reduce_fusion.1
  73.7 1.3 broadcast_select_fusion.12
  76.3 1.1 broadcast_select_fusion.4
  77.5 1.9 %multiply_subtract_fusion.1 = f32[16,2,128,128]{2,3,1,0:T(8,128)S(1)} fusion(f32[16,2,128,128]{2,3,1,0:T(8,128)} %copy-done.2, f32[16,2,128]{2,1,0:T(2,128)S(1)} %bitcast.167, f32[16,2,128]{2,1,0:T(2,128)S(1)} %copy.176), kind=kLoop, calls=%fused_computation.15 | loop fusion | flops 1048576 | bytes 4227072 | tf_op jit(solution)/shard_map/sub | solution.py:206
  79.4 1.3 copy-done.5
  80.8 1.4 gather_fusion.6
  82.2 5.1 %all-to-all-start.3 = ((bf16[4,4,128,128]{2,3,1,0:T(8,128)(2,1)}), bf16[4,4,128,128]{2,3,1,0:T(8,128)(2,1)S(1)}, u32[]{:S(2)}, u32[]{:S(2)}) async-start(bf16[4,4,128,128]{2,3,1,0:T(8,128)(2,1)} %bitcast.61), calls=%async_computation.3 | async-start | bytes 1048576 | tf_op jit(solution)/shard_map/all_to_all | solution.py:160
  87.3 1.3 slice_add_fusion.1
  88.6 2.1 %collective-permute-start.2 = (f32[128]{0:T(128)S(1)}, f32[128]{0:T(128)S(1)}, u32[]{:S(2)}, u32[]{:S(2)}) collective-permute-start(f32[128]{0:T(128)S(1)} %slice_add_fusion.1), channel_id=1, source_target_pairs={{0,2},{2,0},{4,6},{6,4},{1,3},{3,1},{5,7},{7,5},{8,10},{10,8},{12,... | collective-permute-start | bytes 1544 | tf_op jit(solution)/shard_map/ppermute | solution.py:32
  90.7 5.7 %collective-permute-done.2 = f32[128]{0:T(128)S(1)} collective-permute-done((f32[128]{0:T(128)S(1)}, f32[128]{0:T(128)S(1)}, u32[]{:S(2)}, u32[]{:S(2)}) %collective-permute-start.2) | collective-permute-done | bytes 544 | tf_op jit(solution)/shard_map/ppermute | solution.py:32
  96.5 1.3 fusion.80
  97.8 4.5 %collective-permute-start.3 = (f32[128]{0:T(128)S(1)}, f32[128]{0:T(128)S(1)}, u32[]{:S(2)}, u32[]{:S(2)}) collective-permute-start(f32[128]{0:T(128)S(1)} %fusion.80), channel_id=1, source_target_pairs={{0,4},{2,6},{4,0},{6,2},{1,5},{3,7},{5,1},{7,3},{8,12},{10,14},{12... | collective-permute-start | bytes 1544 | tf_op jit(solution)/shard_map/ppermute | solution.py:32
  102.3 1.5 collective-permute-done.3
  103.8 1.5 collective-permute-start.4
  105.3 2.0 %collective-permute-done.4 = f32[128]{0:T(128)S(1)} collective-permute-done((f32[128]{0:T(128)S(1)}, f32[128]{0:T(128)S(1)}, u32[]{:S(2)}, u32[]{:S(2)}) %collective-permute-start.4) | collective-permute-done | bytes 544 | tf_op jit(solution)/shard_map/ppermute | solution.py:32
  107.4 1.5 collective-permute-start.5
  108.9 2.0 %collective-permute-done.5 = f32[128]{0:T(128)S(1)} collective-permute-done((f32[128]{0:T(128)S(1)}, f32[128]{0:T(128)S(1)}, u32[]{:S(2)}, u32[]{:S(2)}) %collective-permute-start.5) | collective-permute-done | bytes 544 | tf_op jit(solution)/shard_map/ppermute | solution.py:32
  112.8 2.1 %convert_reduce_fusion = (f32[]{:T(128)}, bf16[16,1,128,128]{2,3,1,0:T(8,128)(2,1)S(1)}) fusion(f32[16,2,128,128]{2,3,1,0:T(8,128)} %copy-done.5, f32[]{:T(128)} %bitcast.47), kind=kLoop, calls=%fused_computation.37 | loop fusion | flops 1048575 | bytes 1572872 | tf_op jit(solution)/shard_map/reduce_sum | solution.py:188
  115.0 1.4 gather_fusion.5
  116.4 4.4 %all-to-all-start.2 = ((bf16[4,4,128,128]{2,3,1,0:T(8,128)(2,1)}), bf16[4,4,128,128]{2,3,1,0:T(8,128)(2,1)}, u32[]{:S(2)}, u32[]{:S(2)}) async-start(bf16[4,4,128,128]{2,3,1,0:T(8,128)(2,1)} %bitcast.58), calls=%async_computation.2 | async-start | bytes 1048576 | tf_op jit(solution)/shard_map/all_to_all | solution.py:160
  120.7 2.1 %slice.260 = bf16[16,1,128,128]{2,3,1,0:T(8,128)(2,1)} slice(f32[16,2,128,128]{2,3,1,0:T(8,128)} %copy-done.5), slice={[0:16], [1:2], [0:128], [0:128]} | slice | bytes 1048576 | tf_op jit(solution)/shard_map/slice | solution.py:207
  122.9 8.9 %all-to-all-done.2 = bf16[4,4,128,128]{2,3,1,0:T(8,128)(2,1)} async-done(((bf16[4,4,128,128]{2,3,1,0:T(8,128)(2,1)}), bf16[4,4,128,128]{2,3,1,0:T(8,128)(2,1)}, u32[]{:S(2)}, u32[]{:S(2)}) %all-to-all-start.2) | async-done | bytes 524320 | tf_op jit(solution)/shard_map/all_to_all | solution.py:160
  131.7 2.7 %maximum_maximum_fusion = bf16[32,2,128,128]{2,3,1,0:T(8,128)(2,1)} fusion(bf16[16,1,128,128]{2,3,1,0:T(8,128)(2,1)S(1)} %bitcast.156, bf16[16,1,128,128]{2,3,1,0:T(8,128)(2,1)} %bitcast.59, bf16[16,1,128,128]{2,3,1,0:T(8,128)(2,1)} %slice.260, bf16[16,1,128,128]{2,3,1,0:T(8,128)(2,1)S(1)} %get-tuple-element.31), kind=kLoop, calls=%fused_computation.12 | loop fusion | flops 3145728 | bytes 4194304 | tf_op jit(solution)/shard_map/concatenate | solution.py:176
  134.4 2.3 %gather_fusion.10 = bf16[16,2,128,128]{2,3,1,0:T(8,128)(2,1)S(1)} fusion(bf16[32,2,128,128]{2,3,1,0:T(8,128)(2,1)} %maximum_maximum_fusion, s32[1024]{0:T(1024)S(1)} %get-tuple-element.49), kind=kCustom, calls=%fused_computation.10 | custom fusion | bytes 2097216 | tf_op jit(solution)/shard_map/gather | solution.py:182
  136.8 3.2 %gather_fusion.9 = bf16[16,2,128,128]{2,3,1,0:T(8,128)(2,1)} fusion(bf16[32,2,128,128]{2,3,1,0:T(8,128)(2,1)} %maximum_maximum_fusion, s32[1024]{0:T(1024)S(1)} %get-tuple-element.50), kind=kCustom, calls=%fused_computation.9 | custom fusion | bytes 2097216 | tf_op jit(solution)/shard_map/gather | solution.py:182
  140.0 3.3 %gather_fusion.8 = bf16[16,2,128,128]{2,3,1,0:T(8,128)(2,1)} fusion(bf16[32,2,128,128]{2,3,1,0:T(8,128)(2,1)} %maximum_maximum_fusion, s32[1024]{0:T(1024)S(1)} %get-tuple-element.51), kind=kCustom, calls=%fused_computation.8 | custom fusion | bytes 2097216 | tf_op jit(solution)/shard_map/gather | solution.py:182
  143.3 3.2 %gather_fusion.7 = bf16[16,2,128,128]{2,3,1,0:T(8,128)(2,1)} fusion(bf16[32,2,128,128]{2,3,1,0:T(8,128)(2,1)} %maximum_maximum_fusion, s32[1024]{0:T(1024)S(1)} %get-tuple-element.52), kind=kCustom, calls=%fused_computation.7 | custom fusion | bytes 2097216 | tf_op jit(solution)/shard_map/gather | solution.py:182
  146.5 1.9 %fusion.21 = f32[16,2,128,128]{3,2,1,0:T(8,128)S(1)} fusion(bf16[16,2,128,128]{2,3,1,0:T(8,128)(2,1)} %gather_fusion.7, bf16[16,4,128,128]{3,2,1,0:T(8,128)(2,1)} %param.10), kind=kOutput, calls=%fused_computation.51 | convolution fusion | flops 134217728 | bytes 3670016 | tf_op jit(solution)/shard_map/tcd,tfdz->tfcz/dot_general | solution.py:179
  149.3 0.8 copy-done.7
  151.1 3.3 %fusion = f32[16,2,128,128]{2,3,1,0:T(8,128)S(1)} fusion(f32[16,2,128,128]{3,2,1,0:T(8,128)S(1)} %add_add_fusion, f32[16,2,128,128]{2,1,0,3:T(2,128)S(1)} %bitcast.148), kind=kOutput, calls=%fused_computation.17 | convolution fusion | flops 805306368 | bytes 6291456 | tf_op jit(solution)/shard_map/tfcy,tfyz->tfcz/dot_general | solution.py:191
  154.4 0.9 slice_reduce_fusion
  155.3 1.3 broadcast_select_fusion.11
  156.7 1.2 collective-permute-done.7
  157.9 1.3 slice_add_fusion
  159.3 3.5 %collective-permute-done.8 = f32[128]{0:T(128)S(1)} collective-permute-done((f32[128]{0:T(128)S(1)}, f32[128]{0:T(128)S(1)}, u32[]{:S(2)}, u32[]{:S(2)}) %collective-permute-start.8) | collective-permute-done | bytes 544 | tf_op jit(solution)/shard_map/ppermute | solution.py:32
  162.8 1.3 fusion.79
  164.4 4.2 %collective-permute-done.9 = f32[128]{0:T(128)S(1)} collective-permute-done((f32[128]{0:T(128)S(1)}, f32[128]{0:T(128)S(1)}, u32[]{:S(2)}, u32[]{:S(2)}) %collective-permute-start.9) | collective-permute-done | bytes 544 | tf_op jit(solution)/shard_map/ppermute | solution.py:32
  168.6 1.5 collective-permute-start.10
  170.8 1.4 collective-permute-done.10
  172.2 1.5 collective-permute-start.11
  173.8 1.0 copy.182
  174.8 0.9 collective-permute-done.11
  178.3 1.0 copy.181
  (111 shorter events, 16.8 us)
Async XLA Ops:
  0.6 14.9 %copy-start = (f32[2,8]{1,0:T(2,128)S(1)}, f32[2,8]{1,0:T(2,128)}, u32[]{:S(2)}) copy-start(f32[2,8]{1,0:T(2,128)} %param.12) | copy-start | bytes 196
  0.6 15.3 %copy-start.13 = (f32[8]{0:T(128)S(1)}, f32[8]{0:T(128)}, u32[]{:S(2)}) copy-start(f32[8]{0:T(128)} %param.13) | copy-start | bytes 100
  1.4 14.4 %collective-permute-start = (s32[16,1]{0,1:T(1,128)S(1)}, s32[16,1]{0,1:T(1,128)S(1)}, u32[]{:S(2)}, u32[]{:S(2)}) collective-permute-start(s32[16,1]{0,1:T(1,128)S(1)} %slice.124), channel_id=1, source_target_pairs={{1,0},{3,2},{5,4},{7,6},{9,8},{11,10},{13,12},{15,14},{17,16},{19,... | collective-permute-start | bytes 200 | tf_op jit(solution)/shard_map/ppermute | solution.py:17
  4.6 12.3 %all-to-all-start = ((s32[4,1,4]{2,1,0:T(1,128)}), s32[4,1,4]{2,1,0:T(1,128)S(1)}, u32[]{:S(2)}, u32[]{:S(2)}) async-start(s32[4,1,4]{2,1,0:T(1,128)} %bitcast.3), calls=%async_computation | async-start | bytes 4096 | tf_op jit(solution)/shard_map/all_to_all | solution.py:157
  18.8 37.4 %all-to-all-start.1 = ((bf16[4,4,2,128,128]{4,3,1,2,0:T(8,128)(2,1)}), bf16[4,4,2,128,128]{4,3,1,2,0:T(8,128)(2,1)}, u32[]{:S(2)}, u32[]{:S(2)}) async-start(bf16[4,4,2,128,128]{4,3,1,2,0:T(8,128)(2,1)} %copy.149), calls=%async_computation.1 | async-start | bytes 2097152 | tf_op jit(solution)/shard_map/all_to_all | solution.py:160
  51.2 6.3 %copy-start.6 = (bf16[16,128,128]{2,1,0:T(8,128)(2,1)S(1)}, bf16[16,128,128]{2,1,0:T(8,128)(2,1)}, u32[]{:S(2)}) copy-start(bf16[16,128,128]{2,1,0:T(8,128)(2,1)} %param.7) | copy-start | bytes 1572868
  51.2 6.3 %copy-start.11 = (bf16[16,128,128]{2,1,0:T(8,128)(2,1)S(1)}, bf16[16,128,128]{2,1,0:T(8,128)(2,1)}, u32[]{:S(2)}) copy-start(bf16[16,128,128]{2,1,0:T(8,128)(2,1)} %param.8) | copy-start | bytes 1572868
  55.2 0.7 copy-start.12
  55.9 19.5 %collective-permute-start.6 = (f32[16,2]{0,1:T(2,128)S(1)}, f32[16,2]{0,1:T(2,128)S(1)}, u32[]{:S(2)}, u32[]{:S(2)}) collective-permute-start(f32[16,2]{0,1:T(2,128)S(1)} %fusion.58), channel_id=1, source_target_pairs={{0,1},{1,0},{2,3},{3,2},{4,5},{5,4},{6,7},{7,6},{8,9},{9,8},{10,11... | collective-permute-start | bytes 392 | tf_op jit(solution)/shard_map/ppermute | solution.py:21
  63.5 2.1 %copy-start.3 = (bf16[16,4,128,128]{3,2,1,0:T(8,128)(2,1)S(1)}, bf16[16,4,128,128]{3,2,1,0:T(8,128)(2,1)}, u32[]{:S(2)}) copy-start(bf16[16,4,128,128]{3,2,1,0:T(8,128)(2,1)} %param.10) | copy-start | bytes 6291460
  63.5 2.3 %copy-start.10 = (bf16[16,2,128,128]{3,2,1,0:T(8,128)(2,1)S(1)}, bf16[16,2,128,128]{3,2,1,0:T(8,128)(2,1)}, u32[]{:S(2)}) copy-start(bf16[16,2,128,128]{3,2,1,0:T(8,128)(2,1)} %gather_fusion.1) | copy-start | bytes 3145732
  65.8 1.2 copy-start.8
  67.5 1.6 copy-start.1
  72.4 1.3 copy-start.2
  75.1 1.3 collective-permute-start.1
  79.4 1.3 copy-start.5
  82.2 34.1 %all-to-all-start.3 = ((bf16[4,4,128,128]{2,3,1,0:T(8,128)(2,1)}), bf16[4,4,128,128]{2,3,1,0:T(8,128)(2,1)S(1)}, u32[]{:S(2)}, u32[]{:S(2)}) async-start(bf16[4,4,128,128]{2,3,1,0:T(8,128)(2,1)} %bitcast.61), calls=%async_computation.3 | async-start | bytes 1048576 | tf_op jit(solution)/shard_map/all_to_all | solution.py:160
  88.6 7.8 %collective-permute-start.2 = (f32[128]{0:T(128)S(1)}, f32[128]{0:T(128)S(1)}, u32[]{:S(2)}, u32[]{:S(2)}) collective-permute-start(f32[128]{0:T(128)S(1)} %slice_add_fusion.1), channel_id=1, source_target_pairs={{0,2},{2,0},{4,6},{6,4},{1,3},{3,1},{5,7},{7,5},{8,10},{10,8},{12,... | collective-permute-start | bytes 1544 | tf_op jit(solution)/shard_map/ppermute | solution.py:32
  97.8 6.1 %collective-permute-start.3 = (f32[128]{0:T(128)S(1)}, f32[128]{0:T(128)S(1)}, u32[]{:S(2)}, u32[]{:S(2)}) collective-permute-start(f32[128]{0:T(128)S(1)} %fusion.80), channel_id=1, source_target_pairs={{0,4},{2,6},{4,0},{6,2},{1,5},{3,7},{5,1},{7,3},{8,12},{10,14},{12... | collective-permute-start | bytes 1544 | tf_op jit(solution)/shard_map/ppermute | solution.py:32
  103.8 3.5 %collective-permute-start.4 = (f32[128]{0:T(128)S(1)}, f32[128]{0:T(128)S(1)}, u32[]{:S(2)}, u32[]{:S(2)}) collective-permute-start(f32[128]{0:T(128)S(1)} %add.202), channel_id=1, source_target_pairs={{0,8},{8,0},{16,24},{24,16},{1,9},{9,1},{17,25},{25,17},{2,10},{10... | collective-permute-start | bytes 1544 | tf_op jit(solution)/shard_map/ppermute | solution.py:32
  107.4 3.5 %collective-permute-start.5 = (f32[128]{0:T(128)S(1)}, f32[128]{0:T(128)S(1)}, u32[]{:S(2)}, u32[]{:S(2)}) collective-permute-start(f32[128]{0:T(128)S(1)} %add.203), channel_id=1, source_target_pairs={{0,16},{8,24},{16,0},{24,8},{1,17},{9,25},{17,1},{25,9},{2,18},{10... | collective-permute-start | bytes 1544 | tf_op jit(solution)/shard_map/ppermute | solution.py:32
  116.4 15.3 %all-to-all-start.2 = ((bf16[4,4,128,128]{2,3,1,0:T(8,128)(2,1)}), bf16[4,4,128,128]{2,3,1,0:T(8,128)(2,1)}, u32[]{:S(2)}, u32[]{:S(2)}) async-start(bf16[4,4,128,128]{2,3,1,0:T(8,128)(2,1)} %bitcast.58), calls=%async_computation.2 | async-start | bytes 1048576 | tf_op jit(solution)/shard_map/all_to_all | solution.py:160
  146.5 2.1 %copy-start.4 = (bf16[16,4,128,128]{3,2,1,0:T(8,128)(2,1)S(1)}, bf16[16,4,128,128]{3,2,1,0:T(8,128)(2,1)}, u32[]{:S(2)}) copy-start(bf16[16,4,128,128]{3,2,1,0:T(8,128)(2,1)} %param.10) | copy-start | bytes 6291460
  146.5 2.3 %copy-start.9 = (bf16[16,2,128,128]{2,3,1,0:T(8,128)(2,1)S(1)}, bf16[16,2,128,128]{2,3,1,0:T(8,128)(2,1)}, u32[]{:S(2)}) copy-start(bf16[16,2,128,128]{2,3,1,0:T(8,128)(2,1)} %gather_fusion.8) | copy-start | bytes 3145732
  148.9 1.2 copy-start.7
  156.6 1.3 collective-permute-start.7
  159.2 3.6 %collective-permute-start.8 = (f32[128]{0:T(128)S(1)}, f32[128]{0:T(128)S(1)}, u32[]{:S(2)}, u32[]{:S(2)}) collective-permute-start(f32[128]{0:T(128)S(1)} %slice_add_fusion), channel_id=1, source_target_pairs={{0,2},{2,0},{4,6},{6,4},{1,3},{3,1},{5,7},{7,5},{8,10},{10,8},{12,... | collective-permute-start | bytes 1544 | tf_op jit(solution)/shard_map/ppermute | solution.py:32
  164.1 4.5 %collective-permute-start.9 = (f32[128]{0:T(128)S(1)}, f32[128]{0:T(128)S(1)}, u32[]{:S(2)}, u32[]{:S(2)}) collective-permute-start(f32[128]{0:T(128)S(1)} %fusion.79), channel_id=1, source_target_pairs={{0,4},{2,6},{4,0},{6,2},{1,5},{3,7},{5,1},{7,3},{8,12},{10,14},{12... | collective-permute-start | bytes 1544 | tf_op jit(solution)/shard_map/ppermute | solution.py:32
  168.6 3.5 %collective-permute-start.10 = (f32[128]{0:T(128)S(1)}, f32[128]{0:T(128)S(1)}, u32[]{:S(2)}, u32[]{:S(2)}) collective-permute-start(f32[128]{0:T(128)S(1)} %add.213), channel_id=1, source_target_pairs={{0,8},{8,0},{16,24},{24,16},{1,9},{9,1},{17,25},{25,17},{2,10},{10... | collective-permute-start | bytes 1544 | tf_op jit(solution)/shard_map/ppermute | solution.py:32
  172.2 3.5 %collective-permute-start.11 = (f32[128]{0:T(128)S(1)}, f32[128]{0:T(128)S(1)}, u32[]{:S(2)}, u32[]{:S(2)}) collective-permute-start(f32[128]{0:T(128)S(1)} %add.214), channel_id=1, source_target_pairs={{0,16},{8,24},{16,0},{24,8},{1,17},{9,25},{17,1},{25,9},{2,18},{10... | collective-permute-start | bytes 1544 | tf_op jit(solution)/shard_map/ppermute | solution.py:32

commit v7 on v5

--- a/solution.py
+++ b/solution.py
@@ -4,6 +4,7 @@
 from jax.sharding import PartitionSpec as P
 from jax.experimental import pallas as pl
 from jax.experimental.pallas import tpu as pltpu
+from jax.experimental.layout import Layout, with_layout_constraint
 
 STEPS = 2
 
@@ -194,6 +195,7 @@
             precision=HIGHEST,
             preferred_element_type=jnp.float32,
         )
+        solved = with_layout_constraint(solved, Layout((0, 1, 2, 3)))
         edge_value = jnp.where(my_layer == 0, solved[..., -1], solved[..., 0])
         other_value = from_partner(edge_value, "gz", 0)
         low_value = jnp.where(my_layer == 0, edge_value, other_value)

time: 175 us -> 188 us (1.074)
  other arithmetic: 22.4 us -> 29.8 us
  local copies, waits for them, and re-layouts: 56 us -> 59.2 us
  matrix products: 14.2 us -> 17.2 us
    select_n x3 -> x5, local copies, waits for them, and re-layouts: 0.26 us -> 4.58 us  [the longest x2 4.56 us: per_device(): edge_value = jnp.where(my_layer == 0, solved[..., -1], solved[..., 0])]
    select_n x2, other arithmetic: 0.03 us -> 3.88 us  [per_device(): edge_value = jnp.where(my_layer == 0, solved[..., -1], solved[..., 0])]
    dot_general x2, matrix products: 6.61 us -> 9.34 us  [per_device(): jnp.einsum('tfzy,tfcy->tfcz', inverse, advected, precision=HIGHEST, prefe...]
    unnamed x30 -> x38, local copies, waits for them, and re-layouts: 12.1 us -> 10.5 us
  transfers between devices with their start and end apart: 18 -> 18, of which waited for: 12 -> 11; matrix products, arithmetic and copies ran while one was open for 24% -> 25% of each run, Pallas kernels for 5% -> 5%
where the time goes in v7:
time: 188 us; the launch traced here: 187 us
  local copies, waits for them, and re-layouts  59.2 us (31%)
  starting transfers between devices  35.8 us (19%)
  waiting for transfers between devices  31.8 us (17%)
  other arithmetic  29.8 us (16%)
  matrix products  17.2 us (9%)
  Pallas kernels  9.16 us (5%)
  between operations  3.78 us (2%)
    ppermute x10, waiting for transfers between devices, butterfly_sum(): lax.ppermute(value, axis, [(i, i ^ bit) for i in range(devices)])  22 us
    gather x8, local copies, waits for them, and re-layouts, per_device(): tile_pool[pool_index[:, entry_k]]  17.8 us
    all_to_all x3, starting transfers between devices, exchange(): lax.all_to_all(tiles[wanted], 'gy', split_axis=0, concat_axis=0, tiled=True)  14.4 us
    ppermute x10, starting transfers between devices, butterfly_sum(): lax.ppermute(value, axis, [(i, i ^ bit) for i in range(devices)])  12.6 us
    unnamed x38, local copies, waits for them, and re-layouts  10.5 us
    dot_general x2, matrix products, per_device(): jnp.einsum('tfzy,tfcy->tfcz', inverse, advected, precision=HIGHEST, prefe...  9.34 us
    pallas_call x1, Pallas kernels, block_inverse(): pl.pallas_call(thomas_inverse_kernel, out_shape=jax.ShapeDtypeStruct((lev...  9.16 us
    all_to_all x3, waiting for transfers between devices, exchange(): lax.all_to_all(tiles[wanted], 'gy', split_axis=0, concat_axis=0, tiled=True)  8.92 us
  transfers between devices with their start and end apart: 18, of which 11 were waited for; matrix products, arithmetic and copies ran while one was open for 25% of the time, Pallas kernels for 5%

profile of v7, /device:TPU:0, one launch (start us, length us, event | category | flops | bytes accessed | tf_op | source)
XLA Modules:
  0.0 186.7 jit_solution(11091020576326553365)
XLA Ops:
  1.4 1.3 collective-permute-start.5
  4.6 6.3 %all-to-all-start = ((s32[4,1,4]{2,1,0:T(1,128)}), s32[4,1,4]{2,1,0:T(1,128)S(1)}, u32[]{:S(2)}, u32[]{:S(2)}) async-start(s32[4,1,4]{2,1,0:T(1,128)} %bitcast.4), calls=%async_computation | async-start | bytes 4096 | tf_op jit(solution)/shard_map/all_to_all | solution.py:158
  11.8 1.9 %convert_reduce_fusion.1 = f32[]{:T(128)} fusion(bf16[16,128,128]{2,1,0:T(8,128)(2,1)} %param.7), kind=kLoop, calls=%fused_computation.40 | loop fusion | flops 524287 | bytes 524292 | tf_op jit(solution)/shard_map/reduce_sum | solution.py:188
  14.2 1.3 pad_maximum_fusion.1
  17.6 1.0 copy.254
  18.6 5.1 %all-to-all-start.1 = ((bf16[4,4,2,128,128]{4,3,1,2,0:T(8,128)(2,1)}), bf16[4,4,2,128,128]{4,3,1,2,0:T(8,128)(2,1)}, u32[]{:S(2)}, u32[]{:S(2)}) async-start(bf16[4,4,2,128,128]{4,3,1,2,0:T(8,128)(2,1)} %copy.254), calls=%async_computation.1 | async-start | bytes 2097152 | tf_op jit(solution)/shard_map/all_to_all | solution.py:161
  24.1 2.9 %copy.273.lower_ref = f32[128,32,1]{2,1,0:T(8,128)} copy(f32[128,32,1]{0,1,2:T(8,128)S(1)} %bitcast.167) | data formatting | bytes 32768 | tf_op jit(solution)/shard_map/optimization_barrier | solution.py:90
  26.9 2.9 %copy.274.diagonal_ref = f32[128,32,1]{2,1,0:T(8,128)} copy(f32[128,32,1]{0,1,2:T(8,128)S(1)} %bitcast.166) | data formatting | bytes 32768 | tf_op jit(solution)/shard_map/optimization_barrier | solution.py:90
  29.8 2.9 %copy.275.upper_ref = f32[128,32,1]{2,1,0:T(8,128)} copy(f32[128,32,1]{0,1,2:T(8,128)S(1)} %fusion.42) | data formatting | bytes 32768 | tf_op jit(solution)/shard_map/optimization_barrier | solution.py:90
  32.7 9.2 %shard_map.94 = f32[128,32,128]{2,1,0:T(8,128)} custom-call(f32[128,32,1]{2,1,0:T(8,128)} %copy.273.lower_ref, f32[128,32,1]{2,1,0:T(8,128)} %copy.274.diagonal_ref, f32[128,32,1]{2,1,0:T(8,128)} %copy.275.upper_ref), custom_call_target="tpu_custom_call" | custom-call | flops 8388608 | bytes 33554432 | tf_op jit(solution)/shard_map/pallas_call | solution.py:93
  41.8 5.9 %fusion.60 = (f32[16,2,128,1]{3,1,0,2:T(2,128)}, f32[16,2,128,1]{3,1,0,2:T(2,128)S(1)}) fusion(f32[16,2,128,128]{3,1,0,2:T(2,128)} %bitcast.142), kind=kLoop, calls=%fused_computation.148 | loop fusion | bytes 65536 | tf_op jit(solution)/shard_map/slice | solution.py:168
  47.7 2.0 %copy.311 = f32[16,2,128,1]{2,0,1,3:T(8,128)S(1)} copy(f32[16,2,128,1]{3,1,0,2:T(2,128)} %get-tuple-element.22) | data formatting | bytes 32768
  49.7 1.1 copy.312
  52.3 1.3 copy.255
  54.6 1.7 gather_fusion.3
  56.3 1.6 gather_fusion.2
  57.9 1.7 gather_fusion.1
  59.6 2.0 %fusion.15 = f32[16,2,128,128]{3,2,1,0:T(8,128)S(1)} fusion(bf16[16,2,128,128]{3,2,1,0:T(8,128)(2,1)} %gather_fusion.3, bf16[16,4,128,128]{3,2,1,0:T(8,128)(2,1)} %param.10), kind=kOutput, calls=%fused_computation.47 | convolution fusion | flops 134217728 | bytes 3670016 | tf_op jit(solution)/shard_map/tcd,tfdz->tfcz/dot_general | solution.py:180
  64.2 1.0 copy-done.2
  65.2 4.7 %fusion.2 = f32[16,2,128,128]{3,2,1,0:T(8,128)S(1)} fusion(f32[16,2,128,128]{3,2,1,0:T(8,128)S(1)} %add_add_fusion.1, f32[16,2,128,128]{3,1,0,2:T(2,128)S(1)} %bitcast.143), kind=kOutput, calls=%fused_computation.21 | convolution fusion | flops 805306368 | bytes 6291456 | tf_op jit(solution)/shard_map/tfzy,tfcy->tfcz/dot_general | solution.py:191
  69.9 1.3 copy-done.5
  71.2 1.9 %slice_select_fusion.1 = f32[16,2,128,1]{3,2,1,0:T(8,128)} fusion(f32[16,2,128,128]{3,2,1,0:T(8,128)S(1)} %fusion.2, pred[]{:T(512)S(6)} %eq.151), kind=kLoop, calls=%fused_computation.12 | loop fusion | flops 4096 | bytes 49153 | tf_op jit(solution)/shard_map/jit(_where)/select_n | solution.py:199
  73.2 2.2 %copy.283 = f32[16,2,128,1]{2,0,3,1:T(8,128)S(1)} copy(f32[16,2,128,1]{3,2,1,0:T(8,128)} %slice_select_fusion.1) | data formatting | bytes 32768 | tf_op jit(solution)/shard_map/jit(_where)/select_n | solution.py:199
  75.7 2.1 %slice_reduce_fusion.1 = f32[]{:T(128)} fusion(f32[16,2,128,128]{2,3,1,0:T(8,128)} %bitcast.145), kind=kLoop, calls=%fused_computation.37 | loop fusion | flops 262143 | bytes 1048580 | tf_op jit(solution)/shard_map/reduce_sum | solution.py:188
  77.9 1.9 %multiply_subtract_fusion.1 = f32[16,2,128,128]{3,2,1,0:T(8,128)S(1)} fusion(f32[16,2,128,128]{3,2,1,0:T(8,128)} %copy-done.5, f32[16,2,128]{2,1,0:T(2,128)S(1)} %copy.284, f32[16,2,128]{2,1,0:T(2,128)S(1)} %copy.282), kind=kLoop, calls=%fused_computation.17 | loop fusion | flops 1048576 | bytes 4227072 | tf_op jit(solution)/shard_map/sub | solution.py:205
  79.8 1.3 copy-done.9
  81.3 1.4 gather_fusion.6
  82.7 5.0 %all-to-all-start.3 = ((bf16[4,4,128,128]{3,2,1,0:T(8,128)(2,1)}), bf16[4,4,128,128]{3,2,1,0:T(8,128)(2,1)S(1)}, u32[]{:S(2)}, u32[]{:S(2)}) async-start(bf16[4,4,128,128]{3,2,1,0:T(8,128)(2,1)} %bitcast.60), calls=%async_computation.3 | async-start | bytes 1048576 | tf_op jit(solution)/shard_map/all_to_all | solution.py:161
  87.7 1.4 pad_maximum_fusion.3
  89.1 1.1 collective-permute-done
  90.2 1.4 fusion.76
  91.5 2.0 %collective-permute-start.1 = (f32[2]{0:T(128)S(1)}, f32[2]{0:T(128)S(1)}, u32[]{:S(2)}, u32[]{:S(2)}) collective-permute-start(f32[2]{0:T(128)S(1)} %fusion.76), channel_id=1, source_target_pairs={{0,2},{2,0},{4,6},{6,4},{1,3},{3,1},{5,7},{7,5},{8,10},{10,8},{12,... | collective-permute-start | bytes 32 | tf_op jit(solution)/shard_map/ppermute | solution.py:33
  93.6 3.3 %collective-permute-done.1 = f32[2]{0:T(128)S(1)} collective-permute-done((f32[2]{0:T(128)S(1)}, f32[2]{0:T(128)S(1)}, u32[]{:S(2)}, u32[]{:S(2)}) %collective-permute-start.1) | collective-permute-done | bytes 40 | tf_op jit(solution)/shard_map/ppermute | solution.py:33
  96.9 1.4 fusion.78
  98.3 4.5 %collective-permute-start.2 = (f32[2]{0:T(128)S(1)}, f32[2]{0:T(128)S(1)}, u32[]{:S(2)}, u32[]{:S(2)}) collective-permute-start(f32[2]{0:T(128)S(1)} %fusion.78), channel_id=1, source_target_pairs={{0,4},{2,6},{4,0},{6,2},{1,5},{3,7},{5,1},{7,3},{8,12},{10,14},{12... | collective-permute-start | bytes 32 | tf_op jit(solution)/shard_map/ppermute | solution.py:33
  102.7 1.5 collective-permute-done.2
  104.3 1.5 collective-permute-start.3
  105.8 2.0 %collective-permute-done.3 = f32[2]{0:T(128)S(1)} collective-permute-done((f32[2]{0:T(128)S(1)}, f32[2]{0:T(128)S(1)}, u32[]{:S(2)}, u32[]{:S(2)}) %collective-permute-start.3) | collective-permute-done | bytes 40 | tf_op jit(solution)/shard_map/ppermute | solution.py:33
  107.8 1.5 collective-permute-start.4
  109.3 2.0 %collective-permute-done.4 = f32[2]{0:T(128)S(1)} collective-permute-done((f32[2]{0:T(128)S(1)}, f32[2]{0:T(128)S(1)}, u32[]{:S(2)}, u32[]{:S(2)}) %collective-permute-start.4) | collective-permute-done | bytes 40 | tf_op jit(solution)/shard_map/ppermute | solution.py:33
  113.3 2.1 %convert_reduce_fusion = (f32[]{:T(128)}, bf16[16,1,128,128]{3,2,1,0:T(8,128)(2,1)S(1)}) fusion(f32[16,2,128,128]{3,2,1,0:T(8,128)} %copy-done.9, f32[]{:T(128)} %bitcast.22), kind=kLoop, calls=%fused_computation.39 | loop fusion | flops 1048575 | bytes 1572872 | tf_op jit(solution)/shard_map/reduce_sum | solution.py:188
  115.4 1.4 gather_fusion.5
  116.8 4.4 %all-to-all-start.2 = ((bf16[4,4,128,128]{3,2,1,0:T(8,128)(2,1)}), bf16[4,4,128,128]{3,2,1,0:T(8,128)(2,1)}, u32[]{:S(2)}, u32[]{:S(2)}) async-start(bf16[4,4,128,128]{3,2,1,0:T(8,128)(2,1)} %bitcast.57), calls=%async_computation.2 | async-start | bytes 1048576 | tf_op jit(solution)/shard_map/all_to_all | solution.py:161
  121.2 2.1 %slice.238 = bf16[16,1,128,128]{3,2,1,0:T(8,128)(2,1)} slice(f32[16,2,128,128]{3,2,1,0:T(8,128)} %copy-done.9), slice={[0:16], [1:2], [0:128], [0:128]} | slice | bytes 1048576 | tf_op jit(solution)/shard_map/slice | solution.py:206
  123.3 8.9 %all-to-all-done.2 = bf16[4,4,128,128]{3,2,1,0:T(8,128)(2,1)} async-done(((bf16[4,4,128,128]{3,2,1,0:T(8,128)(2,1)}), bf16[4,4,128,128]{3,2,1,0:T(8,128)(2,1)}, u32[]{:S(2)}, u32[]{:S(2)}) %all-to-all-start.2) | async-done | bytes 524320 | tf_op jit(solution)/shard_map/all_to_all | solution.py:161
  132.2 2.7 %maximum_maximum_fusion = bf16[32,2,128,128]{3,2,1,0:T(8,128)(2,1)} fusion(bf16[16,1,128,128]{3,2,1,0:T(8,128)(2,1)S(1)} %bitcast.152, bf16[16,1,128,128]{3,2,1,0:T(8,128)(2,1)} %bitcast.58, bf16[16,1,128,128]{3,2,1,0:T(8,128)(2,1)} %slice.238, bf16[16,1,128,128]{3,2,1,0:T(8,128)(2,1)S(1)} %get-tuple-element.16), kind=kLoop, calls=%fused_computation.14 | loop fusion | flops 3145728 | bytes 4194304 | tf_op jit(solution)/shard_map/concatenate | solution.py:177
  134.9 2.3 %gather_fusion.10 = bf16[16,2,128,128]{3,2,1,0:T(8,128)(2,1)S(1)} fusion(bf16[32,2,128,128]{3,2,1,0:T(8,128)(2,1)} %maximum_maximum_fusion, s32[1024]{0:T(1024)S(1)} %get-tuple-element.34), kind=kCustom, calls=%fused_computation.10 | custom fusion | bytes 2097216 | tf_op jit(solution)/shard_map/gather | solution.py:183
  137.3 3.2 %gather_fusion.9 = bf16[16,2,128,128]{3,2,1,0:T(8,128)(2,1)} fusion(bf16[32,2,128,128]{3,2,1,0:T(8,128)(2,1)} %maximum_maximum_fusion, s32[1024]{0:T(1024)S(1)} %get-tuple-element.35), kind=kCustom, calls=%fused_computation.9 | custom fusion | bytes 2097216 | tf_op jit(solution)/shard_map/gather | solution.py:183
  140.5 3.3 %gather_fusion.8 = bf16[16,2,128,128]{3,2,1,0:T(8,128)(2,1)} fusion(bf16[32,2,128,128]{3,2,1,0:T(8,128)(2,1)} %maximum_maximum_fusion, s32[1024]{0:T(1024)S(1)} %get-tuple-element.36), kind=kCustom, calls=%fused_computation.8 | custom fusion | bytes 2097216 | tf_op jit(solution)/shard_map/gather | solution.py:183
  143.8 3.2 %gather_fusion.7 = bf16[16,2,128,128]{3,2,1,0:T(8,128)(2,1)} fusion(bf16[32,2,128,128]{3,2,1,0:T(8,128)(2,1)} %maximum_maximum_fusion, s32[1024]{0:T(1024)S(1)} %get-tuple-element.37), kind=kCustom, calls=%fused_computation.7 | custom fusion | bytes 2097216 | tf_op jit(solution)/shard_map/gather | solution.py:183
  147.0 2.0 %fusion.21 = f32[16,2,128,128]{3,2,1,0:T(8,128)S(1)} fusion(bf16[16,2,128,128]{3,2,1,0:T(8,128)(2,1)} %gather_fusion.7, bf16[16,4,128,128]{3,2,1,0:T(8,128)(2,1)} %param.10), kind=kOutput, calls=%fused_computation.53 | convolution fusion | flops 134217728 | bytes 3670016 | tf_op jit(solution)/shard_map/tcd,tfdz->tfcz/dot_general | solution.py:180
  151.7 4.7 %fusion = f32[16,2,128,128]{3,2,1,0:T(8,128)S(1)} fusion(f32[16,2,128,128]{3,2,1,0:T(8,128)S(1)} %add_add_fusion, f32[16,2,128,128]{3,1,0,2:T(2,128)S(1)} %bitcast.144), kind=kOutput, calls=%fused_computation.19 | convolution fusion | flops 805306368 | bytes 6291456 | tf_op jit(solution)/shard_map/tfzy,tfcy->tfcz/dot_general | solution.py:191
  156.4 1.1 slice_reduce_fusion
  157.5 1.4 pad_maximum_fusion.4
  158.9 1.9 %slice_select_fusion = f32[16,2,128,1]{3,2,1,0:T(8,128)} fusion(f32[16,2,128,128]{3,2,1,0:T(8,128)S(1)} %fusion, pred[]{:T(512)S(6)} %eq.151), kind=kLoop, calls=%fused_computation.11 | loop fusion | flops 4096 | bytes 49153 | tf_op jit(solution)/shard_map/jit(_where)/select_n | solution.py:199
  160.8 2.4 %copy.291 = f32[16,2,128,1]{2,0,3,1:T(8,128)S(1)} copy(f32[16,2,128,1]{3,2,1,0:T(8,128)} %slice_select_fusion) | data formatting | bytes 32768 | tf_op jit(solution)/shard_map/jit(_where)/select_n | solution.py:199
  163.7 1.4 fusion.75
  165.1 3.5 %collective-permute-done.9 = f32[2]{0:T(128)S(1)} collective-permute-done((f32[2]{0:T(128)S(1)}, f32[2]{0:T(128)S(1)}, u32[]{:S(2)}, u32[]{:S(2)}) %collective-permute-start.9) | collective-permute-done | bytes 40 | tf_op jit(solution)/shard_map/ppermute | solution.py:33
  168.6 1.4 fusion.77
  170.0 4.4 %collective-permute-done.10 = f32[2]{0:T(128)S(1)} collective-permute-done((f32[2]{0:T(128)S(1)}, f32[2]{0:T(128)S(1)}, u32[]{:S(2)}, u32[]{:S(2)}) %collective-permute-start.10) | collective-permute-done | bytes 40 | tf_op jit(solution)/shard_map/ppermute | solution.py:33
  174.4 1.5 collective-permute-start.11
  175.9 2.1 %collective-permute-done.11 = f32[2]{0:T(128)S(1)} collective-permute-done((f32[2]{0:T(128)S(1)}, f32[2]{0:T(128)S(1)}, u32[]{:S(2)}, u32[]{:S(2)}) %collective-permute-start.11) | collective-permute-done | bytes 40 | tf_op jit(solution)/shard_map/ppermute | solution.py:33
  178.0 1.5 collective-permute-start.12
  179.5 2.0 %collective-permute-done.12 = f32[2]{0:T(128)S(1)} collective-permute-done((f32[2]{0:T(128)S(1)}, f32[2]{0:T(128)S(1)}, u32[]{:S(2)}, u32[]{:S(2)}) %collective-permute-start.12) | collective-permute-done | bytes 40 | tf_op jit(solution)/shard_map/ppermute | solution.py:33
  (115 shorter events, 19.5 us)
Async XLA Ops:
  0.6 14.9 %copy-start = (f32[2,8]{1,0:T(2,128)S(1)}, f32[2,8]{1,0:T(2,128)}, u32[]{:S(2)}) copy-start(f32[2,8]{1,0:T(2,128)} %param.12) | copy-start | bytes 196
  0.6 15.3 %copy-start.16 = (f32[8]{0:T(128)S(1)}, f32[8]{0:T(128)}, u32[]{:S(2)}) copy-start(f32[8]{0:T(128)} %param.13) | copy-start | bytes 100
  1.4 14.4 %collective-permute-start.5 = (s32[16,1]{0,1:T(1,128)S(1)}, s32[16,1]{0,1:T(1,128)S(1)}, u32[]{:S(2)}, u32[]{:S(2)}) collective-permute-start(s32[16,1]{0,1:T(1,128)S(1)} %slice.114), channel_id=1, source_target_pairs={{1,0},{3,2},{5,4},{7,6},{9,8},{11,10},{13,12},{15,14},{17,16},{19,... | collective-permute-start | bytes 200 | tf_op jit(solution)/shard_map/ppermute | solution.py:18
  4.6 12.1 %all-to-all-start = ((s32[4,1,4]{2,1,0:T(1,128)}), s32[4,1,4]{2,1,0:T(1,128)S(1)}, u32[]{:S(2)}, u32[]{:S(2)}) async-start(s32[4,1,4]{2,1,0:T(1,128)} %bitcast.4), calls=%async_computation | async-start | bytes 4096 | tf_op jit(solution)/shard_map/all_to_all | solution.py:158
  18.6 33.7 %all-to-all-start.1 = ((bf16[4,4,2,128,128]{4,3,1,2,0:T(8,128)(2,1)}), bf16[4,4,2,128,128]{4,3,1,2,0:T(8,128)(2,1)}, u32[]{:S(2)}, u32[]{:S(2)}) async-start(bf16[4,4,2,128,128]{4,3,1,2,0:T(8,128)(2,1)} %copy.254), calls=%async_computation.1 | async-start | bytes 2097152 | tf_op jit(solution)/shard_map/all_to_all | solution.py:161
  49.7 3.9 %copy-start.10 = (bf16[16,128,128]{2,1,0:T(8,128)(2,1)S(1)}, bf16[16,128,128]{2,1,0:T(8,128)(2,1)}, u32[]{:S(2)}) copy-start(bf16[16,128,128]{2,1,0:T(8,128)(2,1)} %param.7) | copy-start | bytes 1572868
  49.7 3.9 %copy-start.15 = (bf16[16,128,128]{2,1,0:T(8,128)(2,1)S(1)}, bf16[16,128,128]{2,1,0:T(8,128)(2,1)}, u32[]{:S(2)}) copy-start(bf16[16,128,128]{2,1,0:T(8,128)(2,1)} %param.8) | copy-start | bytes 1572868
  51.1 1.1 collective-permute-start.7
  59.6 2.1 %copy-start.7 = (bf16[16,4,128,128]{3,2,1,0:T(8,128)(2,1)S(1)}, bf16[16,4,128,128]{3,2,1,0:T(8,128)(2,1)}, u32[]{:S(2)}) copy-start(bf16[16,4,128,128]{3,2,1,0:T(8,128)(2,1)} %param.10) | copy-start | bytes 6291460
  59.6 2.3 %copy-start.14 = (bf16[16,2,128,128]{3,2,1,0:T(8,128)(2,1)S(1)}, bf16[16,2,128,128]{3,2,1,0:T(8,128)(2,1)}, u32[]{:S(2)}) copy-start(bf16[16,2,128,128]{3,2,1,0:T(8,128)(2,1)} %gather_fusion.1) | copy-start | bytes 3145732
  61.9 1.2 copy-start.12
  63.6 1.6 copy-start.2
  65.2 4.7 %copy-start.6 = (f32[16,2,128,128]{3,2,1,0:T(8,128)}, f32[16,2,128,128]{3,2,1,0:T(8,128)S(1)}, u32[]{:S(2)}) copy-start(f32[16,2,128,128]{3,2,1,0:T(8,128)S(1)} %add_add_fusion.1) | copy-start | bytes 6291460
  69.9 1.3 copy-start.5
  75.4 2.4 %collective-permute-start.6 = (f32[16,2,128]{2,0,1:T(8,128)S(1)}, f32[16,2,128]{2,0,1:T(8,128)S(1)}, u32[]{:S(2)}, u32[]{:S(2)}) collective-permute-start(f32[16,2,128]{2,0,1:T(8,128)S(1)} %bitcast.163), channel_id=1, source_target_pairs={{0,1},{1,0},{2,3},{3,2},{4,5},{5,4},{6,7},{7,6},{8,9},{9,8},{10,11... | collective-permute-start | bytes 49160 | tf_op jit(solution)/shard_map/ppermute | solution.py:22
  79.8 1.3 copy-start.9
  82.7 34.1 %all-to-all-start.3 = ((bf16[4,4,128,128]{3,2,1,0:T(8,128)(2,1)}), bf16[4,4,128,128]{3,2,1,0:T(8,128)(2,1)S(1)}, u32[]{:S(2)}, u32[]{:S(2)}) async-start(bf16[4,4,128,128]{3,2,1,0:T(8,128)(2,1)} %bitcast.60), calls=%async_computation.3 | async-start | bytes 1048576 | tf_op jit(solution)/shard_map/all_to_all | solution.py:161
  89.0 1.1 collective-permute-start
  91.5 5.4 %collective-permute-start.1 = (f32[2]{0:T(128)S(1)}, f32[2]{0:T(128)S(1)}, u32[]{:S(2)}, u32[]{:S(2)}) collective-permute-start(f32[2]{0:T(128)S(1)} %fusion.76), channel_id=1, source_target_pairs={{0,2},{2,0},{4,6},{6,4},{1,3},{3,1},{5,7},{7,5},{8,10},{10,8},{12,... | collective-permute-start | bytes 32 | tf_op jit(solution)/shard_map/ppermute | solution.py:33
  98.3 6.0 %collective-permute-start.2 = (f32[2]{0:T(128)S(1)}, f32[2]{0:T(128)S(1)}, u32[]{:S(2)}, u32[]{:S(2)}) collective-permute-start(f32[2]{0:T(128)S(1)} %fusion.78), channel_id=1, source_target_pairs={{0,4},{2,6},{4,0},{6,2},{1,5},{3,7},{5,1},{7,3},{8,12},{10,14},{12... | collective-permute-start | bytes 32 | tf_op jit(solution)/shard_map/ppermute | solution.py:33
  104.3 3.5 %collective-permute-start.3 = (f32[2]{0:T(128)S(1)}, f32[2]{0:T(128)S(1)}, u32[]{:S(2)}, u32[]{:S(2)}) collective-permute-start(f32[2]{0:T(128)S(1)} %add.195), channel_id=1, source_target_pairs={{0,8},{8,0},{16,24},{24,16},{1,9},{9,1},{17,25},{25,17},{2,10},{10... | collective-permute-start | bytes 32 | tf_op jit(solution)/shard_map/ppermute | solution.py:33
  107.8 3.5 %collective-permute-start.4 = (f32[2]{0:T(128)S(1)}, f32[2]{0:T(128)S(1)}, u32[]{:S(2)}, u32[]{:S(2)}) collective-permute-start(f32[2]{0:T(128)S(1)} %add.196), channel_id=1, source_target_pairs={{0,16},{8,24},{16,0},{24,8},{1,17},{9,25},{17,1},{25,9},{2,18},{10... | collective-permute-start | bytes 32 | tf_op jit(solution)/shard_map/ppermute | solution.py:33
  116.8 15.4 %all-to-all-start.2 = ((bf16[4,4,128,128]{3,2,1,0:T(8,128)(2,1)}), bf16[4,4,128,128]{3,2,1,0:T(8,128)(2,1)}, u32[]{:S(2)}, u32[]{:S(2)}) async-start(bf16[4,4,128,128]{3,2,1,0:T(8,128)(2,1)} %bitcast.57), calls=%async_computation.2 | async-start | bytes 1048576 | tf_op jit(solution)/shard_map/all_to_all | solution.py:161
  147.0 2.1 %copy-start.8 = (bf16[16,4,128,128]{3,2,1,0:T(8,128)(2,1)S(1)}, bf16[16,4,128,128]{3,2,1,0:T(8,128)(2,1)}, u32[]{:S(2)}) copy-start(bf16[16,4,128,128]{3,2,1,0:T(8,128)(2,1)} %param.10) | copy-start | bytes 6291460
  147.0 2.3 %copy-start.13 = (bf16[16,2,128,128]{3,2,1,0:T(8,128)(2,1)S(1)}, bf16[16,2,128,128]{3,2,1,0:T(8,128)(2,1)}, u32[]{:S(2)}) copy-start(bf16[16,2,128,128]{3,2,1,0:T(8,128)(2,1)} %gather_fusion.8) | copy-start | bytes 3145732
  149.4 1.2 copy-start.11
  156.3 2.5 %copy-start.3 = (f32[16,2,128,128]{3,2,1,0:T(8,128)}, f32[16,2,128,128]{3,2,1,0:T(8,128)S(1)}, u32[]{:S(2)}) copy-start(f32[16,2,128,128]{3,2,1,0:T(8,128)S(1)} %fusion) | copy-start | bytes 6291460
  158.8 4.8 %collective-permute-start.8 = (f32[2]{0:T(128)S(1)}, f32[2]{0:T(128)S(1)}, u32[]{:S(2)}, u32[]{:S(2)}) collective-permute-start(f32[2]{0:T(128)S(1)} %pad_maximum_fusion.4), channel_id=1, source_target_pairs={{0,1},{1,0},{2,3},{3,2},{4,5},{5,4},{6,7},{7,6},{8,9},{9,8},{10,11... | collective-permute-start | bytes 32 | tf_op jit(solution)/shard_map/ppermute | solution.py:33
  160.8 23.3 %copy-start.4 = (f32[16,2,128,128]{3,2,1,0:T(8,128)S(1)}, f32[16,2,128,128]{3,2,1,0:T(8,128)}, u32[]{:S(2)}) copy-start(f32[16,2,128,128]{3,2,1,0:T(8,128)} %copy-done.3) | copy-start | bytes 6291460
  163.2 20.9 %collective-permute-start.13 = (f32[16,2,128]{2,0,1:T(8,128)S(1)}, f32[16,2,128]{2,0,1:T(8,128)S(1)}, u32[]{:S(2)}, u32[]{:S(2)}) collective-permute-start(f32[16,2,128]{2,0,1:T(8,128)S(1)} %bitcast.162), channel_id=1, source_target_pairs={{0,1},{1,0},{2,3},{3,2},{4,5},{5,4},{6,7},{7,6},{8,9},{9,8},{10,11... | collective-permute-start | bytes 49160 | tf_op jit(solution)/shard_map/ppermute | solution.py:22
  165.1 3.5 %collective-permute-start.9 = (f32[2]{0:T(128)S(1)}, f32[2]{0:T(128)S(1)}, u32[]{:S(2)}, u32[]{:S(2)}) collective-permute-start(f32[2]{0:T(128)S(1)} %fusion.75), channel_id=1, source_target_pairs={{0,2},{2,0},{4,6},{6,4},{1,3},{3,1},{5,7},{7,5},{8,10},{10,8},{12,... | collective-permute-start | bytes 32 | tf_op jit(solution)/shard_map/ppermute | solution.py:33
  170.0 4.4 %collective-permute-start.10 = (f32[2]{0:T(128)S(1)}, f32[2]{0:T(128)S(1)}, u32[]{:S(2)}, u32[]{:S(2)}) collective-permute-start(f32[2]{0:T(128)S(1)} %fusion.77), channel_id=1, source_target_pairs={{0,4},{2,6},{4,0},{6,2},{1,5},{3,7},{5,1},{7,3},{8,12},{10,14},{12... | collective-permute-start | bytes 32 | tf_op jit(solution)/shard_map/ppermute | solution.py:33
  174.4 3.5 %collective-permute-start.11 = (f32[2]{0:T(128)S(1)}, f32[2]{0:T(128)S(1)}, u32[]{:S(2)}, u32[]{:S(2)}) collective-permute-start(f32[2]{0:T(128)S(1)} %add.213), channel_id=1, source_target_pairs={{0,8},{8,0},{16,24},{24,16},{1,9},{9,1},{17,25},{25,17},{2,10},{10... | collective-permute-start | bytes 32 | tf_op jit(solution)/shard_map/ppermute | solution.py:33
  178.0 3.5 %collective-permute-start.12 = (f32[2]{0:T(128)S(1)}, f32[2]{0:T(128)S(1)}, u32[]{:S(2)}, u32[]{:S(2)}) collective-permute-start(f32[2]{0:T(128)S(1)} %add.214), channel_id=1, source_target_pairs={{0,16},{8,24},{16,0},{24,8},{1,17},{9,25},{17,1},{25,9},{2,18},{10... | collective-permute-start | bytes 32 | tf_op jit(solution)/shard_map/ppermute | solution.py:33
  184.1 2.5 %copy-start.1 = (f32[2,8]{1,0:T(2,128)S(1)}, f32[2,8]{1,0:T(2,128)}, u32[]{:S(2)}) copy-start(f32[2,8]{1,0:T(2,128)} %param.12) | copy-start | bytes 196

commit v8 on v5

--- a/solution.py
+++ b/solution.py
@@ -84,7 +84,9 @@
     systems = diagonal.size // levels
 
     def level_major(band):
-        return jnp.transpose(band.reshape(systems, levels))[:, :, None]
+        return jnp.broadcast_to(
+            jnp.transpose(band.reshape(systems, levels))[:, :, None], (levels, systems, levels)
+        )
 
     bands, ready = lax.optimization_barrier(
         ((level_major(lower), level_major(diagonal), level_major(upper)), ready)
@@ -92,7 +94,7 @@
     inverse = pl.pallas_call(
         thomas_inverse_kernel,
         out_shape=jax.ShapeDtypeStruct((levels, systems, levels), jnp.float32),
-        scratch_shapes=[pltpu.VMEM((levels, systems, 1), jnp.float32)],
+        scratch_shapes=[pltpu.VMEM((levels, systems, levels), jnp.float32)],
         cost_estimate=pl.CostEstimate(
             flops=16 * levels * systems * levels,
             transcendentals=levels * systems,
@@ -162,10 +164,12 @@
 
     arrived = exchange(fields)
     inverse, wanted = block_inverse(block_lower, diagonal, block_upper, wanted)
-    spike_column = jnp.where(
-        my_layer == 0,
-        upper_band[..., -1:] * inverse[..., :, levels - 1],
-        lower_band[..., :1] * inverse[..., :, 0],
+    coupled = lax.broadcasted_iota(jnp.int32, (levels,), 0) == jnp.where(
+        my_layer == 0, levels - 1, 0
+    )
+    inverse_column = jnp.sum(jnp.where(coupled, inverse, 0.0), axis=-1)
+    spike_column = (
+        jnp.where(my_layer == 0, upper_band[..., -1:], lower_band[..., :1]) * inverse_column
     )
     edge_spike = jnp.where(my_layer == 0, spike_column[..., -1], spike_column[..., 0])
     other_spike = from_partner(edge_spike, "gz", 0)

time: 175 us -> 169 us (0.966)
  local copies, waits for them, and re-layouts: 56 us -> 42.4 us
  waiting for transfers between devices: 32.2 us -> 42.9 us
  Pallas kernels: 9.14 us -> 5.92 us
  other arithmetic: 22.4 us -> 24.7 us
  starting transfers between devices: 35.9 us -> 33.8 us
    all_to_all x3, waiting for transfers between devices: 8.84 us -> 19 us  [exchange(): lax.all_to_all(tiles[wanted], 'gy', split_axis=0, concat_axis=0, tiled=True)]
    optimization_barrier x3 -> x0, local copies, waits for them, and re-layouts: 8.6 us -> none  [block_inverse(): lax.optimization_barrier(((level_major(lower), level_major(diagonal), lev...]
    slice x3 -> x0, local copies, waits for them, and re-layouts: 6.03 us -> none  [the longest x1 5.84 us: per_device(): inverse[..., :, levels - 1]]
    broadcast_in_dim x0 -> x3, local copies, waits for them, and re-layouts: none -> 5.81 us  [level_major(): jnp.broadcast_to(jnp.transpose(band.reshape(systems, levels))[:, :, None]...]
    unnamed x30 -> x28, local copies, waits for them, and re-layouts: 12.1 us -> 8.16 us
    pallas_call x1, Pallas kernels: 9.14 us -> 5.92 us  [block_inverse(): pl.pallas_call(thomas_inverse_kernel, out_shape=jax.ShapeDtypeStruct((lev...]
    reduce_sum x0 -> x1, other arithmetic: none -> 2.29 us  [per_device(): inverse_column = jnp.sum(jnp.where(coupled, inverse, 0.0), axis=-1)]
  transfers between devices with their start and end apart: 18 -> 18, of which waited for: 12 -> 14; matrix products, arithmetic and copies ran while one was open for 24% -> 19% of each run, Pallas kernels for 5% -> 4%
where the time goes in v8:
time: 169 us; the launch traced here: 168 us
  waiting for transfers between devices  42.9 us (25%)
  local copies, waits for them, and re-layouts  42.4 us (25%)
  starting transfers between devices  33.8 us (20%)
  other arithmetic  24.7 us (15%)
  matrix products  14.2 us (8%)
  Pallas kernels  5.92 us (4%)
  between operations  3.77 us (2%)
    ppermute x10, waiting for transfers between devices, butterfly_sum(): lax.ppermute(value, axis, [(i, i ^ bit) for i in range(devices)])  22.7 us
    all_to_all x3, waiting for transfers between devices, exchange(): lax.all_to_all(tiles[wanted], 'gy', split_axis=0, concat_axis=0, tiled=True)  19 us
    gather x8, local copies, waits for them, and re-layouts, per_device(): tile_pool[pool_index[:, entry_k]]  17.8 us
    all_to_all x3, starting transfers between devices, exchange(): lax.all_to_all(tiles[wanted], 'gy', split_axis=0, concat_axis=0, tiled=True)  12.9 us
    ppermute x10, starting transfers between devices, butterfly_sum(): lax.ppermute(value, axis, [(i, i ^ bit) for i in range(devices)])  12.4 us
    unnamed x28, local copies, waits for them, and re-layouts  8.16 us
    dot_general x8, matrix products, per_device(): jnp.einsum('tcd,tfdz->tfcz', interp_weights[:, entry_k], tile_pool[pool_i...  6.92 us
    dot_general x2, matrix products, per_device(): jnp.einsum('tfzy,tfcy->tfcz', inverse, advected, precision=HIGHEST, prefe...  6.61 us
  transfers between devices with their start and end apart: 18, of which 14 were waited for; matrix products, arithmetic and copies ran while one was open for 19% of the time, Pallas kernels for 4%

profile of v8, /device:TPU:0, one launch (start us, length us, event | category | flops | bytes accessed | tf_op | source)
XLA Modules:
  0.0 167.7 jit_solution(7984865254368509314)
XLA Ops:
  1.4 1.3 collective-permute-start.5
  2.6 0.8 copy.152
  4.6 6.3 %all-to-all-start = ((s32[4,1,4]{2,1,0:T(1,128)}), s32[4,1,4]{2,1,0:T(1,128)S(1)}, u32[]{:S(2)}, u32[]{:S(2)}) async-start(s32[4,1,4]{2,1,0:T(1,128)} %bitcast.4), calls=%async_computation | async-start | bytes 4096 | tf_op jit(solution)/shard_map/all_to_all | solution.py:159
  11.0 0.8 copy.168
  11.8 1.9 %convert_reduce_fusion.1 = f32[]{:T(128)} fusion(bf16[16,128,128]{2,1,0:T(8,128)(2,1)} %param.7), kind=kLoop, calls=%fused_computation.40 | loop fusion | flops 524287 | bytes 524292 | tf_op jit(solution)/shard_map/reduce_sum | solution.py:191
  14.2 1.3 pad_maximum_fusion.1
  16.7 0.7 gather_fusion
  17.5 1.1 copy.154
  18.6 5.1 %all-to-all-start.1 = ((bf16[4,4,2,128,128]{4,3,1,2,0:T(8,128)(2,1)}), bf16[4,4,2,128,128]{4,3,1,2,0:T(8,128)(2,1)S(1)}, u32[]{:S(2)}, u32[]{:S(2)}) async-start(bf16[4,4,2,128,128]{4,3,1,2,0:T(8,128)(2,1)} %copy.154), calls=%async_computation.1 | async-start | bytes 2097152 | tf_op jit(solution)/shard_map/all_to_all | solution.py:162
  24.4 1.9 %broadcast_in_dim.68.diagonal_ref = f32[128,32,128]{2,1,0:T(8,128)} broadcast(f32[128,32]{1,0:T(8,128)S(1)} %bitcast.147), dimensions={0,1} | broadcast | bytes 2113536 | tf_op jit(solution)/shard_map/broadcast_in_dim | solution.py:87
  26.3 1.9 %broadcast_in_dim.66.lower_ref = f32[128,32,128]{2,1,0:T(8,128)} broadcast(f32[128,32]{1,0:T(8,128)S(1)} %bitcast.146), dimensions={0,1} | broadcast | bytes 2113536 | tf_op jit(solution)/shard_map/broadcast_in_dim | solution.py:87
  28.2 2.0 %broadcast_in_dim.121.upper_ref = f32[128,32,128]{2,1,0:T(8,128)} broadcast(f32[128,32]{1,0:T(8,128)S(1)} %copy.175), dimensions={0,1} | broadcast | bytes 2113536 | tf_op jit(solution)/shard_map/broadcast_in_dim | solution.py:87
  30.3 5.9 %shard_map.94 = f32[128,32,128]{2,1,0:T(8,128)} custom-call(f32[128,32,128]{2,1,0:T(8,128)} %broadcast_in_dim.66.lower_ref, f32[128,32,128]{2,1,0:T(8,128)} %broadcast_in_dim.68.diagonal_ref, f32[128,32,128]{2,1,0:T(8,128)} %broadcast_in_dim.121.upper_ref), custom_call_target="tpu_custom_call" | custom-call | flops 8388608 | bytes 33554432 | tf_op jit(solution)/shard_map/pallas_call | solution.py:94
  36.2 2.3 %fusion = f32[32,128]{0,1:T(8,128)S(1)} fusion(f32[128,32,128]{2,1,0:T(8,128)} %shard_map.94, pred[128]{0:T(512)(128)(4,1)S(1)} %iota_compare_fusion.9), kind=kLoop, calls=%fused_computation.14 | loop fusion | flops 1044480 | bytes 2113664 | tf_op jit(solution)/shard_map/reduce_sum | solution.py:170
  39.1 0.9 collective-permute-done.7
  40.2 9.9 %all-to-all-done.1 = bf16[4,4,2,128,128]{4,3,1,2,0:T(8,128)(2,1)S(1)} async-done(((bf16[4,4,2,128,128]{4,3,1,2,0:T(8,128)(2,1)}), bf16[4,4,2,128,128]{4,3,1,2,0:T(8,128)(2,1)S(1)}, u32[]{:S(2)}, u32[]{:S(2)}) %all-to-all-start.1) | async-done | bytes 1048608 | tf_op jit(solution)/shard_map/all_to_all | solution.py:162
  50.5 0.7 gather_fusion.4
  51.2 1.7 gather_fusion.3
  52.9 1.7 gather_fusion.2
  54.5 1.6 gather_fusion.1
  56.2 2.0 %fusion.16 = f32[16,2,128,128]{3,2,1,0:T(8,128)S(1)} fusion(bf16[16,2,128,128]{3,2,1,0:T(8,128)(2,1)} %gather_fusion.3, bf16[16,4,128,128]{3,2,1,0:T(8,128)(2,1)} %param.10), kind=kOutput, calls=%fused_computation.47 | convolution fusion | flops 134217728 | bytes 3670016 | tf_op jit(solution)/shard_map/tcd,tfdz->tfcz/dot_general | solution.py:183
  60.8 1.0 copy-done.1
  61.8 3.3 %fusion.3 = f32[16,2,128,128]{2,3,1,0:T(8,128)S(1)} fusion(f32[16,2,128,128]{3,2,1,0:T(8,128)S(1)} %add_add_fusion.1, f32[16,2,128,128]{3,1,0,2:T(2,128)S(1)} %bitcast.134), kind=kOutput, calls=%fused_computation.21 | convolution fusion | flops 805306368 | bytes 6291456 | tf_op jit(solution)/shard_map/tfzy,tfcy->tfcz/dot_general | solution.py:194
  65.2 0.9 slice_reduce_fusion.1
  67.3 1.3 copy-done.4
  68.7 1.4 gather_fusion.6
  70.1 3.7 %all-to-all-start.3 = ((bf16[4,4,128,128]{2,3,1,0:T(8,128)(2,1)}), bf16[4,4,128,128]{2,3,1,0:T(8,128)(2,1)S(1)}, u32[]{:S(2)}, u32[]{:S(2)}) async-start(bf16[4,4,128,128]{2,3,1,0:T(8,128)(2,1)} %bitcast.55), calls=%async_computation.3 | async-start | bytes 1048576 | tf_op jit(solution)/shard_map/all_to_all | solution.py:162
  73.8 1.4 pad_maximum_fusion.3
  75.3 0.9 collective-permute-done
  76.3 1.4 fusion.75
  77.6 1.8 %collective-permute-start.1 = (f32[2]{0:T(128)S(1)}, f32[2]{0:T(128)S(1)}, u32[]{:S(2)}, u32[]{:S(2)}) collective-permute-start(f32[2]{0:T(128)S(1)} %fusion.75), channel_id=1, source_target_pairs={{0,2},{2,0},{4,6},{6,4},{1,3},{3,1},{5,7},{7,5},{8,10},{10,8},{12,... | collective-permute-start | bytes 32 | tf_op jit(solution)/shard_map/ppermute | solution.py:32
  79.4 3.7 %collective-permute-done.1 = f32[2]{0:T(128)S(1)} collective-permute-done((f32[2]{0:T(128)S(1)}, f32[2]{0:T(128)S(1)}, u32[]{:S(2)}, u32[]{:S(2)}) %collective-permute-start.1) | collective-permute-done | bytes 40 | tf_op jit(solution)/shard_map/ppermute | solution.py:32
  83.1 1.4 fusion.77
  84.5 4.3 %collective-permute-start.2 = (f32[2]{0:T(128)S(1)}, f32[2]{0:T(128)S(1)}, u32[]{:S(2)}, u32[]{:S(2)}) collective-permute-start(f32[2]{0:T(128)S(1)} %fusion.77), channel_id=1, source_target_pairs={{0,4},{2,6},{4,0},{6,2},{1,5},{3,7},{5,1},{7,3},{8,12},{10,14},{12... | collective-permute-start | bytes 32 | tf_op jit(solution)/shard_map/ppermute | solution.py:32
  88.8 1.5 collective-permute-done.2
  90.3 1.5 collective-permute-start.3
  91.8 2.0 %collective-permute-done.3 = f32[2]{0:T(128)S(1)} collective-permute-done((f32[2]{0:T(128)S(1)}, f32[2]{0:T(128)S(1)}, u32[]{:S(2)}, u32[]{:S(2)}) %collective-permute-start.3) | collective-permute-done | bytes 40 | tf_op jit(solution)/shard_map/ppermute | solution.py:32
  93.8 1.5 collective-permute-start.4
  95.4 2.0 %collective-permute-done.4 = f32[2]{0:T(128)S(1)} collective-permute-done((f32[2]{0:T(128)S(1)}, f32[2]{0:T(128)S(1)}, u32[]{:S(2)}, u32[]{:S(2)}) %collective-permute-start.4) | collective-permute-done | bytes 40 | tf_op jit(solution)/shard_map/ppermute | solution.py:32
  99.3 2.1 %convert_reduce_fusion = (f32[]{:T(128)}, bf16[16,1,128,128]{2,3,1,0:T(8,128)(2,1)S(1)}) fusion(f32[16,2,128,128]{2,3,1,0:T(8,128)} %copy-done.4, f32[]{:T(128)} %bitcast.22), kind=kLoop, calls=%fused_computation.39 | loop fusion | flops 1048575 | bytes 1572872 | tf_op jit(solution)/shard_map/reduce_sum | solution.py:191
  101.4 1.4 gather_fusion.5
  102.9 4.2 %all-to-all-start.2 = ((bf16[4,4,128,128]{2,3,1,0:T(8,128)(2,1)}), bf16[4,4,128,128]{2,3,1,0:T(8,128)(2,1)}, u32[]{:S(2)}, u32[]{:S(2)}) async-start(bf16[4,4,128,128]{2,3,1,0:T(8,128)(2,1)} %bitcast.52), calls=%async_computation.2 | async-start | bytes 1048576 | tf_op jit(solution)/shard_map/all_to_all | solution.py:162
  107.0 2.1 %slice.225 = bf16[16,1,128,128]{2,3,1,0:T(8,128)(2,1)} slice(f32[16,2,128,128]{2,3,1,0:T(8,128)} %copy-done.4), slice={[0:16], [1:2], [0:128], [0:128]} | slice | bytes 1048576 | tf_op jit(solution)/shard_map/slice | solution.py:208
  109.2 9.1 %all-to-all-done.2 = bf16[4,4,128,128]{2,3,1,0:T(8,128)(2,1)} async-done(((bf16[4,4,128,128]{2,3,1,0:T(8,128)(2,1)}), bf16[4,4,128,128]{2,3,1,0:T(8,128)(2,1)}, u32[]{:S(2)}, u32[]{:S(2)}) %all-to-all-start.2) | async-done | bytes 524320 | tf_op jit(solution)/shard_map/all_to_all | solution.py:162
  118.2 2.7 %maximum_maximum_fusion = bf16[32,2,128,128]{2,3,1,0:T(8,128)(2,1)} fusion(bf16[16,1,128,128]{2,3,1,0:T(8,128)(2,1)S(1)} %bitcast.143, bf16[16,1,128,128]{2,3,1,0:T(8,128)(2,1)} %bitcast.53, bf16[16,1,128,128]{2,3,1,0:T(8,128)(2,1)} %slice.225, bf16[16,1,128,128]{2,3,1,0:T(8,128)(2,1)S(1)} %get-tuple-element.31), kind=kLoop, calls=%fused_computation.12 | loop fusion | flops 3145728 | bytes 4194304 | tf_op jit(solution)/shard_map/concatenate | solution.py:180
  121.0 2.3 %gather_fusion.10 = bf16[16,2,128,128]{2,3,1,0:T(8,128)(2,1)S(1)} fusion(bf16[32,2,128,128]{2,3,1,0:T(8,128)(2,1)} %maximum_maximum_fusion, s32[1024]{0:T(1024)S(1)} %get-tuple-element.49), kind=kCustom, calls=%fused_computation.10 | custom fusion | bytes 2097216 | tf_op jit(solution)/shard_map/gather | solution.py:186
  123.3 3.3 %gather_fusion.9 = bf16[16,2,128,128]{2,3,1,0:T(8,128)(2,1)} fusion(bf16[32,2,128,128]{2,3,1,0:T(8,128)(2,1)} %maximum_maximum_fusion, s32[1024]{0:T(1024)S(1)} %get-tuple-element.50), kind=kCustom, calls=%fused_computation.9 | custom fusion | bytes 2097216 | tf_op jit(solution)/shard_map/gather | solution.py:186
  126.5 3.3 %gather_fusion.8 = bf16[16,2,128,128]{2,3,1,0:T(8,128)(2,1)} fusion(bf16[32,2,128,128]{2,3,1,0:T(8,128)(2,1)} %maximum_maximum_fusion, s32[1024]{0:T(1024)S(1)} %get-tuple-element.51), kind=kCustom, calls=%fused_computation.8 | custom fusion | bytes 2097216 | tf_op jit(solution)/shard_map/gather | solution.py:186
  129.8 3.2 %gather_fusion.7 = bf16[16,2,128,128]{2,3,1,0:T(8,128)(2,1)} fusion(bf16[32,2,128,128]{2,3,1,0:T(8,128)(2,1)} %maximum_maximum_fusion, s32[1024]{0:T(1024)S(1)} %get-tuple-element.52), kind=kCustom, calls=%fused_computation.7 | custom fusion | bytes 2097216 | tf_op jit(solution)/shard_map/gather | solution.py:186
  133.0 1.9 %fusion.22 = f32[16,2,128,128]{3,2,1,0:T(8,128)S(1)} fusion(bf16[16,2,128,128]{2,3,1,0:T(8,128)(2,1)} %gather_fusion.7, bf16[16,4,128,128]{3,2,1,0:T(8,128)(2,1)} %param.10), kind=kOutput, calls=%fused_computation.53 | convolution fusion | flops 134217728 | bytes 3670016 | tf_op jit(solution)/shard_map/tcd,tfdz->tfcz/dot_general | solution.py:183
  135.8 0.8 copy-done.6
  137.6 3.3 %fusion.1 = f32[16,2,128,128]{2,3,1,0:T(8,128)S(1)} fusion(f32[16,2,128,128]{3,2,1,0:T(8,128)S(1)} %add_add_fusion, f32[16,2,128,128]{3,1,0,2:T(2,128)S(1)} %bitcast.135), kind=kOutput, calls=%fused_computation.19 | convolution fusion | flops 805306368 | bytes 6291456 | tf_op jit(solution)/shard_map/tfzy,tfcy->tfcz/dot_general | solution.py:194
  140.9 0.9 slice_reduce_fusion
  141.8 1.4 pad_maximum_fusion.4
  144.3 1.4 fusion.74
  145.7 3.5 %collective-permute-done.9 = f32[2]{0:T(128)S(1)} collective-permute-done((f32[2]{0:T(128)S(1)}, f32[2]{0:T(128)S(1)}, u32[]{:S(2)}, u32[]{:S(2)}) %collective-permute-start.9) | collective-permute-done | bytes 40 | tf_op jit(solution)/shard_map/ppermute | solution.py:32
  149.2 1.4 fusion.76
  150.6 4.4 %collective-permute-done.10 = f32[2]{0:T(128)S(1)} collective-permute-done((f32[2]{0:T(128)S(1)}, f32[2]{0:T(128)S(1)}, u32[]{:S(2)}, u32[]{:S(2)}) %collective-permute-start.10) | collective-permute-done | bytes 40 | tf_op jit(solution)/shard_map/ppermute | solution.py:32
  155.0 1.5 collective-permute-start.11
  156.5 2.0 %collective-permute-done.11 = f32[2]{0:T(128)S(1)} collective-permute-done((f32[2]{0:T(128)S(1)}, f32[2]{0:T(128)S(1)}, u32[]{:S(2)}, u32[]{:S(2)}) %collective-permute-start.11) | collective-permute-done | bytes 40 | tf_op jit(solution)/shard_map/ppermute | solution.py:32
  158.6 1.5 collective-permute-start.12
  160.1 2.0 %collective-permute-done.12 = f32[2]{0:T(128)S(1)} collective-permute-done((f32[2]{0:T(128)S(1)}, f32[2]{0:T(128)S(1)}, u32[]{:S(2)}, u32[]{:S(2)}) %collective-permute-start.12) | collective-permute-done | bytes 40 | tf_op jit(solution)/shard_map/ppermute | solution.py:32
  165.7 1.0 copy.189
  166.7 1.0 copy.188
  (110 shorter events, 15.4 us)
Async XLA Ops:
  0.6 14.9 %copy-start = (f32[2,8]{1,0:T(2,128)S(1)}, f32[2,8]{1,0:T(2,128)}, u32[]{:S(2)}) copy-start(f32[2,8]{1,0:T(2,128)} %param.12) | copy-start | bytes 196
  0.6 15.3 %copy-start.11 = (f32[8]{0:T(128)S(1)}, f32[8]{0:T(128)}, u32[]{:S(2)}) copy-start(f32[8]{0:T(128)} %param.13) | copy-start | bytes 100
  1.4 14.4 %collective-permute-start.5 = (s32[16,1]{0,1:T(1,128)S(1)}, s32[16,1]{0,1:T(1,128)S(1)}, u32[]{:S(2)}, u32[]{:S(2)}) collective-permute-start(s32[16,1]{0,1:T(1,128)S(1)} %slice.108), channel_id=1, source_target_pairs={{1,0},{3,2},{5,4},{7,6},{9,8},{11,10},{13,12},{15,14},{17,16},{19,... | collective-permute-start | bytes 200 | tf_op jit(solution)/shard_map/ppermute | solution.py:17
  4.6 12.0 %all-to-all-start = ((s32[4,1,4]{2,1,0:T(1,128)}), s32[4,1,4]{2,1,0:T(1,128)S(1)}, u32[]{:S(2)}, u32[]{:S(2)}) async-start(s32[4,1,4]{2,1,0:T(1,128)} %bitcast.4), calls=%async_computation | async-start | bytes 4096 | tf_op jit(solution)/shard_map/all_to_all | solution.py:159
  18.6 31.5 %all-to-all-start.1 = ((bf16[4,4,2,128,128]{4,3,1,2,0:T(8,128)(2,1)}), bf16[4,4,2,128,128]{4,3,1,2,0:T(8,128)(2,1)S(1)}, u32[]{:S(2)}, u32[]{:S(2)}) async-start(bf16[4,4,2,128,128]{4,3,1,2,0:T(8,128)(2,1)} %copy.154), calls=%async_computation.1 | async-start | bytes 2097152 | tf_op jit(solution)/shard_map/all_to_all | solution.py:162
  36.2 14.0 %copy-start.5 = (bf16[16,128,128]{2,1,0:T(8,128)(2,1)S(1)}, bf16[16,128,128]{2,1,0:T(8,128)(2,1)}, u32[]{:S(2)}) copy-start(bf16[16,128,128]{2,1,0:T(8,128)(2,1)} %param.7) | copy-start | bytes 1572868
  36.2 14.0 %copy-start.10 = (bf16[16,128,128]{2,1,0:T(8,128)(2,1)S(1)}, bf16[16,128,128]{2,1,0:T(8,128)(2,1)}, u32[]{:S(2)}) copy-start(bf16[16,128,128]{2,1,0:T(8,128)(2,1)} %param.8) | copy-start | bytes 1572868
  38.8 1.1 collective-permute-start.7
  56.2 2.1 %copy-start.2 = (bf16[16,4,128,128]{3,2,1,0:T(8,128)(2,1)S(1)}, bf16[16,4,128,128]{3,2,1,0:T(8,128)(2,1)}, u32[]{:S(2)}) copy-start(bf16[16,4,128,128]{3,2,1,0:T(8,128)(2,1)} %param.10) | copy-start | bytes 6291460
  56.2 2.3 %copy-start.9 = (bf16[16,2,128,128]{3,2,1,0:T(8,128)(2,1)S(1)}, bf16[16,2,128,128]{3,2,1,0:T(8,128)(2,1)}, u32[]{:S(2)}) copy-start(bf16[16,2,128,128]{3,2,1,0:T(8,128)(2,1)} %gather_fusion.1) | copy-start | bytes 3145732
  58.5 1.2 copy-start.7
  60.2 1.6 copy-start.1
  65.2 1.2 collective-permute-start.6
  67.3 1.3 copy-start.4
  70.1 32.8 %all-to-all-start.3 = ((bf16[4,4,128,128]{2,3,1,0:T(8,128)(2,1)}), bf16[4,4,128,128]{2,3,1,0:T(8,128)(2,1)S(1)}, u32[]{:S(2)}, u32[]{:S(2)}) async-start(bf16[4,4,128,128]{2,3,1,0:T(8,128)(2,1)} %bitcast.55), calls=%async_computation.3 | async-start | bytes 1048576 | tf_op jit(solution)/shard_map/all_to_all | solution.py:162
  75.1 1.1 collective-permute-start
  77.6 5.5 %collective-permute-start.1 = (f32[2]{0:T(128)S(1)}, f32[2]{0:T(128)S(1)}, u32[]{:S(2)}, u32[]{:S(2)}) collective-permute-start(f32[2]{0:T(128)S(1)} %fusion.75), channel_id=1, source_target_pairs={{0,2},{2,0},{4,6},{6,4},{1,3},{3,1},{5,7},{7,5},{8,10},{10,8},{12,... | collective-permute-start | bytes 32 | tf_op jit(solution)/shard_map/ppermute | solution.py:32
  84.5 5.8 %collective-permute-start.2 = (f32[2]{0:T(128)S(1)}, f32[2]{0:T(128)S(1)}, u32[]{:S(2)}, u32[]{:S(2)}) collective-permute-start(f32[2]{0:T(128)S(1)} %fusion.77), channel_id=1, source_target_pairs={{0,4},{2,6},{4,0},{6,2},{1,5},{3,7},{5,1},{7,3},{8,12},{10,14},{12... | collective-permute-start | bytes 32 | tf_op jit(solution)/shard_map/ppermute | solution.py:32
  90.3 3.5 %collective-permute-start.3 = (f32[2]{0:T(128)S(1)}, f32[2]{0:T(128)S(1)}, u32[]{:S(2)}, u32[]{:S(2)}) collective-permute-start(f32[2]{0:T(128)S(1)} %add.195), channel_id=1, source_target_pairs={{0,8},{8,0},{16,24},{24,16},{1,9},{9,1},{17,25},{25,17},{2,10},{10... | collective-permute-start | bytes 32 | tf_op jit(solution)/shard_map/ppermute | solution.py:32
  93.8 3.5 %collective-permute-start.4 = (f32[2]{0:T(128)S(1)}, f32[2]{0:T(128)S(1)}, u32[]{:S(2)}, u32[]{:S(2)}) collective-permute-start(f32[2]{0:T(128)S(1)} %add.196), channel_id=1, source_target_pairs={{0,16},{8,24},{16,0},{24,8},{1,17},{9,25},{17,1},{25,9},{2,18},{10... | collective-permute-start | bytes 32 | tf_op jit(solution)/shard_map/ppermute | solution.py:32
  102.9 15.4 %all-to-all-start.2 = ((bf16[4,4,128,128]{2,3,1,0:T(8,128)(2,1)}), bf16[4,4,128,128]{2,3,1,0:T(8,128)(2,1)}, u32[]{:S(2)}, u32[]{:S(2)}) async-start(bf16[4,4,128,128]{2,3,1,0:T(8,128)(2,1)} %bitcast.52), calls=%async_computation.2 | async-start | bytes 1048576 | tf_op jit(solution)/shard_map/all_to_all | solution.py:162
  133.0 2.1 %copy-start.3 = (bf16[16,4,128,128]{3,2,1,0:T(8,128)(2,1)S(1)}, bf16[16,4,128,128]{3,2,1,0:T(8,128)(2,1)}, u32[]{:S(2)}) copy-start(bf16[16,4,128,128]{3,2,1,0:T(8,128)(2,1)} %param.10) | copy-start | bytes 6291460
  133.0 2.3 %copy-start.8 = (bf16[16,2,128,128]{2,3,1,0:T(8,128)(2,1)S(1)}, bf16[16,2,128,128]{2,3,1,0:T(8,128)(2,1)}, u32[]{:S(2)}) copy-start(bf16[16,2,128,128]{2,3,1,0:T(8,128)(2,1)} %gather_fusion.8) | copy-start | bytes 3145732
  135.4 1.2 copy-start.6
  143.2 1.1 collective-permute-start.8
  143.2 21.4 %collective-permute-start.13 = (f32[16,2,128]{2,1,0:T(2,128)S(1)}, f32[16,2,128]{2,1,0:T(2,128)S(1)}, u32[]{:S(2)}, u32[]{:S(2)}) collective-permute-start(f32[16,2,128]{2,1,0:T(2,128)S(1)} %select_bitcast_fusion), channel_id=1, source_target_pairs={{0,1},{1,0},{2,3},{3,2},{4,5},{5,4},{6,7},{7,6},{8,9},{9,8},{10,11... | collective-permute-start | bytes 49160 | tf_op jit(solution)/shard_map/ppermute | solution.py:21
  145.7 3.5 %collective-permute-start.9 = (f32[2]{0:T(128)S(1)}, f32[2]{0:T(128)S(1)}, u32[]{:S(2)}, u32[]{:S(2)}) collective-permute-start(f32[2]{0:T(128)S(1)} %fusion.74), channel_id=1, source_target_pairs={{0,2},{2,0},{4,6},{6,4},{1,3},{3,1},{5,7},{7,5},{8,10},{10,8},{12,... | collective-permute-start | bytes 32 | tf_op jit(solution)/shard_map/ppermute | solution.py:32
  150.6 4.4 %collective-permute-start.10 = (f32[2]{0:T(128)S(1)}, f32[2]{0:T(128)S(1)}, u32[]{:S(2)}, u32[]{:S(2)}) collective-permute-start(f32[2]{0:T(128)S(1)} %fusion.76), channel_id=1, source_target_pairs={{0,4},{2,6},{4,0},{6,2},{1,5},{3,7},{5,1},{7,3},{8,12},{10,14},{12... | collective-permute-start | bytes 32 | tf_op jit(solution)/shard_map/ppermute | solution.py:32
  155.0 3.5 %collective-permute-start.11 = (f32[2]{0:T(128)S(1)}, f32[2]{0:T(128)S(1)}, u32[]{:S(2)}, u32[]{:S(2)}) collective-permute-start(f32[2]{0:T(128)S(1)} %add.213), channel_id=1, source_target_pairs={{0,8},{8,0},{16,24},{24,16},{1,9},{9,1},{17,25},{25,17},{2,10},{10... | collective-permute-start | bytes 32 | tf_op jit(solution)/shard_map/ppermute | solution.py:32
  158.6 3.5 %collective-permute-start.12 = (f32[2]{0:T(128)S(1)}, f32[2]{0:T(128)S(1)}, u32[]{:S(2)}, u32[]{:S(2)}) collective-permute-start(f32[2]{0:T(128)S(1)} %add.214), channel_id=1, source_target_pairs={{0,16},{8,24},{16,0},{24,8},{1,17},{9,25},{17,1},{25,9},{2,18},{10... | collective-permute-start | bytes 32 | tf_op jit(solution)/shard_map/ppermute | solution.py:32

commit v9 on v8

--- a/solution.py
+++ b/solution.py
@@ -134,9 +134,28 @@
         & (slot_index[None, None, :] == jnp.arange(capacity, dtype=jnp.int32)[None, :, None])
     )
     requests = jnp.sum(jnp.where(match, local_tile[None, None, :], 0), axis=-1, dtype=jnp.int32)
-    pool_index = jnp.where(
-        remote, tiles_here + owner_lane * capacity + slot_index, local_tile
-    ).reshape(tiles_here, sources_per)
+    entry_count = entries.shape[0]
+    remote_rank = jnp.cumsum(remote.astype(jnp.int32)) - 1
+    picks = remote[None, :] & (
+        remote_rank[None, :] == jnp.arange(remote_count, dtype=jnp.int32)[:, None]
+    )
+    remote_entry = jnp.sum(
+        jnp.where(picks, jnp.arange(entry_count, dtype=jnp.int32)[None, :], 0), axis=1
+    )
+    remote_slot = (owner_lane * capacity + slot_index)[remote_entry]
+    remote_tile = remote_entry // sources_per
+    remote_weights = interp_weights.reshape((entry_count,) + interp_weights.shape[2:])[
+        remote_entry
+    ]
+    remote_owner = (
+        remote_tile[None, :] == jnp.arange(tiles_here, dtype=jnp.int32)[:, None]
+    ).astype(jnp.float32)
+    local_index = jnp.where(remote, 0, local_tile).reshape(tiles_here, sources_per)
+    local_weights = jnp.where(
+        remote.reshape(tiles_here, sources_per)[:, :, None, None],
+        jnp.zeros_like(interp_weights),
+        interp_weights,
+    )
     level_class = jnp.repeat(settle_class, levels // settle_class.shape[1], axis=1)
     both_fall = jnp.stack([fall_table, jnp.zeros_like(fall_table)])
     diffusion = table_lookup(level_class, kappa_table)
@@ -177,15 +196,27 @@
     high_spike = jnp.where(my_layer == 0, other_spike, edge_spike)
     ratios = []
     for step_index in range(STEPS):
-        tile_pool = jnp.concatenate([fields, arrived], axis=0)
         advected = jnp.zeros(fields.shape, jnp.float32)
         for entry_k in range(sources_per):
             advected = advected + jnp.einsum(
                 "tcd,tfdz->tfcz",
-                interp_weights[:, entry_k],
-                tile_pool[pool_index[:, entry_k]],
+                local_weights[:, entry_k],
+                fields[local_index[:, entry_k]],
                 preferred_element_type=jnp.float32,
             )
+        remote_terms = jnp.einsum(
+            "rcd,rfdz->rfcz",
+            remote_weights,
+            arrived[remote_slot],
+            preferred_element_type=jnp.float32,
+        )
+        advected = advected + jnp.einsum(
+            "tr,rfcz->tfcz",
+            remote_owner,
+            remote_terms,
+            precision=HIGHEST,
+            preferred_element_type=jnp.float32,
+        )
         last = step_index + 1 == STEPS
         totals = butterfly_sum(
             jnp.stack([jnp.sum(fields[:, 0], dtype=jnp.float32), jnp.sum(advected[:, 0])]),

time: 169 us -> 195 us (1.15)
  matrix products: 14.2 us -> 40.8 us
  waiting for transfers between devices: 42.9 us -> 30.7 us
  starting transfers between devices: 33.8 us -> 40.4 us
  local copies, waits for them, and re-layouts: 42.4 us -> 46.9 us
    dot_general x8 -> x12, matrix products: 6.92 us -> 33.5 us  [the longest x8 25.8 us: per_device(): jnp.einsum('tcd,tfdz->tfcz', local_weights[:, entry_k], fields[local_inde...]
    all_to_all x3, waiting for transfers between devices: 19 us -> 10.3 us  [exchange(): lax.all_to_all(tiles[wanted], 'gy', split_axis=0, concat_axis=0, tiled=True)]
    ppermute x10, starting transfers between devices: 12.4 us -> 18.2 us  [butterfly_sum(): lax.ppermute(value, axis, [(i, i ^ bit) for i in range(devices)])]
    dot_general x0 -> x2, local copies, waits for them, and re-layouts: none -> 4.88 us  [per_device(): jnp.einsum('tr,rfcz->tfcz', remote_owner, remote_terms, precision=HIGHEST...]
    ppermute x10, waiting for transfers between devices: 22.7 us -> 19.6 us  [butterfly_sum(): lax.ppermute(value, axis, [(i, i ^ bit) for i in range(devices)])]
    concatenate x2 -> x0, other arithmetic: 2.94 us -> none  [per_device(): tile_pool = jnp.concatenate([fields, arrived], axis=0)]
    transpose x0 -> x2, local copies, waits for them, and re-layouts: none -> 2.74 us  [per_device(): jnp.einsum('rcd,rfdz->rfcz', remote_weights, arrived[remote_slot], prefer...]
    another operation x0 -> x3, other arithmetic: none -> 2.69 us  [the longest x1 1.3 us: per_device(): fields = jnp.stack([next_concentration, next_turbulence], axis=1)]
  transfers between devices with their start and end apart: 18 -> 18, of which waited for: 14 -> 11; matrix products, arithmetic and copies ran while one was open for 19% -> 35% of each run, Pallas kernels for 4% -> 3%
where the time goes in v9:
time: 195 us; the launch traced here: 194 us
  local copies, waits for them, and re-layouts  46.9 us (24%)
  matrix products  40.8 us (21%)
  starting transfers between devices  40.4 us (21%)
  waiting for transfers between devices  30.7 us (16%)
  other arithmetic  25.1 us (13%)
  Pallas kernels  5.95 us (3%)
  between operations  3.82 us (2%)
    dot_general x8, matrix products, per_device(): jnp.einsum('tcd,tfdz->tfcz', local_weights[:, entry_k], fields[local_inde...  25.8 us
    ppermute x10, waiting for transfers between devices, butterfly_sum(): lax.ppermute(value, axis, [(i, i ^ bit) for i in range(devices)])  19.6 us
    ppermute x10, starting transfers between devices, butterfly_sum(): lax.ppermute(value, axis, [(i, i ^ bit) for i in range(devices)])  18.2 us
    all_to_all x3, starting transfers between devices, exchange(): lax.all_to_all(tiles[wanted], 'gy', split_axis=0, concat_axis=0, tiled=True)  13.6 us
    gather x8, local copies, waits for them, and re-layouts, per_device(): fields[local_index[:, entry_k]]  12.6 us
    all_to_all x3, waiting for transfers between devices, exchange(): lax.all_to_all(tiles[wanted], 'gy', split_axis=0, concat_axis=0, tiled=True)  10.3 us
    dot_general x2, matrix products, per_device(): jnp.einsum('tfzy,tfcy->tfcz', inverse, advected, precision=HIGHEST, prefe...  6.58 us
    all_to_all x1, starting transfers between devices, per_device(): lax.all_to_all(requests, 'gy', split_axis=0, concat_axis=0, tiled=True)  6.32 us
  transfers between devices with their start and end apart: 18, of which 11 were waited for; matrix products, arithmetic and copies ran while one was open for 35% of the time, Pallas kernels for 3%

profile of v9, /device:TPU:0, one launch (start us, length us, event | category | flops | bytes accessed | tf_op | source)
XLA Modules:
  0.0 193.6 jit_solution(3837400230212736617)
XLA Ops:
  2.7 6.3 %all-to-all-start = ((s32[4,1,4]{2,1,0:T(1,128)}), s32[4,1,4]{2,1,0:T(1,128)S(1)}, u32[]{:S(2)}, u32[]{:S(2)}) async-start(s32[4,1,4]{2,1,0:T(1,128)} %bitcast.23), calls=%async_computation | async-start | bytes 4096 | tf_op jit(solution)/shard_map/all_to_all | solution.py:178
  13.6 2.2 %gather_fusion.7 = bf16[8,128,128]{2,1,0:T(8,128)(2,1)S(1)} fusion(bf16[64,128,128]{2,1,0:T(8,128)(2,1)} %bitcast.165, s32[1024]{0:T(1024)S(1)} %pad_clamp_fusion.2), kind=kCustom, calls=%fused_computation.7 | custom fusion | bytes 524320 | tf_op jit(solution)/shard_map/gather | solution.py:147
  15.8 1.9 copy_select_fusion
  19.0 1.6 gather_fusion.2
  20.6 1.7 gather_fusion
  22.3 3.1 %fusion.17 = f32[16,2,128,128]{3,2,1,0:T(8,128)} fusion(bf16[16,2,128,128]{3,2,1,0:T(8,128)(2,1)} %gather_fusion.2, bf16[16,4,128,128]{3,2,0,1:T(8,128)(2,1)S(1)} %copy_select_fusion), kind=kOutput, calls=%fused_computation.59 | convolution fusion | flops 134217728 | bytes 3670016 | tf_op jit(solution)/shard_map/tcd,tfdz->tfcz/dot_general | solution.py:201
  25.4 1.8 fusion.13
  27.2 1.8 gather_fusion.1
  29.0 3.1 %fusion.15 = f32[16,2,128,128]{3,2,1,0:T(8,128)} fusion(bf16[16,2,128,128]{3,2,1,0:T(8,128)(2,1)} %gather_fusion.1, bf16[16,4,128,128]{3,2,0,1:T(8,128)(2,1)S(1)} %copy_select_fusion), kind=kOutput, calls=%fused_computation.57 | convolution fusion | flops 134217728 | bytes 3670016 | tf_op jit(solution)/shard_map/tcd,tfdz->tfcz/dot_general | solution.py:201
  34.4 1.7 gather_fusion.4
  36.1 5.1 %all-to-all-start.1 = ((bf16[4,4,2,128,128]{4,3,2,1,0:T(8,128)(2,1)}), bf16[4,4,2,128,128]{4,3,2,1,0:T(8,128)(2,1)S(1)}, u32[]{:S(2)}, u32[]{:S(2)}) async-start(bf16[4,4,2,128,128]{4,3,2,1,0:T(8,128)(2,1)} %bitcast.25), calls=%async_computation.1 | async-start | bytes 2097152 | tf_op jit(solution)/shard_map/all_to_all | solution.py:181
  41.7 1.9 %broadcast_in_dim.94.lower_ref = f32[128,32,128]{2,1,0:T(8,128)} broadcast(f32[128,32]{1,0:T(8,128)S(1)} %bitcast.170), dimensions={0,1} | broadcast | bytes 2113536 | tf_op jit(solution)/shard_map/broadcast_in_dim | solution.py:87
  43.6 1.9 %broadcast_in_dim.96.diagonal_ref = f32[128,32,128]{2,1,0:T(8,128)} broadcast(f32[128,32]{1,0:T(8,128)S(1)} %bitcast.171), dimensions={0,1} | broadcast | bytes 2113536 | tf_op jit(solution)/shard_map/broadcast_in_dim | solution.py:87
  45.5 1.9 broadcast_in_dim.160.upper_ref
  47.4 5.9 %shard_map.94 = f32[128,32,128]{2,1,0:T(8,128)} custom-call(f32[128,32,128]{2,1,0:T(8,128)} %broadcast_in_dim.94.lower_ref, f32[128,32,128]{2,1,0:T(8,128)} %broadcast_in_dim.96.diagonal_ref, f32[128,32,128]{2,1,0:T(8,128)} %broadcast_in_dim.160.upper_ref), custom_call_target="tpu_custom_call" | custom-call | flops 8388608 | bytes 33554432 | tf_op jit(solution)/shard_map/pallas_call | solution.py:94
  53.4 2.2 %fusion = f32[32,128]{0,1:T(8,128)S(1)} fusion(f32[128,32,128]{2,1,0:T(8,128)} %shard_map.94, pred[128]{0:T(512)(128)(4,1)S(1)} %iota_compare_fusion.11), kind=kLoop, calls=%fused_computation.17 | loop fusion | flops 1044480 | bytes 2113664 | tf_op jit(solution)/shard_map/reduce_sum | solution.py:189
  57.9 10.3 %all-to-all-done.1 = bf16[4,4,2,128,128]{4,3,2,1,0:T(8,128)(2,1)S(1)} async-done(((bf16[4,4,2,128,128]{4,3,2,1,0:T(8,128)(2,1)}), bf16[4,4,2,128,128]{4,3,2,1,0:T(8,128)(2,1)S(1)}, u32[]{:S(2)}, u32[]{:S(2)}) %all-to-all-start.1) | async-done | bytes 1048608 | tf_op jit(solution)/shard_map/all_to_all | solution.py:181
  69.2 1.3 copy.174
  70.5 2.3 %fusion.40 = f32[16,2,128,128]{3,0,2,1:T(8,128)S(1)} fusion(f32[8,2,128,128]{3,0,2,1:T(8,128)} %copy.174, s32[8]{0:T(128)S(1)} %and_select_fusion.1), kind=kOutput, calls=%fused_computation.120 | convolution fusion | flops 50331776 | bytes 3145760 | tf_op jit(solution)/shard_map/tr,rfcz->tfcz/dot_general | solution.py:213
  72.9 1.9 copy.175
  74.8 4.4 %bitcast_add_fusion.1 = f32[16,2,128,128]{2,3,1,0:T(8,128)S(1)} fusion(f32[16,2,128,128]{2,3,1,0:T(8,128)} %copy.175, f32[16,2,128,128]{3,2,1,0:T(8,128)} %fusion.17, f32[16,2,128,128]{3,2,1,0:T(8,128)} %fusion.13, f32[16,2,128,128]{3,2,1,0:T(8,128)} %fusion.15, bf16[16,2,128,128]{3,2,1,0:T(8,128)(2,1)S(1)} %gather_fusion.3, ...), kind=kOutput, calls=%fused_computation.18 | convolution fusion | flops 136314880 | bytes 12058624 | tf_op jit(solution)/shard_map/tcd,tfdz->tfcz/dot_general | solution.py:201
  80.0 3.3 %fusion.3 = f32[16,2,128,128]{2,3,1,0:T(8,128)S(1)} fusion(f32[16,2,128,128]{2,3,1,0:T(8,128)S(1)} %bitcast_add_fusion.1, f32[16,2,128,128]{3,1,0,2:T(2,128)S(1)} %bitcast.162), kind=kOutput, calls=%fused_computation.24 | convolution fusion | flops 805306368 | bytes 6291456 | tf_op jit(solution)/shard_map/tfzy,tfcy->tfcz/dot_general | solution.py:225
  83.4 1.4 pad_maximum_fusion.4
  87.5 1.4 gather_fusion.13
  88.9 4.1 %all-to-all-start.3 = ((bf16[4,4,128,128]{2,3,1,0:T(8,128)(2,1)}), bf16[4,4,128,128]{2,3,1,0:T(8,128)(2,1)}, u32[]{:S(2)}, u32[]{:S(2)}) async-start(bf16[4,4,128,128]{2,3,1,0:T(8,128)(2,1)} %bitcast.75), calls=%async_computation.3 | async-start | bytes 1048576 | tf_op jit(solution)/shard_map/all_to_all | solution.py:181
  93.1 1.4 fusion.82
  94.5 2.0 %collective-permute-start.1 = (f32[2]{0:T(128)S(1)}, f32[2]{0:T(128)S(1)}, u32[]{:S(2)}, u32[]{:S(2)}) collective-permute-start(f32[2]{0:T(128)S(1)} %fusion.82), channel_id=1, source_target_pairs={{0,2},{2,0},{4,6},{6,4},{1,3},{3,1},{5,7},{7,5},{8,10},{10,8},{12,... | collective-permute-start | bytes 32 | tf_op jit(solution)/shard_map/ppermute | solution.py:32
  96.4 5.8 %collective-permute-done.1 = f32[2]{0:T(128)S(1)} collective-permute-done((f32[2]{0:T(128)S(1)}, f32[2]{0:T(128)S(1)}, u32[]{:S(2)}, u32[]{:S(2)}) %collective-permute-start.1) | collective-permute-done | bytes 40 | tf_op jit(solution)/shard_map/ppermute | solution.py:32
  102.3 1.4 fusion.84
  103.6 4.5 %collective-permute-start.2 = (f32[2]{0:T(128)S(1)}, f32[2]{0:T(128)S(1)}, u32[]{:S(2)}, u32[]{:S(2)}) collective-permute-start(f32[2]{0:T(128)S(1)} %fusion.84), channel_id=1, source_target_pairs={{0,4},{2,6},{4,0},{6,2},{1,5},{3,7},{5,1},{7,3},{8,12},{10,14},{12... | collective-permute-start | bytes 32 | tf_op jit(solution)/shard_map/ppermute | solution.py:32
  108.1 1.5 collective-permute-done.2
  109.6 1.5 collective-permute-start.3
  111.1 2.0 %collective-permute-done.3 = f32[2]{0:T(128)S(1)} collective-permute-done((f32[2]{0:T(128)S(1)}, f32[2]{0:T(128)S(1)}, u32[]{:S(2)}, u32[]{:S(2)}) %collective-permute-start.3) | collective-permute-done | bytes 40 | tf_op jit(solution)/shard_map/ppermute | solution.py:32
  113.2 1.5 collective-permute-start.4
  114.7 2.0 %collective-permute-done.4 = f32[2]{0:T(128)S(1)} collective-permute-done((f32[2]{0:T(128)S(1)}, f32[2]{0:T(128)S(1)}, u32[]{:S(2)}, u32[]{:S(2)}) %collective-permute-start.4) | collective-permute-done | bytes 40 | tf_op jit(solution)/shard_map/ppermute | solution.py:32
  118.6 2.1 %slice.213 = bf16[16,1,128,128]{2,3,1,0:T(8,128)(2,1)} slice(f32[16,2,128,128]{2,3,1,0:T(8,128)} %copy-done.4), slice={[0:16], [1:2], [0:128], [0:128]} | slice | bytes 1048576 | tf_op jit(solution)/shard_map/slice | solution.py:239
  120.8 2.1 %convert_reduce_fusion = (f32[]{:T(128)}, bf16[16,1,128,128]{2,3,1,0:T(8,128)(2,1)S(1)}) fusion(f32[16,2,128,128]{2,3,1,0:T(8,128)} %copy-done.4, f32[]{:T(128)} %bitcast.36), kind=kLoop, calls=%fused_computation.46 | loop fusion | flops 1048575 | bytes 1572872 | tf_op jit(solution)/shard_map/reduce_sum | solution.py:222
  123.7 1.4 gather_fusion.12
  126.4 1.6 gather_fusion.10
  128.0 4.4 %all-to-all-start.2 = ((bf16[4,4,128,128]{2,3,1,0:T(8,128)(2,1)}), bf16[4,4,128,128]{2,3,1,0:T(8,128)(2,1)}, u32[]{:S(2)}, u32[]{:S(2)}) async-start(bf16[4,4,128,128]{2,3,1,0:T(8,128)(2,1)} %bitcast.167), calls=%async_computation.2 | async-start | bytes 1048576 | tf_op jit(solution)/shard_map/all_to_all | solution.py:181
  132.4 3.1 %fusion.16 = f32[16,2,128,128]{3,2,1,0:T(8,128)} fusion(bf16[16,2,128,128]{2,3,1,0:T(8,128)(2,1)} %gather_fusion.10, bf16[16,4,128,128]{3,2,0,1:T(8,128)(2,1)} %copy-done.3), kind=kOutput, calls=%fused_computation.58 | convolution fusion | flops 134217728 | bytes 3670016 | tf_op jit(solution)/shard_map/tcd,tfdz->tfcz/dot_general | solution.py:201
  135.5 1.7 gather_fusion.8
  137.2 1.7 gather_fusion.9
  138.9 1.7 gather_fusion.11
  140.6 3.2 %fusion.12 = f32[16,2,128,128]{3,2,1,0:T(8,128)} fusion(bf16[16,2,128,128]{2,3,1,0:T(8,128)(2,1)} %gather_fusion.8, bf16[16,4,128,128]{3,2,0,1:T(8,128)(2,1)} %copy-done.3), kind=kOutput, calls=%fused_computation.54 | convolution fusion | flops 134217728 | bytes 3670016 | tf_op jit(solution)/shard_map/tcd,tfdz->tfcz/dot_general | solution.py:201
  143.8 2.8 %fusion.14 = f32[16,2,128,128]{3,2,1,0:T(8,128)} fusion(bf16[16,2,128,128]{2,3,1,0:T(8,128)(2,1)S(1)} %copy-done.7, bf16[16,4,128,128]{3,2,0,1:T(8,128)(2,1)} %copy-done.3), kind=kOutput, calls=%fused_computation.56 | convolution fusion | flops 134217728 | bytes 3670016 | tf_op jit(solution)/shard_map/tcd,tfdz->tfcz/dot_general | solution.py:201
  148.0 1.4 gather_fusion.14
  149.4 1.3 convolution_bitcast_fusion
  150.7 1.4 copy.194
  152.1 3.7 %fusion.38 = f32[16,2,128,128]{3,0,2,1:T(8,128)} fusion(f32[8,2,128,128]{3,0,2,1:T(8,128)} %copy.194, s32[8]{0:T(128)S(1)} %and_select_fusion.1), kind=kOutput, calls=%fused_computation.119 | convolution fusion | flops 50331776 | bytes 3145760 | tf_op jit(solution)/shard_map/tr,rfcz->tfcz/dot_general | solution.py:213
  155.8 3.0 %copy.195 = f32[16,2,128,128]{2,3,1,0:T(8,128)} copy(f32[16,2,128,128]{3,0,2,1:T(8,128)} %fusion.38) | data formatting | bytes 4194304 | tf_op jit(solution)/shard_map/tr,rfcz->tfcz/dot_general | solution.py:213
  158.8 4.3 %bitcast_add_fusion = f32[16,2,128,128]{2,3,1,0:T(8,128)S(1)} fusion(f32[16,2,128,128]{2,3,1,0:T(8,128)} %copy.195, f32[16,2,128,128]{3,2,1,0:T(8,128)} %fusion.16, f32[16,2,128,128]{3,2,1,0:T(8,128)} %fusion.12, f32[16,2,128,128]{3,2,1,0:T(8,128)} %fusion.14, bf16[16,2,128,128]{2,3,1,0:T(8,128)(2,1)S(1)} %copy-done.6, bf16[16,4,128,128]{3,2,0,1:T(8,128)(2,1)} %copy-done.3), kind=kOutput, calls=%fused_computation.15 | convolution fusion | flops 136314880 | bytes 12058624 | tf_op jit(solution)/shard_map/tcd,tfdz->tfcz/dot_general | solution.py:201
  163.1 3.3 %fusion.1 = f32[16,2,128,128]{2,3,1,0:T(8,128)S(1)} fusion(f32[16,2,128,128]{2,3,1,0:T(8,128)S(1)} %bitcast_add_fusion, f32[16,2,128,128]{3,1,0,2:T(2,128)S(1)} %bitcast.163), kind=kOutput, calls=%fused_computation.22 | convolution fusion | flops 805306368 | bytes 6291456 | tf_op jit(solution)/shard_map/tfzy,tfcy->tfcz/dot_general | solution.py:225
  167.4 1.4 pad_maximum_fusion.5
  170.1 1.4 fusion.81
  171.5 1.8 collective-permute-start.9
  173.3 1.7 collective-permute-done.9
  175.0 1.4 fusion.83
  176.4 2.9 %collective-permute-start.10 = (f32[2]{0:T(128)S(1)}, f32[2]{0:T(128)S(1)}, u32[]{:S(2)}, u32[]{:S(2)}) collective-permute-start(f32[2]{0:T(128)S(1)} %fusion.83), channel_id=1, source_target_pairs={{0,4},{2,6},{4,0},{6,2},{1,5},{3,7},{5,1},{7,3},{8,12},{10,14},{12... | collective-permute-start | bytes 32 | tf_op jit(solution)/shard_map/ppermute | solution.py:32
  179.3 1.6 collective-permute-done.10
  180.8 1.5 collective-permute-start.11
  182.3 2.1 %collective-permute-done.11 = f32[2]{0:T(128)S(1)} collective-permute-done((f32[2]{0:T(128)S(1)}, f32[2]{0:T(128)S(1)}, u32[]{:S(2)}, u32[]{:S(2)}) %collective-permute-start.11) | collective-permute-done | bytes 40 | tf_op jit(solution)/shard_map/ppermute | solution.py:32
  184.4 1.5 collective-permute-start.12
  185.9 2.0 %collective-permute-done.12 = f32[2]{0:T(128)S(1)} collective-permute-done((f32[2]{0:T(128)S(1)}, f32[2]{0:T(128)S(1)}, u32[]{:S(2)}, u32[]{:S(2)}) %collective-permute-start.12) | collective-permute-done | bytes 40 | tf_op jit(solution)/shard_map/ppermute | solution.py:32
  (131 shorter events, 28.0 us)
Async XLA Ops:
  0.6 32.4 %copy-start = (f32[2,8]{1,0:T(2,128)S(1)}, f32[2,8]{1,0:T(2,128)}, u32[]{:S(2)}) copy-start(f32[2,8]{1,0:T(2,128)} %param.12) | copy-start | bytes 196
  2.7 31.7 %all-to-all-start = ((s32[4,1,4]{2,1,0:T(1,128)}), s32[4,1,4]{2,1,0:T(1,128)S(1)}, u32[]{:S(2)}, u32[]{:S(2)}) async-start(s32[4,1,4]{2,1,0:T(1,128)} %bitcast.23), calls=%async_computation | async-start | bytes 4096 | tf_op jit(solution)/shard_map/all_to_all | solution.py:178
  9.7 23.6 %collective-permute-start.5 = (s32[16,1]{0,1:T(1,128)S(1)}, s32[16,1]{0,1:T(1,128)S(1)}, u32[]{:S(2)}, u32[]{:S(2)}) collective-permute-start(s32[16,1]{0,1:T(1,128)S(1)} %slice.108), channel_id=1, source_target_pairs={{1,0},{3,2},{5,4},{7,6},{9,8},{11,10},{13,12},{15,14},{17,16},{19,... | collective-permute-start | bytes 200 | tf_op jit(solution)/shard_map/ppermute | solution.py:17
  15.8 1.9 copy-start.9
  15.8 3.1 %copy-start.10 = (bf16[16,128,128]{2,1,0:T(8,128)(2,1)S(1)}, bf16[16,128,128]{2,1,0:T(8,128)(2,1)}, u32[]{:S(2)}) copy-start(bf16[16,128,128]{2,1,0:T(8,128)(2,1)} %param.8) | copy-start | bytes 1572868
  17.7 11.3 %copy-start.3 = (bf16[16,4,128,128]{3,2,0,1:T(8,128)(2,1)}, bf16[16,4,128,128]{3,2,0,1:T(8,128)(2,1)S(1)}, u32[]{:S(2)}) copy-start(bf16[16,4,128,128]{3,2,0,1:T(8,128)(2,1)S(1)} %copy_select_fusion) | copy-start | bytes 6291460
  22.3 3.1 %copy-start.8 = (bf16[16,2,128,128]{3,2,1,0:T(8,128)(2,1)S(1)}, bf16[16,2,128,128]{3,2,1,0:T(8,128)(2,1)}, u32[]{:S(2)}) copy-start(bf16[16,2,128,128]{3,2,1,0:T(8,128)(2,1)} %gather_fusion) | copy-start | bytes 3145732
  29.0 4.6 %copy-start.11 = (f32[8]{0:T(128)S(1)}, f32[8]{0:T(128)}, u32[]{:S(2)}) copy-start(f32[8]{0:T(128)} %param.13) | copy-start | bytes 100
  36.1 32.1 %all-to-all-start.1 = ((bf16[4,4,2,128,128]{4,3,2,1,0:T(8,128)(2,1)}), bf16[4,4,2,128,128]{4,3,2,1,0:T(8,128)(2,1)S(1)}, u32[]{:S(2)}, u32[]{:S(2)}) async-start(bf16[4,4,2,128,128]{4,3,2,1,0:T(8,128)(2,1)} %bitcast.25), calls=%async_computation.1 | async-start | bytes 2097152 | tf_op jit(solution)/shard_map/all_to_all | solution.py:181
  55.9 1.7 collective-permute-start.7
  74.8 5.3 %copy-start.2 = (f32[128,32,128]{2,1,0:T(8,128)S(1)}, f32[128,32,128]{2,1,0:T(8,128)}, u32[]{:S(2)}) copy-start(f32[128,32,128]{2,1,0:T(8,128)} %shard_map.94) | copy-start | bytes 6291460
  83.3 1.9 %collective-permute-start.6 = (f32[16,2,128]{2,1,0:T(2,128)S(1)}, f32[16,2,128]{2,1,0:T(2,128)S(1)}, u32[]{:S(2)}, u32[]{:S(2)}) collective-permute-start(f32[16,2,128]{2,1,0:T(2,128)S(1)} %bitcast.180), channel_id=1, source_target_pairs={{0,1},{1,0},{2,3},{3,2},{4,5},{5,4},{6,7},{7,6},{8,9},{9,8},{10,11... | collective-permute-start | bytes 49160 | tf_op jit(solution)/shard_map/ppermute | solution.py:21
  84.8 8.3 %collective-permute-start = (f32[2]{0:T(128)S(1)}, f32[2]{0:T(128)S(1)}, u32[]{:S(2)}, u32[]{:S(2)}) collective-permute-start(f32[2]{0:T(128)S(1)} %pad_maximum_fusion.4), channel_id=1, source_target_pairs={{0,1},{1,0},{2,3},{3,2},{4,5},{5,4},{6,7},{7,6},{8,9},{9,8},{10,11... | collective-permute-start | bytes 32 | tf_op jit(solution)/shard_map/ppermute | solution.py:32
  86.1 1.3 copy-start.4
  88.9 39.1 %all-to-all-start.3 = ((bf16[4,4,128,128]{2,3,1,0:T(8,128)(2,1)}), bf16[4,4,128,128]{2,3,1,0:T(8,128)(2,1)}, u32[]{:S(2)}, u32[]{:S(2)}) async-start(bf16[4,4,128,128]{2,3,1,0:T(8,128)(2,1)} %bitcast.75), calls=%async_computation.3 | async-start | bytes 1048576 | tf_op jit(solution)/shard_map/all_to_all | solution.py:181
  94.5 7.8 %collective-permute-start.1 = (f32[2]{0:T(128)S(1)}, f32[2]{0:T(128)S(1)}, u32[]{:S(2)}, u32[]{:S(2)}) collective-permute-start(f32[2]{0:T(128)S(1)} %fusion.82), channel_id=1, source_target_pairs={{0,2},{2,0},{4,6},{6,4},{1,3},{3,1},{5,7},{7,5},{8,10},{10,8},{12,... | collective-permute-start | bytes 32 | tf_op jit(solution)/shard_map/ppermute | solution.py:32
  103.6 6.0 %collective-permute-start.2 = (f32[2]{0:T(128)S(1)}, f32[2]{0:T(128)S(1)}, u32[]{:S(2)}, u32[]{:S(2)}) collective-permute-start(f32[2]{0:T(128)S(1)} %fusion.84), channel_id=1, source_target_pairs={{0,4},{2,6},{4,0},{6,2},{1,5},{3,7},{5,1},{7,3},{8,12},{10,14},{12... | collective-permute-start | bytes 32 | tf_op jit(solution)/shard_map/ppermute | solution.py:32
  109.6 3.5 %collective-permute-start.3 = (f32[2]{0:T(128)S(1)}, f32[2]{0:T(128)S(1)}, u32[]{:S(2)}, u32[]{:S(2)}) collective-permute-start(f32[2]{0:T(128)S(1)} %add.261), channel_id=1, source_target_pairs={{0,8},{8,0},{16,24},{24,16},{1,9},{9,1},{17,25},{25,17},{2,10},{10... | collective-permute-start | bytes 32 | tf_op jit(solution)/shard_map/ppermute | solution.py:32
  113.2 3.5 %collective-permute-start.4 = (f32[2]{0:T(128)S(1)}, f32[2]{0:T(128)S(1)}, u32[]{:S(2)}, u32[]{:S(2)}) collective-permute-start(f32[2]{0:T(128)S(1)} %add.262), channel_id=1, source_target_pairs={{0,16},{8,24},{16,0},{24,8},{1,17},{9,25},{17,1},{25,9},{2,18},{10... | collective-permute-start | bytes 32 | tf_op jit(solution)/shard_map/ppermute | solution.py:32
  122.9 0.8 copy-start.5
  128.0 18.6 %all-to-all-start.2 = ((bf16[4,4,128,128]{2,3,1,0:T(8,128)(2,1)}), bf16[4,4,128,128]{2,3,1,0:T(8,128)(2,1)}, u32[]{:S(2)}, u32[]{:S(2)}) async-start(bf16[4,4,128,128]{2,3,1,0:T(8,128)(2,1)} %bitcast.167), calls=%async_computation.2 | async-start | bytes 1048576 | tf_op jit(solution)/shard_map/all_to_all | solution.py:181
  140.6 3.2 %copy-start.7 = (bf16[16,2,128,128]{2,3,1,0:T(8,128)(2,1)S(1)}, bf16[16,2,128,128]{2,3,1,0:T(8,128)(2,1)}, u32[]{:S(2)}) copy-start(bf16[16,2,128,128]{2,3,1,0:T(8,128)(2,1)} %gather_fusion.9) | copy-start | bytes 3145732
  155.8 3.0 %copy-start.6 = (bf16[16,2,128,128]{2,3,1,0:T(8,128)(2,1)S(1)}, bf16[16,2,128,128]{2,3,1,0:T(8,128)(2,1)}, u32[]{:S(2)}) copy-start(bf16[16,2,128,128]{2,3,1,0:T(8,128)(2,1)} %gather_fusion.11) | copy-start | bytes 3145732
  167.3 23.1 %collective-permute-start.13 = (f32[16,2,128]{2,1,0:T(2,128)S(1)}, f32[16,2,128]{2,1,0:T(2,128)S(1)}, u32[]{:S(2)}, u32[]{:S(2)}) collective-permute-start(f32[16,2,128]{2,1,0:T(2,128)S(1)} %select_bitcast_fusion), channel_id=1, source_target_pairs={{0,1},{1,0},{2,3},{3,2},{4,5},{5,4},{6,7},{7,6},{8,9},{9,8},{10,11... | collective-permute-start | bytes 49160 | tf_op jit(solution)/shard_map/ppermute | solution.py:21
  168.8 1.3 collective-permute-start.8
  171.5 3.5 %collective-permute-start.9 = (f32[2]{0:T(128)S(1)}, f32[2]{0:T(128)S(1)}, u32[]{:S(2)}, u32[]{:S(2)}) collective-permute-start(f32[2]{0:T(128)S(1)} %fusion.81), channel_id=1, source_target_pairs={{0,2},{2,0},{4,6},{6,4},{1,3},{3,1},{5,7},{7,5},{8,10},{10,8},{12,... | collective-permute-start | bytes 32 | tf_op jit(solution)/shard_map/ppermute | solution.py:32
  176.4 4.4 %collective-permute-start.10 = (f32[2]{0:T(128)S(1)}, f32[2]{0:T(128)S(1)}, u32[]{:S(2)}, u32[]{:S(2)}) collective-permute-start(f32[2]{0:T(128)S(1)} %fusion.83), channel_id=1, source_target_pairs={{0,4},{2,6},{4,0},{6,2},{1,5},{3,7},{5,1},{7,3},{8,12},{10,14},{12... | collective-permute-start | bytes 32 | tf_op jit(solution)/shard_map/ppermute | solution.py:32
  180.8 3.5 %collective-permute-start.11 = (f32[2]{0:T(128)S(1)}, f32[2]{0:T(128)S(1)}, u32[]{:S(2)}, u32[]{:S(2)}) collective-permute-start(f32[2]{0:T(128)S(1)} %add.280), channel_id=1, source_target_pairs={{0,8},{8,0},{16,24},{24,16},{1,9},{9,1},{17,25},{25,17},{2,10},{10... | collective-permute-start | bytes 32 | tf_op jit(solution)/shard_map/ppermute | solution.py:32
  184.4 3.5 %collective-permute-start.12 = (f32[2]{0:T(128)S(1)}, f32[2]{0:T(128)S(1)}, u32[]{:S(2)}, u32[]{:S(2)}) collective-permute-start(f32[2]{0:T(128)S(1)} %add.281), channel_id=1, source_target_pairs={{0,16},{8,24},{16,0},{24,8},{1,17},{9,25},{17,1},{25,9},{2,18},{10... | collective-permute-start | bytes 32 | tf_op jit(solution)/shard_map/ppermute | solution.py:32
  191.3 2.3 %copy-start.1 = (f32[2,8]{1,0:T(2,128)S(1)}, f32[2,8]{1,0:T(2,128)}, u32[]{:S(2)}) copy-start(f32[2,8]{1,0:T(2,128)} %param.12) | copy-start | bytes 196

commit v10 on v8

--- a/solution.py
+++ b/solution.py
@@ -102,6 +102,46 @@
         ),
     )(*bands)
     return jnp.transpose(inverse, (1, 0, 2)).reshape(lead + (levels, levels)), ready
+
+
+def advect_kernel(index_ref, weight_ref, pool_ref, out_ref):
+    tiles, sources = weight_ref.shape[:2]
+    fields = out_ref.shape[1]
+
+    def one_tile(t, carry):
+        picked = [index_ref[t * sources + k] for k in range(sources)]
+        for field in range(fields):
+            total = jnp.dot(
+                weight_ref[t, 0], pool_ref[picked[0], field], preferred_element_type=jnp.float32
+            )
+            for k in range(1, sources):
+                total = total + jnp.dot(
+                    weight_ref[t, k], pool_ref[picked[k], field], preferred_element_type=jnp.float32
+                )
+            out_ref[t, field] = total
+        return carry
+
+    lax.fori_loop(0, tiles, one_tile, 0)
+
+
+def advect(weights, tile_pool, pool_index):
+    tiles, sources = pool_index.shape
+    _, fields, columns, levels = tile_pool.shape
+    return pl.pallas_call(
+        advect_kernel,
+        out_shape=jax.ShapeDtypeStruct((tiles, fields, columns, levels), jnp.float32),
+        in_specs=[
+            pl.BlockSpec(memory_space=pltpu.SMEM),
+            pl.BlockSpec(memory_space=pltpu.VMEM),
+            pl.BlockSpec(memory_space=pltpu.VMEM),
+        ],
+        out_specs=pl.BlockSpec(memory_space=pltpu.VMEM),
+        cost_estimate=pl.CostEstimate(
+            flops=2 * tiles * sources * fields * columns * columns * levels,
+            transcendentals=0,
+            bytes_accessed=weights.size * 2 + tile_pool.size * 2 + tiles * fields * columns * levels * 4,
+        ),
+    )(pool_index.reshape(-1), weights, tile_pool)
 
 
 def interface_values(low_value, low_spike, high_value, high_spike):
@@ -178,14 +218,7 @@
     ratios = []
     for step_index in range(STEPS):
         tile_pool = jnp.concatenate([fields, arrived], axis=0)
-        advected = jnp.zeros(fields.shape, jnp.float32)
-        for entry_k in range(sources_per):
-            advected = advected + jnp.einsum(
-                "tcd,tfdz->tfcz",
-                interp_weights[:, entry_k],
-                tile_pool[pool_index[:, entry_k]],
-                preferred_element_type=jnp.float32,
-            )
+        advected = advect(interp_weights, tile_pool, pool_index)
         last = step_index + 1 == STEPS
         totals = butterfly_sum(
             jnp.stack([jnp.sum(fields[:, 0], dtype=jnp.float32), jnp.sum(advected[:, 0])]),

time: 169 us -> 174 us (1.030)
  local copies, waits for them, and re-layouts: 42.4 us -> 27.4 us
  Pallas kernels: 5.92 us -> 20.3 us
  other arithmetic: 24.7 us -> 29.5 us
    gather x8 -> x0, local copies, waits for them, and re-layouts: 17.8 us -> none  [per_device(): tile_pool[pool_index[:, entry_k]]]
    pallas_call x0 -> x2, Pallas kernels: none -> 14.4 us  [advect(): pl.pallas_call(advect_kernel, out_shape=jax.ShapeDtypeStruct((tiles, fiel...]
    dot_general x2, matrix products: 6.61 us -> 14 us  [per_device(): jnp.einsum('tfzy,tfcy->tfcz', inverse, advected, precision=HIGHEST, prefe...]
    dot_general x8 -> x0, matrix products: 6.92 us -> none  [per_device(): jnp.einsum('tcd,tfdz->tfcz', interp_weights[:, entry_k], tile_pool[pool_i...]
    dot_general x0 -> x2, local copies, waits for them, and re-layouts: none -> 4.85 us  [per_device(): jnp.einsum('tfzy,tfcy->tfcz', inverse, advected, precision=HIGHEST, prefe...]
    unnamed x28 -> x20, local copies, waits for them, and re-layouts: 8.16 us -> 5.53 us
    gather x4 -> x3, local copies, waits for them, and re-layouts: 4.69 us -> 4.56 us  [exchange(): tiles[wanted]]
  transfers between devices with their start and end apart: 18 -> 18, of which waited for: 14 -> 14; matrix products, arithmetic and copies ran while one was open for 19% -> 20% of each run, Pallas kernels for 4% -> 3%
where the time goes in v10:
time: 174 us; the launch traced here: 173 us
  waiting for transfers between devices  42.9 us (25%)
  starting transfers between devices  34.1 us (20%)
  other arithmetic  29.5 us (17%)
  local copies, waits for them, and re-layouts  27.4 us (16%)
  Pallas kernels  20.3 us (12%)
  matrix products  14.7 us (8%)
  between operations  3.6 us (2%)
    ppermute x10, waiting for transfers between devices, butterfly_sum(): lax.ppermute(value, axis, [(i, i ^ bit) for i in range(devices)])  22.8 us
    all_to_all x3, waiting for transfers between devices, exchange(): lax.all_to_all(tiles[wanted], 'gy', split_axis=0, concat_axis=0, tiled=True)  19.1 us
    pallas_call x2, Pallas kernels, advect(): pl.pallas_call(advect_kernel, out_shape=jax.ShapeDtypeStruct((tiles, fiel...  14.4 us
    dot_general x2, matrix products, per_device(): jnp.einsum('tfzy,tfcy->tfcz', inverse, advected, precision=HIGHEST, prefe...  14 us
    ppermute x10, starting transfers between devices, butterfly_sum(): lax.ppermute(value, axis, [(i, i ^ bit) for i in range(devices)])  12.8 us
    all_to_all x3, starting transfers between devices, exchange(): lax.all_to_all(tiles[wanted], 'gy', split_axis=0, concat_axis=0, tiled=True)  12.8 us
    all_to_all x1, starting transfers between devices, per_device(): lax.all_to_all(requests, 'gy', split_axis=0, concat_axis=0, tiled=True)  6.32 us
    pallas_call x1, Pallas kernels, block_inverse(): pl.pallas_call(thomas_inverse_kernel, out_shape=jax.ShapeDtypeStruct((lev...  5.92 us
  transfers between devices with their start and end apart: 18, of which 14 were waited for; matrix products, arithmetic and copies ran while one was open for 20% of the time, Pallas kernels for 3%

profile of v10, /device:TPU:0, one launch (start us, length us, event | category | flops | bytes accessed | tf_op | source)
XLA Modules:
  0.0 172.6 jit_solution(16802310798264773405)
XLA Ops:
  0.7 0.7 slice.68
  1.4 1.3 collective-permute-start.5
  2.6 0.8 copy.76
  4.4 0.7 select_reduce_fusion.1
  5.2 6.3 %all-to-all-start = ((s32[4,1,4]{2,1,0:T(1,128)}), s32[4,1,4]{2,1,0:T(1,128)S(1)}, u32[]{:S(2)}, u32[]{:S(2)}) async-start(s32[4,1,4]{2,1,0:T(1,128)} %bitcast.4), calls=%async_computation | async-start | bytes 4096 | tf_op jit(solution)/shard_map/all_to_all | solution.py:199
  11.5 0.8 copy.78
  12.2 2.0 %convert_reduce_fusion.1 = f32[]{:T(128)} fusion(bf16[16,128,128]{2,1,0:T(8,128)(2,1)} %param.7), kind=kLoop, calls=%fused_computation.30 | loop fusion | flops 524287 | bytes 524292 | tf_op jit(solution)/shard_map/reduce_sum | solution.py:224
  14.4 1.3 pad_maximum_fusion.1
  17.0 1.7 %gather_fusion = bf16[16,2,128,128]{3,2,1,0:T(8,128)(2,1)} fusion(bf16[16,2,128,128]{3,2,1,0:T(8,128)(2,1)S(1)} %pad_maximum_fusion.1, s32[1024]{0:T(1024)S(1)} %pad_clamp_fusion.1), kind=kCustom, calls=%fused_computation | custom fusion | bytes 2097216 | tf_op jit(solution)/shard_map/gather | solution.py:202
  18.8 5.0 %all-to-all-start.1 = ((bf16[4,4,2,128,128]{4,3,2,1,0:T(8,128)(2,1)}), bf16[4,4,2,128,128]{4,3,2,1,0:T(8,128)(2,1)S(1)}, u32[]{:S(2)}, u32[]{:S(2)}) async-start(bf16[4,4,2,128,128]{4,3,2,1,0:T(8,128)(2,1)} %bitcast.6), calls=%async_computation.1 | async-start | bytes 2097152 | tf_op jit(solution)/shard_map/all_to_all | solution.py:202
  24.4 2.0 %broadcast_in_dim.109.diagonal_ref = f32[128,32,128]{2,1,0:T(8,128)} broadcast(f32[128,32]{1,0:T(8,128)S(1)} %bitcast.94), dimensions={0,1} | broadcast | bytes 2113536 | tf_op jit(solution)/shard_map/broadcast_in_dim | solution.py:87
  26.4 1.9 %broadcast_in_dim.107.lower_ref = f32[128,32,128]{2,1,0:T(8,128)} broadcast(f32[128,32]{1,0:T(8,128)S(1)} %bitcast.93), dimensions={0,1} | broadcast | bytes 2113536 | tf_op jit(solution)/shard_map/broadcast_in_dim | solution.py:87
  28.3 2.0 %broadcast_in_dim.113.upper_ref = f32[128,32,128]{2,1,0:T(8,128)} broadcast(f32[128,32]{1,0:T(8,128)S(1)} %copy.85), dimensions={0,1} | broadcast | bytes 2113536 | tf_op jit(solution)/shard_map/broadcast_in_dim | solution.py:87
  30.4 5.9 %shard_map.95 = f32[128,32,128]{2,1,0:T(8,128)} custom-call(f32[128,32,128]{2,1,0:T(8,128)} %broadcast_in_dim.107.lower_ref, f32[128,32,128]{2,1,0:T(8,128)} %broadcast_in_dim.109.diagonal_ref, f32[128,32,128]{2,1,0:T(8,128)} %broadcast_in_dim.113.upper_ref), custom_call_target="tpu_custom_call" | custom-call | flops 8388608 | bytes 33554432 | tf_op jit(solution)/shard_map/pallas_call | solution.py:94
  36.3 2.3 %fusion = f32[32,128]{0,1:T(8,128)S(1)} fusion(f32[128,32,128]{2,1,0:T(8,128)} %shard_map.95, pred[128]{0:T(512)(128)(4,1)S(1)} %iota_compare_fusion.9), kind=kLoop, calls=%fused_computation.6 | loop fusion | flops 1044480 | bytes 2113664 | tf_op jit(solution)/shard_map/reduce_sum | solution.py:210
  39.2 0.9 collective-permute-done.7
  40.3 9.9 %all-to-all-done.1 = bf16[4,4,2,128,128]{4,3,2,1,0:T(8,128)(2,1)S(1)} async-done(((bf16[4,4,2,128,128]{4,3,2,1,0:T(8,128)(2,1)}), bf16[4,4,2,128,128]{4,3,2,1,0:T(8,128)(2,1)S(1)}, u32[]{:S(2)}, u32[]{:S(2)}) %all-to-all-start.1) | async-done | bytes 1048608 | tf_op jit(solution)/shard_map/all_to_all | solution.py:202
  50.2 1.6 pad_maximum_fusion.pool_ref
  51.8 7.3 %shard_map.94 = f32[16,2,128,128]{3,2,1,0:T(8,128)} custom-call(s32[64]{0:T(128)} %get-tuple-element.16.index_ref, bf16[16,4,128,128]{3,2,1,0:T(8,128)(2,1)} %weight_ref.3, bf16[32,2,128,128]{3,2,1,0:T(8,128)(2,1)} %pad_maximum_fusion.pool_ref), custom_call_target="tpu_custom_call" | custom-call | flops 536870912 | bytes 6291456 | tf_op jit(solution)/shard_map/pallas_call | solution.py:130
  59.0 7.1 %fusion.3 = f32[16,2,128,128]{2,3,1,0:T(8,128)S(1)} fusion(f32[16,2,128,128]{3,2,1,0:T(8,128)} %shard_map.94, f32[16,2,128,128]{3,1,0,2:T(2,128)S(1)} %bitcast.84), kind=kOutput, calls=%fused_computation.11 | convolution fusion | flops 805306368 | bytes 6291456 | tf_op jit(solution)/shard_map/tfzy,tfcy->tfcz/dot_general | solution.py:227
  66.1 1.3 copy-done.4
  67.6 0.9 slice_reduce_fusion.1
  68.4 2.9 %copy.95 = f32[16,2,128,128]{3,2,1,0:T(8,128)} copy(f32[16,2,128,128]{2,3,1,0:T(8,128)} %copy-done.4) | data formatting | bytes 4194304 | tf_op jit(solution)/shard_map/tfzy,tfcy->tfcz/dot_general | solution.py:227
  71.5 1.9 %multiply_subtract_fusion.1 = f32[16,2,128,128]{3,2,1,0:T(8,128)S(1)} fusion(f32[16,2,128,128]{3,2,1,0:T(8,128)} %copy.95, f32[16,2,128]{2,1,0:T(2,128)S(1)} %subtract_select_fusion.1, f32[16,2,128]{2,1,0:T(2,128)S(1)} %broadcast_multiply_fusion), kind=kLoop, calls=%fused_computation.8 | loop fusion | flops 1048576 | bytes 4227072 | tf_op jit(solution)/shard_map/sub | solution.py:240
  73.4 1.3 copy-done.5
  74.9 1.4 gather_fusion.2
  76.3 3.5 %all-to-all-start.3 = ((bf16[4,4,128,128]{3,2,1,0:T(8,128)(2,1)}), bf16[4,4,128,128]{3,2,1,0:T(8,128)(2,1)S(1)}, u32[]{:S(2)}, u32[]{:S(2)}) async-start(bf16[4,4,128,128]{3,2,1,0:T(8,128)(2,1)} %bitcast.42), calls=%async_computation.3 | async-start | bytes 1048576 | tf_op jit(solution)/shard_map/all_to_all | solution.py:202
  79.8 1.3 pad_maximum_fusion.3
  81.6 0.8 collective-permute-done
  82.4 1.3 fusion.38
  83.7 1.8 %collective-permute-start.1 = (f32[2]{0:T(128)S(1)}, f32[2]{0:T(128)S(1)}, u32[]{:S(2)}, u32[]{:S(2)}) collective-permute-start(f32[2]{0:T(128)S(1)} %fusion.38), channel_id=1, source_target_pairs={{0,2},{2,0},{4,6},{6,4},{1,3},{3,1},{5,7},{7,5},{8,10},{10,8},{12,... | collective-permute-start | bytes 32 | tf_op jit(solution)/shard_map/ppermute | solution.py:32
  85.5 3.9 %collective-permute-done.1 = f32[2]{0:T(128)S(1)} collective-permute-done((f32[2]{0:T(128)S(1)}, f32[2]{0:T(128)S(1)}, u32[]{:S(2)}, u32[]{:S(2)}) %collective-permute-start.1) | collective-permute-done | bytes 40 | tf_op jit(solution)/shard_map/ppermute | solution.py:32
  89.4 1.3 fusion.40
  90.7 4.5 %collective-permute-start.2 = (f32[2]{0:T(128)S(1)}, f32[2]{0:T(128)S(1)}, u32[]{:S(2)}, u32[]{:S(2)}) collective-permute-start(f32[2]{0:T(128)S(1)} %fusion.40), channel_id=1, source_target_pairs={{0,4},{2,6},{4,0},{6,2},{1,5},{3,7},{5,1},{7,3},{8,12},{10,14},{12... | collective-permute-start | bytes 32 | tf_op jit(solution)/shard_map/ppermute | solution.py:32
  95.2 1.5 collective-permute-done.2
  96.7 1.5 collective-permute-start.3
  98.2 2.0 %collective-permute-done.3 = f32[2]{0:T(128)S(1)} collective-permute-done((f32[2]{0:T(128)S(1)}, f32[2]{0:T(128)S(1)}, u32[]{:S(2)}, u32[]{:S(2)}) %collective-permute-start.3) | collective-permute-done | bytes 40 | tf_op jit(solution)/shard_map/ppermute | solution.py:32
  100.3 1.5 collective-permute-start.4
  101.8 2.0 %collective-permute-done.4 = f32[2]{0:T(128)S(1)} collective-permute-done((f32[2]{0:T(128)S(1)}, f32[2]{0:T(128)S(1)}, u32[]{:S(2)}, u32[]{:S(2)}) %collective-permute-start.4) | collective-permute-done | bytes 40 | tf_op jit(solution)/shard_map/ppermute | solution.py:32
  103.8 0.6 fusion.33
  105.7 2.2 %convert_reduce_fusion = (f32[]{:T(128)}, bf16[16,1,128,128]{3,2,1,0:T(8,128)(2,1)S(1)}) fusion(f32[16,2,128,128]{3,2,1,0:T(8,128)} %copy-done.5, f32[]{:T(128)} %bitcast.9), kind=kLoop, calls=%fused_computation.29 | loop fusion | flops 1048575 | bytes 1572872 | tf_op jit(solution)/shard_map/reduce_sum | solution.py:224
  107.9 1.4 gather_fusion.1
  109.3 4.3 %all-to-all-start.2 = ((bf16[4,4,128,128]{3,2,1,0:T(8,128)(2,1)}), bf16[4,4,128,128]{3,2,1,0:T(8,128)(2,1)}, u32[]{:S(2)}, u32[]{:S(2)}) async-start(bf16[4,4,128,128]{3,2,1,0:T(8,128)(2,1)} %bitcast.39), calls=%async_computation.2 | async-start | bytes 1048576 | tf_op jit(solution)/shard_map/all_to_all | solution.py:202
  113.6 2.1 %slice.129 = bf16[16,1,128,128]{3,2,1,0:T(8,128)(2,1)} slice(f32[16,2,128,128]{3,2,1,0:T(8,128)} %copy-done.5), slice={[0:16], [1:2], [0:128], [0:128]} | slice | bytes 1048576 | tf_op jit(solution)/shard_map/slice | solution.py:241
  115.8 9.3 %all-to-all-done.2 = bf16[4,4,128,128]{3,2,1,0:T(8,128)(2,1)} async-done(((bf16[4,4,128,128]{3,2,1,0:T(8,128)(2,1)}), bf16[4,4,128,128]{3,2,1,0:T(8,128)(2,1)}, u32[]{:S(2)}, u32[]{:S(2)}) %all-to-all-start.2) | async-done | bytes 524320 | tf_op jit(solution)/shard_map/all_to_all | solution.py:202
  125.0 2.7 %maximum_maximum_fusion.pool_ref = bf16[32,2,128,128]{3,2,1,0:T(8,128)(2,1)} fusion(bf16[16,1,128,128]{3,2,1,0:T(8,128)(2,1)S(1)} %bitcast.90, bf16[16,1,128,128]{3,2,1,0:T(8,128)(2,1)} %bitcast.40, bf16[16,1,128,128]{3,2,1,0:T(8,128)(2,1)} %slice.129, bf16[16,1,128,128]{3,2,1,0:T(8,128)(2,1)S(1)} %get-tuple-element.12), kind=kLoop, calls=%fused_computation.4 | loop fusion | flops 3145728 | bytes 4194304 | tf_op jit(solution)/shard_map/concatenate | solution.py:220
  127.7 7.1 %shard_map.96 = f32[16,2,128,128]{3,2,1,0:T(8,128)} custom-call(s32[64]{0:T(128)} %get-tuple-element.16.index_ref, bf16[16,4,128,128]{3,2,1,0:T(8,128)(2,1)} %weight_ref.3, bf16[32,2,128,128]{3,2,1,0:T(8,128)(2,1)} %maximum_maximum_fusion.pool_ref), custom_call_target="tpu_custom_call" | custom-call | flops 536870912 | bytes 6291456 | tf_op jit(solution)/shard_map/pallas_call | solution.py:130
  134.8 2.1 %slice_reduce_fusion = f32[]{:T(128)} fusion(f32[16,2,128,128]{3,2,1,0:T(8,128)} %shard_map.96), kind=kLoop, calls=%fused_computation.23 | loop fusion | flops 262143 | bytes 1048580 | tf_op jit(solution)/shard_map/reduce_sum | solution.py:224
  136.9 6.9 %fusion.1 = f32[16,2,128,128]{2,3,1,0:T(8,128)S(1)} fusion(f32[16,2,128,128]{3,2,1,0:T(8,128)} %shard_map.96, f32[16,2,128,128]{3,1,0,2:T(2,128)S(1)} %bitcast.85), kind=kOutput, calls=%fused_computation.9 | convolution fusion | flops 805306368 | bytes 6291456 | tf_op jit(solution)/shard_map/tfzy,tfcy->tfcz/dot_general | solution.py:227
  143.9 1.3 copy-done.3
  145.2 1.9 %copy.99 = f32[16,2,128,128]{3,2,1,0:T(8,128)S(1)} copy(f32[16,2,128,128]{2,3,1,0:T(8,128)} %copy-done.3) | data formatting | bytes 4194304 | tf_op jit(solution)/shard_map/tfzy,tfcy->tfcz/dot_general | solution.py:227
  147.2 1.4 pad_maximum_fusion.4
  149.7 1.3 fusion.37
  151.0 3.5 %collective-permute-done.9 = f32[2]{0:T(128)S(1)} collective-permute-done((f32[2]{0:T(128)S(1)}, f32[2]{0:T(128)S(1)}, u32[]{:S(2)}, u32[]{:S(2)}) %collective-permute-start.9) | collective-permute-done | bytes 40 | tf_op jit(solution)/shard_map/ppermute | solution.py:32
  154.5 1.3 fusion.39
  155.9 4.4 %collective-permute-done.10 = f32[2]{0:T(128)S(1)} collective-permute-done((f32[2]{0:T(128)S(1)}, f32[2]{0:T(128)S(1)}, u32[]{:S(2)}, u32[]{:S(2)}) %collective-permute-start.10) | collective-permute-done | bytes 40 | tf_op jit(solution)/shard_map/ppermute | solution.py:32
  160.3 1.5 collective-permute-start.11
  161.8 2.1 %collective-permute-done.11 = f32[2]{0:T(128)S(1)} collective-permute-done((f32[2]{0:T(128)S(1)}, f32[2]{0:T(128)S(1)}, u32[]{:S(2)}, u32[]{:S(2)}) %collective-permute-start.11) | collective-permute-done | bytes 40 | tf_op jit(solution)/shard_map/ppermute | solution.py:32
  163.9 1.5 collective-permute-start.12
  165.4 2.0 %collective-permute-done.12 = f32[2]{0:T(128)S(1)} collective-permute-done((f32[2]{0:T(128)S(1)}, f32[2]{0:T(128)S(1)}, u32[]{:S(2)}, u32[]{:S(2)}) %collective-permute-start.12) | collective-permute-done | bytes 40 | tf_op jit(solution)/shard_map/ppermute | solution.py:32
  169.4 0.6 pad_maximum_fusion.5
  170.1 0.7 multiply_subtract_fusion
  170.8 0.9 fusion.11
  171.7 0.9 fusion.10
  (83 shorter events, 6.8 us)
Async XLA Ops:
  0.6 15.1 %copy-start = (f32[2,8]{1,0:T(2,128)S(1)}, f32[2,8]{1,0:T(2,128)}, u32[]{:S(2)}) copy-start(f32[2,8]{1,0:T(2,128)} %param.12) | copy-start | bytes 196
  0.6 15.5 %copy-start.8 = (f32[8]{0:T(128)S(1)}, f32[8]{0:T(128)}, u32[]{:S(2)}) copy-start(f32[8]{0:T(128)} %param.13) | copy-start | bytes 100
  1.4 14.6 %collective-permute-start.5 = (s32[16,1]{0,1:T(1,128)S(1)}, s32[16,1]{0,1:T(1,128)S(1)}, u32[]{:S(2)}, u32[]{:S(2)}) collective-permute-start(s32[16,1]{0,1:T(1,128)S(1)} %slice.68), channel_id=1, source_target_pairs={{1,0},{3,2},{5,4},{7,6},{9,8},{11,10},{13,12},{15,14},{17,16},{19,... | collective-permute-start | bytes 200 | tf_op jit(solution)/shard_map/ppermute | solution.py:17
  5.2 11.8 %all-to-all-start = ((s32[4,1,4]{2,1,0:T(1,128)}), s32[4,1,4]{2,1,0:T(1,128)S(1)}, u32[]{:S(2)}, u32[]{:S(2)}) async-start(s32[4,1,4]{2,1,0:T(1,128)} %bitcast.4), calls=%async_computation | async-start | bytes 4096 | tf_op jit(solution)/shard_map/all_to_all | solution.py:199
  18.8 31.4 %all-to-all-start.1 = ((bf16[4,4,2,128,128]{4,3,2,1,0:T(8,128)(2,1)}), bf16[4,4,2,128,128]{4,3,2,1,0:T(8,128)(2,1)S(1)}, u32[]{:S(2)}, u32[]{:S(2)}) async-start(bf16[4,4,2,128,128]{4,3,2,1,0:T(8,128)(2,1)} %bitcast.6), calls=%async_computation.1 | async-start | bytes 2097152 | tf_op jit(solution)/shard_map/all_to_all | solution.py:202
  36.3 13.9 %copy-start.6 = (bf16[16,128,128]{2,1,0:T(8,128)(2,1)S(1)}, bf16[16,128,128]{2,1,0:T(8,128)(2,1)}, u32[]{:S(2)}) copy-start(bf16[16,128,128]{2,1,0:T(8,128)(2,1)} %param.7) | copy-start | bytes 1572868
  36.3 13.9 %copy-start.7 = (bf16[16,128,128]{2,1,0:T(8,128)(2,1)S(1)}, bf16[16,128,128]{2,1,0:T(8,128)(2,1)}, u32[]{:S(2)}) copy-start(bf16[16,128,128]{2,1,0:T(8,128)(2,1)} %param.8) | copy-start | bytes 1572868
  38.9 1.1 collective-permute-start.7
  51.8 7.3 %copy-start.1 = (f32[128,32,128]{2,1,0:T(8,128)S(1)}, f32[128,32,128]{2,1,0:T(8,128)}, u32[]{:S(2)}) copy-start(f32[128,32,128]{2,1,0:T(8,128)} %shard_map.95) | copy-start | bytes 6291460
  59.0 8.5 %copy-start.2 = (f32[16,2,128,128]{3,2,1,0:T(8,128)S(1)}, f32[16,2,128,128]{3,2,1,0:T(8,128)}, u32[]{:S(2)}) copy-start(f32[16,2,128,128]{3,2,1,0:T(8,128)} %shard_map.94) | copy-start | bytes 6291460
  66.1 1.3 copy-start.4
  67.5 3.9 %collective-permute-start.6 = (f32[16,2,128]{2,1,0:T(2,128)S(1)}, f32[16,2,128]{2,1,0:T(2,128)S(1)}, u32[]{:S(2)}, u32[]{:S(2)}) collective-permute-start(f32[16,2,128]{2,1,0:T(2,128)S(1)} %bitcast.103), channel_id=1, source_target_pairs={{0,1},{1,0},{2,3},{3,2},{4,5},{5,4},{6,7},{7,6},{8,9},{9,8},{10,11... | collective-permute-start | bytes 49160 | tf_op jit(solution)/shard_map/ppermute | solution.py:21
  73.4 1.3 copy-start.5
  76.3 33.0 %all-to-all-start.3 = ((bf16[4,4,128,128]{3,2,1,0:T(8,128)(2,1)}), bf16[4,4,128,128]{3,2,1,0:T(8,128)(2,1)S(1)}, u32[]{:S(2)}, u32[]{:S(2)}) async-start(bf16[4,4,128,128]{3,2,1,0:T(8,128)(2,1)} %bitcast.42), calls=%async_computation.3 | async-start | bytes 1048576 | tf_op jit(solution)/shard_map/all_to_all | solution.py:202
  81.1 1.3 collective-permute-start
  83.7 5.7 %collective-permute-start.1 = (f32[2]{0:T(128)S(1)}, f32[2]{0:T(128)S(1)}, u32[]{:S(2)}, u32[]{:S(2)}) collective-permute-start(f32[2]{0:T(128)S(1)} %fusion.38), channel_id=1, source_target_pairs={{0,2},{2,0},{4,6},{6,4},{1,3},{3,1},{5,7},{7,5},{8,10},{10,8},{12,... | collective-permute-start | bytes 32 | tf_op jit(solution)/shard_map/ppermute | solution.py:32
  90.7 6.0 %collective-permute-start.2 = (f32[2]{0:T(128)S(1)}, f32[2]{0:T(128)S(1)}, u32[]{:S(2)}, u32[]{:S(2)}) collective-permute-start(f32[2]{0:T(128)S(1)} %fusion.40), channel_id=1, source_target_pairs={{0,4},{2,6},{4,0},{6,2},{1,5},{3,7},{5,1},{7,3},{8,12},{10,14},{12... | collective-permute-start | bytes 32 | tf_op jit(solution)/shard_map/ppermute | solution.py:32
  96.7 3.5 %collective-permute-start.3 = (f32[2]{0:T(128)S(1)}, f32[2]{0:T(128)S(1)}, u32[]{:S(2)}, u32[]{:S(2)}) collective-permute-start(f32[2]{0:T(128)S(1)} %add.128), channel_id=1, source_target_pairs={{0,8},{8,0},{16,24},{24,16},{1,9},{9,1},{17,25},{25,17},{2,10},{10... | collective-permute-start | bytes 32 | tf_op jit(solution)/shard_map/ppermute | solution.py:32
  100.3 3.5 %collective-permute-start.4 = (f32[2]{0:T(128)S(1)}, f32[2]{0:T(128)S(1)}, u32[]{:S(2)}, u32[]{:S(2)}) collective-permute-start(f32[2]{0:T(128)S(1)} %add.129), channel_id=1, source_target_pairs={{0,16},{8,24},{16,0},{24,8},{1,17},{9,25},{17,1},{25,9},{2,18},{10... | collective-permute-start | bytes 32 | tf_op jit(solution)/shard_map/ppermute | solution.py:32
  109.3 15.7 %all-to-all-start.2 = ((bf16[4,4,128,128]{3,2,1,0:T(8,128)(2,1)}), bf16[4,4,128,128]{3,2,1,0:T(8,128)(2,1)}, u32[]{:S(2)}, u32[]{:S(2)}) async-start(bf16[4,4,128,128]{3,2,1,0:T(8,128)(2,1)} %bitcast.39), calls=%async_computation.2 | async-start | bytes 1048576 | tf_op jit(solution)/shard_map/all_to_all | solution.py:202
  143.9 1.3 copy-start.3
  148.5 1.1 collective-permute-start.8
  148.6 21.4 %collective-permute-start.13 = (f32[16,2,128]{2,1,0:T(2,128)S(1)}, f32[16,2,128]{2,1,0:T(2,128)S(1)}, u32[]{:S(2)}, u32[]{:S(2)}) collective-permute-start(f32[16,2,128]{2,1,0:T(2,128)S(1)} %select_bitcast_fusion), channel_id=1, source_target_pairs={{0,1},{1,0},{2,3},{3,2},{4,5},{5,4},{6,7},{7,6},{8,9},{9,8},{10,11... | collective-permute-start | bytes 49160 | tf_op jit(solution)/shard_map/ppermute | solution.py:21
  151.0 3.5 %collective-permute-start.9 = (f32[2]{0:T(128)S(1)}, f32[2]{0:T(128)S(1)}, u32[]{:S(2)}, u32[]{:S(2)}) collective-permute-start(f32[2]{0:T(128)S(1)} %fusion.37), channel_id=1, source_target_pairs={{0,2},{2,0},{4,6},{6,4},{1,3},{3,1},{5,7},{7,5},{8,10},{10,8},{12,... | collective-permute-start | bytes 32 | tf_op jit(solution)/shard_map/ppermute | solution.py:32
  155.9 4.4 %collective-permute-start.10 = (f32[2]{0:T(128)S(1)}, f32[2]{0:T(128)S(1)}, u32[]{:S(2)}, u32[]{:S(2)}) collective-permute-start(f32[2]{0:T(128)S(1)} %fusion.39), channel_id=1, source_target_pairs={{0,4},{2,6},{4,0},{6,2},{1,5},{3,7},{5,1},{7,3},{8,12},{10,14},{12... | collective-permute-start | bytes 32 | tf_op jit(solution)/shard_map/ppermute | solution.py:32
  160.3 3.5 %collective-permute-start.11 = (f32[2]{0:T(128)S(1)}, f32[2]{0:T(128)S(1)}, u32[]{:S(2)}, u32[]{:S(2)}) collective-permute-start(f32[2]{0:T(128)S(1)} %add.142), channel_id=1, source_target_pairs={{0,8},{8,0},{16,24},{24,16},{1,9},{9,1},{17,25},{25,17},{2,10},{10... | collective-permute-start | bytes 32 | tf_op jit(solution)/shard_map/ppermute | solution.py:32
  163.9 3.5 %collective-permute-start.12 = (f32[2]{0:T(128)S(1)}, f32[2]{0:T(128)S(1)}, u32[]{:S(2)}, u32[]{:S(2)}) collective-permute-start(f32[2]{0:T(128)S(1)} %add.143), channel_id=1, source_target_pairs={{0,16},{8,24},{16,0},{24,8},{1,17},{9,25},{17,1},{25,9},{2,18},{10... | collective-permute-start | bytes 32 | tf_op jit(solution)/shard_map/ppermute | solution.py:32

commit v11 on v10

--- a/solution.py
+++ b/solution.py
@@ -104,9 +104,9 @@
     return jnp.transpose(inverse, (1, 0, 2)).reshape(lead + (levels, levels)), ready
 
 
-def advect_kernel(index_ref, weight_ref, pool_ref, out_ref):
+def advect_solve_kernel(index_ref, weight_ref, pool_ref, inverse_ref, solved_ref, sums_ref):
     tiles, sources = weight_ref.shape[:2]
-    fields = out_ref.shape[1]
+    fields = solved_ref.shape[1]
 
     def one_tile(t, carry):
         picked = [index_ref[t * sources + k] for k in range(sources)]
@@ -118,30 +118,43 @@
                 total = total + jnp.dot(
                     weight_ref[t, k], pool_ref[picked[k], field], preferred_element_type=jnp.float32
                 )
-            out_ref[t, field] = total
+            if field == 0:
+                sums_ref[t] = jnp.sum(total, axis=0, keepdims=True)
+            solved_ref[t, field] = lax.dot_general(
+                total,
+                inverse_ref[t, field],
+                (((1,), (1,)), ((), ())),
+                precision=HIGHEST,
+                preferred_element_type=jnp.float32,
+            )
         return carry
 
     lax.fori_loop(0, tiles, one_tile, 0)
 
 
-def advect(weights, tile_pool, pool_index):
+def advect_solve(weights, tile_pool, pool_index, inverse):
     tiles, sources = pool_index.shape
     _, fields, columns, levels = tile_pool.shape
     return pl.pallas_call(
-        advect_kernel,
-        out_shape=jax.ShapeDtypeStruct((tiles, fields, columns, levels), jnp.float32),
+        advect_solve_kernel,
+        out_shape=(
+            jax.ShapeDtypeStruct((tiles, fields, columns, levels), jnp.float32),
+            jax.ShapeDtypeStruct((tiles, 1, levels), jnp.float32),
+        ),
         in_specs=[
             pl.BlockSpec(memory_space=pltpu.SMEM),
             pl.BlockSpec(memory_space=pltpu.VMEM),
             pl.BlockSpec(memory_space=pltpu.VMEM),
+            pl.BlockSpec(memory_space=pltpu.VMEM),
         ],
-        out_specs=pl.BlockSpec(memory_space=pltpu.VMEM),
+        out_specs=(pl.BlockSpec(memory_space=pltpu.VMEM), pl.BlockSpec(memory_space=pltpu.VMEM)),
         cost_estimate=pl.CostEstimate(
-            flops=2 * tiles * sources * fields * columns * columns * levels,
+            flops=2 * tiles * (sources + 6) * fields * columns * columns * levels,
             transcendentals=0,
-            bytes_accessed=weights.size * 2 + tile_pool.size * 2 + tiles * fields * columns * levels * 4,
-        ),
-    )(pool_index.reshape(-1), weights, tile_pool)
+            bytes_accessed=weights.size * 2 + tile_pool.size * 2 + inverse.size * 4
+            + tiles * fields * columns * levels * 4,
+        ),
+    )(pool_index.reshape(-1), weights, tile_pool, inverse)
 
 
 def interface_values(low_value, low_spike, high_value, high_spike):
@@ -218,18 +231,11 @@
     ratios = []
     for step_index in range(STEPS):
         tile_pool = jnp.concatenate([fields, arrived], axis=0)
-        advected = advect(interp_weights, tile_pool, pool_index)
+        solved, advected_sums = advect_solve(interp_weights, tile_pool, pool_index, inverse)
         last = step_index + 1 == STEPS
         totals = butterfly_sum(
-            jnp.stack([jnp.sum(fields[:, 0], dtype=jnp.float32), jnp.sum(advected[:, 0])]),
+            jnp.stack([jnp.sum(fields[:, 0], dtype=jnp.float32), jnp.sum(advected_sums)]),
             ("gz", "gy", "gx"),
-        )
-        solved = jnp.einsum(
-            "tfzy,tfcy->tfcz",
-            inverse,
-            advected,
-            precision=HIGHEST,
-            preferred_element_type=jnp.float32,
         )
         edge_value = jnp.where(my_layer == 0, solved[..., -1], solved[..., 0])
         other_value = from_partner(edge_value, "gz", 0)

time: 174 us -> 180 us (1.034)
  matrix products: 14.7 us -> 0.72 us
  Pallas kernels: 20.3 us -> 33.7 us
  waiting for transfers between devices: 42.9 us -> 50.6 us
  other arithmetic: 29.5 us -> 36.5 us
  starting transfers between devices: 34.1 us -> 28.5 us
    dot_general x2 -> x0, matrix products: 14 us -> none  [per_device(): jnp.einsum('tfzy,tfcy->tfcz', inverse, advected, precision=HIGHEST, prefe...]
    pallas_call x2, Pallas kernels: 14.4 us -> 27.8 us  [advect_solve(): pl.pallas_call(advect_solve_kernel, out_shape=(jax.ShapeDtypeStruct((tile...]
    select_n x2, other arithmetic: 0.03 us -> 8.36 us  [per_device(): edge_value = jnp.where(my_layer == 0, solved[..., -1], solved[..., 0])]
    all_to_all x3, waiting for transfers between devices: 19.1 us -> 26.7 us  [exchange(): lax.all_to_all(tiles[wanted], 'gy', split_axis=0, concat_axis=0, tiled=True)]
    ppermute x10, starting transfers between devices: 12.8 us -> 6.28 us  [butterfly_sum(): lax.ppermute(value, axis, [(i, i ^ bit) for i in range(devices)])]
    dot_general x2 -> x0, local copies, waits for them, and re-layouts: 4.85 us -> none  [per_device(): jnp.einsum('tfzy,tfcy->tfcz', inverse, advected, precision=HIGHEST, prefe...]
    select_n x2 -> x4, local copies, waits for them, and re-layouts: 0.17 us -> 4.73 us  [the longest x2 4.71 us: per_device(): edge_value = jnp.where(my_layer == 0, solved[..., -1], solved[..., 0])]
    unnamed x20, local copies, waits for them, and re-layouts: 5.53 us -> 2.88 us
  transfers between devices with their start and end apart: 18 -> 18, of which waited for: 14 -> 11; matrix products, arithmetic and copies ran while one was open for 20% -> 23% of each run, Pallas kernels for 3% -> 3%
where the time goes in v11:
time: 180 us; the launch traced here: 179 us
  waiting for transfers between devices  50.6 us (28%)
  other arithmetic  36.5 us (20%)
  Pallas kernels  33.7 us (19%)
  starting transfers between devices  28.5 us (16%)
  local copies, waits for them, and re-layouts  25.6 us (14%)
  between operations  3.66 us (2%)
    pallas_call x2, Pallas kernels, advect_solve(): pl.pallas_call(advect_solve_kernel, out_shape=(jax.ShapeDtypeStruct((tile...  27.8 us
    all_to_all x3, waiting for transfers between devices, exchange(): lax.all_to_all(tiles[wanted], 'gy', split_axis=0, concat_axis=0, tiled=True)  26.7 us
    ppermute x10, waiting for transfers between devices, butterfly_sum(): lax.ppermute(value, axis, [(i, i ^ bit) for i in range(devices)])  23.9 us
    all_to_all x3, starting transfers between devices, exchange(): lax.all_to_all(tiles[wanted], 'gy', split_axis=0, concat_axis=0, tiled=True)  12.7 us
    select_n x2, other arithmetic, per_device(): edge_value = jnp.where(my_layer == 0, solved[..., -1], solved[..., 0])  8.36 us
    all_to_all x1, starting transfers between devices, per_device(): lax.all_to_all(requests, 'gy', split_axis=0, concat_axis=0, tiled=True)  6.32 us
    ppermute x10, starting transfers between devices, butterfly_sum(): lax.ppermute(value, axis, [(i, i ^ bit) for i in range(devices)])  6.28 us
    pallas_call x1, Pallas kernels, block_inverse(): pl.pallas_call(thomas_inverse_kernel, out_shape=jax.ShapeDtypeStruct((lev...  5.93 us
  transfers between devices with their start and end apart: 18, of which 11 were waited for; matrix products, arithmetic and copies ran while one was open for 23% of the time, Pallas kernels for 3%

profile of v11, /device:TPU:0, one launch (start us, length us, event | category | flops | bytes accessed | tf_op | source)
XLA Modules:
  0.0 179.3 jit_solution(10265445532386162941)
XLA Ops:
  0.7 0.8 copy.82
  2.4 0.7 select_reduce_fusion.2
  3.2 6.3 %all-to-all-start = ((s32[4,1,4]{2,1,0:T(1,128)}), s32[4,1,4]{2,1,0:T(1,128)S(1)}, u32[]{:S(2)}, u32[]{:S(2)}) async-start(s32[4,1,4]{2,1,0:T(1,128)} %bitcast.4), calls=%async_computation | async-start | bytes 4096 | tf_op jit(solution)/shard_map/all_to_all | solution.py:212
  9.5 0.7 slice.59
  10.2 1.3 collective-permute-start
  11.5 0.8 copy.84
  12.7 1.9 %convert_reduce_fusion.1 = f32[]{:T(128)} fusion(bf16[16,128,128]{2,1,0:T(8,128)(2,1)} %param.7), kind=kLoop, calls=%fused_computation.25 | loop fusion | flops 524287 | bytes 524292 | tf_op jit(solution)/shard_map/reduce_sum | solution.py:237
  14.6 1.3 pad_maximum_fusion.1
  16.9 1.7 gather_fusion
  18.6 5.1 %all-to-all-start.1 = ((bf16[4,4,2,128,128]{4,3,2,1,0:T(8,128)(2,1)}), bf16[4,4,2,128,128]{4,3,2,1,0:T(8,128)(2,1)}, u32[]{:S(2)}, u32[]{:S(2)}) async-start(bf16[4,4,2,128,128]{4,3,2,1,0:T(8,128)(2,1)} %bitcast.6), calls=%async_computation.1 | async-start | bytes 2097152 | tf_op jit(solution)/shard_map/all_to_all | solution.py:215
  24.3 2.0 %broadcast_in_dim.113.upper_ref = f32[128,32,128]{2,1,0:T(8,128)} broadcast(f32[128,32]{1,0:T(8,128)S(1)} %copy.91), dimensions={0,1} | broadcast | bytes 2113536 | tf_op jit(solution)/shard_map/broadcast_in_dim | solution.py:87
  26.3 1.9 %broadcast_in_dim.107.lower_ref = f32[128,32,128]{2,1,0:T(8,128)} broadcast(f32[128,32]{1,0:T(8,128)S(1)} %bitcast.87), dimensions={0,1} | broadcast | bytes 2113536 | tf_op jit(solution)/shard_map/broadcast_in_dim | solution.py:87
  28.2 1.9 %broadcast_in_dim.109.diagonal_ref = f32[128,32,128]{2,1,0:T(8,128)} broadcast(f32[128,32]{1,0:T(8,128)S(1)} %bitcast.88), dimensions={0,1} | broadcast | bytes 2113536 | tf_op jit(solution)/shard_map/broadcast_in_dim | solution.py:87
  30.2 5.9 %shard_map.94 = f32[128,32,128]{2,1,0:T(8,128)} custom-call(f32[128,32,128]{2,1,0:T(8,128)} %broadcast_in_dim.107.lower_ref, f32[128,32,128]{2,1,0:T(8,128)} %broadcast_in_dim.109.diagonal_ref, f32[128,32,128]{2,1,0:T(8,128)} %broadcast_in_dim.113.upper_ref), custom_call_target="tpu_custom_call" | custom-call | flops 8388608 | bytes 33554432 | tf_op jit(solution)/shard_map/pallas_call | solution.py:94
  36.1 2.4 %select_reduce_fusion = f32[32,128]{0,1:T(8,128)S(1)} fusion(pred[128]{0:T(512)(128)(4,1)S(1)} %iota_compare_fusion.9, f32[128,32,128]{2,1,0:T(8,128)} %shard_map.94), kind=kLoop, calls=%fused_computation.9 | loop fusion | flops 1044480 | bytes 2113664 | tf_op jit(solution)/shard_map/reduce_sum | solution.py:223
  38.8 0.8 collective-permute-start.7
  39.8 2.6 %copy.92 = f32[32,128,128]{2,1,0:T(8,128)} copy(f32[32,128,128]{2,0,1:T(8,128)S(1)} %bitcast.80) | data formatting | bytes 4194304 | tf_op jit(solution)/shard_map/transpose | solution.py:104
  42.3 8.4 %all-to-all-done.1 = bf16[4,4,2,128,128]{4,3,2,1,0:T(8,128)(2,1)} async-done(((bf16[4,4,2,128,128]{4,3,2,1,0:T(8,128)(2,1)}), bf16[4,4,2,128,128]{4,3,2,1,0:T(8,128)(2,1)}, u32[]{:S(2)}, u32[]{:S(2)}) %all-to-all-start.1) | async-done | bytes 1048608 | tf_op jit(solution)/shard_map/all_to_all | solution.py:215
  50.8 2.8 %pad_maximum_fusion.pool_ref = bf16[32,2,128,128]{3,2,1,0:T(8,128)(2,1)} fusion(bf16[16,2,128,128]{3,2,1,0:T(8,128)(2,1)} %bitcast.7, bf16[16,1,128,128]{3,2,1,0:T(8,128)(2,1)S(1)} %bitcast.86, bf16[16,1,128,128]{3,2,1,0:T(8,128)(2,1)S(1)} %bitcast.82), kind=kLoop, calls=%fused_computation.3 | loop fusion | flops 2097152 | bytes 4194304 | tf_op jit(solution)/shard_map/concatenate | solution.py:233
  53.6 13.9 %shard_map.95 = (f32[16,2,128,128]{3,2,1,0:T(8,128)}, f32[16,1,128]{2,1,0:T(1,128)}) custom-call(s32[64]{0:T(128)} %get-tuple-element.24.index_ref, bf16[16,4,128,128]{3,2,1,0:T(8,128)(2,1)} %weight_ref.3, bf16[32,2,128,128]{3,2,1,0:T(8,128)(2,1)} %pad_maximum_fusion.pool_ref, f32[16,2,128,128]{3,2,1,0:T(8,128)} %bitcast.78), custom_call_target="tpu_custom_call" | custom-call | flops 1342177280 | bytes 8388608 | tf_op jit(solution)/shard_map/pallas_call | solution.py:138
  67.5 1.3 reduce_sum.68
  68.8 1.4 pad_maximum_fusion.3
  70.1 4.2 %slice_select_fusion.1 = f32[16,2,128,1]{3,2,1,0:T(8,128)} fusion(f32[16,2,128,128]{3,2,1,0:T(8,128)} %get-tuple-element.15, pred[]{:T(512)S(6)} %eq.158), kind=kLoop, calls=%fused_computation.8 | loop fusion | flops 4096 | bytes 49153 | tf_op jit(solution)/shard_map/jit(_where)/select_n | solution.py:240
  74.3 2.4 %copy.96 = f32[16,2,128,1]{2,0,3,1:T(8,128)S(1)} copy(f32[16,2,128,1]{3,2,1,0:T(8,128)} %slice_select_fusion.1) | data formatting | bytes 32768 | tf_op jit(solution)/shard_map/jit(_where)/select_n | solution.py:240
  76.7 0.5 collective-permute-start.6
  77.2 1.4 fusion.30
  78.6 3.5 %collective-permute-done.2 = f32[2]{0:T(128)S(1)} collective-permute-done((f32[2]{0:T(128)S(1)}, f32[2]{0:T(128)S(1)}, u32[]{:S(2)}, u32[]{:S(2)}) %collective-permute-start.2) | collective-permute-done | bytes 40 | tf_op jit(solution)/shard_map/ppermute | solution.py:32
  82.1 1.4 fusion.32
  83.5 4.4 %collective-permute-done.3 = f32[2]{0:T(128)S(1)} collective-permute-done((f32[2]{0:T(128)S(1)}, f32[2]{0:T(128)S(1)}, u32[]{:S(2)}, u32[]{:S(2)}) %collective-permute-start.3) | collective-permute-done | bytes 40 | tf_op jit(solution)/shard_map/ppermute | solution.py:32
  87.9 1.5 collective-permute-start.4
  89.4 2.1 %collective-permute-done.4 = f32[2]{0:T(128)S(1)} collective-permute-done((f32[2]{0:T(128)S(1)}, f32[2]{0:T(128)S(1)}, u32[]{:S(2)}, u32[]{:S(2)}) %collective-permute-start.4) | collective-permute-done | bytes 40 | tf_op jit(solution)/shard_map/ppermute | solution.py:32
  91.5 1.5 collective-permute-start.5
  93.0 2.0 %collective-permute-done.5 = f32[2]{0:T(128)S(1)} collective-permute-done((f32[2]{0:T(128)S(1)}, f32[2]{0:T(128)S(1)}, u32[]{:S(2)}, u32[]{:S(2)}) %collective-permute-start.5) | collective-permute-done | bytes 40 | tf_op jit(solution)/shard_map/ppermute | solution.py:32
  95.0 0.6 fusion.27
  97.1 0.7 multiply_subtract_fusion.1
  97.8 1.3 copy-done.4
  99.1 1.0 convert_reduce_fusion
  100.1 1.4 gather_fusion.1
  101.5 4.1 %all-to-all-start.2 = ((bf16[4,4,128,128]{3,2,1,0:T(8,128)(2,1)}), bf16[4,4,128,128]{3,2,1,0:T(8,128)(2,1)}, u32[]{:S(2)}, u32[]{:S(2)}) async-start(bf16[4,4,128,128]{3,2,1,0:T(8,128)(2,1)} %bitcast.39), calls=%async_computation.2 | async-start | bytes 1048576 | tf_op jit(solution)/shard_map/all_to_all | solution.py:215
  105.7 1.4 gather_fusion.2
  107.1 8.9 %all-to-all-done.2 = bf16[4,4,128,128]{3,2,1,0:T(8,128)(2,1)} async-done(((bf16[4,4,128,128]{3,2,1,0:T(8,128)(2,1)}), bf16[4,4,128,128]{3,2,1,0:T(8,128)(2,1)}, u32[]{:S(2)}, u32[]{:S(2)}) %all-to-all-start.2) | async-done | bytes 524320 | tf_op jit(solution)/shard_map/all_to_all | solution.py:215
  116.0 3.5 %all-to-all-start.3 = ((bf16[4,4,128,128]{3,2,1,0:T(8,128)(2,1)}), bf16[4,4,128,128]{3,2,1,0:T(8,128)(2,1)S(1)}, u32[]{:S(2)}, u32[]{:S(2)}) async-start(bf16[4,4,128,128]{3,2,1,0:T(8,128)(2,1)} %bitcast.42), calls=%async_computation.3 | async-start | bytes 1048576 | tf_op jit(solution)/shard_map/all_to_all | solution.py:215
  119.5 0.9 slice.115
  120.4 9.4 %all-to-all-done.3 = bf16[4,4,128,128]{3,2,1,0:T(8,128)(2,1)S(1)} async-done(((bf16[4,4,128,128]{3,2,1,0:T(8,128)(2,1)}), bf16[4,4,128,128]{3,2,1,0:T(8,128)(2,1)S(1)}, u32[]{:S(2)}, u32[]{:S(2)}) %all-to-all-start.3) | async-done | bytes 524320 | tf_op jit(solution)/shard_map/all_to_all | solution.py:215
  129.8 2.7 %maximum_maximum_fusion.pool_ref = bf16[32,2,128,128]{3,2,1,0:T(8,128)(2,1)} fusion(bf16[16,1,128,128]{3,2,1,0:T(8,128)(2,1)S(1)} %bitcast.84, bf16[16,1,128,128]{3,2,1,0:T(8,128)(2,1)} %bitcast.40, bf16[16,1,128,128]{3,2,1,0:T(8,128)(2,1)} %slice.115, bf16[16,1,128,128]{3,2,1,0:T(8,128)(2,1)S(1)} %get-tuple-element.20), kind=kLoop, calls=%fused_computation.4 | loop fusion | flops 3145728 | bytes 4194304 | tf_op jit(solution)/shard_map/concatenate | solution.py:233
  132.5 13.9 %shard_map.96 = (f32[16,2,128,128]{3,2,1,0:T(8,128)}, f32[16,1,128]{2,1,0:T(1,128)}) custom-call(s32[64]{0:T(128)} %get-tuple-element.24.index_ref, bf16[16,4,128,128]{3,2,1,0:T(8,128)(2,1)} %weight_ref.3, bf16[32,2,128,128]{3,2,1,0:T(8,128)(2,1)} %maximum_maximum_fusion.pool_ref, f32[16,2,128,128]{3,2,1,0:T(8,128)} %bitcast.79), custom_call_target="tpu_custom_call" | custom-call | flops 1342177280 | bytes 8388608 | tf_op jit(solution)/shard_map/pallas_call | solution.py:138
  146.4 1.3 reduce_sum.72
  147.7 1.4 pad_maximum_fusion.4
  149.2 4.2 %slice_select_fusion = f32[16,2,128,1]{3,2,1,0:T(8,128)} fusion(f32[16,2,128,128]{3,2,1,0:T(8,128)} %get-tuple-element.18, pred[]{:T(512)S(6)} %eq.158), kind=kLoop, calls=%fused_computation.6 | loop fusion | flops 4096 | bytes 49153 | tf_op jit(solution)/shard_map/jit(_where)/select_n | solution.py:240
  153.3 2.4 %copy.99 = f32[16,2,128,1]{2,0,3,1:T(8,128)S(1)} copy(f32[16,2,128,1]{3,2,1,0:T(8,128)} %slice_select_fusion) | data formatting | bytes 32768 | tf_op jit(solution)/shard_map/jit(_where)/select_n | solution.py:240
  155.7 0.5 collective-permute-start.13
  156.2 1.4 fusion.29
  157.8 3.3 %collective-permute-done.9 = f32[2]{0:T(128)S(1)} collective-permute-done((f32[2]{0:T(128)S(1)}, f32[2]{0:T(128)S(1)}, u32[]{:S(2)}, u32[]{:S(2)}) %collective-permute-start.9) | collective-permute-done | bytes 40 | tf_op jit(solution)/shard_map/ppermute | solution.py:32
  161.2 1.4 fusion.31
  162.6 4.4 %collective-permute-done.10 = f32[2]{0:T(128)S(1)} collective-permute-done((f32[2]{0:T(128)S(1)}, f32[2]{0:T(128)S(1)}, u32[]{:S(2)}, u32[]{:S(2)}) %collective-permute-start.10) | collective-permute-done | bytes 40 | tf_op jit(solution)/shard_map/ppermute | solution.py:32
  167.0 1.5 collective-permute-start.11
  168.5 2.1 %collective-permute-done.11 = f32[2]{0:T(128)S(1)} collective-permute-done((f32[2]{0:T(128)S(1)}, f32[2]{0:T(128)S(1)}, u32[]{:S(2)}, u32[]{:S(2)}) %collective-permute-start.11) | collective-permute-done | bytes 40 | tf_op jit(solution)/shard_map/ppermute | solution.py:32
  170.6 1.5 collective-permute-start.12
  172.1 2.0 %collective-permute-done.12 = f32[2]{0:T(128)S(1)} collective-permute-done((f32[2]{0:T(128)S(1)}, f32[2]{0:T(128)S(1)}, u32[]{:S(2)}, u32[]{:S(2)}) %collective-permute-start.12) | collective-permute-done | bytes 40 | tf_op jit(solution)/shard_map/ppermute | solution.py:32
  174.1 0.6 fusion.26
  176.0 0.6 pad_maximum_fusion.5
  176.7 0.7 multiply_subtract_fusion
  177.5 0.9 fusion.6
  178.3 0.9 fusion.5
  (80 shorter events, 4.0 us)
Async XLA Ops:
  0.6 11.8 %copy-start = (f32[2,8]{1,0:T(2,128)S(1)}, f32[2,8]{1,0:T(2,128)}, u32[]{:S(2)}) copy-start(f32[2,8]{1,0:T(2,128)} %param.12) | copy-start | bytes 196
  0.6 15.6 %copy-start.8 = (f32[8]{0:T(128)S(1)}, f32[8]{0:T(128)}, u32[]{:S(2)}) copy-start(f32[8]{0:T(128)} %param.13) | copy-start | bytes 100
  3.2 13.6 %all-to-all-start = ((s32[4,1,4]{2,1,0:T(1,128)}), s32[4,1,4]{2,1,0:T(1,128)S(1)}, u32[]{:S(2)}, u32[]{:S(2)}) async-start(s32[4,1,4]{2,1,0:T(1,128)} %bitcast.4), calls=%async_computation | async-start | bytes 4096 | tf_op jit(solution)/shard_map/all_to_all | solution.py:212
  10.2 5.8 %collective-permute-start = (s32[16,1]{0,1:T(1,128)S(1)}, s32[16,1]{0,1:T(1,128)S(1)}, u32[]{:S(2)}, u32[]{:S(2)}) collective-permute-start(s32[16,1]{0,1:T(1,128)S(1)} %slice.59), channel_id=1, source_target_pairs={{1,0},{3,2},{5,4},{7,6},{9,8},{11,10},{13,12},{15,14},{17,16},{19,... | collective-permute-start | bytes 200 | tf_op jit(solution)/shard_map/ppermute | solution.py:17
  18.6 32.2 %all-to-all-start.1 = ((bf16[4,4,2,128,128]{4,3,2,1,0:T(8,128)(2,1)}), bf16[4,4,2,128,128]{4,3,2,1,0:T(8,128)(2,1)}, u32[]{:S(2)}, u32[]{:S(2)}) async-start(bf16[4,4,2,128,128]{4,3,2,1,0:T(8,128)(2,1)} %bitcast.6), calls=%async_computation.1 | async-start | bytes 2097152 | tf_op jit(solution)/shard_map/all_to_all | solution.py:215
  36.1 3.7 %copy-start.3 = (f32[128,32,128]{2,1,0:T(8,128)S(1)}, f32[128,32,128]{2,1,0:T(8,128)}, u32[]{:S(2)}) copy-start(f32[128,32,128]{2,1,0:T(8,128)} %shard_map.94) | copy-start | bytes 6291460
  38.8 3.5 %collective-permute-start.7 = (f32[16,2]{0,1:T(2,128)S(1)}, f32[16,2]{0,1:T(2,128)S(1)}, u32[]{:S(2)}, u32[]{:S(2)}) collective-permute-start(f32[16,2]{0,1:T(2,128)S(1)} %bitcast.104), channel_id=1, source_target_pairs={{0,1},{1,0},{2,3},{3,2},{4,5},{5,4},{6,7},{7,6},{8,9},{9,8},{10,11... | collective-permute-start | bytes 392 | tf_op jit(solution)/shard_map/ppermute | solution.py:21
  39.7 11.0 %copy-start.6 = (bf16[16,128,128]{2,1,0:T(8,128)(2,1)S(1)}, bf16[16,128,128]{2,1,0:T(8,128)(2,1)}, u32[]{:S(2)}) copy-start(bf16[16,128,128]{2,1,0:T(8,128)(2,1)} %param.7) | copy-start | bytes 1572868
  39.8 11.0 %copy-start.7 = (bf16[16,128,128]{2,1,0:T(8,128)(2,1)S(1)}, bf16[16,128,128]{2,1,0:T(8,128)(2,1)}, u32[]{:S(2)}) copy-start(bf16[16,128,128]{2,1,0:T(8,128)(2,1)} %param.8) | copy-start | bytes 1572868
  70.1 7.1 %collective-permute-start.1 = (f32[2]{0:T(128)S(1)}, f32[2]{0:T(128)S(1)}, u32[]{:S(2)}, u32[]{:S(2)}) collective-permute-start(f32[2]{0:T(128)S(1)} %pad_maximum_fusion.3), channel_id=1, source_target_pairs={{0,1},{1,0},{2,3},{3,2},{4,5},{5,4},{6,7},{7,6},{8,9},{9,8},{10,11... | collective-permute-start | bytes 32 | tf_op jit(solution)/shard_map/ppermute | solution.py:32
  74.3 22.7 %copy-start.2 = (f32[16,2,128,128]{3,2,1,0:T(8,128)S(1)}, f32[16,2,128,128]{3,2,1,0:T(8,128)}, u32[]{:S(2)}) copy-start(f32[16,2,128,128]{3,2,1,0:T(8,128)} %get-tuple-element.15) | copy-start | bytes 6291460
  76.7 20.3 %collective-permute-start.6 = (f32[16,2,128]{2,0,1:T(8,128)S(1)}, f32[16,2,128]{2,0,1:T(8,128)S(1)}, u32[]{:S(2)}, u32[]{:S(2)}) collective-permute-start(f32[16,2,128]{2,0,1:T(8,128)S(1)} %bitcast.97), channel_id=1, source_target_pairs={{0,1},{1,0},{2,3},{3,2},{4,5},{5,4},{6,7},{7,6},{8,9},{9,8},{10,11... | collective-permute-start | bytes 49160 | tf_op jit(solution)/shard_map/ppermute | solution.py:21
  78.6 3.5 %collective-permute-start.2 = (f32[2]{0:T(128)S(1)}, f32[2]{0:T(128)S(1)}, u32[]{:S(2)}, u32[]{:S(2)}) collective-permute-start(f32[2]{0:T(128)S(1)} %fusion.30), channel_id=1, source_target_pairs={{0,2},{2,0},{4,6},{6,4},{1,3},{3,1},{5,7},{7,5},{8,10},{10,8},{12,... | collective-permute-start | bytes 32 | tf_op jit(solution)/shard_map/ppermute | solution.py:32
  83.5 4.4 %collective-permute-start.3 = (f32[2]{0:T(128)S(1)}, f32[2]{0:T(128)S(1)}, u32[]{:S(2)}, u32[]{:S(2)}) collective-permute-start(f32[2]{0:T(128)S(1)} %fusion.32), channel_id=1, source_target_pairs={{0,4},{2,6},{4,0},{6,2},{1,5},{3,7},{5,1},{7,3},{8,12},{10,14},{12... | collective-permute-start | bytes 32 | tf_op jit(solution)/shard_map/ppermute | solution.py:32
  87.9 3.5 %collective-permute-start.4 = (f32[2]{0:T(128)S(1)}, f32[2]{0:T(128)S(1)}, u32[]{:S(2)}, u32[]{:S(2)}) collective-permute-start(f32[2]{0:T(128)S(1)} %add.135), channel_id=1, source_target_pairs={{0,8},{8,0},{16,24},{24,16},{1,9},{9,1},{17,25},{25,17},{2,10},{10... | collective-permute-start | bytes 32 | tf_op jit(solution)/shard_map/ppermute | solution.py:32
  91.5 3.5 %collective-permute-start.5 = (f32[2]{0:T(128)S(1)}, f32[2]{0:T(128)S(1)}, u32[]{:S(2)}, u32[]{:S(2)}) collective-permute-start(f32[2]{0:T(128)S(1)} %add.136), channel_id=1, source_target_pairs={{0,16},{8,24},{16,0},{24,8},{1,17},{9,25},{17,1},{25,9},{2,18},{10... | collective-permute-start | bytes 32 | tf_op jit(solution)/shard_map/ppermute | solution.py:32
  97.8 1.3 copy-start.4
  100.1 5.6 %copy-start.5 = (f32[16,2,128,128]{3,2,1,0:T(8,128)S(1)}, f32[16,2,128,128]{3,2,1,0:T(8,128)}, u32[]{:S(2)}) copy-start(f32[16,2,128,128]{3,2,1,0:T(8,128)} %copy-done.4) | copy-start | bytes 6291460
  101.5 14.6 %all-to-all-start.2 = ((bf16[4,4,128,128]{3,2,1,0:T(8,128)(2,1)}), bf16[4,4,128,128]{3,2,1,0:T(8,128)(2,1)}, u32[]{:S(2)}, u32[]{:S(2)}) async-start(bf16[4,4,128,128]{3,2,1,0:T(8,128)(2,1)} %bitcast.39), calls=%async_computation.2 | async-start | bytes 1048576 | tf_op jit(solution)/shard_map/all_to_all | solution.py:215
  116.0 13.7 %all-to-all-start.3 = ((bf16[4,4,128,128]{3,2,1,0:T(8,128)(2,1)}), bf16[4,4,128,128]{3,2,1,0:T(8,128)(2,1)S(1)}, u32[]{:S(2)}, u32[]{:S(2)}) async-start(bf16[4,4,128,128]{3,2,1,0:T(8,128)(2,1)} %bitcast.42), calls=%async_computation.3 | async-start | bytes 1048576 | tf_op jit(solution)/shard_map/all_to_all | solution.py:215
  149.1 7.1 %collective-permute-start.8 = (f32[2]{0:T(128)S(1)}, f32[2]{0:T(128)S(1)}, u32[]{:S(2)}, u32[]{:S(2)}) collective-permute-start(f32[2]{0:T(128)S(1)} %pad_maximum_fusion.4), channel_id=1, source_target_pairs={{0,1},{1,0},{2,3},{3,2},{4,5},{5,4},{6,7},{7,6},{8,9},{9,8},{10,11... | collective-permute-start | bytes 32 | tf_op jit(solution)/shard_map/ppermute | solution.py:32
  153.3 23.4 %copy-start.1 = (f32[16,2,128,128]{3,2,1,0:T(8,128)S(1)}, f32[16,2,128,128]{3,2,1,0:T(8,128)}, u32[]{:S(2)}) copy-start(f32[16,2,128,128]{3,2,1,0:T(8,128)} %get-tuple-element.18) | copy-start | bytes 6291460
  155.7 21.0 %collective-permute-start.13 = (f32[16,2,128]{2,0,1:T(8,128)S(1)}, f32[16,2,128]{2,0,1:T(8,128)S(1)}, u32[]{:S(2)}, u32[]{:S(2)}) collective-permute-start(f32[16,2,128]{2,0,1:T(8,128)S(1)} %bitcast.96), channel_id=1, source_target_pairs={{0,1},{1,0},{2,3},{3,2},{4,5},{5,4},{6,7},{7,6},{8,9},{9,8},{10,11... | collective-permute-start | bytes 49160 | tf_op jit(solution)/shard_map/ppermute | solution.py:21
  157.6 3.5 %collective-permute-start.9 = (f32[2]{0:T(128)S(1)}, f32[2]{0:T(128)S(1)}, u32[]{:S(2)}, u32[]{:S(2)}) collective-permute-start(f32[2]{0:T(128)S(1)} %fusion.29), channel_id=1, source_target_pairs={{0,2},{2,0},{4,6},{6,4},{1,3},{3,1},{5,7},{7,5},{8,10},{10,8},{12,... | collective-permute-start | bytes 32 | tf_op jit(solution)/shard_map/ppermute | solution.py:32
  162.6 4.4 %collective-permute-start.10 = (f32[2]{0:T(128)S(1)}, f32[2]{0:T(128)S(1)}, u32[]{:S(2)}, u32[]{:S(2)}) collective-permute-start(f32[2]{0:T(128)S(1)} %fusion.31), channel_id=1, source_target_pairs={{0,4},{2,6},{4,0},{6,2},{1,5},{3,7},{5,1},{7,3},{8,12},{10,14},{12... | collective-permute-start | bytes 32 | tf_op jit(solution)/shard_map/ppermute | solution.py:32
  167.0 3.5 %collective-permute-start.11 = (f32[2]{0:T(128)S(1)}, f32[2]{0:T(128)S(1)}, u32[]{:S(2)}, u32[]{:S(2)}) collective-permute-start(f32[2]{0:T(128)S(1)} %add.142), channel_id=1, source_target_pairs={{0,8},{8,0},{16,24},{24,16},{1,9},{9,1},{17,25},{25,17},{2,10},{10... | collective-permute-start | bytes 32 | tf_op jit(solution)/shard_map/ppermute | solution.py:32
  170.6 3.5 %collective-permute-start.12 = (f32[2]{0:T(128)S(1)}, f32[2]{0:T(128)S(1)}, u32[]{:S(2)}, u32[]{:S(2)}) collective-permute-start(f32[2]{0:T(128)S(1)} %add.143), channel_id=1, source_target_pairs={{0,16},{8,24},{16,0},{24,8},{1,17},{9,25},{17,1},{25,9},{2,18},{10... | collective-permute-start | bytes 32 | tf_op jit(solution)/shard_map/ppermute | solution.py:32

commit v12 on v8

--- a/solution.py
+++ b/solution.py
@@ -123,17 +123,22 @@
     my_layer = lax.axis_index("gz")
     remote_count = tiles_here // 2
     capacity = max(2, 3 * remote_count // (2 * (lane_count - 1)))
-    entries = src_list.reshape(-1)
+    lane_rows = src_list.reshape(lane_count, tiles_here * sources_per)
+    entries = lax.dynamic_index_in_dim(lane_rows, my_lane, 0, keepdims=False)
     owner_lane = entries // tiles_here % lane_count
     local_tile = entries % tiles_here
     remote = owner_lane != my_lane
     slot_index = bucket_ranks(owner_lane, remote, lane_count)
-    match = (
-        remote[None, None, :]
-        & (owner_lane[None, None, :] == jnp.arange(lane_count, dtype=jnp.int32)[:, None, None])
-        & (slot_index[None, None, :] == jnp.arange(capacity, dtype=jnp.int32)[None, :, None])
-    )
-    requests = jnp.sum(jnp.where(match, local_tile[None, None, :], 0), axis=-1, dtype=jnp.int32)
+    reader_owner = lane_rows // tiles_here % lane_count
+    reader_tile = lane_rows % tiles_here
+    reader_remote = reader_owner != jnp.arange(lane_count, dtype=jnp.int32)[:, None]
+    reader_slot = bucket_ranks(reader_owner, reader_remote, lane_count)
+    hit = (
+        reader_remote[:, None, :]
+        & (reader_owner[:, None, :] == my_lane)
+        & (reader_slot[:, None, :] == jnp.arange(capacity, dtype=jnp.int32)[None, :, None])
+    )
+    wanted = jnp.sum(jnp.where(hit, reader_tile[:, None, :], 0), axis=-1, dtype=jnp.int32)
     pool_index = jnp.where(
         remote, tiles_here + owner_lane * capacity + slot_index, local_tile
     ).reshape(tiles_here, sources_per)
@@ -156,7 +161,6 @@
     block_lower = jnp.where(level_index == 0, 0.0, lower_band)
     block_upper = jnp.where(level_index == levels - 1, 0.0, upper_band)
     fields = jnp.stack([concentration, turbulence], axis=1)
-    wanted = lax.all_to_all(requests, "gy", split_axis=0, concat_axis=0, tiled=True)
 
     def exchange(tiles):
         sent = lax.all_to_all(tiles[wanted], "gy", split_axis=0, concat_axis=0, tiled=True)
@@ -224,7 +228,7 @@
         in_specs=(
             P(("gx", "gy"), None, "gz"),
             P(("gx", "gy"), None, "gz"),
-            P(("gx", "gy"), None),
+            P("gx", None),
             P(("gx", "gy"), None, None, None),
             P(("gx", "gy"), "gz"),
             P(),

time: 169 us -> 167 us (0.988)
  blocking collectives: 0 us -> 13.7 us
  starting transfers between devices: 33.8 us -> 26 us
  waiting for transfers between devices: 42.9 us -> 38 us
    unnamed x0 -> x1, blocking collectives: none -> 13.7 us
    all_to_all x1 -> x0, starting transfers between devices: 6.32 us -> none  [per_device(): lax.all_to_all(requests, 'gy', split_axis=0, concat_axis=0, tiled=True)]
    all_to_all x3, waiting for transfers between devices: 19 us -> 14 us  [exchange(): lax.all_to_all(tiles[wanted], 'gy', split_axis=0, concat_axis=0, tiled=True)]
    unnamed x28 -> x30, local copies, waits for them, and re-layouts: 8.16 us -> 6.84 us
  transfers between devices with their start and end apart: 18 -> 17, of which waited for: 14 -> 14; matrix products, arithmetic and copies ran while one was open for 19% -> 19% of each run, Pallas kernels for 4% -> 4%
where the time goes in v12:
time: 167 us
  local copies, waits for them, and re-layouts  41.2 us (25%)
  waiting for transfers between devices  38 us (23%)
  starting transfers between devices  26 us (16%)
  other arithmetic  23.7 us (14%)
  matrix products  14.3 us (9%)
  blocking collectives  13.7 us (8%)
  Pallas kernels  5.94 us (4%)
  between operations  3.83 us (2%)
    ppermute x10, waiting for transfers between devices, butterfly_sum(): lax.ppermute(value, axis, [(i, i ^ bit) for i in range(devices)])  22.5 us
    gather x8, local copies, waits for them, and re-layouts, per_device(): tile_pool[pool_index[:, entry_k]]  17.8 us
    all_to_all x3, waiting for transfers between devices, exchange(): lax.all_to_all(tiles[wanted], 'gy', split_axis=0, concat_axis=0, tiled=True)  14 us
    unnamed x1, blocking collectives  13.7 us
    ppermute x10, starting transfers between devices, butterfly_sum(): lax.ppermute(value, axis, [(i, i ^ bit) for i in range(devices)])  12.7 us
    all_to_all x3, starting transfers between devices, exchange(): lax.all_to_all(tiles[wanted], 'gy', split_axis=0, concat_axis=0, tiled=True)  11.4 us
    dot_general x8, matrix products, per_device(): jnp.einsum('tcd,tfdz->tfcz', interp_weights[:, entry_k], tile_pool[pool_i...  6.92 us
    unnamed x30, local copies, waits for them, and re-layouts  6.84 us
  transfers between devices with their start and end apart: 17, of which 14 were waited for; matrix products, arithmetic and copies ran while one was open for 19% of the time, Pallas kernels for 4%

profile of v12, /device:TPU:0, one launch (start us, length us, event | category | flops | bytes accessed | tf_op | source)
XLA Modules:
  0.0 166.6 jit_solution(8465595057870538694)
XLA Ops:
  1.3 1.3 collective-permute-start.5
  2.6 13.7 %all-gather.1 = s32[4,16,4]{1,2,0:T(4,128)S(1)} all-gather(s32[1,16,4]{1,2,0:T(4,128)} %bitcast.173), channel_id=3, replica_groups=[8,4]<=[4,4,2]T(0,2,1), dimensions={0}, use_global_device_ids=true | all-gather | bytes 1280 | tf_op args[2]
  17.3 1.3 pad_maximum_fusion.1
  18.7 0.7 gather_fusion
  19.5 1.1 copy.134
  20.6 3.5 %all-to-all-start = ((bf16[4,4,2,128,128]{4,3,1,2,0:T(8,128)(2,1)}), bf16[4,4,2,128,128]{4,3,1,2,0:T(8,128)(2,1)S(1)}, u32[]{:S(2)}, u32[]{:S(2)}) async-start(bf16[4,4,2,128,128]{4,3,1,2,0:T(8,128)(2,1)} %copy.134), calls=%async_computation | async-start | bytes 2097152 | tf_op jit(solution)/shard_map/all_to_all | solution.py:166
  24.1 0.9 convert_reduce_fusion.1
  28.0 1.9 %broadcast_in_dim.68.diagonal_ref = f32[128,32,128]{2,1,0:T(8,128)} broadcast(f32[128,32]{1,0:T(8,128)S(1)} %bitcast.156), dimensions={0,1} | broadcast | bytes 2113536 | tf_op jit(solution)/shard_map/broadcast_in_dim | solution.py:87
  29.9 1.9 %broadcast_in_dim.66.lower_ref = f32[128,32,128]{2,1,0:T(8,128)} broadcast(f32[128,32]{1,0:T(8,128)S(1)} %bitcast.155), dimensions={0,1} | broadcast | bytes 2113536 | tf_op jit(solution)/shard_map/broadcast_in_dim | solution.py:87
  31.8 1.9 %broadcast_in_dim.72.upper_ref = f32[128,32,128]{2,1,0:T(8,128)} broadcast(f32[128,32]{1,0:T(8,128)S(1)} %copy.151), dimensions={0,1} | broadcast | bytes 2113536 | tf_op jit(solution)/shard_map/broadcast_in_dim | solution.py:87
  33.8 5.9 %shard_map.94 = f32[128,32,128]{2,1,0:T(8,128)} custom-call(f32[128,32,128]{2,1,0:T(8,128)} %broadcast_in_dim.66.lower_ref, f32[128,32,128]{2,1,0:T(8,128)} %broadcast_in_dim.68.diagonal_ref, f32[128,32,128]{2,1,0:T(8,128)} %broadcast_in_dim.72.upper_ref), custom_call_target="tpu_custom_call" | custom-call | flops 8388608 | bytes 33554432 | tf_op jit(solution)/shard_map/pallas_call | solution.py:94
  39.8 2.3 %fusion = f32[32,128]{0,1:T(8,128)S(1)} fusion(f32[128,32,128]{2,1,0:T(8,128)} %shard_map.94, pred[128]{0:T(512)(128)(4,1)S(1)} %iota_compare_fusion.10), kind=kLoop, calls=%fused_computation.14 | loop fusion | flops 1044480 | bytes 2113664 | tf_op jit(solution)/shard_map/reduce_sum | solution.py:174
  42.4 1.1 collective-permute-done.7
  43.8 5.0 %all-to-all-done = bf16[4,4,2,128,128]{4,3,1,2,0:T(8,128)(2,1)S(1)} async-done(((bf16[4,4,2,128,128]{4,3,1,2,0:T(8,128)(2,1)}), bf16[4,4,2,128,128]{4,3,1,2,0:T(8,128)(2,1)S(1)}, u32[]{:S(2)}, u32[]{:S(2)}) %all-to-all-start) | async-done | bytes 1048608 | tf_op jit(solution)/shard_map/all_to_all | solution.py:166
  49.1 0.7 gather_fusion.4
  49.8 1.7 gather_fusion.3
  51.5 1.7 gather_fusion.2
  53.2 1.7 gather_fusion.1
  54.8 2.0 %fusion.16 = f32[16,2,128,128]{3,2,1,0:T(8,128)S(1)} fusion(bf16[16,2,128,128]{3,2,1,0:T(8,128)(2,1)} %gather_fusion.3, bf16[16,4,128,128]{3,2,1,0:T(8,128)(2,1)} %param.10), kind=kOutput, calls=%fused_computation.47 | convolution fusion | flops 134217728 | bytes 3670016 | tf_op jit(solution)/shard_map/tcd,tfdz->tfcz/dot_general | solution.py:187
  57.6 0.7 copy-done.7
  59.5 1.0 copy-done.1
  60.4 3.3 %fusion.3 = f32[16,2,128,128]{2,3,1,0:T(8,128)S(1)} fusion(f32[16,2,128,128]{3,2,1,0:T(8,128)S(1)} %add_add_fusion.1, f32[16,2,128,128]{3,1,0,2:T(2,128)S(1)} %bitcast.143), kind=kOutput, calls=%fused_computation.21 | convolution fusion | flops 805306368 | bytes 6291456 | tf_op jit(solution)/shard_map/tfzy,tfcy->tfcz/dot_general | solution.py:198
  63.9 0.9 slice_reduce_fusion.1
  65.2 0.7 multiply_subtract_fusion.1
  65.9 1.3 copy-done.4
  67.3 1.4 gather_fusion.6
  68.7 3.7 %all-to-all-start.2 = ((bf16[4,4,128,128]{2,3,1,0:T(8,128)(2,1)}), bf16[4,4,128,128]{2,3,1,0:T(8,128)(2,1)S(1)}, u32[]{:S(2)}, u32[]{:S(2)}) async-start(bf16[4,4,128,128]{2,3,1,0:T(8,128)(2,1)} %bitcast.54), calls=%async_computation.2 | async-start | bytes 1048576 | tf_op jit(solution)/shard_map/all_to_all | solution.py:166
  72.4 1.4 pad_maximum_fusion.3
  74.0 0.9 collective-permute-done
  74.9 1.4 fusion.80
  76.3 2.0 %collective-permute-start.1 = (f32[2]{0:T(128)S(1)}, f32[2]{0:T(128)S(1)}, u32[]{:S(2)}, u32[]{:S(2)}) collective-permute-start(f32[2]{0:T(128)S(1)} %fusion.80), channel_id=1, source_target_pairs={{0,2},{2,0},{4,6},{6,4},{1,3},{3,1},{5,7},{7,5},{8,10},{10,8},{12,... | collective-permute-start | bytes 32 | tf_op jit(solution)/shard_map/ppermute | solution.py:32
  78.2 3.5 %collective-permute-done.1 = f32[2]{0:T(128)S(1)} collective-permute-done((f32[2]{0:T(128)S(1)}, f32[2]{0:T(128)S(1)}, u32[]{:S(2)}, u32[]{:S(2)}) %collective-permute-start.1) | collective-permute-done | bytes 40 | tf_op jit(solution)/shard_map/ppermute | solution.py:32
  81.7 1.4 fusion.82
  83.1 4.5 %collective-permute-start.2 = (f32[2]{0:T(128)S(1)}, f32[2]{0:T(128)S(1)}, u32[]{:S(2)}, u32[]{:S(2)}) collective-permute-start(f32[2]{0:T(128)S(1)} %fusion.82), channel_id=1, source_target_pairs={{0,4},{2,6},{4,0},{6,2},{1,5},{3,7},{5,1},{7,3},{8,12},{10,14},{12... | collective-permute-start | bytes 32 | tf_op jit(solution)/shard_map/ppermute | solution.py:32
  87.6 1.5 collective-permute-done.2
  89.1 1.5 collective-permute-start.3
  90.6 2.0 %collective-permute-done.3 = f32[2]{0:T(128)S(1)} collective-permute-done((f32[2]{0:T(128)S(1)}, f32[2]{0:T(128)S(1)}, u32[]{:S(2)}, u32[]{:S(2)}) %collective-permute-start.3) | collective-permute-done | bytes 40 | tf_op jit(solution)/shard_map/ppermute | solution.py:32
  92.7 1.5 collective-permute-start.4
  94.2 2.0 %collective-permute-done.4 = f32[2]{0:T(128)S(1)} collective-permute-done((f32[2]{0:T(128)S(1)}, f32[2]{0:T(128)S(1)}, u32[]{:S(2)}, u32[]{:S(2)}) %collective-permute-start.4) | collective-permute-done | bytes 40 | tf_op jit(solution)/shard_map/ppermute | solution.py:32
  98.1 2.1 %convert_reduce_fusion = (f32[]{:T(128)}, bf16[16,1,128,128]{2,3,1,0:T(8,128)(2,1)S(1)}) fusion(f32[16,2,128,128]{2,3,1,0:T(8,128)} %copy-done.4, f32[]{:T(128)} %bitcast.22), kind=kLoop, calls=%fused_computation.39 | loop fusion | flops 1048575 | bytes 1572872 | tf_op jit(solution)/shard_map/reduce_sum | solution.py:195
  100.3 1.4 gather_fusion.5
  101.7 4.2 %all-to-all-start.1 = ((bf16[4,4,128,128]{2,3,1,0:T(8,128)(2,1)}), bf16[4,4,128,128]{2,3,1,0:T(8,128)(2,1)}, u32[]{:S(2)}, u32[]{:S(2)}) async-start(bf16[4,4,128,128]{2,3,1,0:T(8,128)(2,1)} %bitcast.51), calls=%async_computation.1 | async-start | bytes 1048576 | tf_op jit(solution)/shard_map/all_to_all | solution.py:166
  105.9 2.1 %slice.225 = bf16[16,1,128,128]{2,3,1,0:T(8,128)(2,1)} slice(f32[16,2,128,128]{2,3,1,0:T(8,128)} %copy-done.4), slice={[0:16], [1:2], [0:128], [0:128]} | slice | bytes 1048576 | tf_op jit(solution)/shard_map/slice | solution.py:212
  108.0 9.0 %all-to-all-done.1 = bf16[4,4,128,128]{2,3,1,0:T(8,128)(2,1)} async-done(((bf16[4,4,128,128]{2,3,1,0:T(8,128)(2,1)}), bf16[4,4,128,128]{2,3,1,0:T(8,128)(2,1)}, u32[]{:S(2)}, u32[]{:S(2)}) %all-to-all-start.1) | async-done | bytes 524320 | tf_op jit(solution)/shard_map/all_to_all | solution.py:166
  117.0 2.7 %maximum_maximum_fusion = bf16[32,2,128,128]{2,3,1,0:T(8,128)(2,1)} fusion(bf16[16,1,128,128]{2,3,1,0:T(8,128)(2,1)S(1)} %bitcast.152, bf16[16,1,128,128]{2,3,1,0:T(8,128)(2,1)} %bitcast.52, bf16[16,1,128,128]{2,3,1,0:T(8,128)(2,1)} %slice.225, bf16[16,1,128,128]{2,3,1,0:T(8,128)(2,1)S(1)} %get-tuple-element.31), kind=kLoop, calls=%fused_computation.12 | loop fusion | flops 3145728 | bytes 4194304 | tf_op jit(solution)/shard_map/concatenate | solution.py:184
  119.8 2.3 %gather_fusion.10 = bf16[16,2,128,128]{2,3,1,0:T(8,128)(2,1)S(1)} fusion(bf16[32,2,128,128]{2,3,1,0:T(8,128)(2,1)} %maximum_maximum_fusion, s32[1024]{0:T(1024)S(1)} %get-tuple-element.50), kind=kCustom, calls=%fused_computation.10 | custom fusion | bytes 2097216 | tf_op jit(solution)/shard_map/gather | solution.py:190
  122.1 3.3 %gather_fusion.9 = bf16[16,2,128,128]{2,3,1,0:T(8,128)(2,1)} fusion(bf16[32,2,128,128]{2,3,1,0:T(8,128)(2,1)} %maximum_maximum_fusion, s32[1024]{0:T(1024)S(1)} %get-tuple-element.51), kind=kCustom, calls=%fused_computation.9 | custom fusion | bytes 2097216 | tf_op jit(solution)/shard_map/gather | solution.py:190
  125.4 3.3 %gather_fusion.8 = bf16[16,2,128,128]{2,3,1,0:T(8,128)(2,1)} fusion(bf16[32,2,128,128]{2,3,1,0:T(8,128)(2,1)} %maximum_maximum_fusion, s32[1024]{0:T(1024)S(1)} %get-tuple-element.52), kind=kCustom, calls=%fused_computation.8 | custom fusion | bytes 2097216 | tf_op jit(solution)/shard_map/gather | solution.py:190
  128.6 3.2 %gather_fusion.7 = bf16[16,2,128,128]{2,3,1,0:T(8,128)(2,1)} fusion(bf16[32,2,128,128]{2,3,1,0:T(8,128)(2,1)} %maximum_maximum_fusion, s32[1024]{0:T(1024)S(1)} %get-tuple-element.53), kind=kCustom, calls=%fused_computation.7 | custom fusion | bytes 2097216 | tf_op jit(solution)/shard_map/gather | solution.py:190
  131.9 1.9 %fusion.22 = f32[16,2,128,128]{3,2,1,0:T(8,128)S(1)} fusion(bf16[16,2,128,128]{2,3,1,0:T(8,128)(2,1)} %gather_fusion.7, bf16[16,4,128,128]{3,2,1,0:T(8,128)(2,1)} %param.10), kind=kOutput, calls=%fused_computation.53 | convolution fusion | flops 134217728 | bytes 3670016 | tf_op jit(solution)/shard_map/tcd,tfdz->tfcz/dot_general | solution.py:187
  134.6 0.8 copy-done.6
  136.4 3.3 %fusion.1 = f32[16,2,128,128]{2,3,1,0:T(8,128)S(1)} fusion(f32[16,2,128,128]{3,2,1,0:T(8,128)S(1)} %add_add_fusion, f32[16,2,128,128]{3,1,0,2:T(2,128)S(1)} %bitcast.144), kind=kOutput, calls=%fused_computation.19 | convolution fusion | flops 805306368 | bytes 6291456 | tf_op jit(solution)/shard_map/tfzy,tfcy->tfcz/dot_general | solution.py:198
  139.7 0.9 slice_reduce_fusion
  140.6 1.4 pad_maximum_fusion.4
  143.1 1.4 fusion.79
  144.5 3.5 %collective-permute-done.9 = f32[2]{0:T(128)S(1)} collective-permute-done((f32[2]{0:T(128)S(1)}, f32[2]{0:T(128)S(1)}, u32[]{:S(2)}, u32[]{:S(2)}) %collective-permute-start.9) | collective-permute-done | bytes 40 | tf_op jit(solution)/shard_map/ppermute | solution.py:32
  148.0 1.4 fusion.81
  149.4 4.4 %collective-permute-done.10 = f32[2]{0:T(128)S(1)} collective-permute-done((f32[2]{0:T(128)S(1)}, f32[2]{0:T(128)S(1)}, u32[]{:S(2)}, u32[]{:S(2)}) %collective-permute-start.10) | collective-permute-done | bytes 40 | tf_op jit(solution)/shard_map/ppermute | solution.py:32
  153.8 1.5 collective-permute-start.11
  155.3 2.0 %collective-permute-done.11 = f32[2]{0:T(128)S(1)} collective-permute-done((f32[2]{0:T(128)S(1)}, f32[2]{0:T(128)S(1)}, u32[]{:S(2)}, u32[]{:S(2)}) %collective-permute-start.11) | collective-permute-done | bytes 40 | tf_op jit(solution)/shard_map/ppermute | solution.py:32
  157.4 1.5 collective-permute-start.12
  158.9 2.0 %collective-permute-done.12 = f32[2]{0:T(128)S(1)} collective-permute-done((f32[2]{0:T(128)S(1)}, f32[2]{0:T(128)S(1)}, u32[]{:S(2)}, u32[]{:S(2)}) %collective-permute-start.12) | collective-permute-done | bytes 40 | tf_op jit(solution)/shard_map/ppermute | solution.py:32
  164.5 1.0 copy.165
  165.5 1.0 copy.164
  (116 shorter events, 14.0 us)
Async XLA Ops:
  0.6 25.5 %copy-start = (f32[2,8]{1,0:T(2,128)S(1)}, f32[2,8]{1,0:T(2,128)}, u32[]{:S(2)}) copy-start(f32[2,8]{1,0:T(2,128)} %param.12) | copy-start | bytes 196
  1.3 25.1 %collective-permute-start.5 = (s32[16,1]{0,1:T(1,128)S(1)}, s32[16,1]{0,1:T(1,128)S(1)}, u32[]{:S(2)}, u32[]{:S(2)}) collective-permute-start(s32[16,1]{0,1:T(1,128)S(1)} %slice.108), channel_id=1, source_target_pairs={{1,0},{3,2},{5,4},{7,6},{9,8},{11,10},{13,12},{15,14},{17,16},{19,... | collective-permute-start | bytes 200 | tf_op jit(solution)/shard_map/ppermute | solution.py:17
  19.4 4.7 %copy-start.5 = (bf16[16,128,128]{2,1,0:T(8,128)(2,1)S(1)}, bf16[16,128,128]{2,1,0:T(8,128)(2,1)}, u32[]{:S(2)}) copy-start(bf16[16,128,128]{2,1,0:T(8,128)(2,1)} %param.7) | copy-start | bytes 1572868
  19.4 5.6 %copy-start.11 = (s32[16,4]{0,1:T(4,128)S(1)}, s32[16,4]{0,1:T(4,128)}, u32[]{:S(2)}) copy-start(s32[16,4]{0,1:T(4,128)} %param.11) | copy-start | bytes 772
  19.4 7.2 %copy-start.12 = (f32[8]{0:T(128)S(1)}, f32[8]{0:T(128)}, u32[]{:S(2)}) copy-start(f32[8]{0:T(128)} %param.13) | copy-start | bytes 100
  20.6 28.2 %all-to-all-start = ((bf16[4,4,2,128,128]{4,3,1,2,0:T(8,128)(2,1)}), bf16[4,4,2,128,128]{4,3,1,2,0:T(8,128)(2,1)S(1)}, u32[]{:S(2)}, u32[]{:S(2)}) async-start(bf16[4,4,2,128,128]{4,3,1,2,0:T(8,128)(2,1)} %copy.134), calls=%async_computation | async-start | bytes 2097152 | tf_op jit(solution)/shard_map/all_to_all | solution.py:166
  39.8 9.1 %copy-start.10 = (bf16[16,128,128]{2,1,0:T(8,128)(2,1)S(1)}, bf16[16,128,128]{2,1,0:T(8,128)(2,1)}, u32[]{:S(2)}) copy-start(bf16[16,128,128]{2,1,0:T(8,128)(2,1)} %param.8) | copy-start | bytes 1572868
  42.4 1.1 collective-permute-start.7
  54.8 2.1 %copy-start.2 = (bf16[16,4,128,128]{3,2,1,0:T(8,128)(2,1)S(1)}, bf16[16,4,128,128]{3,2,1,0:T(8,128)(2,1)}, u32[]{:S(2)}) copy-start(bf16[16,4,128,128]{3,2,1,0:T(8,128)(2,1)} %param.10) | copy-start | bytes 6291460
  54.8 2.3 %copy-start.9 = (bf16[16,2,128,128]{3,2,1,0:T(8,128)(2,1)S(1)}, bf16[16,2,128,128]{3,2,1,0:T(8,128)(2,1)}, u32[]{:S(2)}) copy-start(bf16[16,2,128,128]{3,2,1,0:T(8,128)(2,1)} %gather_fusion.1) | copy-start | bytes 3145732
  57.1 1.2 copy-start.7
  58.9 1.6 copy-start.1
  63.8 1.2 collective-permute-start.6
  65.9 1.4 copy-start.4
  68.7 32.9 %all-to-all-start.2 = ((bf16[4,4,128,128]{2,3,1,0:T(8,128)(2,1)}), bf16[4,4,128,128]{2,3,1,0:T(8,128)(2,1)S(1)}, u32[]{:S(2)}, u32[]{:S(2)}) async-start(bf16[4,4,128,128]{2,3,1,0:T(8,128)(2,1)} %bitcast.54), calls=%async_computation.2 | async-start | bytes 1048576 | tf_op jit(solution)/shard_map/all_to_all | solution.py:166
  73.8 1.1 collective-permute-start
  76.3 5.5 %collective-permute-start.1 = (f32[2]{0:T(128)S(1)}, f32[2]{0:T(128)S(1)}, u32[]{:S(2)}, u32[]{:S(2)}) collective-permute-start(f32[2]{0:T(128)S(1)} %fusion.80), channel_id=1, source_target_pairs={{0,2},{2,0},{4,6},{6,4},{1,3},{3,1},{5,7},{7,5},{8,10},{10,8},{12,... | collective-permute-start | bytes 32 | tf_op jit(solution)/shard_map/ppermute | solution.py:32
  83.1 6.0 %collective-permute-start.2 = (f32[2]{0:T(128)S(1)}, f32[2]{0:T(128)S(1)}, u32[]{:S(2)}, u32[]{:S(2)}) collective-permute-start(f32[2]{0:T(128)S(1)} %fusion.82), channel_id=1, source_target_pairs={{0,4},{2,6},{4,0},{6,2},{1,5},{3,7},{5,1},{7,3},{8,12},{10,14},{12... | collective-permute-start | bytes 32 | tf_op jit(solution)/shard_map/ppermute | solution.py:32
  89.1 3.5 %collective-permute-start.3 = (f32[2]{0:T(128)S(1)}, f32[2]{0:T(128)S(1)}, u32[]{:S(2)}, u32[]{:S(2)}) collective-permute-start(f32[2]{0:T(128)S(1)} %add.219), channel_id=1, source_target_pairs={{0,8},{8,0},{16,24},{24,16},{1,9},{9,1},{17,25},{25,17},{2,10},{10... | collective-permute-start | bytes 32 | tf_op jit(solution)/shard_map/ppermute | solution.py:32
  92.7 3.5 %collective-permute-start.4 = (f32[2]{0:T(128)S(1)}, f32[2]{0:T(128)S(1)}, u32[]{:S(2)}, u32[]{:S(2)}) collective-permute-start(f32[2]{0:T(128)S(1)} %add.220), channel_id=1, source_target_pairs={{0,16},{8,24},{16,0},{24,8},{1,17},{9,25},{17,1},{25,9},{2,18},{10... | collective-permute-start | bytes 32 | tf_op jit(solution)/shard_map/ppermute | solution.py:32
  101.7 15.3 %all-to-all-start.1 = ((bf16[4,4,128,128]{2,3,1,0:T(8,128)(2,1)}), bf16[4,4,128,128]{2,3,1,0:T(8,128)(2,1)}, u32[]{:S(2)}, u32[]{:S(2)}) async-start(bf16[4,4,128,128]{2,3,1,0:T(8,128)(2,1)} %bitcast.51), calls=%async_computation.1 | async-start | bytes 1048576 | tf_op jit(solution)/shard_map/all_to_all | solution.py:166
  131.9 2.1 %copy-start.3 = (bf16[16,4,128,128]{3,2,1,0:T(8,128)(2,1)S(1)}, bf16[16,4,128,128]{3,2,1,0:T(8,128)(2,1)}, u32[]{:S(2)}) copy-start(bf16[16,4,128,128]{3,2,1,0:T(8,128)(2,1)} %param.10) | copy-start | bytes 6291460
  131.9 2.3 %copy-start.8 = (bf16[16,2,128,128]{2,3,1,0:T(8,128)(2,1)S(1)}, bf16[16,2,128,128]{2,3,1,0:T(8,128)(2,1)}, u32[]{:S(2)}) copy-start(bf16[16,2,128,128]{2,3,1,0:T(8,128)(2,1)} %gather_fusion.8) | copy-start | bytes 3145732
  134.2 1.2 copy-start.6
  142.0 1.1 collective-permute-start.8
  142.0 21.4 %collective-permute-start.13 = (f32[16,2,128]{2,1,0:T(2,128)S(1)}, f32[16,2,128]{2,1,0:T(2,128)S(1)}, u32[]{:S(2)}, u32[]{:S(2)}) collective-permute-start(f32[16,2,128]{2,1,0:T(2,128)S(1)} %select_bitcast_fusion), channel_id=1, source_target_pairs={{0,1},{1,0},{2,3},{3,2},{4,5},{5,4},{6,7},{7,6},{8,9},{9,8},{10,11... | collective-permute-start | bytes 49160 | tf_op jit(solution)/shard_map/ppermute | solution.py:21
  144.5 3.5 %collective-permute-start.9 = (f32[2]{0:T(128)S(1)}, f32[2]{0:T(128)S(1)}, u32[]{:S(2)}, u32[]{:S(2)}) collective-permute-start(f32[2]{0:T(128)S(1)} %fusion.79), channel_id=1, source_target_pairs={{0,2},{2,0},{4,6},{6,4},{1,3},{3,1},{5,7},{7,5},{8,10},{10,8},{12,... | collective-permute-start | bytes 32 | tf_op jit(solution)/shard_map/ppermute | solution.py:32
  149.4 4.4 %collective-permute-start.10 = (f32[2]{0:T(128)S(1)}, f32[2]{0:T(128)S(1)}, u32[]{:S(2)}, u32[]{:S(2)}) collective-permute-start(f32[2]{0:T(128)S(1)} %fusion.81), channel_id=1, source_target_pairs={{0,4},{2,6},{4,0},{6,2},{1,5},{3,7},{5,1},{7,3},{8,12},{10,14},{12... | collective-permute-start | bytes 32 | tf_op jit(solution)/shard_map/ppermute | solution.py:32
  153.8 3.5 %collective-permute-start.11 = (f32[2]{0:T(128)S(1)}, f32[2]{0:T(128)S(1)}, u32[]{:S(2)}, u32[]{:S(2)}) collective-permute-start(f32[2]{0:T(128)S(1)} %add.237), channel_id=1, source_target_pairs={{0,8},{8,0},{16,24},{24,16},{1,9},{9,1},{17,25},{25,17},{2,10},{10... | collective-permute-start | bytes 32 | tf_op jit(solution)/shard_map/ppermute | solution.py:32
  157.4 3.5 %collective-permute-start.12 = (f32[2]{0:T(128)S(1)}, f32[2]{0:T(128)S(1)}, u32[]{:S(2)}, u32[]{:S(2)}) collective-permute-start(f32[2]{0:T(128)S(1)} %add.238), channel_id=1, source_target_pairs={{0,16},{8,24},{16,0},{24,8},{1,17},{9,25},{17,1},{25,9},{2,18},{10... | collective-permute-start | bytes 32 | tf_op jit(solution)/shard_map/ppermute | solution.py:32

commit v13 on v12

--- a/solution.py
+++ b/solution.py
@@ -123,7 +123,12 @@
     my_layer = lax.axis_index("gz")
     remote_count = tiles_here // 2
     capacity = max(2, 3 * remote_count // (2 * (lane_count - 1)))
-    lane_rows = src_list.reshape(lane_count, tiles_here * sources_per)
+    own_rows = src_list.reshape(-1)
+    by_hop = [own_rows] + [
+        lax.ppermute(own_rows, "gy", [(i, (i + hop) % lane_count) for i in range(lane_count)])
+        for hop in range(1, lane_count)
+    ]
+    lane_rows = jnp.stack(by_hop)[(my_lane - jnp.arange(lane_count)) % lane_count]
     entries = lax.dynamic_index_in_dim(lane_rows, my_lane, 0, keepdims=False)
     owner_lane = entries // tiles_here % lane_count
     local_tile = entries % tiles_here
@@ -228,7 +233,7 @@
         in_specs=(
             P(("gx", "gy"), None, "gz"),
             P(("gx", "gy"), None, "gz"),
-            P("gx", None),
+            P(("gx", "gy"), None),
             P(("gx", "gy"), None, None, None),
             P(("gx", "gy"), "gz"),
             P(),

time: 167 us -> 169 us (1.012)
  blocking collectives: 13.7 us -> 0 us
  starting transfers between devices: 26 us -> 33.5 us
  waiting for transfers between devices: 38 us -> 42.7 us
  local copies, waits for them, and re-layouts: 41.2 us -> 43.1 us
    unnamed x1 -> x0, blocking collectives: 13.7 us -> none
    ppermute x0 -> x3, starting transfers between devices: none -> 6.11 us  [per_device(): lax.ppermute(own_rows, 'gy', [(i, (i + hop) % lane_count) for i in range(...]
    all_to_all x3, waiting for transfers between devices: 14 us -> 19.3 us  [exchange(): lax.all_to_all(tiles[wanted], 'gy', split_axis=0, concat_axis=0, tiled=True)]
    unnamed x30 -> x28, local copies, waits for them, and re-layouts: 6.84 us -> 8.17 us
  transfers between devices with their start and end apart: 17 -> 20, of which waited for: 14 -> 14; matrix products, arithmetic and copies ran while one was open for 19% -> 19% of each run, Pallas kernels for 4% -> 4%
where the time goes in v13:
time: 169 us; the launch traced here: 168 us
  local copies, waits for them, and re-layouts  43.1 us (26%)
  waiting for transfers between devices  42.7 us (25%)
  starting transfers between devices  33.5 us (20%)
  other arithmetic  24.7 us (15%)
  matrix products  14.3 us (8%)
  Pallas kernels  5.94 us (4%)
  between operations  3.84 us (2%)
    ppermute x10, waiting for transfers between devices, butterfly_sum(): lax.ppermute(value, axis, [(i, i ^ bit) for i in range(devices)])  22.5 us
    all_to_all x3, waiting for transfers between devices, exchange(): lax.all_to_all(tiles[wanted], 'gy', split_axis=0, concat_axis=0, tiled=True)  19.3 us
    gather x8, local copies, waits for them, and re-layouts, per_device(): tile_pool[pool_index[:, entry_k]]  17.8 us
    ppermute x10, starting transfers between devices, butterfly_sum(): lax.ppermute(value, axis, [(i, i ^ bit) for i in range(devices)])  12.7 us
    all_to_all x3, starting transfers between devices, exchange(): lax.all_to_all(tiles[wanted], 'gy', split_axis=0, concat_axis=0, tiled=True)  11.9 us
    unnamed x28, local copies, waits for them, and re-layouts  8.17 us
    dot_general x8, matrix products, per_device(): jnp.einsum('tcd,tfdz->tfcz', interp_weights[:, entry_k], tile_pool[pool_i...  6.92 us
    dot_general x2, matrix products, per_device(): jnp.einsum('tfzy,tfcy->tfcz', inverse, advected, precision=HIGHEST, prefe...  6.61 us
  transfers between devices with their start and end apart: 20, of which 14 were waited for; matrix products, arithmetic and copies ran while one was open for 19% of the time, Pallas kernels for 4%

profile of v13, /device:TPU:0, one launch (start us, length us, event | category | flops | bytes accessed | tf_op | source)
XLA Modules:
  0.0 168.1 jit_solution(11697974200517732006)
XLA Ops:
  0.7 0.8 copy.138
  1.5 5.1 %collective-permute-start.2 = (s32[64]{0:T(128)S(1)}, s32[64]{0:T(128)S(1)}, u32[]{:S(2)}, u32[]{:S(2)}) collective-permute-start(s32[64]{0:T(128)S(1)} %reshape.289), channel_id=1, source_target_pairs={{0,6},{2,0},{4,2},{6,4},{1,7},{3,1},{5,3},{7,5},{8,14},{10,8},{12,... | collective-permute-start | bytes 776 | tf_op jit(solution)/shard_map/ppermute | solution.py:128
  6.6 1.0 collective-permute-start
  8.3 1.3 collective-permute-start.8
  9.7 0.8 copy.150
  10.5 1.9 %convert_reduce_fusion.1 = f32[]{:T(128)} fusion(bf16[16,128,128]{2,1,0:T(8,128)(2,1)} %param.7), kind=kLoop, calls=%fused_computation.41 | loop fusion | flops 524287 | bytes 524292 | tf_op jit(solution)/shard_map/reduce_sum | solution.py:200
  12.9 1.3 pad_maximum_fusion.1
  17.4 0.8 gather_fusion.1
  18.1 1.1 copy.140
  19.2 4.1 %all-to-all-start = ((bf16[4,4,2,128,128]{4,3,1,2,0:T(8,128)(2,1)}), bf16[4,4,2,128,128]{4,3,1,2,0:T(8,128)(2,1)S(1)}, u32[]{:S(2)}, u32[]{:S(2)}) async-start(bf16[4,4,2,128,128]{4,3,1,2,0:T(8,128)(2,1)} %copy.140), calls=%async_computation | async-start | bytes 2097152 | tf_op jit(solution)/shard_map/all_to_all | solution.py:171
  23.3 1.9 %broadcast_in_dim.68.diagonal_ref = f32[128,32,128]{2,1,0:T(8,128)} broadcast(f32[128,32]{1,0:T(8,128)S(1)} %bitcast.160), dimensions={0,1} | broadcast | bytes 2113536 | tf_op jit(solution)/shard_map/broadcast_in_dim | solution.py:87
  25.3 1.9 %broadcast_in_dim.66.lower_ref = f32[128,32,128]{2,1,0:T(8,128)} broadcast(f32[128,32]{1,0:T(8,128)S(1)} %bitcast.159), dimensions={0,1} | broadcast | bytes 2113536 | tf_op jit(solution)/shard_map/broadcast_in_dim | solution.py:87
  27.2 1.9 %broadcast_in_dim.72.upper_ref = f32[128,32,128]{2,1,0:T(8,128)} broadcast(f32[128,32]{1,0:T(8,128)S(1)} %copy.157), dimensions={0,1} | broadcast | bytes 2113536 | tf_op jit(solution)/shard_map/broadcast_in_dim | solution.py:87
  29.6 5.9 %shard_map.94 = f32[128,32,128]{2,1,0:T(8,128)} custom-call(f32[128,32,128]{2,1,0:T(8,128)} %broadcast_in_dim.66.lower_ref, f32[128,32,128]{2,1,0:T(8,128)} %broadcast_in_dim.68.diagonal_ref, f32[128,32,128]{2,1,0:T(8,128)} %broadcast_in_dim.72.upper_ref), custom_call_target="tpu_custom_call" | custom-call | flops 8388608 | bytes 33554432 | tf_op jit(solution)/shard_map/pallas_call | solution.py:94
  35.5 2.3 %fusion = f32[32,128]{0,1:T(8,128)S(1)} fusion(f32[128,32,128]{2,1,0:T(8,128)} %shard_map.94, pred[128]{0:T(512)(128)(4,1)S(1)} %iota_compare_fusion.10), kind=kLoop, calls=%fused_computation.15 | loop fusion | flops 1044480 | bytes 2113664 | tf_op jit(solution)/shard_map/reduce_sum | solution.py:179
  38.2 0.8 collective-permute-start.10
  40.1 10.3 %all-to-all-done = bf16[4,4,2,128,128]{4,3,1,2,0:T(8,128)(2,1)S(1)} async-done(((bf16[4,4,2,128,128]{4,3,1,2,0:T(8,128)(2,1)}), bf16[4,4,2,128,128]{4,3,1,2,0:T(8,128)(2,1)S(1)}, u32[]{:S(2)}, u32[]{:S(2)}) %all-to-all-start) | async-done | bytes 1048608 | tf_op jit(solution)/shard_map/all_to_all | solution.py:171
  51.4 1.7 gather_fusion.4
  53.1 1.7 gather_fusion.3
  54.7 1.6 gather_fusion.2
  56.4 2.0 %fusion.16 = f32[16,2,128,128]{3,2,1,0:T(8,128)S(1)} fusion(bf16[16,2,128,128]{3,2,1,0:T(8,128)(2,1)} %gather_fusion.4, bf16[16,4,128,128]{3,2,1,0:T(8,128)(2,1)} %param.10), kind=kOutput, calls=%fused_computation.48 | convolution fusion | flops 134217728 | bytes 3670016 | tf_op jit(solution)/shard_map/tcd,tfdz->tfcz/dot_general | solution.py:192
  61.0 1.0 copy-done.1
  62.0 3.3 %fusion.3 = f32[16,2,128,128]{2,3,1,0:T(8,128)S(1)} fusion(f32[16,2,128,128]{3,2,1,0:T(8,128)S(1)} %add_add_fusion.1, f32[16,2,128,128]{3,1,0,2:T(2,128)S(1)} %bitcast.147), kind=kOutput, calls=%fused_computation.22 | convolution fusion | flops 805306368 | bytes 6291456 | tf_op jit(solution)/shard_map/tfzy,tfcy->tfcz/dot_general | solution.py:203
  65.4 0.9 slice_reduce_fusion.1
  67.5 1.3 copy-done.4
  68.9 1.4 gather_fusion.7
  70.3 3.5 %all-to-all-start.2 = ((bf16[4,4,128,128]{2,3,1,0:T(8,128)(2,1)}), bf16[4,4,128,128]{2,3,1,0:T(8,128)(2,1)S(1)}, u32[]{:S(2)}, u32[]{:S(2)}) async-start(bf16[4,4,128,128]{2,3,1,0:T(8,128)(2,1)} %bitcast.57), calls=%async_computation.2 | async-start | bytes 1048576 | tf_op jit(solution)/shard_map/all_to_all | solution.py:171
  73.8 1.4 pad_maximum_fusion.3
  75.3 0.9 collective-permute-done.3
  76.3 1.4 fusion.82
  77.6 2.0 %collective-permute-start.4 = (f32[2]{0:T(128)S(1)}, f32[2]{0:T(128)S(1)}, u32[]{:S(2)}, u32[]{:S(2)}) collective-permute-start(f32[2]{0:T(128)S(1)} %fusion.82), channel_id=1, source_target_pairs={{0,2},{2,0},{4,6},{6,4},{1,3},{3,1},{5,7},{7,5},{8,10},{10,8},{12,... | collective-permute-start | bytes 32 | tf_op jit(solution)/shard_map/ppermute | solution.py:32
  79.6 3.5 %collective-permute-done.4 = f32[2]{0:T(128)S(1)} collective-permute-done((f32[2]{0:T(128)S(1)}, f32[2]{0:T(128)S(1)}, u32[]{:S(2)}, u32[]{:S(2)}) %collective-permute-start.4) | collective-permute-done | bytes 40 | tf_op jit(solution)/shard_map/ppermute | solution.py:32
  83.1 1.4 fusion.84
  84.5 4.5 %collective-permute-start.5 = (f32[2]{0:T(128)S(1)}, f32[2]{0:T(128)S(1)}, u32[]{:S(2)}, u32[]{:S(2)}) collective-permute-start(f32[2]{0:T(128)S(1)} %fusion.84), channel_id=1, source_target_pairs={{0,4},{2,6},{4,0},{6,2},{1,5},{3,7},{5,1},{7,3},{8,12},{10,14},{12... | collective-permute-start | bytes 32 | tf_op jit(solution)/shard_map/ppermute | solution.py:32
  89.0 1.5 collective-permute-done.5
  90.5 1.5 collective-permute-start.6
  92.0 2.1 %collective-permute-done.6 = f32[2]{0:T(128)S(1)} collective-permute-done((f32[2]{0:T(128)S(1)}, f32[2]{0:T(128)S(1)}, u32[]{:S(2)}, u32[]{:S(2)}) %collective-permute-start.6) | collective-permute-done | bytes 40 | tf_op jit(solution)/shard_map/ppermute | solution.py:32
  94.0 1.5 collective-permute-start.7
  95.6 2.0 %collective-permute-done.7 = f32[2]{0:T(128)S(1)} collective-permute-done((f32[2]{0:T(128)S(1)}, f32[2]{0:T(128)S(1)}, u32[]{:S(2)}, u32[]{:S(2)}) %collective-permute-start.7) | collective-permute-done | bytes 40 | tf_op jit(solution)/shard_map/ppermute | solution.py:32
  99.5 2.1 %convert_reduce_fusion = (f32[]{:T(128)}, bf16[16,1,128,128]{2,3,1,0:T(8,128)(2,1)S(1)}) fusion(f32[16,2,128,128]{2,3,1,0:T(8,128)} %copy-done.4, f32[]{:T(128)} %bitcast.25), kind=kLoop, calls=%fused_computation.40 | loop fusion | flops 1048575 | bytes 1572872 | tf_op jit(solution)/shard_map/reduce_sum | solution.py:200
  101.6 1.4 gather_fusion.6
  103.0 4.4 %all-to-all-start.1 = ((bf16[4,4,128,128]{2,3,1,0:T(8,128)(2,1)}), bf16[4,4,128,128]{2,3,1,0:T(8,128)(2,1)}, u32[]{:S(2)}, u32[]{:S(2)}) async-start(bf16[4,4,128,128]{2,3,1,0:T(8,128)(2,1)} %bitcast.54), calls=%async_computation.1 | async-start | bytes 1048576 | tf_op jit(solution)/shard_map/all_to_all | solution.py:171
  107.4 2.1 %slice.227 = bf16[16,1,128,128]{2,3,1,0:T(8,128)(2,1)} slice(f32[16,2,128,128]{2,3,1,0:T(8,128)} %copy-done.4), slice={[0:16], [1:2], [0:128], [0:128]} | slice | bytes 1048576 | tf_op jit(solution)/shard_map/slice | solution.py:217
  109.5 9.1 %all-to-all-done.1 = bf16[4,4,128,128]{2,3,1,0:T(8,128)(2,1)} async-done(((bf16[4,4,128,128]{2,3,1,0:T(8,128)(2,1)}), bf16[4,4,128,128]{2,3,1,0:T(8,128)(2,1)}, u32[]{:S(2)}, u32[]{:S(2)}) %all-to-all-start.1) | async-done | bytes 524320 | tf_op jit(solution)/shard_map/all_to_all | solution.py:171
  118.6 2.7 %maximum_maximum_fusion = bf16[32,2,128,128]{2,3,1,0:T(8,128)(2,1)} fusion(bf16[16,1,128,128]{2,3,1,0:T(8,128)(2,1)S(1)} %bitcast.156, bf16[16,1,128,128]{2,3,1,0:T(8,128)(2,1)} %bitcast.55, bf16[16,1,128,128]{2,3,1,0:T(8,128)(2,1)} %slice.227, bf16[16,1,128,128]{2,3,1,0:T(8,128)(2,1)S(1)} %get-tuple-element.31), kind=kLoop, calls=%fused_computation.13 | loop fusion | flops 3145728 | bytes 4194304 | tf_op jit(solution)/shard_map/concatenate | solution.py:189
  121.3 2.3 %gather_fusion.11 = bf16[16,2,128,128]{2,3,1,0:T(8,128)(2,1)S(1)} fusion(bf16[32,2,128,128]{2,3,1,0:T(8,128)(2,1)} %maximum_maximum_fusion, s32[1024]{0:T(1024)S(1)} %get-tuple-element.50), kind=kCustom, calls=%fused_computation.11 | custom fusion | bytes 2097216 | tf_op jit(solution)/shard_map/gather | solution.py:195
  123.7 3.3 %gather_fusion.10 = bf16[16,2,128,128]{2,3,1,0:T(8,128)(2,1)} fusion(bf16[32,2,128,128]{2,3,1,0:T(8,128)(2,1)} %maximum_maximum_fusion, s32[1024]{0:T(1024)S(1)} %get-tuple-element.51), kind=kCustom, calls=%fused_computation.10 | custom fusion | bytes 2097216 | tf_op jit(solution)/shard_map/gather | solution.py:195
  127.0 3.2 %gather_fusion.9 = bf16[16,2,128,128]{2,3,1,0:T(8,128)(2,1)} fusion(bf16[32,2,128,128]{2,3,1,0:T(8,128)(2,1)} %maximum_maximum_fusion, s32[1024]{0:T(1024)S(1)} %get-tuple-element.52), kind=kCustom, calls=%fused_computation.9 | custom fusion | bytes 2097216 | tf_op jit(solution)/shard_map/gather | solution.py:195
  130.2 3.2 %gather_fusion.8 = bf16[16,2,128,128]{2,3,1,0:T(8,128)(2,1)} fusion(bf16[32,2,128,128]{2,3,1,0:T(8,128)(2,1)} %maximum_maximum_fusion, s32[1024]{0:T(1024)S(1)} %get-tuple-element.53), kind=kCustom, calls=%fused_computation.8 | custom fusion | bytes 2097216 | tf_op jit(solution)/shard_map/gather | solution.py:195
  133.4 1.9 %fusion.22 = f32[16,2,128,128]{3,2,1,0:T(8,128)S(1)} fusion(bf16[16,2,128,128]{2,3,1,0:T(8,128)(2,1)} %gather_fusion.8, bf16[16,4,128,128]{3,2,1,0:T(8,128)(2,1)} %param.10), kind=kOutput, calls=%fused_computation.54 | convolution fusion | flops 134217728 | bytes 3670016 | tf_op jit(solution)/shard_map/tcd,tfdz->tfcz/dot_general | solution.py:192
  136.2 0.8 copy-done.6
  138.0 3.3 %fusion.1 = f32[16,2,128,128]{2,3,1,0:T(8,128)S(1)} fusion(f32[16,2,128,128]{3,2,1,0:T(8,128)S(1)} %add_add_fusion, f32[16,2,128,128]{3,1,0,2:T(2,128)S(1)} %bitcast.148), kind=kOutput, calls=%fused_computation.20 | convolution fusion | flops 805306368 | bytes 6291456 | tf_op jit(solution)/shard_map/tfzy,tfcy->tfcz/dot_general | solution.py:203
  141.3 0.9 slice_reduce_fusion
  142.2 1.4 pad_maximum_fusion.4
  144.7 1.4 fusion.81
  146.1 3.5 %collective-permute-done.12 = f32[2]{0:T(128)S(1)} collective-permute-done((f32[2]{0:T(128)S(1)}, f32[2]{0:T(128)S(1)}, u32[]{:S(2)}, u32[]{:S(2)}) %collective-permute-start.12) | collective-permute-done | bytes 40 | tf_op jit(solution)/shard_map/ppermute | solution.py:32
  149.6 1.4 fusion.83
  151.0 4.4 %collective-permute-done.13 = f32[2]{0:T(128)S(1)} collective-permute-done((f32[2]{0:T(128)S(1)}, f32[2]{0:T(128)S(1)}, u32[]{:S(2)}, u32[]{:S(2)}) %collective-permute-start.13) | collective-permute-done | bytes 40 | tf_op jit(solution)/shard_map/ppermute | solution.py:32
  155.4 1.5 collective-permute-start.14
  156.9 2.1 %collective-permute-done.14 = f32[2]{0:T(128)S(1)} collective-permute-done((f32[2]{0:T(128)S(1)}, f32[2]{0:T(128)S(1)}, u32[]{:S(2)}, u32[]{:S(2)}) %collective-permute-start.14) | collective-permute-done | bytes 40 | tf_op jit(solution)/shard_map/ppermute | solution.py:32
  159.0 1.5 collective-permute-start.15
  160.5 2.0 %collective-permute-done.15 = f32[2]{0:T(128)S(1)} collective-permute-done((f32[2]{0:T(128)S(1)}, f32[2]{0:T(128)S(1)}, u32[]{:S(2)}, u32[]{:S(2)}) %collective-permute-start.15) | collective-permute-done | bytes 40 | tf_op jit(solution)/shard_map/ppermute | solution.py:32
  166.1 1.0 copy.171
  167.1 1.0 copy.170
  (124 shorter events, 17.2 us)
Async XLA Ops:
  0.6 12.0 %copy-start = (f32[2,8]{1,0:T(2,128)S(1)}, f32[2,8]{1,0:T(2,128)}, u32[]{:S(2)}) copy-start(f32[2,8]{1,0:T(2,128)} %param.12) | copy-start | bytes 196
  0.6 13.7 %copy-start.11 = (f32[8]{0:T(128)S(1)}, f32[8]{0:T(128)}, u32[]{:S(2)}) copy-start(f32[8]{0:T(128)} %param.13) | copy-start | bytes 100
  1.5 14.2 %collective-permute-start.2 = (s32[64]{0:T(128)S(1)}, s32[64]{0:T(128)S(1)}, u32[]{:S(2)}, u32[]{:S(2)}) collective-permute-start(s32[64]{0:T(128)S(1)} %reshape.289), channel_id=1, source_target_pairs={{0,6},{2,0},{4,2},{6,4},{1,7},{3,1},{5,3},{7,5},{8,14},{10,8},{12,... | collective-permute-start | bytes 776 | tf_op jit(solution)/shard_map/ppermute | solution.py:128
  6.6 9.1 %collective-permute-start.1 = (s32[64]{0:T(128)S(1)}, s32[64]{0:T(128)S(1)}, u32[]{:S(2)}, u32[]{:S(2)}) collective-permute-start(s32[64]{0:T(128)S(1)} %reshape.289), channel_id=1, source_target_pairs={{0,4},{2,6},{4,0},{6,2},{1,5},{3,7},{5,1},{7,3},{8,12},{10,14},{12... | collective-permute-start | bytes 776 | tf_op jit(solution)/shard_map/ppermute | solution.py:128
  6.6 9.1 %collective-permute-start = (s32[64]{0:T(128)S(1)}, s32[64]{0:T(128)S(1)}, u32[]{:S(2)}, u32[]{:S(2)}) collective-permute-start(s32[64]{0:T(128)S(1)} %reshape.289), channel_id=1, source_target_pairs={{0,2},{2,4},{4,6},{6,0},{1,3},{3,5},{5,7},{7,1},{8,10},{10,12},{12... | collective-permute-start | bytes 776 | tf_op jit(solution)/shard_map/ppermute | solution.py:128
  8.3 5.9 %collective-permute-start.8 = (s32[16,1]{0,1:T(1,128)S(1)}, s32[16,1]{0,1:T(1,128)S(1)}, u32[]{:S(2)}, u32[]{:S(2)}) collective-permute-start(s32[16,1]{0,1:T(1,128)S(1)} %slice.108), channel_id=1, source_target_pairs={{1,0},{3,2},{5,4},{7,6},{9,8},{11,10},{13,12},{15,14},{17,16},{19,... | collective-permute-start | bytes 200 | tf_op jit(solution)/shard_map/ppermute | solution.py:17
  19.2 31.1 %all-to-all-start = ((bf16[4,4,2,128,128]{4,3,1,2,0:T(8,128)(2,1)}), bf16[4,4,2,128,128]{4,3,1,2,0:T(8,128)(2,1)S(1)}, u32[]{:S(2)}, u32[]{:S(2)}) async-start(bf16[4,4,2,128,128]{4,3,1,2,0:T(8,128)(2,1)} %copy.140), calls=%async_computation | async-start | bytes 2097152 | tf_op jit(solution)/shard_map/all_to_all | solution.py:171
  35.5 14.9 %copy-start.5 = (bf16[16,128,128]{2,1,0:T(8,128)(2,1)S(1)}, bf16[16,128,128]{2,1,0:T(8,128)(2,1)}, u32[]{:S(2)}) copy-start(bf16[16,128,128]{2,1,0:T(8,128)(2,1)} %param.7) | copy-start | bytes 1572868
  35.5 14.9 %copy-start.10 = (bf16[16,128,128]{2,1,0:T(8,128)(2,1)S(1)}, bf16[16,128,128]{2,1,0:T(8,128)(2,1)}, u32[]{:S(2)}) copy-start(bf16[16,128,128]{2,1,0:T(8,128)(2,1)} %param.8) | copy-start | bytes 1572868
  38.2 1.7 collective-permute-start.10
  56.4 2.1 %copy-start.2 = (bf16[16,4,128,128]{3,2,1,0:T(8,128)(2,1)S(1)}, bf16[16,4,128,128]{3,2,1,0:T(8,128)(2,1)}, u32[]{:S(2)}) copy-start(bf16[16,4,128,128]{3,2,1,0:T(8,128)(2,1)} %param.10) | copy-start | bytes 6291460
  56.4 2.3 %copy-start.9 = (bf16[16,2,128,128]{3,2,1,0:T(8,128)(2,1)S(1)}, bf16[16,2,128,128]{3,2,1,0:T(8,128)(2,1)}, u32[]{:S(2)}) copy-start(bf16[16,2,128,128]{3,2,1,0:T(8,128)(2,1)} %gather_fusion.2) | copy-start | bytes 3145732
  58.7 1.2 copy-start.7
  60.4 1.6 copy-start.1
  65.4 1.2 collective-permute-start.9
  67.4 1.3 copy-start.4
  70.3 32.8 %all-to-all-start.2 = ((bf16[4,4,128,128]{2,3,1,0:T(8,128)(2,1)}), bf16[4,4,128,128]{2,3,1,0:T(8,128)(2,1)S(1)}, u32[]{:S(2)}, u32[]{:S(2)}) async-start(bf16[4,4,128,128]{2,3,1,0:T(8,128)(2,1)} %bitcast.57), calls=%async_computation.2 | async-start | bytes 1048576 | tf_op jit(solution)/shard_map/all_to_all | solution.py:171
  75.1 1.1 collective-permute-start.3
  77.6 5.5 %collective-permute-start.4 = (f32[2]{0:T(128)S(1)}, f32[2]{0:T(128)S(1)}, u32[]{:S(2)}, u32[]{:S(2)}) collective-permute-start(f32[2]{0:T(128)S(1)} %fusion.82), channel_id=1, source_target_pairs={{0,2},{2,0},{4,6},{6,4},{1,3},{3,1},{5,7},{7,5},{8,10},{10,8},{12,... | collective-permute-start | bytes 32 | tf_op jit(solution)/shard_map/ppermute | solution.py:32
  84.5 6.0 %collective-permute-start.5 = (f32[2]{0:T(128)S(1)}, f32[2]{0:T(128)S(1)}, u32[]{:S(2)}, u32[]{:S(2)}) collective-permute-start(f32[2]{0:T(128)S(1)} %fusion.84), channel_id=1, source_target_pairs={{0,4},{2,6},{4,0},{6,2},{1,5},{3,7},{5,1},{7,3},{8,12},{10,14},{12... | collective-permute-start | bytes 32 | tf_op jit(solution)/shard_map/ppermute | solution.py:32
  90.5 3.5 %collective-permute-start.6 = (f32[2]{0:T(128)S(1)}, f32[2]{0:T(128)S(1)}, u32[]{:S(2)}, u32[]{:S(2)}) collective-permute-start(f32[2]{0:T(128)S(1)} %add.244), channel_id=1, source_target_pairs={{0,8},{8,0},{16,24},{24,16},{1,9},{9,1},{17,25},{25,17},{2,10},{10... | collective-permute-start | bytes 32 | tf_op jit(solution)/shard_map/ppermute | solution.py:32
  94.0 3.5 %collective-permute-start.7 = (f32[2]{0:T(128)S(1)}, f32[2]{0:T(128)S(1)}, u32[]{:S(2)}, u32[]{:S(2)}) collective-permute-start(f32[2]{0:T(128)S(1)} %add.245), channel_id=1, source_target_pairs={{0,16},{8,24},{16,0},{24,8},{1,17},{9,25},{17,1},{25,9},{2,18},{10... | collective-permute-start | bytes 32 | tf_op jit(solution)/shard_map/ppermute | solution.py:32
  103.0 15.6 %all-to-all-start.1 = ((bf16[4,4,128,128]{2,3,1,0:T(8,128)(2,1)}), bf16[4,4,128,128]{2,3,1,0:T(8,128)(2,1)}, u32[]{:S(2)}, u32[]{:S(2)}) async-start(bf16[4,4,128,128]{2,3,1,0:T(8,128)(2,1)} %bitcast.54), calls=%async_computation.1 | async-start | bytes 1048576 | tf_op jit(solution)/shard_map/all_to_all | solution.py:171
  133.4 2.1 %copy-start.3 = (bf16[16,4,128,128]{3,2,1,0:T(8,128)(2,1)S(1)}, bf16[16,4,128,128]{3,2,1,0:T(8,128)(2,1)}, u32[]{:S(2)}) copy-start(bf16[16,4,128,128]{3,2,1,0:T(8,128)(2,1)} %param.10) | copy-start | bytes 6291460
  133.4 2.3 %copy-start.8 = (bf16[16,2,128,128]{2,3,1,0:T(8,128)(2,1)S(1)}, bf16[16,2,128,128]{2,3,1,0:T(8,128)(2,1)}, u32[]{:S(2)}) copy-start(bf16[16,2,128,128]{2,3,1,0:T(8,128)(2,1)} %gather_fusion.9) | copy-start | bytes 3145732
  135.8 1.2 copy-start.6
  143.6 1.1 collective-permute-start.11
  143.6 21.4 %collective-permute-start.16 = (f32[16,2,128]{2,1,0:T(2,128)S(1)}, f32[16,2,128]{2,1,0:T(2,128)S(1)}, u32[]{:S(2)}, u32[]{:S(2)}) collective-permute-start(f32[16,2,128]{2,1,0:T(2,128)S(1)} %select_bitcast_fusion), channel_id=1, source_target_pairs={{0,1},{1,0},{2,3},{3,2},{4,5},{5,4},{6,7},{7,6},{8,9},{9,8},{10,11... | collective-permute-start | bytes 49160 | tf_op jit(solution)/shard_map/ppermute | solution.py:21
  146.1 3.5 %collective-permute-start.12 = (f32[2]{0:T(128)S(1)}, f32[2]{0:T(128)S(1)}, u32[]{:S(2)}, u32[]{:S(2)}) collective-permute-start(f32[2]{0:T(128)S(1)} %fusion.81), channel_id=1, source_target_pairs={{0,2},{2,0},{4,6},{6,4},{1,3},{3,1},{5,7},{7,5},{8,10},{10,8},{12,... | collective-permute-start | bytes 32 | tf_op jit(solution)/shard_map/ppermute | solution.py:32
  151.0 4.4 %collective-permute-start.13 = (f32[2]{0:T(128)S(1)}, f32[2]{0:T(128)S(1)}, u32[]{:S(2)}, u32[]{:S(2)}) collective-permute-start(f32[2]{0:T(128)S(1)} %fusion.83), channel_id=1, source_target_pairs={{0,4},{2,6},{4,0},{6,2},{1,5},{3,7},{5,1},{7,3},{8,12},{10,14},{12... | collective-permute-start | bytes 32 | tf_op jit(solution)/shard_map/ppermute | solution.py:32
  155.4 3.5 %collective-permute-start.14 = (f32[2]{0:T(128)S(1)}, f32[2]{0:T(128)S(1)}, u32[]{:S(2)}, u32[]{:S(2)}) collective-permute-start(f32[2]{0:T(128)S(1)} %add.262), channel_id=1, source_target_pairs={{0,8},{8,0},{16,24},{24,16},{1,9},{9,1},{17,25},{25,17},{2,10},{10... | collective-permute-start | bytes 32 | tf_op jit(solution)/shard_map/ppermute | solution.py:32
  159.0 3.5 %collective-permute-start.15 = (f32[2]{0:T(128)S(1)}, f32[2]{0:T(128)S(1)}, u32[]{:S(2)}, u32[]{:S(2)}) collective-permute-start(f32[2]{0:T(128)S(1)} %add.263), channel_id=1, source_target_pairs={{0,16},{8,24},{16,0},{24,8},{1,17},{9,25},{17,1},{25,9},{2,18},{10... | collective-permute-start | bytes 32 | tf_op jit(solution)/shard_map/ppermute | solution.py:32

commit v14 on v12

--- a/solution.py
+++ b/solution.py
@@ -191,10 +191,7 @@
                 preferred_element_type=jnp.float32,
             )
         last = step_index + 1 == STEPS
-        totals = butterfly_sum(
-            jnp.stack([jnp.sum(fields[:, 0], dtype=jnp.float32), jnp.sum(advected[:, 0])]),
-            ("gz", "gy", "gx"),
-        )
+        partial = jnp.stack([jnp.sum(fields[:, 0], dtype=jnp.float32), jnp.sum(advected[:, 0])])
         solved = jnp.einsum(
             "tfzy,tfcy->tfcz",
             inverse,
@@ -203,7 +200,9 @@
             preferred_element_type=jnp.float32,
         )
         edge_value = jnp.where(my_layer == 0, solved[..., -1], solved[..., 0])
-        other_value = from_partner(edge_value, "gz", 0)
+        carried = from_partner(jnp.concatenate([edge_value.reshape(-1), partial]), "gz", 0)
+        other_value = carried[: edge_value.size].reshape(edge_value.shape)
+        totals = butterfly_sum(partial + carried[edge_value.size :], ("gy", "gx"))
         low_value = jnp.where(my_layer == 0, edge_value, other_value)
         high_value = jnp.where(my_layer == 0, other_value, edge_value)
         lower_end, upper_end = interface_values(low_value, low_spike, high_value, high_spike)

time: 167 us -> 172 us (1.030)
  local copies, waits for them, and re-layouts: 41.2 us -> 44.6 us
  waiting for transfers between devices: 38 us -> 35.7 us
  other arithmetic: 23.7 us -> 25.7 us
    ppermute x10 -> x8, waiting for transfers between devices: 22.5 us -> 18.2 us  [butterfly_sum(): lax.ppermute(value, axis, [(i, i ^ bit) for i in range(devices)])]
    concatenate x0 -> x2, local copies, waits for them, and re-layouts: none -> 2.75 us  [per_device(): jnp.concatenate([edge_value.reshape(-1), partial])]
    add x0 -> x2, other arithmetic: none -> 2.74 us  [per_device(): totals = butterfly_sum(partial + carried[edge_value.size:], ('gy', 'gx'))]
    another operation x2 -> x0, other arithmetic: 2.73 us -> none  [per_device(): jnp.stack([jnp.sum(fields[:, 0], dtype=jnp.float32), jnp.sum(advected[:,...]
    add x10 -> x8, other arithmetic: 5.49 us -> 2.75 us  [butterfly_sum(): value + lax.ppermute(value, axis, [(i, i ^ bit) for i in range(devices)])]
    sub x2, other arithmetic: 1.41 us -> 3.87 us  [per_device(): unscaled = solved - spike_column[:, :, None, :] * needed[..., None]]
    select_n x2, other arithmetic: 0.23 us -> 2.28 us  [per_device(): needed = jnp.where(my_layer == 0, upper_end, lower_end)]
    ppermute x10 -> x8, starting transfers between devices: 12.7 us -> 14.3 us  [butterfly_sum(): lax.ppermute(value, axis, [(i, i ^ bit) for i in range(devices)])]
  transfers between devices with their start and end apart: 17 -> 15, of which waited for: 14 -> 11; matrix products, arithmetic and copies ran while one was open for 19% -> 26% of each run, Pallas kernels for 4% -> 3%
where the time goes in v14:
time: 172 us; the launch traced here: 171 us
  local copies, waits for them, and re-layouts  44.6 us (26%)
  waiting for transfers between devices  35.7 us (21%)
  starting transfers between devices  26.9 us (16%)
  other arithmetic  25.7 us (15%)
  matrix products  14.2 us (8%)
  blocking collectives  13.7 us (8%)
  Pallas kernels  5.94 us (3%)
  between operations  3.85 us (2%)
    ppermute x8, waiting for transfers between devices, butterfly_sum(): lax.ppermute(value, axis, [(i, i ^ bit) for i in range(devices)])  18.2 us
    gather x8, local copies, waits for them, and re-layouts, per_device(): tile_pool[pool_index[:, entry_k]]  17.8 us
    all_to_all x3, waiting for transfers between devices, exchange(): lax.all_to_all(tiles[wanted], 'gy', split_axis=0, concat_axis=0, tiled=True)  15.4 us
    ppermute x8, starting transfers between devices, butterfly_sum(): lax.ppermute(value, axis, [(i, i ^ bit) for i in range(devices)])  14.3 us
    unnamed x1, blocking collectives  13.7 us
    all_to_all x3, starting transfers between devices, exchange(): lax.all_to_all(tiles[wanted], 'gy', split_axis=0, concat_axis=0, tiled=True)  11.3 us
    unnamed x34, local copies, waits for them, and re-layouts  7.51 us
    dot_general x8, matrix products, per_device(): jnp.einsum('tcd,tfdz->tfcz', interp_weights[:, entry_k], tile_pool[pool_i...  6.96 us
  transfers between devices with their start and end apart: 15, of which 11 were waited for; matrix products, arithmetic and copies ran while one was open for 26% of the time, Pallas kernels for 3%

profile of v14, /device:TPU:0, one launch (start us, length us, event | category | flops | bytes accessed | tf_op | source)
XLA Modules:
  0.0 170.7 jit_solution(5952539532031751921)
XLA Ops:
  1.3 1.3 collective-permute-start
  2.6 13.7 %all-gather.1 = s32[4,16,4]{1,2,0:T(4,128)S(1)} all-gather(s32[1,16,4]{1,2,0:T(4,128)} %bitcast.176), channel_id=3, replica_groups=[8,4]<=[4,4,2]T(0,2,1), dimensions={0}, use_global_device_ids=true | all-gather | bytes 1280 | tf_op args[2]
  17.3 1.3 pad_maximum_fusion.1
  19.5 1.1 copy.122
  20.6 3.5 %all-to-all-start = ((bf16[4,4,2,128,128]{4,3,1,2,0:T(8,128)(2,1)}), bf16[4,4,2,128,128]{4,3,1,2,0:T(8,128)(2,1)S(1)}, u32[]{:S(2)}, u32[]{:S(2)}) async-start(bf16[4,4,2,128,128]{4,3,1,2,0:T(8,128)(2,1)} %copy.122), calls=%async_computation | async-start | bytes 2097152 | tf_op jit(solution)/shard_map/all_to_all | solution.py:166
  24.1 0.9 convert_reduce_fusion.1
  28.0 1.9 %broadcast_in_dim.68.diagonal_ref = f32[128,32,128]{2,1,0:T(8,128)} broadcast(f32[128,32]{1,0:T(8,128)S(1)} %bitcast.157), dimensions={0,1} | broadcast | bytes 2113536 | tf_op jit(solution)/shard_map/broadcast_in_dim | solution.py:87
  29.9 1.9 %broadcast_in_dim.66.lower_ref = f32[128,32,128]{2,1,0:T(8,128)} broadcast(f32[128,32]{1,0:T(8,128)S(1)} %bitcast.156), dimensions={0,1} | broadcast | bytes 2113536 | tf_op jit(solution)/shard_map/broadcast_in_dim | solution.py:87
  31.8 1.9 %broadcast_in_dim.72.upper_ref = f32[128,32,128]{2,1,0:T(8,128)} broadcast(f32[128,32]{1,0:T(8,128)S(1)} %copy.139), dimensions={0,1} | broadcast | bytes 2113536 | tf_op jit(solution)/shard_map/broadcast_in_dim | solution.py:87
  33.8 5.9 %shard_map.94 = f32[128,32,128]{2,1,0:T(8,128)} custom-call(f32[128,32,128]{2,1,0:T(8,128)} %broadcast_in_dim.66.lower_ref, f32[128,32,128]{2,1,0:T(8,128)} %broadcast_in_dim.68.diagonal_ref, f32[128,32,128]{2,1,0:T(8,128)} %broadcast_in_dim.72.upper_ref), custom_call_target="tpu_custom_call" | custom-call | flops 8388608 | bytes 33554432 | tf_op jit(solution)/shard_map/pallas_call | solution.py:94
  39.8 2.3 %fusion = f32[32,128]{0,1:T(8,128)S(1)} fusion(f32[128,32,128]{2,1,0:T(8,128)} %shard_map.94, pred[128]{0:T(512)(128)(4,1)S(1)} %iota_compare_fusion.10), kind=kLoop, calls=%fused_computation.14 | loop fusion | flops 1044480 | bytes 2113664 | tf_op jit(solution)/shard_map/reduce_sum | solution.py:174
  42.4 6.4 %all-to-all-done = bf16[4,4,2,128,128]{4,3,1,2,0:T(8,128)(2,1)S(1)} async-done(((bf16[4,4,2,128,128]{4,3,1,2,0:T(8,128)(2,1)}), bf16[4,4,2,128,128]{4,3,1,2,0:T(8,128)(2,1)S(1)}, u32[]{:S(2)}, u32[]{:S(2)}) %all-to-all-start) | async-done | bytes 1048608 | tf_op jit(solution)/shard_map/all_to_all | solution.py:166
  49.8 1.7 gather_fusion.3
  51.5 1.7 gather_fusion.2
  53.2 1.7 gather_fusion.1
  54.8 2.0 %fusion.16 = f32[16,2,128,128]{3,2,1,0:T(8,128)S(1)} fusion(bf16[16,2,128,128]{3,2,1,0:T(8,128)(2,1)} %gather_fusion.3, bf16[16,4,128,128]{3,2,1,0:T(8,128)(2,1)} %param.10), kind=kOutput, calls=%fused_computation.47 | convolution fusion | flops 134217728 | bytes 3670016 | tf_op jit(solution)/shard_map/tcd,tfdz->tfcz/dot_general | solution.py:187
  59.5 0.9 slice_reduce_fusion.1
  60.5 3.3 %fusion.3 = f32[16,2,128,128]{2,3,1,0:T(8,128)S(1)} fusion(f32[16,2,128,128]{3,2,1,0:T(8,128)S(1)} %add_add_fusion.1, f32[16,2,128,128]{3,1,0,2:T(2,128)S(1)} %bitcast.144), kind=kOutput, calls=%fused_computation.21 | convolution fusion | flops 805306368 | bytes 6291456 | tf_op jit(solution)/shard_map/tfzy,tfcy->tfcz/dot_general | solution.py:195
  63.7 1.3 copy-done.2
  65.1 1.4 concatenate.42
  66.7 0.9 collective-permute-done.1
  67.7 1.1 broadcast_select_fusion.4
  68.8 1.9 %multiply_subtract_fusion.1 = f32[16,2,128,128]{2,3,1,0:T(8,128)S(1)} fusion(f32[16,2,128,128]{2,3,1,0:T(8,128)} %copy-done.2, f32[16,2,128]{2,1,0:T(2,128)S(1)} %bitcast.166, f32[16,2,128]{2,1,0:T(2,128)S(1)} %broadcast_multiply_fusion), kind=kLoop, calls=%fused_computation.17 | loop fusion | flops 1048576 | bytes 4227072 | tf_op jit(solution)/shard_map/sub | solution.py:210
  70.8 1.3 copy-done.6
  72.2 1.4 gather_fusion.6
  73.6 3.5 %all-to-all-start.2 = ((bf16[4,4,128,128]{2,3,1,0:T(8,128)(2,1)}), bf16[4,4,128,128]{2,3,1,0:T(8,128)(2,1)S(1)}, u32[]{:S(2)}, u32[]{:S(2)}) async-start(bf16[4,4,128,128]{2,3,1,0:T(8,128)(2,1)} %bitcast.56), calls=%async_computation.2 | async-start | bytes 1048576 | tf_op jit(solution)/shard_map/all_to_all | solution.py:166
  77.1 1.4 slice_add_fusion.1
  78.4 2.0 %collective-permute-start.2 = (f32[2]{0:T(128)S(1)}, f32[2]{0:T(128)S(1)}, u32[]{:S(2)}, u32[]{:S(2)}) collective-permute-start(f32[2]{0:T(128)S(1)} %slice_add_fusion.1), channel_id=1, source_target_pairs={{0,2},{2,0},{4,6},{6,4},{1,3},{3,1},{5,7},{7,5},{8,10},{10,8},{12,... | collective-permute-start | bytes 32 | tf_op jit(solution)/shard_map/ppermute | solution.py:32
  80.4 6.0 %collective-permute-done.2 = f32[2]{0:T(128)S(1)} collective-permute-done((f32[2]{0:T(128)S(1)}, f32[2]{0:T(128)S(1)}, u32[]{:S(2)}, u32[]{:S(2)}) %collective-permute-start.2) | collective-permute-done | bytes 40 | tf_op jit(solution)/shard_map/ppermute | solution.py:32
  86.4 1.4 fusion.83
  87.8 4.5 %collective-permute-start.3 = (f32[2]{0:T(128)S(1)}, f32[2]{0:T(128)S(1)}, u32[]{:S(2)}, u32[]{:S(2)}) collective-permute-start(f32[2]{0:T(128)S(1)} %fusion.83), channel_id=1, source_target_pairs={{0,4},{2,6},{4,0},{6,2},{1,5},{3,7},{5,1},{7,3},{8,12},{10,14},{12... | collective-permute-start | bytes 32 | tf_op jit(solution)/shard_map/ppermute | solution.py:32
  92.2 1.5 collective-permute-done.3
  93.8 1.5 collective-permute-start.4
  95.3 2.0 %collective-permute-done.4 = f32[2]{0:T(128)S(1)} collective-permute-done((f32[2]{0:T(128)S(1)}, f32[2]{0:T(128)S(1)}, u32[]{:S(2)}, u32[]{:S(2)}) %collective-permute-start.4) | collective-permute-done | bytes 40 | tf_op jit(solution)/shard_map/ppermute | solution.py:32
  97.3 1.5 collective-permute-start.5
  98.8 2.0 %collective-permute-done.5 = f32[2]{0:T(128)S(1)} collective-permute-done((f32[2]{0:T(128)S(1)}, f32[2]{0:T(128)S(1)}, u32[]{:S(2)}, u32[]{:S(2)}) %collective-permute-start.5) | collective-permute-done | bytes 40 | tf_op jit(solution)/shard_map/ppermute | solution.py:32
  102.8 2.1 %convert_reduce_fusion = (f32[]{:T(128)}, bf16[16,1,128,128]{2,3,1,0:T(8,128)(2,1)S(1)}) fusion(f32[16,2,128,128]{2,3,1,0:T(8,128)} %copy-done.6, f32[]{:T(128)} %bitcast.45), kind=kLoop, calls=%fused_computation.39 | loop fusion | flops 1048575 | bytes 1572872 | tf_op jit(solution)/shard_map/reduce_sum | solution.py:194
  104.9 1.4 gather_fusion.5
  106.3 4.3 %all-to-all-start.1 = ((bf16[4,4,128,128]{2,3,1,0:T(8,128)(2,1)}), bf16[4,4,128,128]{2,3,1,0:T(8,128)(2,1)}, u32[]{:S(2)}, u32[]{:S(2)}) async-start(bf16[4,4,128,128]{2,3,1,0:T(8,128)(2,1)} %bitcast.53), calls=%async_computation.1 | async-start | bytes 1048576 | tf_op jit(solution)/shard_map/all_to_all | solution.py:166
  110.7 2.1 %slice.249 = bf16[16,1,128,128]{2,3,1,0:T(8,128)(2,1)} slice(f32[16,2,128,128]{2,3,1,0:T(8,128)} %copy-done.6), slice={[0:16], [1:2], [0:128], [0:128]} | slice | bytes 1048576 | tf_op jit(solution)/shard_map/slice | solution.py:211
  112.8 9.0 %all-to-all-done.1 = bf16[4,4,128,128]{2,3,1,0:T(8,128)(2,1)} async-done(((bf16[4,4,128,128]{2,3,1,0:T(8,128)(2,1)}), bf16[4,4,128,128]{2,3,1,0:T(8,128)(2,1)}, u32[]{:S(2)}, u32[]{:S(2)}) %all-to-all-start.1) | async-done | bytes 524320 | tf_op jit(solution)/shard_map/all_to_all | solution.py:166
  121.8 2.7 %maximum_maximum_fusion = bf16[32,2,128,128]{2,3,1,0:T(8,128)(2,1)} fusion(bf16[16,1,128,128]{2,3,1,0:T(8,128)(2,1)S(1)} %bitcast.153, bf16[16,1,128,128]{2,3,1,0:T(8,128)(2,1)} %bitcast.54, bf16[16,1,128,128]{2,3,1,0:T(8,128)(2,1)} %slice.249, bf16[16,1,128,128]{2,3,1,0:T(8,128)(2,1)S(1)} %get-tuple-element.31), kind=kLoop, calls=%fused_computation.12 | loop fusion | flops 3145728 | bytes 4194304 | tf_op jit(solution)/shard_map/concatenate | solution.py:184
  124.6 2.3 %gather_fusion.10 = bf16[16,2,128,128]{2,3,1,0:T(8,128)(2,1)S(1)} fusion(bf16[32,2,128,128]{2,3,1,0:T(8,128)(2,1)} %maximum_maximum_fusion, s32[1024]{0:T(1024)S(1)} %get-tuple-element.48), kind=kCustom, calls=%fused_computation.10 | custom fusion | bytes 2097216 | tf_op jit(solution)/shard_map/gather | solution.py:190
  126.9 3.3 %gather_fusion.9 = bf16[16,2,128,128]{2,3,1,0:T(8,128)(2,1)} fusion(bf16[32,2,128,128]{2,3,1,0:T(8,128)(2,1)} %maximum_maximum_fusion, s32[1024]{0:T(1024)S(1)} %get-tuple-element.49), kind=kCustom, calls=%fused_computation.9 | custom fusion | bytes 2097216 | tf_op jit(solution)/shard_map/gather | solution.py:190
  130.2 3.3 %gather_fusion.8 = bf16[16,2,128,128]{2,3,1,0:T(8,128)(2,1)} fusion(bf16[32,2,128,128]{2,3,1,0:T(8,128)(2,1)} %maximum_maximum_fusion, s32[1024]{0:T(1024)S(1)} %get-tuple-element.50), kind=kCustom, calls=%fused_computation.8 | custom fusion | bytes 2097216 | tf_op jit(solution)/shard_map/gather | solution.py:190
  133.4 3.2 %gather_fusion.7 = bf16[16,2,128,128]{2,3,1,0:T(8,128)(2,1)} fusion(bf16[32,2,128,128]{2,3,1,0:T(8,128)(2,1)} %maximum_maximum_fusion, s32[1024]{0:T(1024)S(1)} %get-tuple-element.51), kind=kCustom, calls=%fused_computation.7 | custom fusion | bytes 2097216 | tf_op jit(solution)/shard_map/gather | solution.py:190
  136.7 1.9 %fusion.22 = f32[16,2,128,128]{3,2,1,0:T(8,128)S(1)} fusion(bf16[16,2,128,128]{2,3,1,0:T(8,128)(2,1)} %gather_fusion.7, bf16[16,4,128,128]{3,2,1,0:T(8,128)(2,1)} %param.10), kind=kOutput, calls=%fused_computation.53 | convolution fusion | flops 134217728 | bytes 3670016 | tf_op jit(solution)/shard_map/tcd,tfdz->tfcz/dot_general | solution.py:187
  139.4 0.8 copy-done.8
  141.2 3.3 %fusion.1 = f32[16,2,128,128]{2,3,1,0:T(8,128)S(1)} fusion(f32[16,2,128,128]{3,2,1,0:T(8,128)S(1)} %add_add_fusion, f32[16,2,128,128]{3,1,0,2:T(2,128)S(1)} %bitcast.145), kind=kOutput, calls=%fused_computation.19 | convolution fusion | flops 805306368 | bytes 6291456 | tf_op jit(solution)/shard_map/tfzy,tfcy->tfcz/dot_general | solution.py:195
  144.6 1.1 slice_reduce_fusion
  145.9 1.4 concatenate.45
  147.3 1.2 collective-permute-done.7
  148.5 1.4 slice_add_fusion
  149.9 1.1 broadcast_select_fusion
  151.0 1.9 %multiply_subtract_fusion = f32[16,2,128,128]{2,3,1,0:T(8,128)S(1)} fusion(f32[16,2,128,128]{2,3,1,0:T(8,128)} %copy-done.3, f32[16,2,128]{2,1,0:T(2,128)S(1)} %bitcast.165, f32[16,2,128]{2,1,0:T(2,128)S(1)} %broadcast_multiply_fusion), kind=kLoop, calls=%fused_computation.15 | loop fusion | flops 1048576 | bytes 4227072 | tf_op jit(solution)/shard_map/sub | solution.py:210
  153.1 1.0 copy.150
  154.1 1.4 fusion.82
  155.5 1.8 %collective-permute-start.9 = (f32[2]{0:T(128)S(1)}, f32[2]{0:T(128)S(1)}, u32[]{:S(2)}, u32[]{:S(2)}) collective-permute-start(f32[2]{0:T(128)S(1)} %fusion.82), channel_id=1, source_target_pairs={{0,4},{2,6},{4,0},{6,2},{1,5},{3,7},{5,1},{7,3},{8,12},{10,14},{12... | collective-permute-start | bytes 32 | tf_op jit(solution)/shard_map/ppermute | solution.py:32
  157.3 2.6 %collective-permute-done.9 = f32[2]{0:T(128)S(1)} collective-permute-done((f32[2]{0:T(128)S(1)}, f32[2]{0:T(128)S(1)}, u32[]{:S(2)}, u32[]{:S(2)}) %collective-permute-start.9) | collective-permute-done | bytes 40 | tf_op jit(solution)/shard_map/ppermute | solution.py:32
  159.9 1.5 collective-permute-start.10
  161.4 2.0 %collective-permute-done.10 = f32[2]{0:T(128)S(1)} collective-permute-done((f32[2]{0:T(128)S(1)}, f32[2]{0:T(128)S(1)}, u32[]{:S(2)}, u32[]{:S(2)}) %collective-permute-start.10) | collective-permute-done | bytes 40 | tf_op jit(solution)/shard_map/ppermute | solution.py:32
  163.5 1.5 collective-permute-start.11
  165.0 2.0 %collective-permute-done.11 = f32[2]{0:T(128)S(1)} collective-permute-done((f32[2]{0:T(128)S(1)}, f32[2]{0:T(128)S(1)}, u32[]{:S(2)}, u32[]{:S(2)}) %collective-permute-start.11) | collective-permute-done | bytes 40 | tf_op jit(solution)/shard_map/ppermute | solution.py:32
  169.6 1.0 copy.149
  (117 shorter events, 14.0 us)
Async XLA Ops:
  0.6 25.5 %copy-start = (f32[2,8]{1,0:T(2,128)S(1)}, f32[2,8]{1,0:T(2,128)}, u32[]{:S(2)}) copy-start(f32[2,8]{1,0:T(2,128)} %param.12) | copy-start | bytes 196
  1.3 25.1 %collective-permute-start = (s32[16,1]{0,1:T(1,128)S(1)}, s32[16,1]{0,1:T(1,128)S(1)}, u32[]{:S(2)}, u32[]{:S(2)}) collective-permute-start(s32[16,1]{0,1:T(1,128)S(1)} %slice.118), channel_id=1, source_target_pairs={{1,0},{3,2},{5,4},{7,6},{9,8},{11,10},{13,12},{15,14},{17,16},{19,... | collective-permute-start | bytes 200 | tf_op jit(solution)/shard_map/ppermute | solution.py:17
  19.4 4.7 %copy-start.7 = (bf16[16,128,128]{2,1,0:T(8,128)(2,1)S(1)}, bf16[16,128,128]{2,1,0:T(8,128)(2,1)}, u32[]{:S(2)}) copy-start(bf16[16,128,128]{2,1,0:T(8,128)(2,1)} %param.7) | copy-start | bytes 1572868
  19.4 5.6 %copy-start.13 = (s32[16,4]{0,1:T(4,128)S(1)}, s32[16,4]{0,1:T(4,128)}, u32[]{:S(2)}) copy-start(s32[16,4]{0,1:T(4,128)} %param.11) | copy-start | bytes 772
  19.4 7.2 %copy-start.14 = (f32[8]{0:T(128)S(1)}, f32[8]{0:T(128)}, u32[]{:S(2)}) copy-start(f32[8]{0:T(128)} %param.13) | copy-start | bytes 100
  20.6 28.2 %all-to-all-start = ((bf16[4,4,2,128,128]{4,3,1,2,0:T(8,128)(2,1)}), bf16[4,4,2,128,128]{4,3,1,2,0:T(8,128)(2,1)S(1)}, u32[]{:S(2)}, u32[]{:S(2)}) async-start(bf16[4,4,2,128,128]{4,3,1,2,0:T(8,128)(2,1)} %copy.122), calls=%async_computation | async-start | bytes 2097152 | tf_op jit(solution)/shard_map/all_to_all | solution.py:166
  39.8 9.1 %copy-start.12 = (bf16[16,128,128]{2,1,0:T(8,128)(2,1)S(1)}, bf16[16,128,128]{2,1,0:T(8,128)(2,1)}, u32[]{:S(2)}) copy-start(bf16[16,128,128]{2,1,0:T(8,128)(2,1)} %param.8) | copy-start | bytes 1572868
  42.4 24.1 %collective-permute-start.6 = (f32[16,2]{0,1:T(2,128)S(1)}, f32[16,2]{0,1:T(2,128)S(1)}, u32[]{:S(2)}, u32[]{:S(2)}) collective-permute-start(f32[16,2]{0,1:T(2,128)S(1)} %bitcast.175), channel_id=1, source_target_pairs={{0,1},{1,0},{2,3},{3,2},{4,5},{5,4},{6,7},{7,6},{8,9},{9,8},{10,11... | collective-permute-start | bytes 392 | tf_op jit(solution)/shard_map/ppermute | solution.py:21
  54.8 2.1 %copy-start.4 = (bf16[16,4,128,128]{3,2,1,0:T(8,128)(2,1)S(1)}, bf16[16,4,128,128]{3,2,1,0:T(8,128)(2,1)}, u32[]{:S(2)}) copy-start(bf16[16,4,128,128]{3,2,1,0:T(8,128)(2,1)} %param.10) | copy-start | bytes 6291460
  54.8 2.3 %copy-start.11 = (bf16[16,2,128,128]{3,2,1,0:T(8,128)(2,1)S(1)}, bf16[16,2,128,128]{3,2,1,0:T(8,128)(2,1)}, u32[]{:S(2)}) copy-start(bf16[16,2,128,128]{3,2,1,0:T(8,128)(2,1)} %gather_fusion.1) | copy-start | bytes 3145732
  57.1 1.2 copy-start.9
  58.9 1.6 copy-start.1
  63.7 1.4 copy-start.2
  66.5 1.2 collective-permute-start.1
  70.7 1.4 copy-start.6
  73.6 32.7 %all-to-all-start.2 = ((bf16[4,4,128,128]{2,3,1,0:T(8,128)(2,1)}), bf16[4,4,128,128]{2,3,1,0:T(8,128)(2,1)S(1)}, u32[]{:S(2)}, u32[]{:S(2)}) async-start(bf16[4,4,128,128]{2,3,1,0:T(8,128)(2,1)} %bitcast.56), calls=%async_computation.2 | async-start | bytes 1048576 | tf_op jit(solution)/shard_map/all_to_all | solution.py:166
  78.4 8.0 %collective-permute-start.2 = (f32[2]{0:T(128)S(1)}, f32[2]{0:T(128)S(1)}, u32[]{:S(2)}, u32[]{:S(2)}) collective-permute-start(f32[2]{0:T(128)S(1)} %slice_add_fusion.1), channel_id=1, source_target_pairs={{0,2},{2,0},{4,6},{6,4},{1,3},{3,1},{5,7},{7,5},{8,10},{10,8},{12,... | collective-permute-start | bytes 32 | tf_op jit(solution)/shard_map/ppermute | solution.py:32
  87.8 6.0 %collective-permute-start.3 = (f32[2]{0:T(128)S(1)}, f32[2]{0:T(128)S(1)}, u32[]{:S(2)}, u32[]{:S(2)}) collective-permute-start(f32[2]{0:T(128)S(1)} %fusion.83), channel_id=1, source_target_pairs={{0,4},{2,6},{4,0},{6,2},{1,5},{3,7},{5,1},{7,3},{8,12},{10,14},{12... | collective-permute-start | bytes 32 | tf_op jit(solution)/shard_map/ppermute | solution.py:32
  93.8 3.5 %collective-permute-start.4 = (f32[2]{0:T(128)S(1)}, f32[2]{0:T(128)S(1)}, u32[]{:S(2)}, u32[]{:S(2)}) collective-permute-start(f32[2]{0:T(128)S(1)} %add.226), channel_id=1, source_target_pairs={{0,8},{8,0},{16,24},{24,16},{1,9},{9,1},{17,25},{25,17},{2,10},{10... | collective-permute-start | bytes 32 | tf_op jit(solution)/shard_map/ppermute | solution.py:32
  97.3 3.5 %collective-permute-start.5 = (f32[2]{0:T(128)S(1)}, f32[2]{0:T(128)S(1)}, u32[]{:S(2)}, u32[]{:S(2)}) collective-permute-start(f32[2]{0:T(128)S(1)} %add.227), channel_id=1, source_target_pairs={{0,16},{8,24},{16,0},{24,8},{1,17},{9,25},{17,1},{25,9},{2,18},{10... | collective-permute-start | bytes 32 | tf_op jit(solution)/shard_map/ppermute | solution.py:32
  106.3 15.5 %all-to-all-start.1 = ((bf16[4,4,128,128]{2,3,1,0:T(8,128)(2,1)}), bf16[4,4,128,128]{2,3,1,0:T(8,128)(2,1)}, u32[]{:S(2)}, u32[]{:S(2)}) async-start(bf16[4,4,128,128]{2,3,1,0:T(8,128)(2,1)} %bitcast.53), calls=%async_computation.1 | async-start | bytes 1048576 | tf_op jit(solution)/shard_map/all_to_all | solution.py:166
  136.7 2.1 %copy-start.5 = (bf16[16,4,128,128]{3,2,1,0:T(8,128)(2,1)S(1)}, bf16[16,4,128,128]{3,2,1,0:T(8,128)(2,1)}, u32[]{:S(2)}) copy-start(bf16[16,4,128,128]{3,2,1,0:T(8,128)(2,1)} %param.10) | copy-start | bytes 6291460
  136.7 2.3 %copy-start.10 = (bf16[16,2,128,128]{2,3,1,0:T(8,128)(2,1)S(1)}, bf16[16,2,128,128]{2,3,1,0:T(8,128)(2,1)}, u32[]{:S(2)}) copy-start(bf16[16,2,128,128]{2,3,1,0:T(8,128)(2,1)} %gather_fusion.8) | copy-start | bytes 3145732
  139.0 1.2 copy-start.8
  144.6 1.4 copy-start.3
  147.3 1.2 collective-permute-start.7
  149.9 4.2 %collective-permute-start.8 = (f32[2]{0:T(128)S(1)}, f32[2]{0:T(128)S(1)}, u32[]{:S(2)}, u32[]{:S(2)}) collective-permute-start(f32[2]{0:T(128)S(1)} %slice_add_fusion), channel_id=1, source_target_pairs={{0,2},{2,0},{4,6},{6,4},{1,3},{3,1},{5,7},{7,5},{8,10},{10,8},{12,... | collective-permute-start | bytes 32 | tf_op jit(solution)/shard_map/ppermute | solution.py:32
  155.5 4.4 %collective-permute-start.9 = (f32[2]{0:T(128)S(1)}, f32[2]{0:T(128)S(1)}, u32[]{:S(2)}, u32[]{:S(2)}) collective-permute-start(f32[2]{0:T(128)S(1)} %fusion.82), channel_id=1, source_target_pairs={{0,4},{2,6},{4,0},{6,2},{1,5},{3,7},{5,1},{7,3},{8,12},{10,14},{12... | collective-permute-start | bytes 32 | tf_op jit(solution)/shard_map/ppermute | solution.py:32
  159.9 3.5 %collective-permute-start.10 = (f32[2]{0:T(128)S(1)}, f32[2]{0:T(128)S(1)}, u32[]{:S(2)}, u32[]{:S(2)}) collective-permute-start(f32[2]{0:T(128)S(1)} %add.237), channel_id=1, source_target_pairs={{0,8},{8,0},{16,24},{24,16},{1,9},{9,1},{17,25},{25,17},{2,10},{10... | collective-permute-start | bytes 32 | tf_op jit(solution)/shard_map/ppermute | solution.py:32
  163.5 3.5 %collective-permute-start.11 = (f32[2]{0:T(128)S(1)}, f32[2]{0:T(128)S(1)}, u32[]{:S(2)}, u32[]{:S(2)}) collective-permute-start(f32[2]{0:T(128)S(1)} %add.238), channel_id=1, source_target_pairs={{0,16},{8,24},{16,0},{24,8},{1,17},{9,25},{17,1},{25,9},{2,18},{10... | collective-permute-start | bytes 32 | tf_op jit(solution)/shard_map/ppermute | solution.py:32

commit v15 on v12

--- a/solution.py
+++ b/solution.py
@@ -181,15 +181,19 @@
     high_spike = jnp.where(my_layer == 0, other_spike, edge_spike)
     ratios = []
     for step_index in range(STEPS):
-        tile_pool = jnp.concatenate([fields, arrived], axis=0)
-        advected = jnp.zeros(fields.shape, jnp.float32)
-        for entry_k in range(sources_per):
-            advected = advected + jnp.einsum(
-                "tcd,tfdz->tfcz",
-                interp_weights[:, entry_k],
-                tile_pool[pool_index[:, entry_k]],
-                preferred_element_type=jnp.float32,
-            )
+        per_field = []
+        for field_id in range(fields.shape[1]):
+            tile_pool = jnp.concatenate([fields[:, field_id], arrived[:, field_id]], axis=0)
+            field_sum = jnp.zeros(fields[:, field_id].shape, jnp.float32)
+            for entry_k in range(sources_per):
+                field_sum = field_sum + jnp.einsum(
+                    "tcd,tdz->tcz",
+                    interp_weights[:, entry_k],
+                    tile_pool[pool_index[:, entry_k]],
+                    preferred_element_type=jnp.float32,
+                )
+            per_field.append(field_sum)
+        advected = jnp.stack(per_field, axis=1)
         last = step_index + 1 == STEPS
         totals = butterfly_sum(
             jnp.stack([jnp.sum(fields[:, 0], dtype=jnp.float32), jnp.sum(advected[:, 0])]),

time: 167 us -> 178 us (1.066)
  local copies, waits for them, and re-layouts: 41.2 us -> 48.9 us
  matrix products: 14.3 us -> 21.2 us
  waiting for transfers between devices: 38 us -> 34.8 us
  other arithmetic: 23.7 us -> 21.9 us
    gather x8 -> x16, local copies, waits for them, and re-layouts: 17.8 us -> 25.2 us  [per_device(): tile_pool[pool_index[:, entry_k]]]
    dot_general x8 -> x16, matrix products: 6.92 us -> 13.9 us  [per_device(): jnp.einsum('tcd,tdz->tcz', interp_weights[:, entry_k], tile_pool[pool_ind...]
    all_to_all x3, waiting for transfers between devices: 14 us -> 9.32 us  [exchange(): lax.all_to_all(tiles[wanted], 'gy', split_axis=0, concat_axis=0, tiled=True)]
    unnamed x30 -> x54, local copies, waits for them, and re-layouts: 6.84 us -> 9.11 us
    slice x1 -> x0, local copies, waits for them, and re-layouts: 2.11 us -> none  [per_device(): next_turbulence = unscaled[:, 1].astype(jnp.bfloat16)]
    ppermute x10, waiting for transfers between devices: 22.5 us -> 24.4 us  [butterfly_sum(): lax.ppermute(value, axis, [(i, i ^ bit) for i in range(devices)])]
  transfers between devices with their start and end apart: 17 -> 17, of which waited for: 14 -> 12; matrix products, arithmetic and copies ran while one was open for 19% -> 22% of each run, Pallas kernels for 4% -> 3%
where the time goes in v15:
time: 178 us; the launch traced here: 177 us
  local copies, waits for them, and re-layouts  48.9 us (27%)
  waiting for transfers between devices  34.8 us (20%)
  starting transfers between devices  26.7 us (15%)
  other arithmetic  21.9 us (12%)
  matrix products  21.2 us (12%)
  blocking collectives  13.7 us (8%)
  Pallas kernels  5.92 us (3%)
  between operations  3.89 us (2%)
    gather x16, local copies, waits for them, and re-layouts, per_device(): tile_pool[pool_index[:, entry_k]]  25.2 us
    ppermute x10, waiting for transfers between devices, butterfly_sum(): lax.ppermute(value, axis, [(i, i ^ bit) for i in range(devices)])  24.4 us
    dot_general x16, matrix products, per_device(): jnp.einsum('tcd,tdz->tcz', interp_weights[:, entry_k], tile_pool[pool_ind...  13.9 us
    unnamed x1, blocking collectives  13.7 us
    ppermute x10, starting transfers between devices, butterfly_sum(): lax.ppermute(value, axis, [(i, i ^ bit) for i in range(devices)])  13.1 us
    all_to_all x3, starting transfers between devices, exchange(): lax.all_to_all(tiles[wanted], 'gy', split_axis=0, concat_axis=0, tiled=True)  12.1 us
    all_to_all x3, waiting for transfers between devices, exchange(): lax.all_to_all(tiles[wanted], 'gy', split_axis=0, concat_axis=0, tiled=True)  9.32 us
    unnamed x54, local copies, waits for them, and re-layouts  9.11 us
  transfers between devices with their start and end apart: 17, of which 12 were waited for; matrix products, arithmetic and copies ran while one was open for 22% of the time, Pallas kernels for 3%

profile of v15, /device:TPU:0, one launch (start us, length us, event | category | flops | bytes accessed | tf_op | source)
XLA Modules:
  0.0 177.0 jit_solution(9884583236666020150)
XLA Ops:
  1.3 1.3 collective-permute-start.5
  2.6 13.7 %all-gather.1 = s32[4,16,4]{1,2,0:T(4,128)S(1)} all-gather(s32[1,16,4]{1,2,0:T(4,128)} %bitcast.201), channel_id=3, replica_groups=[8,4]<=[4,4,2]T(0,2,1), dimensions={0}, use_global_device_ids=true | all-gather | bytes 1280 | tf_op args[2]
  17.3 1.3 pad_maximum_fusion.2
  19.4 1.1 copy.158
  20.6 3.6 %all-to-all-start = ((bf16[4,4,2,128,128]{4,3,1,2,0:T(8,128)(2,1)}), bf16[4,4,2,128,128]{4,3,1,2,0:T(8,128)(2,1)S(1)}, u32[]{:S(2)}, u32[]{:S(2)}) async-start(bf16[4,4,2,128,128]{4,3,1,2,0:T(8,128)(2,1)} %copy.158), calls=%async_computation | async-start | bytes 2097152 | tf_op jit(solution)/shard_map/all_to_all | solution.py:166
  27.9 1.9 %broadcast_in_dim.66.lower_ref = f32[128,32,128]{2,1,0:T(8,128)} broadcast(f32[128,32]{1,0:T(8,128)S(1)} %bitcast.183), dimensions={0,1} | broadcast | bytes 2113536 | tf_op jit(solution)/shard_map/broadcast_in_dim | solution.py:87
  29.8 1.9 %broadcast_in_dim.68.diagonal_ref = f32[128,32,128]{2,1,0:T(8,128)} broadcast(f32[128,32]{1,0:T(8,128)S(1)} %bitcast.184), dimensions={0,1} | broadcast | bytes 2113536 | tf_op jit(solution)/shard_map/broadcast_in_dim | solution.py:87
  31.7 1.9 %broadcast_in_dim.72.upper_ref = f32[128,32,128]{2,1,0:T(8,128)} broadcast(f32[128,32]{1,0:T(8,128)S(1)} %copy.179), dimensions={0,1} | broadcast | bytes 2113536 | tf_op jit(solution)/shard_map/broadcast_in_dim | solution.py:87
  33.7 5.9 %shard_map.94 = f32[128,32,128]{2,1,0:T(8,128)} custom-call(f32[128,32,128]{2,1,0:T(8,128)} %broadcast_in_dim.66.lower_ref, f32[128,32,128]{2,1,0:T(8,128)} %broadcast_in_dim.68.diagonal_ref, f32[128,32,128]{2,1,0:T(8,128)} %broadcast_in_dim.72.upper_ref), custom_call_target="tpu_custom_call" | custom-call | flops 8388608 | bytes 33554432 | tf_op jit(solution)/shard_map/pallas_call | solution.py:94
  39.6 2.2 %fusion.2 = f32[32,128]{0,1:T(8,128)S(1)} fusion(f32[128,32,128]{2,1,0:T(8,128)} %shard_map.94, pred[128]{0:T(512)(128)(4,1)S(1)} %iota_compare_fusion.10), kind=kLoop, calls=%fused_computation.24 | loop fusion | flops 1044480 | bytes 2113664 | tf_op jit(solution)/shard_map/reduce_sum | solution.py:174
  42.6 1.0 collective-permute-done.7
  43.9 5.0 %all-to-all-done = bf16[4,4,2,128,128]{4,3,1,2,0:T(8,128)(2,1)S(1)} async-done(((bf16[4,4,2,128,128]{4,3,1,2,0:T(8,128)(2,1)}), bf16[4,4,2,128,128]{4,3,1,2,0:T(8,128)(2,1)S(1)}, u32[]{:S(2)}, u32[]{:S(2)}) %all-to-all-start) | async-done | bytes 1048608 | tf_op jit(solution)/shard_map/all_to_all | solution.py:166
  49.3 1.4 gather_fusion.5
  50.7 1.4 gather_fusion.6
  52.1 1.4 gather_fusion.1
  53.5 1.4 gather_fusion.2
  54.9 2.8 %gather_fusion.7 = bf16[16,128,128]{2,1,0:T(8,128)(2,1)} fusion(bf16[32,128,128]{2,1,0:T(8,128)(2,1)} %copy-done.4, s32[1024]{0:T(1024)S(1)} %get-tuple-element.59), kind=kCustom, calls=%fused_computation.7 | custom fusion | bytes 1048640 | tf_op jit(solution)/shard_map/gather | solution.py:192
  57.7 1.4 gather_fusion.3
  59.1 2.7 %gather_fusion.8 = bf16[16,128,128]{2,1,0:T(8,128)(2,1)} fusion(bf16[32,128,128]{2,1,0:T(8,128)(2,1)} %copy-done.4, s32[1024]{0:T(1024)S(1)} %get-tuple-element.58), kind=kCustom, calls=%fused_computation.8 | custom fusion | bytes 1048640 | tf_op jit(solution)/shard_map/gather | solution.py:192
  61.8 1.4 gather_fusion.4
  63.2 1.6 fusion.34
  70.6 2.3 %fusion.88 = (f32[]{:T(128)}, f32[16,128,128]{2,1,0:T(8,128)S(1)}) fusion(f32[16,128,128]{2,1,0:T(8,128)S(1)} %convolution_add_fusion.10, bf16[16,128,128]{2,1,0:T(8,128)(2,1)S(1)} %copy-done.13, bf16[16,4,128,128]{3,2,1,0:T(8,128)(2,1)} %param.10), kind=kOutput, calls=%fused_computation.214 | convolution fusion | flops 67633152 | bytes 3145732 | tf_op jit(solution)/shard_map/tcd,tdz->tcz/dot_general | solution.py:189
  72.9 3.3 %fusion.3 = f32[16,2,128,128]{2,3,1,0:T(8,128)S(1)} fusion(f32[16,2,128,128]{3,1,0,2:T(2,128)S(1)} %bitcast.174, f32[16,1,128,128]{2,3,0,1:T(8,128)S(1)} %fusion.8, f32[16,1,128,128]{2,3,0,1:T(8,128)S(1)} %bitcast.180), kind=kOutput, calls=%fused_computation.25 | convolution fusion | flops 805830656 | bytes 6291456 | tf_op jit(solution)/shard_map/tfzy,tfcy->tfcz/dot_general | solution.py:202
  76.3 1.4 pad_maximum_fusion.8
  79.1 1.3 copy-done.5
  80.5 1.4 gather_fusion.14
  81.9 4.3 %all-to-all-start.2 = ((bf16[4,4,128,128]{2,3,1,0:T(8,128)(2,1)}), bf16[4,4,128,128]{2,3,1,0:T(8,128)(2,1)}, u32[]{:S(2)}, u32[]{:S(2)}) async-start(bf16[4,4,128,128]{2,3,1,0:T(8,128)(2,1)} %bitcast.55), calls=%async_computation.2 | async-start | bytes 1048576 | tf_op jit(solution)/shard_map/all_to_all | solution.py:166
  86.2 1.4 fusion.108
  87.7 1.8 %collective-permute-start.1 = (f32[2]{0:T(128)S(1)}, f32[2]{0:T(128)S(1)}, u32[]{:S(2)}, u32[]{:S(2)}) collective-permute-start(f32[2]{0:T(128)S(1)} %fusion.108), channel_id=1, source_target_pairs={{0,2},{2,0},{4,6},{6,4},{1,3},{3,1},{5,7},{7,5},{8,10},{10,8},{12,... | collective-permute-start | bytes 32 | tf_op jit(solution)/shard_map/ppermute | solution.py:32
  89.4 6.0 %collective-permute-done.1 = f32[2]{0:T(128)S(1)} collective-permute-done((f32[2]{0:T(128)S(1)}, f32[2]{0:T(128)S(1)}, u32[]{:S(2)}, u32[]{:S(2)}) %collective-permute-start.1) | collective-permute-done | bytes 40 | tf_op jit(solution)/shard_map/ppermute | solution.py:32
  95.4 1.4 fusion.110
  96.8 4.3 %collective-permute-start.2 = (f32[2]{0:T(128)S(1)}, f32[2]{0:T(128)S(1)}, u32[]{:S(2)}, u32[]{:S(2)}) collective-permute-start(f32[2]{0:T(128)S(1)} %fusion.110), channel_id=1, source_target_pairs={{0,4},{2,6},{4,0},{6,2},{1,5},{3,7},{5,1},{7,3},{8,12},{10,14},{12... | collective-permute-start | bytes 32 | tf_op jit(solution)/shard_map/ppermute | solution.py:32
  101.1 1.5 collective-permute-done.2
  102.6 1.5 collective-permute-start.3
  104.1 2.1 %collective-permute-done.3 = f32[2]{0:T(128)S(1)} collective-permute-done((f32[2]{0:T(128)S(1)}, f32[2]{0:T(128)S(1)}, u32[]{:S(2)}, u32[]{:S(2)}) %collective-permute-start.3) | collective-permute-done | bytes 40 | tf_op jit(solution)/shard_map/ppermute | solution.py:32
  106.2 1.5 collective-permute-start.4
  107.7 2.0 %collective-permute-done.4 = f32[2]{0:T(128)S(1)} collective-permute-done((f32[2]{0:T(128)S(1)}, f32[2]{0:T(128)S(1)}, u32[]{:S(2)}, u32[]{:S(2)}) %collective-permute-start.4) | collective-permute-done | bytes 40 | tf_op jit(solution)/shard_map/ppermute | solution.py:32
  111.7 2.1 %convert_reduce_fusion = (f32[]{:T(128)}, bf16[16,128,128]{1,2,0:T(8,128)(2,1)S(1)}) fusion(f32[16,2,128,128]{2,3,1,0:T(8,128)} %copy-done.5, f32[]{:T(128)} %bitcast.14), kind=kLoop, calls=%fused_computation.63 | loop fusion | flops 1048575 | bytes 1572872 | tf_op jit(solution)/shard_map/reduce_sum | solution.py:199
  113.8 1.4 gather_fusion.9
  115.2 4.2 %all-to-all-start.1 = ((bf16[4,4,128,128]{2,3,1,0:T(8,128)(2,1)}), bf16[4,4,128,128]{2,3,1,0:T(8,128)(2,1)}, u32[]{:S(2)}, u32[]{:S(2)}) async-start(bf16[4,4,128,128]{2,3,1,0:T(8,128)(2,1)} %bitcast.181), calls=%async_computation.1 | async-start | bytes 1048576 | tf_op jit(solution)/shard_map/all_to_all | solution.py:166
  119.4 1.3 pad_maximum_fusion.6
  120.7 1.4 gather_fusion.15
  122.1 1.4 gather_fusion.16
  123.5 1.4 gather_fusion.17
  124.9 1.4 gather_fusion.18
  126.3 4.3 %all-to-all-done.1 = bf16[4,4,128,128]{2,3,1,0:T(8,128)(2,1)} async-done(((bf16[4,4,128,128]{2,3,1,0:T(8,128)(2,1)}), bf16[4,4,128,128]{2,3,1,0:T(8,128)(2,1)}, u32[]{:S(2)}, u32[]{:S(2)}) %all-to-all-start.1) | async-done | bytes 524320 | tf_op jit(solution)/shard_map/all_to_all | solution.py:166
  130.6 1.3 pad_maximum_fusion.5
  131.9 1.4 gather_fusion.10
  133.3 1.4 gather_fusion.11
  134.8 1.4 gather_fusion.12
  136.2 1.4 gather_fusion.13
  137.6 1.8 %fusion.30 = f32[16,128,128]{2,1,0:T(8,128)S(1)} fusion(bf16[16,128,128]{1,2,0:T(8,128)(2,1)} %gather_fusion.15, bf16[16,4,128,128]{3,2,1,0:T(8,128)(2,1)} %param.10), kind=kOutput, calls=%fused_computation.83 | convolution fusion | flops 67108864 | bytes 2097152 | tf_op jit(solution)/shard_map/tcd,tdz->tcz/dot_general | solution.py:189
  139.5 1.5 fusion.32
  146.3 1.1 fusion.89
  147.4 3.3 %fusion = f32[16,2,128,128]{2,3,1,0:T(8,128)S(1)} fusion(f32[16,2,128,128]{3,1,0,2:T(2,128)S(1)} %bitcast.175, f32[16,1,128,128]{2,3,0,1:T(8,128)S(1)} %fusion.7, f32[16,1,128,128]{2,3,0,1:T(8,128)S(1)} %bitcast.179), kind=kOutput, calls=%fused_computation.21 | convolution fusion | flops 805830656 | bytes 6291456 | tf_op jit(solution)/shard_map/tfzy,tfcy->tfcz/dot_general | solution.py:202
  150.8 1.4 pad_maximum_fusion.9
  153.5 1.4 fusion.107
  154.9 3.5 %collective-permute-done.9 = f32[2]{0:T(128)S(1)} collective-permute-done((f32[2]{0:T(128)S(1)}, f32[2]{0:T(128)S(1)}, u32[]{:S(2)}, u32[]{:S(2)}) %collective-permute-start.9) | collective-permute-done | bytes 40 | tf_op jit(solution)/shard_map/ppermute | solution.py:32
  158.4 1.4 fusion.109
  159.8 4.4 %collective-permute-done.10 = f32[2]{0:T(128)S(1)} collective-permute-done((f32[2]{0:T(128)S(1)}, f32[2]{0:T(128)S(1)}, u32[]{:S(2)}, u32[]{:S(2)}) %collective-permute-start.10) | collective-permute-done | bytes 40 | tf_op jit(solution)/shard_map/ppermute | solution.py:32
  164.2 1.5 collective-permute-start.11
  165.7 2.1 %collective-permute-done.11 = f32[2]{0:T(128)S(1)} collective-permute-done((f32[2]{0:T(128)S(1)}, f32[2]{0:T(128)S(1)}, u32[]{:S(2)}, u32[]{:S(2)}) %collective-permute-start.11) | collective-permute-done | bytes 40 | tf_op jit(solution)/shard_map/ppermute | solution.py:32
  167.8 1.5 collective-permute-start.12
  169.3 2.0 %collective-permute-done.12 = f32[2]{0:T(128)S(1)} collective-permute-done((f32[2]{0:T(128)S(1)}, f32[2]{0:T(128)S(1)}, u32[]{:S(2)}, u32[]{:S(2)}) %collective-permute-start.12) | collective-permute-done | bytes 40 | tf_op jit(solution)/shard_map/ppermute | solution.py:32
  (155 shorter events, 26.1 us)
Async XLA Ops:
  0.6 25.7 %copy-start = (f32[2,8]{1,0:T(2,128)S(1)}, f32[2,8]{1,0:T(2,128)}, u32[]{:S(2)}) copy-start(f32[2,8]{1,0:T(2,128)} %param.12) | copy-start | bytes 196
  1.3 25.3 %collective-permute-start.5 = (s32[16,1]{0,1:T(1,128)S(1)}, s32[16,1]{0,1:T(1,128)S(1)}, u32[]{:S(2)}, u32[]{:S(2)}) collective-permute-start(s32[16,1]{0,1:T(1,128)S(1)} %slice.126), channel_id=1, source_target_pairs={{1,0},{3,2},{5,4},{7,6},{9,8},{11,10},{13,12},{15,14},{17,16},{19,... | collective-permute-start | bytes 200 | tf_op jit(solution)/shard_map/ppermute | solution.py:17
  19.4 4.8 %copy-start.23 = (s32[16,4]{0,1:T(4,128)S(1)}, s32[16,4]{0,1:T(4,128)}, u32[]{:S(2)}) copy-start(s32[16,4]{0,1:T(4,128)} %param.11) | copy-start | bytes 772
  19.4 5.0 %copy-start.8 = (bf16[16,128,128]{2,1,0:T(8,128)(2,1)S(1)}, bf16[16,128,128]{2,1,0:T(8,128)(2,1)}, u32[]{:S(2)}) copy-start(bf16[16,128,128]{2,1,0:T(8,128)(2,1)} %param.7) | copy-start | bytes 1572868
  20.6 6.3 %copy-start.24 = (f32[8]{0:T(128)S(1)}, f32[8]{0:T(128)}, u32[]{:S(2)}) copy-start(f32[8]{0:T(128)} %param.13) | copy-start | bytes 100
  20.6 28.3 %all-to-all-start = ((bf16[4,4,2,128,128]{4,3,1,2,0:T(8,128)(2,1)}), bf16[4,4,2,128,128]{4,3,1,2,0:T(8,128)(2,1)S(1)}, u32[]{:S(2)}, u32[]{:S(2)}) async-start(bf16[4,4,2,128,128]{4,3,1,2,0:T(8,128)(2,1)} %copy.158), calls=%async_computation | async-start | bytes 2097152 | tf_op jit(solution)/shard_map/all_to_all | solution.py:166
  42.5 1.1 collective-permute-start.7
  43.9 5.2 %copy-start.22 = (bf16[16,128,128]{2,1,0:T(8,128)(2,1)S(1)}, bf16[16,128,128]{2,1,0:T(8,128)(2,1)}, u32[]{:S(2)}) copy-start(bf16[16,128,128]{2,1,0:T(8,128)(2,1)} %param.8) | copy-start | bytes 1572868
  49.3 5.6 %copy-start.4 = (bf16[32,128,128]{2,1,0:T(8,128)(2,1)}, bf16[32,128,128]{2,1,0:T(8,128)(2,1)S(1)}, u32[]{:S(2)}) copy-start(bf16[32,128,128]{2,1,0:T(8,128)(2,1)S(1)} %get-tuple-element.57) | copy-start | bytes 3145732
  54.9 8.3 %copy-start.2 = (bf16[16,4,128,128]{3,2,1,0:T(8,128)(2,1)S(1)}, bf16[16,4,128,128]{3,2,1,0:T(8,128)(2,1)}, u32[]{:S(2)}) copy-start(bf16[16,4,128,128]{3,2,1,0:T(8,128)(2,1)} %param.10) | copy-start | bytes 6291460
  63.2 1.7 copy-start.21
  63.2 2.2 %copy-start.18 = (bf16[16,128,128]{2,1,0:T(8,128)(2,1)S(1)}, bf16[16,128,128]{2,1,0:T(8,128)(2,1)}, u32[]{:S(2)}) copy-start(bf16[16,128,128]{2,1,0:T(8,128)(2,1)} %gather_fusion.6) | copy-start | bytes 1572868
  65.4 1.0 copy-start.19
  66.4 1.0 copy-start.20
  67.5 1.0 copy-start.15
  68.5 1.0 copy-start.14
  69.6 1.0 copy-start.13
  70.6 2.3 %copy-start.1 = (f32[128,32,128]{2,1,0:T(8,128)S(1)}, f32[128,32,128]{2,1,0:T(8,128)}, u32[]{:S(2)}) copy-start(f32[128,32,128]{2,1,0:T(8,128)} %shard_map.94) | copy-start | bytes 6291460
  76.2 2.0 %collective-permute-start.6 = (f32[16,2,128]{2,1,0:T(2,128)S(1)}, f32[16,2,128]{2,1,0:T(2,128)S(1)}, u32[]{:S(2)}, u32[]{:S(2)}) collective-permute-start(f32[16,2,128]{2,1,0:T(2,128)S(1)} %bitcast.193), channel_id=1, source_target_pairs={{0,1},{1,0},{2,3},{3,2},{4,5},{5,4},{6,7},{7,6},{8,9},{9,8},{10,11... | collective-permute-start | bytes 49160 | tf_op jit(solution)/shard_map/ppermute | solution.py:21
  77.7 8.5 %collective-permute-start = (f32[2]{0:T(128)S(1)}, f32[2]{0:T(128)S(1)}, u32[]{:S(2)}, u32[]{:S(2)}) collective-permute-start(f32[2]{0:T(128)S(1)} %pad_maximum_fusion.8), channel_id=1, source_target_pairs={{0,1},{1,0},{2,3},{3,2},{4,5},{5,4},{6,7},{7,6},{8,9},{9,8},{10,11... | collective-permute-start | bytes 32 | tf_op jit(solution)/shard_map/ppermute | solution.py:32
  79.1 1.3 copy-start.5
  80.5 34.7 %copy-start.6 = (bf16[16,128,128]{1,2,0:T(8,128)(2,1)}, bf16[16,128,128]{1,2,0:T(8,128)(2,1)S(1)}, u32[]{:S(2)}) copy-start(bf16[16,128,128]{1,2,0:T(8,128)(2,1)S(1)} %fusion.15) | copy-start | bytes 1572868
  81.9 33.3 %all-to-all-start.2 = ((bf16[4,4,128,128]{2,3,1,0:T(8,128)(2,1)}), bf16[4,4,128,128]{2,3,1,0:T(8,128)(2,1)}, u32[]{:S(2)}, u32[]{:S(2)}) async-start(bf16[4,4,128,128]{2,3,1,0:T(8,128)(2,1)} %bitcast.55), calls=%async_computation.2 | async-start | bytes 1048576 | tf_op jit(solution)/shard_map/all_to_all | solution.py:166
  87.7 7.8 %collective-permute-start.1 = (f32[2]{0:T(128)S(1)}, f32[2]{0:T(128)S(1)}, u32[]{:S(2)}, u32[]{:S(2)}) collective-permute-start(f32[2]{0:T(128)S(1)} %fusion.108), channel_id=1, source_target_pairs={{0,2},{2,0},{4,6},{6,4},{1,3},{3,1},{5,7},{7,5},{8,10},{10,8},{12,... | collective-permute-start | bytes 32 | tf_op jit(solution)/shard_map/ppermute | solution.py:32
  96.8 5.8 %collective-permute-start.2 = (f32[2]{0:T(128)S(1)}, f32[2]{0:T(128)S(1)}, u32[]{:S(2)}, u32[]{:S(2)}) collective-permute-start(f32[2]{0:T(128)S(1)} %fusion.110), channel_id=1, source_target_pairs={{0,4},{2,6},{4,0},{6,2},{1,5},{3,7},{5,1},{7,3},{8,12},{10,14},{12... | collective-permute-start | bytes 32 | tf_op jit(solution)/shard_map/ppermute | solution.py:32
  102.6 3.5 %collective-permute-start.3 = (f32[2]{0:T(128)S(1)}, f32[2]{0:T(128)S(1)}, u32[]{:S(2)}, u32[]{:S(2)}) collective-permute-start(f32[2]{0:T(128)S(1)} %add.254), channel_id=1, source_target_pairs={{0,8},{8,0},{16,24},{24,16},{1,9},{9,1},{17,25},{25,17},{2,10},{10... | collective-permute-start | bytes 32 | tf_op jit(solution)/shard_map/ppermute | solution.py:32
  106.2 3.5 %collective-permute-start.4 = (f32[2]{0:T(128)S(1)}, f32[2]{0:T(128)S(1)}, u32[]{:S(2)}, u32[]{:S(2)}) collective-permute-start(f32[2]{0:T(128)S(1)} %add.255), channel_id=1, source_target_pairs={{0,16},{8,24},{16,0},{24,8},{1,17},{9,25},{17,1},{25,9},{2,18},{10... | collective-permute-start | bytes 32 | tf_op jit(solution)/shard_map/ppermute | solution.py:32
  113.8 5.6 %copy-start.7 = (bf16[16,128,128]{1,2,0:T(8,128)(2,1)}, bf16[16,128,128]{1,2,0:T(8,128)(2,1)S(1)}, u32[]{:S(2)}) copy-start(bf16[16,128,128]{1,2,0:T(8,128)(2,1)S(1)} %get-tuple-element.31) | copy-start | bytes 1572868
  115.2 15.4 %all-to-all-start.1 = ((bf16[4,4,128,128]{2,3,1,0:T(8,128)(2,1)}), bf16[4,4,128,128]{2,3,1,0:T(8,128)(2,1)}, u32[]{:S(2)}, u32[]{:S(2)}) async-start(bf16[4,4,128,128]{2,3,1,0:T(8,128)(2,1)} %bitcast.181), calls=%async_computation.1 | async-start | bytes 1048576 | tf_op jit(solution)/shard_map/all_to_all | solution.py:166
  137.6 1.9 %copy-start.3 = (bf16[16,4,128,128]{3,2,1,0:T(8,128)(2,1)S(1)}, bf16[16,4,128,128]{3,2,1,0:T(8,128)(2,1)}, u32[]{:S(2)}) copy-start(bf16[16,4,128,128]{3,2,1,0:T(8,128)(2,1)} %param.10) | copy-start | bytes 6291460
  137.6 3.4 %copy-start.11 = (bf16[16,128,128]{1,2,0:T(8,128)(2,1)S(1)}, bf16[16,128,128]{1,2,0:T(8,128)(2,1)}, u32[]{:S(2)}) copy-start(bf16[16,128,128]{1,2,0:T(8,128)(2,1)} %gather_fusion.16) | copy-start | bytes 1572868
  141.1 1.0 copy-start.10
  142.1 1.0 copy-start.9
  143.2 1.0 copy-start.17
  144.2 1.0 copy-start.16
  145.2 1.0 copy-start.12
  150.8 23.1 %collective-permute-start.13 = (f32[16,2,128]{2,1,0:T(2,128)S(1)}, f32[16,2,128]{2,1,0:T(2,128)S(1)}, u32[]{:S(2)}, u32[]{:S(2)}) collective-permute-start(f32[16,2,128]{2,1,0:T(2,128)S(1)} %select_bitcast_fusion), channel_id=1, source_target_pairs={{0,1},{1,0},{2,3},{3,2},{4,5},{5,4},{6,7},{7,6},{8,9},{9,8},{10,11... | collective-permute-start | bytes 49160 | tf_op jit(solution)/shard_map/ppermute | solution.py:21
  152.2 1.3 collective-permute-start.8
  154.9 3.5 %collective-permute-start.9 = (f32[2]{0:T(128)S(1)}, f32[2]{0:T(128)S(1)}, u32[]{:S(2)}, u32[]{:S(2)}) collective-permute-start(f32[2]{0:T(128)S(1)} %fusion.107), channel_id=1, source_target_pairs={{0,2},{2,0},{4,6},{6,4},{1,3},{3,1},{5,7},{7,5},{8,10},{10,8},{12,... | collective-permute-start | bytes 32 | tf_op jit(solution)/shard_map/ppermute | solution.py:32
  159.8 4.4 %collective-permute-start.10 = (f32[2]{0:T(128)S(1)}, f32[2]{0:T(128)S(1)}, u32[]{:S(2)}, u32[]{:S(2)}) collective-permute-start(f32[2]{0:T(128)S(1)} %fusion.109), channel_id=1, source_target_pairs={{0,4},{2,6},{4,0},{6,2},{1,5},{3,7},{5,1},{7,3},{8,12},{10,14},{12... | collective-permute-start | bytes 32 | tf_op jit(solution)/shard_map/ppermute | solution.py:32
  164.2 3.5 %collective-permute-start.11 = (f32[2]{0:T(128)S(1)}, f32[2]{0:T(128)S(1)}, u32[]{:S(2)}, u32[]{:S(2)}) collective-permute-start(f32[2]{0:T(128)S(1)} %add.276), channel_id=1, source_target_pairs={{0,8},{8,0},{16,24},{24,16},{1,9},{9,1},{17,25},{25,17},{2,10},{10... | collective-permute-start | bytes 32 | tf_op jit(solution)/shard_map/ppermute | solution.py:32
  167.8 3.5 %collective-permute-start.12 = (f32[2]{0:T(128)S(1)}, f32[2]{0:T(128)S(1)}, u32[]{:S(2)}, u32[]{:S(2)}) collective-permute-start(f32[2]{0:T(128)S(1)} %add.277), channel_id=1, source_target_pairs={{0,16},{8,24},{16,0},{24,8},{1,17},{9,25},{17,1},{25,9},{2,18},{10... | collective-permute-start | bytes 32 | tf_op jit(solution)/shard_map/ppermute | solution.py:32

commit v16 on v12

--- a/solution.py
+++ b/solution.py
@@ -216,7 +216,13 @@
         ratios.append(mass_fixer)
         next_concentration = (mass_fixer * unscaled[:, 0]).astype(jnp.bfloat16)
         if not last:
-            arrived = jnp.stack([exchange(next_concentration), arrived_turbulence], axis=1)
+            payload, next_concentration = lax.optimization_barrier(
+                (next_concentration[wanted], next_concentration)
+            )
+            sent = lax.all_to_all(payload, "gy", split_axis=0, concat_axis=0, tiled=True)
+            arrived = jnp.stack(
+                [sent.reshape((-1,) + next_concentration.shape[1:]), arrived_turbulence], axis=1
+            )
         fields = jnp.stack([next_concentration, next_turbulence], axis=1)
     return (fields[:, 0], fields[:, 1], jnp.stack(ratios))
 

time: 167 us -> 168 us (level)
  waiting for transfers between devices: 38 us -> 45.2 us
  starting transfers between devices: 26 us -> 20 us
    all_to_all x0 -> x1, waiting for transfers between devices: none -> 7.68 us  [per_device(): lax.all_to_all(payload, 'gy', split_axis=0, concat_axis=0, tiled=True)]
    ppermute x10, starting transfers between devices: 12.7 us -> 6.29 us  [butterfly_sum(): lax.ppermute(value, axis, [(i, i ^ bit) for i in range(devices)])]
    all_to_all x3 -> x2, starting transfers between devices: 11.4 us -> 7.17 us  [exchange(): lax.all_to_all(tiles[wanted], 'gy', split_axis=0, concat_axis=0, tiled=True)]
    all_to_all x0 -> x1, starting transfers between devices: none -> 4.14 us  [per_device(): lax.all_to_all(payload, 'gy', split_axis=0, concat_axis=0, tiled=True)]
    all_to_all x3 -> x2, waiting for transfers between devices: 14 us -> 12 us  [exchange(): lax.all_to_all(tiles[wanted], 'gy', split_axis=0, concat_axis=0, tiled=True)]
    ppermute x10, waiting for transfers between devices: 22.5 us -> 24.3 us  [butterfly_sum(): lax.ppermute(value, axis, [(i, i ^ bit) for i in range(devices)])]
    gather x4 -> x3, local copies, waits for them, and re-layouts: 4.71 us -> 3.3 us  [exchange(): tiles[wanted]]
  transfers between devices with their start and end apart: 17 -> 17, of which waited for: 14 -> 13; matrix products, arithmetic and copies ran while one was open for 19% -> 20% of each run, Pallas kernels for 4% -> 4%
where the time goes in v16:
time: 168 us; the launch traced here: 167 us
  waiting for transfers between devices  45.2 us (27%)
  local copies, waits for them, and re-layouts  41.5 us (25%)
  other arithmetic  22.5 us (13%)
  starting transfers between devices  20 us (12%)
  matrix products  14.3 us (9%)
  blocking collectives  13.7 us (8%)
  Pallas kernels  5.94 us (4%)
  between operations  3.86 us (2%)
    ppermute x10, waiting for transfers between devices, butterfly_sum(): lax.ppermute(value, axis, [(i, i ^ bit) for i in range(devices)])  24.3 us
    gather x8, local copies, waits for them, and re-layouts, per_device(): tile_pool[pool_index[:, entry_k]]  17.8 us
    unnamed x1, blocking collectives  13.7 us
    all_to_all x2, waiting for transfers between devices, exchange(): lax.all_to_all(tiles[wanted], 'gy', split_axis=0, concat_axis=0, tiled=True)  12 us
    all_to_all x1, waiting for transfers between devices, per_device(): lax.all_to_all(payload, 'gy', split_axis=0, concat_axis=0, tiled=True)  7.68 us
    all_to_all x2, starting transfers between devices, exchange(): lax.all_to_all(tiles[wanted], 'gy', split_axis=0, concat_axis=0, tiled=True)  7.17 us
    dot_general x8, matrix products, per_device(): jnp.einsum('tcd,tfdz->tfcz', interp_weights[:, entry_k], tile_pool[pool_i...  6.92 us
    dot_general x2, matrix products, per_device(): jnp.einsum('tfzy,tfcy->tfcz', inverse, advected, precision=HIGHEST, prefe...  6.62 us
  transfers between devices with their start and end apart: 17, of which 13 were waited for; matrix products, arithmetic and copies ran while one was open for 20% of the time, Pallas kernels for 4%

profile of v16, /device:TPU:0, one launch (start us, length us, event | category | flops | bytes accessed | tf_op | source)
XLA Modules:
  0.0 166.9 jit_solution(2047915005376896793)
XLA Ops:
  0.6 0.7 slice.108
  1.3 1.3 collective-permute-start.5
  2.6 13.7 %all-gather.1 = s32[4,16,4]{1,2,0:T(4,128)S(1)} all-gather(s32[1,16,4]{1,2,0:T(4,128)} %bitcast.182), channel_id=3, replica_groups=[8,4]<=[4,4,2]T(0,2,1), dimensions={0}, use_global_device_ids=true | all-gather | bytes 1280 | tf_op args[2]
  17.3 1.3 pad_maximum_fusion.1
  18.7 0.7 gather_fusion
  19.5 1.1 copy.138
  20.6 3.5 %all-to-all-start = ((bf16[4,4,2,128,128]{4,3,1,2,0:T(8,128)(2,1)}), bf16[4,4,2,128,128]{4,3,1,2,0:T(8,128)(2,1)S(1)}, u32[]{:S(2)}, u32[]{:S(2)}) async-start(bf16[4,4,2,128,128]{4,3,1,2,0:T(8,128)(2,1)} %copy.138), calls=%async_computation | async-start | bytes 2097152 | tf_op jit(solution)/shard_map/all_to_all | solution.py:166
  24.1 0.9 convert_reduce_fusion.1
  28.0 1.9 %broadcast_in_dim.68.diagonal_ref = f32[128,32,128]{2,1,0:T(8,128)} broadcast(f32[128,32]{1,0:T(8,128)S(1)} %bitcast.165), dimensions={0,1} | broadcast | bytes 2113536 | tf_op jit(solution)/shard_map/broadcast_in_dim | solution.py:87
  29.9 1.9 %broadcast_in_dim.66.lower_ref = f32[128,32,128]{2,1,0:T(8,128)} broadcast(f32[128,32]{1,0:T(8,128)S(1)} %bitcast.164), dimensions={0,1} | broadcast | bytes 2113536 | tf_op jit(solution)/shard_map/broadcast_in_dim | solution.py:87
  31.8 1.9 %broadcast_in_dim.72.upper_ref = f32[128,32,128]{2,1,0:T(8,128)} broadcast(f32[128,32]{1,0:T(8,128)S(1)} %copy.155), dimensions={0,1} | broadcast | bytes 2113536 | tf_op jit(solution)/shard_map/broadcast_in_dim | solution.py:87
  33.8 5.9 %shard_map.94 = f32[128,32,128]{2,1,0:T(8,128)} custom-call(f32[128,32,128]{2,1,0:T(8,128)} %broadcast_in_dim.66.lower_ref, f32[128,32,128]{2,1,0:T(8,128)} %broadcast_in_dim.68.diagonal_ref, f32[128,32,128]{2,1,0:T(8,128)} %broadcast_in_dim.72.upper_ref), custom_call_target="tpu_custom_call" | custom-call | flops 8388608 | bytes 33554432 | tf_op jit(solution)/shard_map/pallas_call | solution.py:94
  39.8 2.3 %fusion = f32[32,128]{0,1:T(8,128)S(1)} fusion(f32[128,32,128]{2,1,0:T(8,128)} %shard_map.94, pred[128]{0:T(512)(128)(4,1)S(1)} %iota_compare_fusion.10), kind=kLoop, calls=%fused_computation.14 | loop fusion | flops 1044480 | bytes 2113664 | tf_op jit(solution)/shard_map/reduce_sum | solution.py:174
  42.4 1.1 collective-permute-done.7
  43.8 5.0 %all-to-all-done = bf16[4,4,2,128,128]{4,3,1,2,0:T(8,128)(2,1)S(1)} async-done(((bf16[4,4,2,128,128]{4,3,1,2,0:T(8,128)(2,1)}), bf16[4,4,2,128,128]{4,3,1,2,0:T(8,128)(2,1)S(1)}, u32[]{:S(2)}, u32[]{:S(2)}) %all-to-all-start) | async-done | bytes 1048608 | tf_op jit(solution)/shard_map/all_to_all | solution.py:166
  49.1 0.7 gather_fusion.4
  49.8 1.7 gather_fusion.3
  51.5 1.7 gather_fusion.2
  53.2 1.7 gather_fusion.1
  54.8 2.0 %fusion.18 = f32[16,2,128,128]{3,2,1,0:T(8,128)S(1)} fusion(bf16[16,2,128,128]{3,2,1,0:T(8,128)(2,1)} %gather_fusion.3, bf16[16,4,128,128]{3,2,1,0:T(8,128)(2,1)} %param.10), kind=kOutput, calls=%fused_computation.49 | convolution fusion | flops 134217728 | bytes 3670016 | tf_op jit(solution)/shard_map/tcd,tfdz->tfcz/dot_general | solution.py:187
  57.6 0.7 copy-done.7
  59.5 0.9 slice_reduce_fusion.1
  60.3 1.4 pad_maximum_fusion.3
  61.7 3.3 %fusion.3 = f32[16,2,128,128]{2,3,1,0:T(8,128)S(1)} fusion(f32[16,2,128,128]{3,2,1,0:T(8,128)S(1)} %add_add_fusion.1, f32[16,2,128,128]{3,1,0,2:T(2,128)S(1)} %bitcast.152), kind=kOutput, calls=%fused_computation.21 | convolution fusion | flops 805306368 | bytes 6291456 | tf_op jit(solution)/shard_map/tfzy,tfcy->tfcz/dot_general | solution.py:198
  65.6 1.4 fusion.81
  67.0 3.5 %collective-permute-done.1 = f32[2]{0:T(128)S(1)} collective-permute-done((f32[2]{0:T(128)S(1)}, f32[2]{0:T(128)S(1)}, u32[]{:S(2)}, u32[]{:S(2)}) %collective-permute-start.1) | collective-permute-done | bytes 40 | tf_op jit(solution)/shard_map/ppermute | solution.py:32
  70.5 1.4 fusion.83
  71.9 4.4 %collective-permute-done.2 = f32[2]{0:T(128)S(1)} collective-permute-done((f32[2]{0:T(128)S(1)}, f32[2]{0:T(128)S(1)}, u32[]{:S(2)}, u32[]{:S(2)}) %collective-permute-start.2) | collective-permute-done | bytes 40 | tf_op jit(solution)/shard_map/ppermute | solution.py:32
  76.4 1.5 collective-permute-start.3
  77.9 2.0 %collective-permute-done.3 = f32[2]{0:T(128)S(1)} collective-permute-done((f32[2]{0:T(128)S(1)}, f32[2]{0:T(128)S(1)}, u32[]{:S(2)}, u32[]{:S(2)}) %collective-permute-start.3) | collective-permute-done | bytes 40 | tf_op jit(solution)/shard_map/ppermute | solution.py:32
  79.9 1.5 collective-permute-start.4
  81.4 2.0 %collective-permute-done.4 = f32[2]{0:T(128)S(1)} collective-permute-done((f32[2]{0:T(128)S(1)}, f32[2]{0:T(128)S(1)}, u32[]{:S(2)}, u32[]{:S(2)}) %collective-permute-start.4) | collective-permute-done | bytes 40 | tf_op jit(solution)/shard_map/ppermute | solution.py:32
  85.5 0.7 multiply_subtract_fusion.1
  86.2 1.3 copy-done.4
  87.7 1.4 gather_fusion.5
  89.1 4.1 %all-to-all-start.1 = ((bf16[4,4,128,128]{2,3,1,0:T(8,128)(2,1)}), bf16[4,4,128,128]{2,3,1,0:T(8,128)(2,1)}, u32[]{:S(2)}, u32[]{:S(2)}) async-start(bf16[4,4,128,128]{2,3,1,0:T(8,128)(2,1)} %bitcast.50), calls=%async_computation.1 | async-start | bytes 1048576 | tf_op jit(solution)/shard_map/all_to_all | solution.py:222
  93.3 1.3 slice_bitcast_fusion.1
  94.6 1.4 gather_fusion.6
  96.0 7.7 %all-to-all-done.1 = bf16[4,4,128,128]{2,3,1,0:T(8,128)(2,1)} async-done(((bf16[4,4,128,128]{2,3,1,0:T(8,128)(2,1)}), bf16[4,4,128,128]{2,3,1,0:T(8,128)(2,1)}, u32[]{:S(2)}, u32[]{:S(2)}) %all-to-all-start.1) | async-done | bytes 524320 | tf_op jit(solution)/shard_map/all_to_all | solution.py:222
  103.7 3.7 %all-to-all-start.2 = ((bf16[4,4,128,128]{2,3,1,0:T(8,128)(2,1)}), bf16[4,4,128,128]{2,3,1,0:T(8,128)(2,1)S(1)}, u32[]{:S(2)}, u32[]{:S(2)}) async-start(bf16[4,4,128,128]{2,3,1,0:T(8,128)(2,1)} %bitcast.55), calls=%async_computation.2 | async-start | bytes 1048576 | tf_op jit(solution)/shard_map/all_to_all | solution.py:166
  107.3 2.1 %slice.229 = bf16[16,1,128,128]{2,3,1,0:T(8,128)(2,1)} slice(f32[16,2,128,128]{2,3,1,0:T(8,128)} %copy-done.4), slice={[0:16], [1:2], [0:128], [0:128]} | slice | bytes 1048576 | tf_op jit(solution)/shard_map/slice | solution.py:212
  109.5 0.9 convert_reduce_fusion
  110.4 7.0 %all-to-all-done.2 = bf16[4,4,128,128]{2,3,1,0:T(8,128)(2,1)S(1)} async-done(((bf16[4,4,128,128]{2,3,1,0:T(8,128)(2,1)}), bf16[4,4,128,128]{2,3,1,0:T(8,128)(2,1)S(1)}, u32[]{:S(2)}, u32[]{:S(2)}) %all-to-all-start.2) | async-done | bytes 524320 | tf_op jit(solution)/shard_map/all_to_all | solution.py:166
  117.4 2.7 %maximum_maximum_fusion = bf16[32,2,128,128]{2,3,1,0:T(8,128)(2,1)} fusion(bf16[16,1,128,128]{2,3,1,0:T(8,128)(2,1)S(1)} %bitcast.161, bf16[16,1,128,128]{2,3,1,0:T(8,128)(2,1)} %bitcast.53, bf16[16,1,128,128]{2,3,1,0:T(8,128)(2,1)} %slice.229, bf16[16,1,128,128]{2,3,1,0:T(8,128)(2,1)S(1)} %bitcast.156), kind=kLoop, calls=%fused_computation.12 | loop fusion | flops 3145728 | bytes 4194304 | tf_op jit(solution)/shard_map/concatenate | solution.py:184
  120.2 2.3 %gather_fusion.10 = bf16[16,2,128,128]{2,3,1,0:T(8,128)(2,1)S(1)} fusion(bf16[32,2,128,128]{2,3,1,0:T(8,128)(2,1)} %maximum_maximum_fusion, s32[1024]{0:T(1024)S(1)} %get-tuple-element.52), kind=kCustom, calls=%fused_computation.10 | custom fusion | bytes 2097216 | tf_op jit(solution)/shard_map/gather | solution.py:190
  122.5 3.3 %gather_fusion.9 = bf16[16,2,128,128]{2,3,1,0:T(8,128)(2,1)} fusion(bf16[32,2,128,128]{2,3,1,0:T(8,128)(2,1)} %maximum_maximum_fusion, s32[1024]{0:T(1024)S(1)} %get-tuple-element.53), kind=kCustom, calls=%fused_computation.9 | custom fusion | bytes 2097216 | tf_op jit(solution)/shard_map/gather | solution.py:190
  125.8 3.3 %gather_fusion.8 = bf16[16,2,128,128]{2,3,1,0:T(8,128)(2,1)} fusion(bf16[32,2,128,128]{2,3,1,0:T(8,128)(2,1)} %maximum_maximum_fusion, s32[1024]{0:T(1024)S(1)} %get-tuple-element.54), kind=kCustom, calls=%fused_computation.8 | custom fusion | bytes 2097216 | tf_op jit(solution)/shard_map/gather | solution.py:190
  129.0 3.2 %gather_fusion.7 = bf16[16,2,128,128]{2,3,1,0:T(8,128)(2,1)} fusion(bf16[32,2,128,128]{2,3,1,0:T(8,128)(2,1)} %maximum_maximum_fusion, s32[1024]{0:T(1024)S(1)} %get-tuple-element.55), kind=kCustom, calls=%fused_computation.7 | custom fusion | bytes 2097216 | tf_op jit(solution)/shard_map/gather | solution.py:190
  132.3 1.9 %fusion.24 = f32[16,2,128,128]{3,2,1,0:T(8,128)S(1)} fusion(bf16[16,2,128,128]{2,3,1,0:T(8,128)(2,1)} %gather_fusion.7, bf16[16,4,128,128]{3,2,1,0:T(8,128)(2,1)} %param.10), kind=kOutput, calls=%fused_computation.55 | convolution fusion | flops 134217728 | bytes 3670016 | tf_op jit(solution)/shard_map/tcd,tfdz->tfcz/dot_general | solution.py:187
  135.0 0.8 copy-done.6
  136.8 3.3 %fusion.1 = f32[16,2,128,128]{2,3,1,0:T(8,128)S(1)} fusion(f32[16,2,128,128]{3,2,1,0:T(8,128)S(1)} %add_add_fusion, f32[16,2,128,128]{3,1,0,2:T(2,128)S(1)} %bitcast.153), kind=kOutput, calls=%fused_computation.19 | convolution fusion | flops 805306368 | bytes 6291456 | tf_op jit(solution)/shard_map/tfzy,tfcy->tfcz/dot_general | solution.py:198
  140.1 0.9 slice_reduce_fusion
  141.0 1.4 pad_maximum_fusion.4
  143.5 1.4 fusion.80
  145.0 3.3 %collective-permute-done.9 = f32[2]{0:T(128)S(1)} collective-permute-done((f32[2]{0:T(128)S(1)}, f32[2]{0:T(128)S(1)}, u32[]{:S(2)}, u32[]{:S(2)}) %collective-permute-start.9) | collective-permute-done | bytes 40 | tf_op jit(solution)/shard_map/ppermute | solution.py:32
  148.4 1.4 fusion.82
  149.8 4.4 %collective-permute-done.10 = f32[2]{0:T(128)S(1)} collective-permute-done((f32[2]{0:T(128)S(1)}, f32[2]{0:T(128)S(1)}, u32[]{:S(2)}, u32[]{:S(2)}) %collective-permute-start.10) | collective-permute-done | bytes 40 | tf_op jit(solution)/shard_map/ppermute | solution.py:32
  154.2 1.5 collective-permute-start.11
  155.7 2.0 %collective-permute-done.11 = f32[2]{0:T(128)S(1)} collective-permute-done((f32[2]{0:T(128)S(1)}, f32[2]{0:T(128)S(1)}, u32[]{:S(2)}, u32[]{:S(2)}) %collective-permute-start.11) | collective-permute-done | bytes 40 | tf_op jit(solution)/shard_map/ppermute | solution.py:32
  157.7 1.5 collective-permute-start.12
  159.3 2.0 %collective-permute-done.12 = f32[2]{0:T(128)S(1)} collective-permute-done((f32[2]{0:T(128)S(1)}, f32[2]{0:T(128)S(1)}, u32[]{:S(2)}, u32[]{:S(2)}) %collective-permute-start.12) | collective-permute-done | bytes 40 | tf_op jit(solution)/shard_map/ppermute | solution.py:32
  163.9 0.7 multiply_subtract_fusion
  164.9 1.0 copy.170
  165.9 1.0 copy.169
  (117 shorter events, 12.8 us)
Async XLA Ops:
  0.6 25.5 %copy-start = (f32[2,8]{1,0:T(2,128)S(1)}, f32[2,8]{1,0:T(2,128)}, u32[]{:S(2)}) copy-start(f32[2,8]{1,0:T(2,128)} %param.12) | copy-start | bytes 196
  1.3 25.1 %collective-permute-start.5 = (s32[16,1]{0,1:T(1,128)S(1)}, s32[16,1]{0,1:T(1,128)S(1)}, u32[]{:S(2)}, u32[]{:S(2)}) collective-permute-start(s32[16,1]{0,1:T(1,128)S(1)} %slice.108), channel_id=1, source_target_pairs={{1,0},{3,2},{5,4},{7,6},{9,8},{11,10},{13,12},{15,14},{17,16},{19,... | collective-permute-start | bytes 200 | tf_op jit(solution)/shard_map/ppermute | solution.py:17
  19.4 4.7 %copy-start.5 = (bf16[16,128,128]{2,1,0:T(8,128)(2,1)S(1)}, bf16[16,128,128]{2,1,0:T(8,128)(2,1)}, u32[]{:S(2)}) copy-start(bf16[16,128,128]{2,1,0:T(8,128)(2,1)} %param.7) | copy-start | bytes 1572868
  19.4 5.6 %copy-start.11 = (s32[16,4]{0,1:T(4,128)S(1)}, s32[16,4]{0,1:T(4,128)}, u32[]{:S(2)}) copy-start(s32[16,4]{0,1:T(4,128)} %param.11) | copy-start | bytes 772
  19.4 7.2 %copy-start.12 = (f32[8]{0:T(128)S(1)}, f32[8]{0:T(128)}, u32[]{:S(2)}) copy-start(f32[8]{0:T(128)} %param.13) | copy-start | bytes 100
  20.6 28.2 %all-to-all-start = ((bf16[4,4,2,128,128]{4,3,1,2,0:T(8,128)(2,1)}), bf16[4,4,2,128,128]{4,3,1,2,0:T(8,128)(2,1)S(1)}, u32[]{:S(2)}, u32[]{:S(2)}) async-start(bf16[4,4,2,128,128]{4,3,1,2,0:T(8,128)(2,1)} %copy.138), calls=%async_computation | async-start | bytes 2097152 | tf_op jit(solution)/shard_map/all_to_all | solution.py:166
  39.8 9.1 %copy-start.10 = (bf16[16,128,128]{2,1,0:T(8,128)(2,1)S(1)}, bf16[16,128,128]{2,1,0:T(8,128)(2,1)}, u32[]{:S(2)}) copy-start(bf16[16,128,128]{2,1,0:T(8,128)(2,1)} %param.8) | copy-start | bytes 1572868
  42.4 1.1 collective-permute-start.7
  54.8 2.1 %copy-start.2 = (bf16[16,4,128,128]{3,2,1,0:T(8,128)(2,1)S(1)}, bf16[16,4,128,128]{3,2,1,0:T(8,128)(2,1)}, u32[]{:S(2)}) copy-start(bf16[16,4,128,128]{3,2,1,0:T(8,128)(2,1)} %param.10) | copy-start | bytes 6291460
  54.8 2.3 %copy-start.9 = (bf16[16,2,128,128]{3,2,1,0:T(8,128)(2,1)S(1)}, bf16[16,2,128,128]{3,2,1,0:T(8,128)(2,1)}, u32[]{:S(2)}) copy-start(bf16[16,2,128,128]{3,2,1,0:T(8,128)(2,1)} %gather_fusion.1) | copy-start | bytes 3145732
  57.1 1.2 copy-start.7
  58.9 2.9 %copy-start.1 = (f32[128,32,128]{2,1,0:T(8,128)S(1)}, f32[128,32,128]{2,1,0:T(8,128)}, u32[]{:S(2)}) copy-start(f32[128,32,128]{2,1,0:T(8,128)} %shard_map.94) | copy-start | bytes 6291460
  61.7 3.9 %collective-permute-start = (f32[2]{0:T(128)S(1)}, f32[2]{0:T(128)S(1)}, u32[]{:S(2)}, u32[]{:S(2)}) collective-permute-start(f32[2]{0:T(128)S(1)} %pad_maximum_fusion.3), channel_id=1, source_target_pairs={{0,1},{1,0},{2,3},{3,2},{4,5},{5,4},{6,7},{7,6},{8,9},{9,8},{10,11... | collective-permute-start | bytes 32 | tf_op jit(solution)/shard_map/ppermute | solution.py:32
  65.1 20.3 %collective-permute-start.6 = (f32[16,2,128]{2,1,0:T(2,128)S(1)}, f32[16,2,128]{2,1,0:T(2,128)S(1)}, u32[]{:S(2)}, u32[]{:S(2)}) collective-permute-start(f32[16,2,128]{2,1,0:T(2,128)S(1)} %bitcast.174), channel_id=1, source_target_pairs={{0,1},{1,0},{2,3},{3,2},{4,5},{5,4},{6,7},{7,6},{8,9},{9,8},{10,11... | collective-permute-start | bytes 49160 | tf_op jit(solution)/shard_map/ppermute | solution.py:21
  67.0 3.5 %collective-permute-start.1 = (f32[2]{0:T(128)S(1)}, f32[2]{0:T(128)S(1)}, u32[]{:S(2)}, u32[]{:S(2)}) collective-permute-start(f32[2]{0:T(128)S(1)} %fusion.81), channel_id=1, source_target_pairs={{0,2},{2,0},{4,6},{6,4},{1,3},{3,1},{5,7},{7,5},{8,10},{10,8},{12,... | collective-permute-start | bytes 32 | tf_op jit(solution)/shard_map/ppermute | solution.py:32
  71.9 4.4 %collective-permute-start.2 = (f32[2]{0:T(128)S(1)}, f32[2]{0:T(128)S(1)}, u32[]{:S(2)}, u32[]{:S(2)}) collective-permute-start(f32[2]{0:T(128)S(1)} %fusion.83), channel_id=1, source_target_pairs={{0,4},{2,6},{4,0},{6,2},{1,5},{3,7},{5,1},{7,3},{8,12},{10,14},{12... | collective-permute-start | bytes 32 | tf_op jit(solution)/shard_map/ppermute | solution.py:32
  76.4 3.5 %collective-permute-start.3 = (f32[2]{0:T(128)S(1)}, f32[2]{0:T(128)S(1)}, u32[]{:S(2)}, u32[]{:S(2)}) collective-permute-start(f32[2]{0:T(128)S(1)} %add.219), channel_id=1, source_target_pairs={{0,8},{8,0},{16,24},{24,16},{1,9},{9,1},{17,25},{25,17},{2,10},{10... | collective-permute-start | bytes 32 | tf_op jit(solution)/shard_map/ppermute | solution.py:32
  79.9 3.5 %collective-permute-start.4 = (f32[2]{0:T(128)S(1)}, f32[2]{0:T(128)S(1)}, u32[]{:S(2)}, u32[]{:S(2)}) collective-permute-start(f32[2]{0:T(128)S(1)} %add.220), channel_id=1, source_target_pairs={{0,16},{8,24},{16,0},{24,8},{1,17},{9,25},{17,1},{25,9},{2,18},{10... | collective-permute-start | bytes 32 | tf_op jit(solution)/shard_map/ppermute | solution.py:32
  86.2 1.4 copy-start.4
  89.1 14.6 %all-to-all-start.1 = ((bf16[4,4,128,128]{2,3,1,0:T(8,128)(2,1)}), bf16[4,4,128,128]{2,3,1,0:T(8,128)(2,1)}, u32[]{:S(2)}, u32[]{:S(2)}) async-start(bf16[4,4,128,128]{2,3,1,0:T(8,128)(2,1)} %bitcast.50), calls=%async_computation.1 | async-start | bytes 1048576 | tf_op jit(solution)/shard_map/all_to_all | solution.py:222
  103.7 13.7 %all-to-all-start.2 = ((bf16[4,4,128,128]{2,3,1,0:T(8,128)(2,1)}), bf16[4,4,128,128]{2,3,1,0:T(8,128)(2,1)S(1)}, u32[]{:S(2)}, u32[]{:S(2)}) async-start(bf16[4,4,128,128]{2,3,1,0:T(8,128)(2,1)} %bitcast.55), calls=%async_computation.2 | async-start | bytes 1048576 | tf_op jit(solution)/shard_map/all_to_all | solution.py:166
  132.3 2.1 %copy-start.3 = (bf16[16,4,128,128]{3,2,1,0:T(8,128)(2,1)S(1)}, bf16[16,4,128,128]{3,2,1,0:T(8,128)(2,1)}, u32[]{:S(2)}) copy-start(bf16[16,4,128,128]{3,2,1,0:T(8,128)(2,1)} %param.10) | copy-start | bytes 6291460
  132.3 2.3 %copy-start.8 = (bf16[16,2,128,128]{2,3,1,0:T(8,128)(2,1)S(1)}, bf16[16,2,128,128]{2,3,1,0:T(8,128)(2,1)}, u32[]{:S(2)}) copy-start(bf16[16,2,128,128]{2,3,1,0:T(8,128)(2,1)} %gather_fusion.8) | copy-start | bytes 3145732
  134.6 1.2 copy-start.6
  142.4 1.1 collective-permute-start.8
  142.4 21.4 %collective-permute-start.13 = (f32[16,2,128]{2,1,0:T(2,128)S(1)}, f32[16,2,128]{2,1,0:T(2,128)S(1)}, u32[]{:S(2)}, u32[]{:S(2)}) collective-permute-start(f32[16,2,128]{2,1,0:T(2,128)S(1)} %select_bitcast_fusion), channel_id=1, source_target_pairs={{0,1},{1,0},{2,3},{3,2},{4,5},{5,4},{6,7},{7,6},{8,9},{9,8},{10,11... | collective-permute-start | bytes 49160 | tf_op jit(solution)/shard_map/ppermute | solution.py:21
  144.8 3.5 %collective-permute-start.9 = (f32[2]{0:T(128)S(1)}, f32[2]{0:T(128)S(1)}, u32[]{:S(2)}, u32[]{:S(2)}) collective-permute-start(f32[2]{0:T(128)S(1)} %fusion.80), channel_id=1, source_target_pairs={{0,2},{2,0},{4,6},{6,4},{1,3},{3,1},{5,7},{7,5},{8,10},{10,8},{12,... | collective-permute-start | bytes 32 | tf_op jit(solution)/shard_map/ppermute | solution.py:32
  149.7 4.4 %collective-permute-start.10 = (f32[2]{0:T(128)S(1)}, f32[2]{0:T(128)S(1)}, u32[]{:S(2)}, u32[]{:S(2)}) collective-permute-start(f32[2]{0:T(128)S(1)} %fusion.82), channel_id=1, source_target_pairs={{0,4},{2,6},{4,0},{6,2},{1,5},{3,7},{5,1},{7,3},{8,12},{10,14},{12... | collective-permute-start | bytes 32 | tf_op jit(solution)/shard_map/ppermute | solution.py:32
  154.2 3.5 %collective-permute-start.11 = (f32[2]{0:T(128)S(1)}, f32[2]{0:T(128)S(1)}, u32[]{:S(2)}, u32[]{:S(2)}) collective-permute-start(f32[2]{0:T(128)S(1)} %add.237), channel_id=1, source_target_pairs={{0,8},{8,0},{16,24},{24,16},{1,9},{9,1},{17,25},{25,17},{2,10},{10... | collective-permute-start | bytes 32 | tf_op jit(solution)/shard_map/ppermute | solution.py:32
  157.7 3.5 %collective-permute-start.12 = (f32[2]{0:T(128)S(1)}, f32[2]{0:T(128)S(1)}, u32[]{:S(2)}, u32[]{:S(2)}) collective-permute-start(f32[2]{0:T(128)S(1)} %add.238), channel_id=1, source_target_pairs={{0,16},{8,24},{16,0},{24,8},{1,17},{9,25},{17,1},{25,9},{2,18},{10... | collective-permute-start | bytes 32 | tf_op jit(solution)/shard_map/ppermute | solution.py:32

commit v17 on v14

--- a/solution.py
+++ b/solution.py
@@ -192,6 +192,12 @@
             )
         last = step_index + 1 == STEPS
         partial = jnp.stack([jnp.sum(fields[:, 0], dtype=jnp.float32), jnp.sum(advected[:, 0])])
+        if last:
+            partial = butterfly_sum(partial, ("gz",))
+            advected, partial = lax.optimization_barrier((advected, partial))
+            totals = butterfly_sum(partial, ("gy", "gx"))
+        else:
+            totals = butterfly_sum(partial, ("gz", "gy", "gx"))
         solved = jnp.einsum(
             "tfzy,tfcy->tfcz",
             inverse,
@@ -200,9 +206,7 @@
             preferred_element_type=jnp.float32,
         )
         edge_value = jnp.where(my_layer == 0, solved[..., -1], solved[..., 0])
-        carried = from_partner(jnp.concatenate([edge_value.reshape(-1), partial]), "gz", 0)
-        other_value = carried[: edge_value.size].reshape(edge_value.shape)
-        totals = butterfly_sum(partial + carried[edge_value.size :], ("gy", "gx"))
+        other_value = from_partner(edge_value, "gz", 0)
         low_value = jnp.where(my_layer == 0, edge_value, other_value)
         high_value = jnp.where(my_layer == 0, other_value, edge_value)
         lower_end, upper_end = interface_values(low_value, low_spike, high_value, high_spike)

time: 172 us -> 166 us (0.965)
  other arithmetic: 25.7 us -> 22.3 us
  local copies, waits for them, and re-layouts: 44.6 us -> 41.2 us
  waiting for transfers between devices: 35.7 us -> 38.3 us
    ppermute x8 -> x10, waiting for transfers between devices: 18.2 us -> 22.8 us  [butterfly_sum(): lax.ppermute(value, axis, [(i, i ^ bit) for i in range(devices)])]
    concatenate x2 -> x0, local copies, waits for them, and re-layouts: 2.75 us -> none  [per_device(): jnp.concatenate([edge_value.reshape(-1), partial])]
    add x2 -> x0, other arithmetic: 2.74 us -> none  [per_device(): totals = butterfly_sum(partial + carried[edge_value.size:], ('gy', 'gx'))]
    another operation x0 -> x2, other arithmetic: none -> 2.73 us  [per_device(): jnp.stack([jnp.sum(fields[:, 0], dtype=jnp.float32), jnp.sum(advected[:,...]
    sub x2, other arithmetic: 3.87 us -> 1.41 us  [per_device(): unscaled = solved - spike_column[:, :, None, :] * needed[..., None]]
    select_n x2, other arithmetic: 2.28 us -> 0.23 us  [per_device(): needed = jnp.where(my_layer == 0, upper_end, lower_end)]
    ppermute x8 -> x10, starting transfers between devices: 14.3 us -> 12.8 us  [butterfly_sum(): lax.ppermute(value, axis, [(i, i ^ bit) for i in range(devices)])]
    add x8 -> x10, other arithmetic: 2.75 us -> 4.12 us  [butterfly_sum(): value + lax.ppermute(value, axis, [(i, i ^ bit) for i in range(devices)])]
  transfers between devices with their start and end apart: 15 -> 17, of which waited for: 11 -> 14; matrix products, arithmetic and copies ran while one was open for 26% -> 18% of each run, Pallas kernels for 3% -> 4%
where the time goes in v17:
time: 166 us; the launch traced here: 165 us
  local copies, waits for them, and re-layouts  41.2 us (25%)
  waiting for transfers between devices  38.3 us (23%)
  starting transfers between devices  25.8 us (16%)
  other arithmetic  22.3 us (13%)
  matrix products  14.2 us (9%)
  blocking collectives  13.7 us (8%)
  Pallas kernels  5.94 us (4%)
  between operations  3.82 us (2%)
    ppermute x10, waiting for transfers between devices, butterfly_sum(): lax.ppermute(value, axis, [(i, i ^ bit) for i in range(devices)])  22.8 us
    gather x8, local copies, waits for them, and re-layouts, per_device(): tile_pool[pool_index[:, entry_k]]  17.8 us
    all_to_all x3, waiting for transfers between devices, exchange(): lax.all_to_all(tiles[wanted], 'gy', split_axis=0, concat_axis=0, tiled=True)  14 us
    unnamed x1, blocking collectives  13.7 us
    ppermute x10, starting transfers between devices, butterfly_sum(): lax.ppermute(value, axis, [(i, i ^ bit) for i in range(devices)])  12.8 us
    all_to_all x3, starting transfers between devices, exchange(): lax.all_to_all(tiles[wanted], 'gy', split_axis=0, concat_axis=0, tiled=True)  11.4 us
    dot_general x8, matrix products, per_device(): jnp.einsum('tcd,tfdz->tfcz', interp_weights[:, entry_k], tile_pool[pool_i...  6.92 us
    unnamed x30, local copies, waits for them, and re-layouts  6.84 us
  transfers between devices with their start and end apart: 17, of which 14 were waited for; matrix products, arithmetic and copies ran while one was open for 18% of the time, Pallas kernels for 4%

profile of v17, /device:TPU:0, one launch (start us, length us, event | category | flops | bytes accessed | tf_op | source)
XLA Modules:
  0.0 165.2 jit_solution(12473538044349414152)
XLA Ops:
  1.3 1.3 collective-permute-start.5
  2.6 13.7 %all-gather.1 = s32[4,16,4]{1,2,0:T(4,128)S(1)} all-gather(s32[1,16,4]{1,2,0:T(4,128)} %bitcast.173), channel_id=3, replica_groups=[8,4]<=[4,4,2]T(0,2,1), dimensions={0}, use_global_device_ids=true | all-gather | bytes 1280 | tf_op args[2]
  17.3 1.3 pad_maximum_fusion.1
  18.7 0.7 gather_fusion
  19.5 1.1 copy.138
  20.6 3.5 %all-to-all-start = ((bf16[4,4,2,128,128]{4,3,1,2,0:T(8,128)(2,1)}), bf16[4,4,2,128,128]{4,3,1,2,0:T(8,128)(2,1)S(1)}, u32[]{:S(2)}, u32[]{:S(2)}) async-start(bf16[4,4,2,128,128]{4,3,1,2,0:T(8,128)(2,1)} %copy.138), calls=%async_computation | async-start | bytes 2097152 | tf_op jit(solution)/shard_map/all_to_all | solution.py:166
  24.1 0.9 convert_reduce_fusion.1
  28.0 1.9 %broadcast_in_dim.68.diagonal_ref = f32[128,32,128]{2,1,0:T(8,128)} broadcast(f32[128,32]{1,0:T(8,128)S(1)} %bitcast.156), dimensions={0,1} | broadcast | bytes 2113536 | tf_op jit(solution)/shard_map/broadcast_in_dim | solution.py:87
  29.9 1.9 %broadcast_in_dim.66.lower_ref = f32[128,32,128]{2,1,0:T(8,128)} broadcast(f32[128,32]{1,0:T(8,128)S(1)} %bitcast.155), dimensions={0,1} | broadcast | bytes 2113536 | tf_op jit(solution)/shard_map/broadcast_in_dim | solution.py:87
  31.8 1.9 %broadcast_in_dim.72.upper_ref = f32[128,32,128]{2,1,0:T(8,128)} broadcast(f32[128,32]{1,0:T(8,128)S(1)} %copy.155), dimensions={0,1} | broadcast | bytes 2113536 | tf_op jit(solution)/shard_map/broadcast_in_dim | solution.py:87
  33.8 5.9 %shard_map.94 = f32[128,32,128]{2,1,0:T(8,128)} custom-call(f32[128,32,128]{2,1,0:T(8,128)} %broadcast_in_dim.66.lower_ref, f32[128,32,128]{2,1,0:T(8,128)} %broadcast_in_dim.68.diagonal_ref, f32[128,32,128]{2,1,0:T(8,128)} %broadcast_in_dim.72.upper_ref), custom_call_target="tpu_custom_call" | custom-call | flops 8388608 | bytes 33554432 | tf_op jit(solution)/shard_map/pallas_call | solution.py:94
  39.8 2.3 %fusion = f32[32,128]{0,1:T(8,128)S(1)} fusion(f32[128,32,128]{2,1,0:T(8,128)} %shard_map.94, pred[128]{0:T(512)(128)(4,1)S(1)} %iota_compare_fusion.10), kind=kLoop, calls=%fused_computation.14 | loop fusion | flops 1044480 | bytes 2113664 | tf_op jit(solution)/shard_map/reduce_sum | solution.py:174
  42.4 1.1 collective-permute-done.7
  43.8 5.0 %all-to-all-done = bf16[4,4,2,128,128]{4,3,1,2,0:T(8,128)(2,1)S(1)} async-done(((bf16[4,4,2,128,128]{4,3,1,2,0:T(8,128)(2,1)}), bf16[4,4,2,128,128]{4,3,1,2,0:T(8,128)(2,1)S(1)}, u32[]{:S(2)}, u32[]{:S(2)}) %all-to-all-start) | async-done | bytes 1048608 | tf_op jit(solution)/shard_map/all_to_all | solution.py:166
  49.1 0.7 gather_fusion.4
  49.8 1.7 %gather_fusion.3 = bf16[16,2,128,128]{3,2,1,0:T(8,128)(2,1)} fusion(bf16[32,2,128,128]{3,2,1,0:T(8,128)(2,1)S(1)} %pad_maximum_fusion, s32[1024]{0:T(1024)S(1)} %get-tuple-element.55), kind=kCustom, calls=%fused_computation.3 | custom fusion | bytes 2097216 | tf_op jit(solution)/shard_map/gather | solution.py:190
  51.5 1.7 %gather_fusion.2 = bf16[16,2,128,128]{3,2,1,0:T(8,128)(2,1)} fusion(bf16[32,2,128,128]{3,2,1,0:T(8,128)(2,1)S(1)} %pad_maximum_fusion, s32[1024]{0:T(1024)S(1)} %get-tuple-element.56), kind=kCustom, calls=%fused_computation.2 | custom fusion | bytes 2097216 | tf_op jit(solution)/shard_map/gather | solution.py:190
  53.2 1.7 %gather_fusion.1 = bf16[16,2,128,128]{3,2,1,0:T(8,128)(2,1)} fusion(bf16[32,2,128,128]{3,2,1,0:T(8,128)(2,1)S(1)} %pad_maximum_fusion, s32[1024]{0:T(1024)S(1)} %get-tuple-element.57), kind=kCustom, calls=%fused_computation.1 | custom fusion | bytes 2097216 | tf_op jit(solution)/shard_map/gather | solution.py:190
  54.8 2.0 %fusion.16 = f32[16,2,128,128]{3,2,1,0:T(8,128)S(1)} fusion(bf16[16,2,128,128]{3,2,1,0:T(8,128)(2,1)} %gather_fusion.3, bf16[16,4,128,128]{3,2,1,0:T(8,128)(2,1)} %param.10), kind=kOutput, calls=%fused_computation.47 | convolution fusion | flops 134217728 | bytes 3670016 | tf_op jit(solution)/shard_map/tcd,tfdz->tfcz/dot_general | solution.py:187
  57.6 0.7 copy-done.7
  59.5 1.0 copy-done.1
  60.4 3.3 %fusion.3 = f32[16,2,128,128]{2,3,1,0:T(8,128)S(1)} fusion(f32[16,2,128,128]{3,2,1,0:T(8,128)S(1)} %add_add_fusion, f32[16,2,128,128]{3,1,0,2:T(2,128)S(1)} %bitcast.144), kind=kOutput, calls=%fused_computation.21 | convolution fusion | flops 805306368 | bytes 6291456 | tf_op jit(solution)/shard_map/tfzy,tfcy->tfcz/dot_general | solution.py:201
  63.9 0.9 slice_reduce_fusion.1
  65.2 0.7 multiply_subtract_fusion.1
  65.9 1.3 copy-done.4
  67.3 1.4 gather_fusion.6
  68.7 3.7 %all-to-all-start.2 = ((bf16[4,4,128,128]{2,3,1,0:T(8,128)(2,1)}), bf16[4,4,128,128]{2,3,1,0:T(8,128)(2,1)S(1)}, u32[]{:S(2)}, u32[]{:S(2)}) async-start(bf16[4,4,128,128]{2,3,1,0:T(8,128)(2,1)} %bitcast.53), calls=%async_computation.2 | async-start | bytes 1048576 | tf_op jit(solution)/shard_map/all_to_all | solution.py:166
  72.4 1.4 pad_maximum_fusion.3
  74.0 0.9 collective-permute-done
  74.9 1.4 fusion.80
  76.3 2.0 %collective-permute-start.1 = (f32[2]{0:T(128)S(1)}, f32[2]{0:T(128)S(1)}, u32[]{:S(2)}, u32[]{:S(2)}) collective-permute-start(f32[2]{0:T(128)S(1)} %fusion.80), channel_id=1, source_target_pairs={{0,2},{2,0},{4,6},{6,4},{1,3},{3,1},{5,7},{7,5},{8,10},{10,8},{12,... | collective-permute-start | bytes 32 | tf_op jit(solution)/shard_map/ppermute | solution.py:32
  78.2 3.5 %collective-permute-done.1 = f32[2]{0:T(128)S(1)} collective-permute-done((f32[2]{0:T(128)S(1)}, f32[2]{0:T(128)S(1)}, u32[]{:S(2)}, u32[]{:S(2)}) %collective-permute-start.1) | collective-permute-done | bytes 40 | tf_op jit(solution)/shard_map/ppermute | solution.py:32
  81.7 1.4 fusion.81
  83.1 4.5 %collective-permute-start.2 = (f32[2]{0:T(128)S(1)}, f32[2]{0:T(128)S(1)}, u32[]{:S(2)}, u32[]{:S(2)}) collective-permute-start(f32[2]{0:T(128)S(1)} %fusion.81), channel_id=1, source_target_pairs={{0,4},{2,6},{4,0},{6,2},{1,5},{3,7},{5,1},{7,3},{8,12},{10,14},{12... | collective-permute-start | bytes 32 | tf_op jit(solution)/shard_map/ppermute | solution.py:32
  87.6 1.5 collective-permute-done.2
  89.1 1.5 collective-permute-start.3
  90.6 2.0 %collective-permute-done.3 = f32[2]{0:T(128)S(1)} collective-permute-done((f32[2]{0:T(128)S(1)}, f32[2]{0:T(128)S(1)}, u32[]{:S(2)}, u32[]{:S(2)}) %collective-permute-start.3) | collective-permute-done | bytes 40 | tf_op jit(solution)/shard_map/ppermute | solution.py:32
  92.7 1.5 collective-permute-start.4
  94.2 2.0 %collective-permute-done.4 = f32[2]{0:T(128)S(1)} collective-permute-done((f32[2]{0:T(128)S(1)}, f32[2]{0:T(128)S(1)}, u32[]{:S(2)}, u32[]{:S(2)}) %collective-permute-start.4) | collective-permute-done | bytes 40 | tf_op jit(solution)/shard_map/ppermute | solution.py:32
  98.1 2.1 %convert_reduce_fusion = (f32[]{:T(128)}, bf16[16,1,128,128]{2,3,1,0:T(8,128)(2,1)S(1)}) fusion(f32[16,2,128,128]{2,3,1,0:T(8,128)} %copy-done.4, f32[]{:T(128)} %bitcast.22), kind=kLoop, calls=%fused_computation.39 | loop fusion | flops 1048575 | bytes 1572872 | tf_op jit(solution)/shard_map/reduce_sum | solution.py:194
  100.3 1.4 gather_fusion.5
  101.7 4.2 %all-to-all-start.1 = ((bf16[4,4,128,128]{2,3,1,0:T(8,128)(2,1)}), bf16[4,4,128,128]{2,3,1,0:T(8,128)(2,1)}, u32[]{:S(2)}, u32[]{:S(2)}) async-start(bf16[4,4,128,128]{2,3,1,0:T(8,128)(2,1)} %bitcast.50), calls=%async_computation.1 | async-start | bytes 1048576 | tf_op jit(solution)/shard_map/all_to_all | solution.py:166
  105.9 2.1 %slice.225 = bf16[16,1,128,128]{2,3,1,0:T(8,128)(2,1)} slice(f32[16,2,128,128]{2,3,1,0:T(8,128)} %copy-done.4), slice={[0:16], [1:2], [0:128], [0:128]} | slice | bytes 1048576 | tf_op jit(solution)/shard_map/slice | solution.py:215
  108.0 9.0 %all-to-all-done.1 = bf16[4,4,128,128]{2,3,1,0:T(8,128)(2,1)} async-done(((bf16[4,4,128,128]{2,3,1,0:T(8,128)(2,1)}), bf16[4,4,128,128]{2,3,1,0:T(8,128)(2,1)}, u32[]{:S(2)}, u32[]{:S(2)}) %all-to-all-start.1) | async-done | bytes 524320 | tf_op jit(solution)/shard_map/all_to_all | solution.py:166
  117.0 2.7 %maximum_maximum_fusion = bf16[32,2,128,128]{2,3,1,0:T(8,128)(2,1)} fusion(bf16[16,1,128,128]{2,3,1,0:T(8,128)(2,1)S(1)} %bitcast.152, bf16[16,1,128,128]{2,3,1,0:T(8,128)(2,1)} %bitcast.51, bf16[16,1,128,128]{2,3,1,0:T(8,128)(2,1)} %slice.225, bf16[16,1,128,128]{2,3,1,0:T(8,128)(2,1)S(1)} %get-tuple-element.35), kind=kLoop, calls=%fused_computation.12 | loop fusion | flops 3145728 | bytes 4194304 | tf_op jit(solution)/shard_map/concatenate | solution.py:184
  119.8 2.3 %gather_fusion.10 = bf16[16,2,128,128]{2,3,1,0:T(8,128)(2,1)S(1)} fusion(bf16[32,2,128,128]{2,3,1,0:T(8,128)(2,1)} %maximum_maximum_fusion, s32[1024]{0:T(1024)S(1)} %get-tuple-element.54), kind=kCustom, calls=%fused_computation.10 | custom fusion | bytes 2097216 | tf_op jit(solution)/shard_map/gather | solution.py:190
  122.1 3.3 %gather_fusion.9 = bf16[16,2,128,128]{2,3,1,0:T(8,128)(2,1)} fusion(bf16[32,2,128,128]{2,3,1,0:T(8,128)(2,1)} %maximum_maximum_fusion, s32[1024]{0:T(1024)S(1)} %get-tuple-element.55), kind=kCustom, calls=%fused_computation.9 | custom fusion | bytes 2097216 | tf_op jit(solution)/shard_map/gather | solution.py:190
  125.4 3.3 %gather_fusion.8 = bf16[16,2,128,128]{2,3,1,0:T(8,128)(2,1)} fusion(bf16[32,2,128,128]{2,3,1,0:T(8,128)(2,1)} %maximum_maximum_fusion, s32[1024]{0:T(1024)S(1)} %get-tuple-element.56), kind=kCustom, calls=%fused_computation.8 | custom fusion | bytes 2097216 | tf_op jit(solution)/shard_map/gather | solution.py:190
  128.6 3.2 %gather_fusion.7 = bf16[16,2,128,128]{2,3,1,0:T(8,128)(2,1)} fusion(bf16[32,2,128,128]{2,3,1,0:T(8,128)(2,1)} %maximum_maximum_fusion, s32[1024]{0:T(1024)S(1)} %get-tuple-element.57), kind=kCustom, calls=%fused_computation.7 | custom fusion | bytes 2097216 | tf_op jit(solution)/shard_map/gather | solution.py:190
  131.9 1.9 %fusion.22 = f32[16,2,128,128]{3,2,1,0:T(8,128)S(1)} fusion(bf16[16,2,128,128]{2,3,1,0:T(8,128)(2,1)} %gather_fusion.7, bf16[16,4,128,128]{3,2,1,0:T(8,128)(2,1)} %param.10), kind=kOutput, calls=%fused_computation.53 | convolution fusion | flops 134217728 | bytes 3670016 | tf_op jit(solution)/shard_map/tcd,tfdz->tfcz/dot_general | solution.py:187
  134.6 0.8 copy-done.6
  136.4 0.9 slice_reduce_fusion
  137.3 1.4 pad_maximum_fusion.4
  138.7 1.1 collective-permute-done.8
  139.8 1.4 fusion.79
  141.2 3.3 %fusion.1 = f32[16,2,128,128]{2,3,1,0:T(8,128)S(1)} fusion(f32[16,2,128,128]{2,3,1,0:T(8,128)S(1)} %add_bitcast_fusion, f32[16,2,128,128]{3,1,0,2:T(2,128)S(1)} %bitcast.145), kind=kOutput, calls=%fused_computation.19 | convolution fusion | flops 805306368 | bytes 6291456 | tf_op jit(solution)/shard_map/tfzy,tfcy->tfcz/dot_general | solution.py:201
  144.9 3.2 %collective-permute-done.9 = f32[2]{0:T(128)S(1)} collective-permute-done((f32[2]{0:T(128)S(1)}, f32[2]{0:T(128)S(1)}, u32[]{:S(2)}, u32[]{:S(2)}) %collective-permute-start.9) | collective-permute-done | bytes 40 | tf_op jit(solution)/shard_map/ppermute | solution.py:32
  148.1 4.4 %collective-permute-done.10 = f32[2]{0:T(128)S(1)} collective-permute-done((f32[2]{0:T(128)S(1)}, f32[2]{0:T(128)S(1)}, u32[]{:S(2)}, u32[]{:S(2)}) %collective-permute-start.10) | collective-permute-done | bytes 40 | tf_op jit(solution)/shard_map/ppermute | solution.py:32
  152.5 1.5 collective-permute-start.11
  154.0 2.0 %collective-permute-done.11 = f32[2]{0:T(128)S(1)} collective-permute-done((f32[2]{0:T(128)S(1)}, f32[2]{0:T(128)S(1)}, u32[]{:S(2)}, u32[]{:S(2)}) %collective-permute-start.11) | collective-permute-done | bytes 40 | tf_op jit(solution)/shard_map/ppermute | solution.py:32
  156.1 1.5 collective-permute-start.12
  157.6 2.0 %collective-permute-done.12 = f32[2]{0:T(128)S(1)} collective-permute-done((f32[2]{0:T(128)S(1)}, f32[2]{0:T(128)S(1)}, u32[]{:S(2)}, u32[]{:S(2)}) %collective-permute-start.12) | collective-permute-done | bytes 40 | tf_op jit(solution)/shard_map/ppermute | solution.py:32
  163.2 1.0 copy.170
  164.2 1.0 copy.169
  (116 shorter events, 13.2 us)
Async XLA Ops:
  0.6 25.5 %copy-start = (f32[2,8]{1,0:T(2,128)S(1)}, f32[2,8]{1,0:T(2,128)}, u32[]{:S(2)}) copy-start(f32[2,8]{1,0:T(2,128)} %param.12) | copy-start | bytes 196
  1.3 25.1 %collective-permute-start.5 = (s32[16,1]{0,1:T(1,128)S(1)}, s32[16,1]{0,1:T(1,128)S(1)}, u32[]{:S(2)}, u32[]{:S(2)}) collective-permute-start(s32[16,1]{0,1:T(1,128)S(1)} %slice.108), channel_id=1, source_target_pairs={{1,0},{3,2},{5,4},{7,6},{9,8},{11,10},{13,12},{15,14},{17,16},{19,... | collective-permute-start | bytes 200 | tf_op jit(solution)/shard_map/ppermute | solution.py:17
  19.4 4.7 %copy-start.5 = (bf16[16,128,128]{2,1,0:T(8,128)(2,1)S(1)}, bf16[16,128,128]{2,1,0:T(8,128)(2,1)}, u32[]{:S(2)}) copy-start(bf16[16,128,128]{2,1,0:T(8,128)(2,1)} %param.7) | copy-start | bytes 1572868
  19.4 5.6 %copy-start.11 = (s32[16,4]{0,1:T(4,128)S(1)}, s32[16,4]{0,1:T(4,128)}, u32[]{:S(2)}) copy-start(s32[16,4]{0,1:T(4,128)} %param.11) | copy-start | bytes 772
  19.4 7.2 %copy-start.12 = (f32[8]{0:T(128)S(1)}, f32[8]{0:T(128)}, u32[]{:S(2)}) copy-start(f32[8]{0:T(128)} %param.13) | copy-start | bytes 100
  20.6 28.2 %all-to-all-start = ((bf16[4,4,2,128,128]{4,3,1,2,0:T(8,128)(2,1)}), bf16[4,4,2,128,128]{4,3,1,2,0:T(8,128)(2,1)S(1)}, u32[]{:S(2)}, u32[]{:S(2)}) async-start(bf16[4,4,2,128,128]{4,3,1,2,0:T(8,128)(2,1)} %copy.138), calls=%async_computation | async-start | bytes 2097152 | tf_op jit(solution)/shard_map/all_to_all | solution.py:166
  39.8 9.1 %copy-start.10 = (bf16[16,128,128]{2,1,0:T(8,128)(2,1)S(1)}, bf16[16,128,128]{2,1,0:T(8,128)(2,1)}, u32[]{:S(2)}) copy-start(bf16[16,128,128]{2,1,0:T(8,128)(2,1)} %param.8) | copy-start | bytes 1572868
  42.4 1.1 collective-permute-start.7
  54.8 2.1 %copy-start.2 = (bf16[16,4,128,128]{3,2,1,0:T(8,128)(2,1)S(1)}, bf16[16,4,128,128]{3,2,1,0:T(8,128)(2,1)}, u32[]{:S(2)}) copy-start(bf16[16,4,128,128]{3,2,1,0:T(8,128)(2,1)} %param.10) | copy-start | bytes 6291460
  54.8 2.3 %copy-start.9 = (bf16[16,2,128,128]{3,2,1,0:T(8,128)(2,1)S(1)}, bf16[16,2,128,128]{3,2,1,0:T(8,128)(2,1)}, u32[]{:S(2)}) copy-start(bf16[16,2,128,128]{3,2,1,0:T(8,128)(2,1)} %gather_fusion.1) | copy-start | bytes 3145732
  57.1 1.2 copy-start.7
  58.9 1.6 copy-start.1
  63.8 1.2 collective-permute-start.6
  65.9 1.4 copy-start.4
  68.7 32.9 %all-to-all-start.2 = ((bf16[4,4,128,128]{2,3,1,0:T(8,128)(2,1)}), bf16[4,4,128,128]{2,3,1,0:T(8,128)(2,1)S(1)}, u32[]{:S(2)}, u32[]{:S(2)}) async-start(bf16[4,4,128,128]{2,3,1,0:T(8,128)(2,1)} %bitcast.53), calls=%async_computation.2 | async-start | bytes 1048576 | tf_op jit(solution)/shard_map/all_to_all | solution.py:166
  73.8 1.1 collective-permute-start
  76.3 5.5 %collective-permute-start.1 = (f32[2]{0:T(128)S(1)}, f32[2]{0:T(128)S(1)}, u32[]{:S(2)}, u32[]{:S(2)}) collective-permute-start(f32[2]{0:T(128)S(1)} %fusion.80), channel_id=1, source_target_pairs={{0,2},{2,0},{4,6},{6,4},{1,3},{3,1},{5,7},{7,5},{8,10},{10,8},{12,... | collective-permute-start | bytes 32 | tf_op jit(solution)/shard_map/ppermute | solution.py:32
  83.1 6.0 %collective-permute-start.2 = (f32[2]{0:T(128)S(1)}, f32[2]{0:T(128)S(1)}, u32[]{:S(2)}, u32[]{:S(2)}) collective-permute-start(f32[2]{0:T(128)S(1)} %fusion.81), channel_id=1, source_target_pairs={{0,4},{2,6},{4,0},{6,2},{1,5},{3,7},{5,1},{7,3},{8,12},{10,14},{12... | collective-permute-start | bytes 32 | tf_op jit(solution)/shard_map/ppermute | solution.py:32
  89.1 3.5 %collective-permute-start.3 = (f32[2]{0:T(128)S(1)}, f32[2]{0:T(128)S(1)}, u32[]{:S(2)}, u32[]{:S(2)}) collective-permute-start(f32[2]{0:T(128)S(1)} %add.219), channel_id=1, source_target_pairs={{0,8},{8,0},{16,24},{24,16},{1,9},{9,1},{17,25},{25,17},{2,10},{10... | collective-permute-start | bytes 32 | tf_op jit(solution)/shard_map/ppermute | solution.py:32
  92.7 3.5 %collective-permute-start.4 = (f32[2]{0:T(128)S(1)}, f32[2]{0:T(128)S(1)}, u32[]{:S(2)}, u32[]{:S(2)}) collective-permute-start(f32[2]{0:T(128)S(1)} %add.220), channel_id=1, source_target_pairs={{0,16},{8,24},{16,0},{24,8},{1,17},{9,25},{17,1},{25,9},{2,18},{10... | collective-permute-start | bytes 32 | tf_op jit(solution)/shard_map/ppermute | solution.py:32
  101.7 15.3 %all-to-all-start.1 = ((bf16[4,4,128,128]{2,3,1,0:T(8,128)(2,1)}), bf16[4,4,128,128]{2,3,1,0:T(8,128)(2,1)}, u32[]{:S(2)}, u32[]{:S(2)}) async-start(bf16[4,4,128,128]{2,3,1,0:T(8,128)(2,1)} %bitcast.50), calls=%async_computation.1 | async-start | bytes 1048576 | tf_op jit(solution)/shard_map/all_to_all | solution.py:166
  131.9 2.1 %copy-start.3 = (bf16[16,4,128,128]{3,2,1,0:T(8,128)(2,1)S(1)}, bf16[16,4,128,128]{3,2,1,0:T(8,128)(2,1)}, u32[]{:S(2)}) copy-start(bf16[16,4,128,128]{3,2,1,0:T(8,128)(2,1)} %param.10) | copy-start | bytes 6291460
  131.9 2.3 %copy-start.8 = (bf16[16,2,128,128]{2,3,1,0:T(8,128)(2,1)S(1)}, bf16[16,2,128,128]{2,3,1,0:T(8,128)(2,1)}, u32[]{:S(2)}) copy-start(bf16[16,2,128,128]{2,3,1,0:T(8,128)(2,1)} %gather_fusion.8) | copy-start | bytes 3145732
  134.2 1.2 copy-start.6
  138.7 1.1 collective-permute-start.8
  144.5 3.6 %collective-permute-start.9 = (f32[2]{0:T(128)S(1)}, f32[2]{0:T(128)S(1)}, u32[]{:S(2)}, u32[]{:S(2)}) collective-permute-start(f32[2]{0:T(128)S(1)} %fusion.79), channel_id=1, source_target_pairs={{0,2},{2,0},{4,6},{6,4},{1,3},{3,1},{5,7},{7,5},{8,10},{10,8},{12,... | collective-permute-start | bytes 32 | tf_op jit(solution)/shard_map/ppermute | solution.py:32
  144.6 17.5 %collective-permute-start.13 = (f32[16,2,128]{2,1,0:T(2,128)S(1)}, f32[16,2,128]{2,1,0:T(2,128)S(1)}, u32[]{:S(2)}, u32[]{:S(2)}) collective-permute-start(f32[16,2,128]{2,1,0:T(2,128)S(1)} %select_bitcast_fusion), channel_id=1, source_target_pairs={{0,1},{1,0},{2,3},{3,2},{4,5},{5,4},{6,7},{7,6},{8,9},{9,8},{10,11... | collective-permute-start | bytes 49160 | tf_op jit(solution)/shard_map/ppermute | solution.py:21
  148.1 4.4 %collective-permute-start.10 = (f32[2]{0:T(128)S(1)}, f32[2]{0:T(128)S(1)}, u32[]{:S(2)}, u32[]{:S(2)}) collective-permute-start(f32[2]{0:T(128)S(1)} %add.236), channel_id=1, source_target_pairs={{0,4},{2,6},{4,0},{6,2},{1,5},{3,7},{5,1},{7,3},{8,12},{10,14},{12... | collective-permute-start | bytes 32 | tf_op jit(solution)/shard_map/ppermute | solution.py:32
  152.5 3.5 %collective-permute-start.11 = (f32[2]{0:T(128)S(1)}, f32[2]{0:T(128)S(1)}, u32[]{:S(2)}, u32[]{:S(2)}) collective-permute-start(f32[2]{0:T(128)S(1)} %add.237), channel_id=1, source_target_pairs={{0,8},{8,0},{16,24},{24,16},{1,9},{9,1},{17,25},{25,17},{2,10},{10... | collective-permute-start | bytes 32 | tf_op jit(solution)/shard_map/ppermute | solution.py:32
  156.1 3.5 %collective-permute-start.12 = (f32[2]{0:T(128)S(1)}, f32[2]{0:T(128)S(1)}, u32[]{:S(2)}, u32[]{:S(2)}) collective-permute-start(f32[2]{0:T(128)S(1)} %add.238), channel_id=1, source_target_pairs={{0,16},{8,24},{16,0},{24,8},{1,17},{9,25},{17,1},{25,9},{2,18},{10... | collective-permute-start | bytes 32 | tf_op jit(solution)/shard_map/ppermute | solution.py:32
